TPU v7x, 32 devices: a whole 2x2x4 slice. The times are simulated.
32 devices in a mesh: ctx: 4 (over y, core), ep: 8 (over z, x).
Axes of the slice: x: 2, y: 2, z: 4, core: 2. Of those that a mesh axis runs over, the one named last changes fastest.
Arguments:
- tokens: bfloat16 [1024, 3584], P('ep', 'ctx'), may hold values from -6 to 6
- cotangent: bfloat16 [1024, 3584], P('ep', 'ctx'), may hold values from -0.8984375 to 0.8984375
- expert_ids: int32 [1024, 1], P('ep'), may hold values from 0 to 7; in each aligned block of 128 rows (0 to 127, 128 to 255, ...) at most 24 rows name the same one
- route_gates: float32 [1024, 1], P('ep'), may hold values from 0.1 to 1
- w_gate: bfloat16 [8, 3584, 2048], P('ep', None, 'ctx'), may hold values from -0.125 to 0.125
- w_up: bfloat16 [8, 3584, 2048], P('ep', None, 'ctx'), may hold values from -0.09375 to 0.09375
- w_down: bfloat16 [8, 2048, 3584], P('ep', 'ctx'), may hold values from -0.1875 to 0.1875
Outputs:
- layer_out: bfloat16 [1024, 3584], P('ep', 'ctx')
- input_grad: bfloat16 [1024, 3584], P('ep', 'ctx')
- gate_grad: float32 [1024, 1], P('ep')
- w_gate_grad: bfloat16 [8, 3584, 2048], P('ep', None, 'ctx')
- w_up_grad: bfloat16 [8, 3584, 2048], P('ep', None, 'ctx')
Inputs may be any that keep to these rules, and one draw needn't show every extreme that they name: `expert_ids`: within each aligned block of 128 tokens (the tokens of one index of ep) no expert is named more than 24 times, a bound that some block reaches; the routes of one token name different experts.
All inputs are finite; a program needn't handle non-finite values.
Results may differ from a plain program's by a relative error of at most 0.015.
Values may be sent and summed in bfloat16 or wider, within the bound.
No kernel may reach another device: no remote copies, remote signals or barrier semaphores. Data moves between devices by JAX's collectives and lax.ppermute only.
A program may use at most 128 MiB of HBM per device.

v0:
```python
import jax
import jax.numpy as jnp
from jax import lax
from jax.sharding import PartitionSpec as P


def route_tables(expert_ids, experts, capacity):
    tok_rows, routes = expert_ids.shape
    flat_ids = expert_ids.reshape(-1)
    labels = jnp.arange(experts, dtype=jnp.int32)
    onehot = (flat_ids[:, None] == labels[None, :]).astype(jnp.int32)
    earlier = jnp.cumsum(onehot, axis=0) - onehot
    slot_rank = jnp.sum(earlier * onehot, axis=1)
    slot_ids = (flat_ids * capacity + slot_rank).reshape(tok_rows, routes)
    positions = jnp.arange(experts * capacity, dtype=jnp.int32)
    return [slot_ids[:, 0][:, None] == positions[None, :]]


def shards(tokens, cotangent, expert_ids, route_gates, w_gate, w_up, w_down):
    tok_rows, routes = expert_ids.shape
    experts = lax.axis_size("ep")
    capacity = 3 * tok_rows * routes // (2 * experts)
    slot_count = experts * capacity
    col_width = tokens.shape[1]
    route_maps = route_tables(expert_ids, experts, capacity)
    chosen = route_maps[0].astype(jnp.bfloat16)
    slot_gates = jnp.sum(jnp.where(route_maps[0], route_gates[:, 0][:, None], 0.0), axis=0)
    slot_gates = slot_gates.reshape(experts, capacity)

    def place_rows(values):
        placed = jnp.einsum("ts,tc->sc", chosen, values, preferred_element_type=jnp.float32)
        return placed.astype(jnp.bfloat16).reshape(experts, capacity, values.shape[1])

    sent_inputs = place_rows(tokens)
    sent_grads = place_rows(cotangent)
    got_inputs, got_grads, got_gates = (
        lax.all_to_all(sent_inputs, "ep", split_axis=0, concat_axis=0, tiled=True),
        lax.all_to_all(sent_grads, "ep", split_axis=0, concat_axis=0, tiled=True),
        lax.all_to_all(
            slot_gates.astype(jnp.bfloat16), "ep", split_axis=0, concat_axis=0, tiled=True
        ).astype(slot_gates.dtype),
    )
    slot_inputs, slot_grads = (
        lax.all_gather(got_inputs, "ctx", axis=2, tiled=True),
        lax.all_gather(got_grads, "ctx", axis=2, tiled=True),
    )
    width = slot_inputs.shape[2]
    rows_in = slot_inputs.reshape(slot_count, width)
    grads_in = slot_grads.reshape(slot_count, width)
    gate_column = got_gates.reshape(slot_count, 1)
    gate_w = w_gate[0]
    up_w = w_up[0]
    down_w = w_down[0]
    pre_gate = jnp.dot(rows_in, gate_w, preferred_element_type=jnp.float32)
    pre_up = jnp.dot(rows_in, up_w, preferred_element_type=jnp.float32)
    sigma = jax.nn.sigmoid(pre_gate)
    activated = pre_gate * sigma
    hidden = (activated * pre_up).astype(jnp.bfloat16)
    partial_out = jnp.dot(hidden, down_w, preferred_element_type=jnp.float32).reshape(
        experts, capacity, width
    )
    expert_out = lax.psum_scatter(
        partial_out.astype(jnp.bfloat16), "ctx", scatter_dimension=2, tiled=True
    )
    contract_last = (((1,), (1,)), ((), ()))
    hidden_grad = gate_column * lax.dot_general(
        grads_in, down_w, contract_last, preferred_element_type=jnp.float32
    )
    grad_gate = (hidden_grad * pre_up * sigma * (1.0 + pre_gate * (1.0 - sigma))).astype(
        jnp.bfloat16
    )
    grad_up = (hidden_grad * activated).astype(jnp.bfloat16)
    contract_first = (((0,), (0,)), ((), ()))
    w_gate_grad = lax.dot_general(
        rows_in, grad_gate, contract_first, preferred_element_type=jnp.float32
    ).astype(jnp.bfloat16)[None]
    w_up_grad = lax.dot_general(
        rows_in, grad_up, contract_first, preferred_element_type=jnp.float32
    ).astype(jnp.bfloat16)[None]
    back_out = lax.all_to_all(expert_out, "ep", split_axis=0, concat_axis=0, tiled=True)
    back_terms = lax.dot_general(
        grad_gate, gate_w, contract_last, preferred_element_type=jnp.float32
    )
    back_terms = back_terms + lax.dot_general(
        grad_up, up_w, contract_last, preferred_element_type=jnp.float32
    )
    summed = lax.psum_scatter(
        back_terms.reshape(experts, capacity, width).astype(jnp.bfloat16),
        "ctx",
        scatter_dimension=2,
        tiled=True,
    )
    back_grad = lax.all_to_all(summed, "ep", split_axis=0, concat_axis=0, tiled=True)
    out_rows = back_out.reshape(slot_count, col_width)
    grad_rows = back_grad.reshape(slot_count, col_width)
    cotangent_wide = cotangent.astype(jnp.float32)
    route_matrix = route_maps[0].astype(jnp.bfloat16)
    picked = jnp.dot(route_matrix, out_rows, preferred_element_type=jnp.float32)
    layer_out = route_gates[:, 0][:, None] * picked
    gate_terms = [jnp.sum(picked * cotangent_wide, axis=1)]
    input_grad = jnp.dot(route_matrix, grad_rows, preferred_element_type=jnp.float32)
    gate_grad = lax.psum(jnp.stack(gate_terms, axis=1), "ctx")
    return (
        layer_out.astype(jnp.bfloat16),
        input_grad.astype(jnp.bfloat16),
        gate_grad,
        w_gate_grad,
        w_up_grad,
    )


def solution(mesh):
    in_specs = (
        P("ep", "ctx"),
        P("ep", "ctx"),
        P("ep", None),
        P("ep", None),
        P("ep", None, "ctx"),
        P("ep", None, "ctx"),
        P("ep", "ctx", None),
    )
    out_specs = (
        P("ep", "ctx"),
        P("ep", "ctx"),
        P("ep", None),
        P("ep", None, "ctx"),
        P("ep", None, "ctx"),
    )
    return jax.shard_map(shards, mesh=mesh, in_specs=in_specs, out_specs=out_specs, check_vma=False)
```

profile of v0, /device:TPU:0, one launch (start us, length us, event | category | flops | bytes accessed | tf_op | source)
XLA Modules:
  0.0 184.7 jit_solution(12868758092519926794)
XLA Ops:
  7.2 0.8 fusion.18
  8.2 0.8 select_reduce_fusion.1
  9.0 0.7 fusion.23
  10.0 18.3 %all_to_all.26 = bf16[8,24,896]{2,1,0:T(8,128)(2,1)} all-to-all(bf16[8,24,896]{2,1,0:T(8,128)(2,1)S(1)} %bitcast.69), channel_id=1, replica_groups=mesh['ctx'=4,'ep'=8] {'ep'}, dimensions={0} | all-to-all | bytes 688128 | tf_op jit(solution)/shard_map/all_to_all | solution.py:37
  28.4 1.2 convolution_convert_fusion.3
  29.6 14.0 %all_to_all.27 = bf16[8,24,896]{2,1,0:T(8,128)(2,1)} all-to-all(bf16[8,24,896]{2,1,0:T(8,128)(2,1)S(1)} %bitcast.70), channel_id=1, replica_groups=mesh['ctx'=4,'ep'=8] {'ep'}, dimensions={0} | all-to-all | bytes 688128 | tf_op jit(solution)/shard_map/all_to_all | solution.py:38
  43.9 9.3 %all_to_all.28 = bf16[8,1,24]{2,1,0:T(2,128)(2,1)S(1)} all-to-all(bf16[8,1,24]{2,1,0:T(2,128)(2,1)S(1)} %convert_element_type.86), channel_id=1, replica_groups=mesh['ctx'=4,'ep'=8] {'ep'}, dimensions={0} | all-to-all | bytes 768 | tf_op jit(solution)/shard_map/all_to_all | solution.py:39
  53.3 3.8 %fusion.11 = f32[192,512]{1,0:T(8,128)S(1)} fusion(bf16[192,3584]{1,0:T(8,128)(2,1)} %bitcast.63, bf16[1,3584,512]{2,1,0:T(8,128)(2,1)} %param.11), kind=kOutput, calls=%fused_computation.15 | convolution fusion | flops 704643072 | bytes 5439488 | tf_op jit(solution)/shard_map/dot_general | solution.py:54
  57.6 0.9 fusion.7
  58.4 7.3 %all-gather.5.cloned.1.call-done = bf16[8,24,3584]{2,1,0:T(8,128)(2,1)} async-done(((bf16[8,24,896]{2,1,0:T(8,128)(2,1)}), bf16[8,24,3584]{2,1,0:T(8,128)(2,1)}) %all-gather.5.cloned.1.call-update) | async-done | bytes 1376272 | tf_op jit(solution)/shard_map/all_gather | solution.py:45
  65.7 4.0 %multiply_convert_fusion.1 = (bf16[192,512]{1,0:T(8,128)(2,1)S(1)}, bf16[192,512]{1,0:T(8,128)(2,1)S(1)}, bf16[192,512]{1,0:T(8,128)(2,1)S(1)}) fusion(f32[192,512]{1,0:T(8,128)S(1)} %fusion.11, f32[192,512]{1,0:T(8,128)S(1)} %fusion.7, bf16[192,3584]{1,0:T(8,128)(2,1)} %bitcast.77, bf16[1,512,3584]{2,1,0:T(8,128)(2,1)} %param.13, f32[192]{0:T(256)S(1)} %reshape.62), kind=kOutput, calls=%fused_computation.23 | convolution fusion | flops 706215936 | bytes 6423296 | tf_op jit(solution)/shard_map/dot_general | solution.py:66
  69.8 0.9 convolution_convert_fusion.2
  70.7 6.4 %copy.14 = bf16[8,24,3584]{1,0,2:T(8,128)(2,1)} copy(bf16[8,24,3584]{2,1,0:T(8,128)(2,1)S(1)} %convolution_convert_fusion.2) | data formatting | bytes 2752512
  77.1 9.6 %reshape.64 = bf16[3584,192]{1,0:T(8,128)(2,1)} reshape(bf16[3584,8,24]{2,1,0:T(8,128)(2,1)} %bitcast.59) | data formatting | bytes 2752512
  86.8 3.5 %fusion.9 = f32[192,3584]{1,0:T(8,128)S(1)} fusion(bf16[192,512]{1,0:T(8,128)(2,1)S(1)} %get-tuple-element.6, bf16[1,3584,512]{2,1,0:T(8,128)(2,1)} %param.11), kind=kOutput, calls=%fused_computation.13 | convolution fusion | flops 704643072 | bytes 6619136 | tf_op jit(solution)/shard_map/dot_general | solution.py:81
  90.4 1.3 fusion.2
  91.7 6.4 %copy.16 = bf16[8,24,3584]{1,0,2:T(8,128)(2,1)} copy(bf16[8,24,3584]{2,1,0:T(8,128)(2,1)S(1)} %bitcast.67) | data formatting | bytes 2752512
  98.1 9.6 %reshape.66 = bf16[3584,192]{1,0:T(8,128)(2,1)} reshape(bf16[3584,8,24]{2,1,0:T(8,128)(2,1)} %bitcast.60) | data formatting | bytes 2752512
  107.7 9.0 %reduce-scatter.7.cloned.1.call-done = bf16[896,192]{1,0:T(8,128)(2,1)} async-done(((bf16[3584,192]{1,0:T(8,128)(2,1)}), bf16[896,192]{1,0:T(8,128)(2,1)}) %reduce-scatter.7.cloned.1.call-update) | async-done | bytes 344080
  116.7 2.6 %reshape.65 = bf16[896,8,24]{2,1,0:T(8,128)(2,1)S(1)} reshape(bf16[896,192]{1,0:T(8,128)(2,1)} %reduce-scatter.7.cloned.1.call-done) | data formatting | bytes 688128
  119.3 2.4 %copy.15 = bf16[8,24,896]{2,1,0:T(8,128)(2,1)} copy(bf16[8,24,896]{1,0,2:T(8,128)(2,1)S(1)} %bitcast.61) | data formatting | bytes 688128
  121.6 5.5 %all-to-all-start.1 = ((bf16[8,24,896]{2,1,0:T(8,128)(2,1)}), bf16[8,24,896]{2,1,0:T(8,128)(2,1)}, u32[]{:S(2)}, u32[]{:S(2)}) async-start(bf16[8,24,896]{2,1,0:T(8,128)(2,1)} %copy.15), calls=%async_computation.1 | async-start | bytes 688128 | tf_op jit(solution)/shard_map/all_to_all | solution.py:80
  127.1 22.6 %reduce-scatter.9.cloned.1.call-done = bf16[896,192]{1,0:T(8,128)(2,1)} async-done(((bf16[3584,192]{1,0:T(8,128)(2,1)}), bf16[896,192]{1,0:T(8,128)(2,1)}) %reduce-scatter.9.cloned.1.call-update) | async-done | bytes 344080
  149.7 2.6 %reshape.67 = bf16[896,8,24]{2,1,0:T(8,128)(2,1)S(1)} reshape(bf16[896,192]{1,0:T(8,128)(2,1)} %reduce-scatter.9.cloned.1.call-done) | data formatting | bytes 688128
  152.2 2.4 %copy.17 = bf16[8,24,896]{2,1,0:T(8,128)(2,1)} copy(bf16[8,24,896]{1,0,2:T(8,128)(2,1)S(1)} %bitcast.62) | data formatting | bytes 688128
  154.6 5.5 %all-to-all-start.4 = ((bf16[8,24,896]{2,1,0:T(8,128)(2,1)}), bf16[8,24,896]{2,1,0:T(8,128)(2,1)S(1)}, u32[]{:S(2)}, u32[]{:S(2)}) async-start(bf16[8,24,896]{2,1,0:T(8,128)(2,1)} %copy.17), calls=%async_computation.4 | async-start | bytes 688128 | tf_op jit(solution)/shard_map/all_to_all | solution.py:93
  160.1 4.0 %fusion = bf16[1,3584,512]{2,1,0:T(8,128)(2,1)} fusion(bf16[192,3584]{1,0:T(8,128)(2,1)S(1)} %bitcast.65, bf16[192,512]{1,0:T(8,128)(2,1)} %copy-done.6), kind=kOutput, calls=%fused_computation.2 | convolution fusion | flops 706478080 | bytes 5242880 | tf_op jit(solution)/shard_map/dot_general | solution.py:74
  164.1 3.0 %fusion.1 = bf16[1,3584,512]{2,1,0:T(8,128)(2,1)} fusion(bf16[192,3584]{1,0:T(8,128)(2,1)S(1)} %bitcast.66, bf16[192,512]{1,0:T(8,128)(2,1)S(1)} %copy-done.8), kind=kOutput, calls=%fused_computation.3 | convolution fusion | flops 706478080 | bytes 5242880 | tf_op jit(solution)/shard_map/dot_general | solution.py:77
  167.1 2.0 %multiply_reduce_fusion = (f32[128]{0:T(128)S(1)}, bf16[128,896]{1,0:T(8,128)(2,1)}) fusion(bf16[128,896]{1,0:T(8,128)(2,1)S(1)} %copy-done.5, f32[128]{0:T(128)S(1)} %bitcast.75, bf16[192,896]{1,0:T(8,128)(2,1)} %bitcast.11, s32[128]{0:T(128)S(1)} %fusion.23), kind=kOutput, calls=%fused_computation.21 | convolution fusion | flops 44638080 | bytes 804352 | tf_op jit(solution)/shard_map/dot_general | solution.py:98
  169.1 1.6 all-to-all-done.4
  170.8 1.0 convolution_convert_fusion.5
  171.7 6.4 %psum.7 = f32[128,1]{0,1:T(1,128)} all-reduce(f32[128,1]{0,1:T(1,128)S(1)} %bitcast.76), channel_id=1, replica_groups=mesh['ctx'=4,'ep'=8] {'ctx'}, use_global_device_ids=true, to_apply=%region_6.7 | all-reduce | flops 128 | bytes 1024 | tf_op jit(solution)/shard_map/psum | solution.py:102
  (36 shorter events, 1.5 us)
Async XLA Ops:
  7.2 2.5 %copy-start = (bf16[128,896]{1,0:T(8,128)(2,1)S(1)}, bf16[128,896]{1,0:T(8,128)(2,1)}, u32[]{:S(2)}) copy-start(bf16[128,896]{1,0:T(8,128)(2,1)} %param.7) | copy-start | bytes 688132
  7.2 36.5 %copy-start.9 = (f32[128,1]{0,1:T(1,128)S(1)}, f32[128,1]{0,1:T(1,128)}, u32[]{:S(2)}) copy-start(f32[128,1]{0,1:T(1,128)} %param.10) | copy-start | bytes 1540
  7.2 46.1 %all-gather.3.cloned.1.call-start = ((), (), s32[]{:S(2)}) async-start(), calls=%async_computation.7 | async-start | bytes 1720320 | tf_op jit(solution)/shard_map/all_gather | solution.py:44
  28.3 37.4 %all-gather.5.cloned.1.call-start = ((), (), s32[]{:S(2)}) async-start(), calls=%async_computation.8 | async-start | bytes 1720320 | tf_op jit(solution)/shard_map/all_gather | solution.py:45
  43.7 73.0 %reduce-scatter.7.cloned.1.call-start = ((), (), s32[]{:S(2)}) async-start(), calls=%async_computation.9 | async-start | bytes 2293760
  53.3 3.9 %copy-start.1 = (bf16[1,3584,512]{2,1,0:T(8,128)(2,1)S(1)}, bf16[1,3584,512]{2,1,0:T(8,128)(2,1)}, u32[]{:S(2)}) copy-start(bf16[1,3584,512]{2,1,0:T(8,128)(2,1)} %param.12) | copy-start | bytes 11010052
  53.3 4.3 %copy-start.3 = (bf16[8,24,3584]{2,1,0:T(8,128)(2,1)S(1)}, bf16[8,24,3584]{2,1,0:T(8,128)(2,1)}, u32[]{:S(2)}) copy-start(bf16[8,24,3584]{2,1,0:T(8,128)(2,1)} %all-gather.3.cloned.1.call-done) | copy-start | bytes 4128772
  65.7 4.1 %copy-start.4 = (bf16[1,512,3584]{2,1,0:T(8,128)(2,1)S(1)}, bf16[1,512,3584]{2,1,0:T(8,128)(2,1)}, u32[]{:S(2)}) copy-start(bf16[1,512,3584]{2,1,0:T(8,128)(2,1)} %param.13) | copy-start | bytes 11010052
  69.8 17.0 %copy-start.6 = (bf16[192,512]{1,0:T(8,128)(2,1)}, bf16[192,512]{1,0:T(8,128)(2,1)S(1)}, u32[]{:S(2)}) copy-start(bf16[192,512]{1,0:T(8,128)(2,1)S(1)} %get-tuple-element.6) | copy-start | bytes 589828
  69.8 20.6 %copy-start.7 = (bf16[192,512]{1,0:T(8,128)(2,1)}, bf16[192,512]{1,0:T(8,128)(2,1)S(1)}, u32[]{:S(2)}) copy-start(bf16[192,512]{1,0:T(8,128)(2,1)S(1)} %get-tuple-element.5) | copy-start | bytes 589828
  86.7 62.9 %reduce-scatter.9.cloned.1.call-start = ((), (), s32[]{:S(2)}) async-start(), calls=%async_computation.10 | async-start | bytes 2293760
  86.8 3.6 %copy-start.2 = (bf16[1,3584,512]{2,1,0:T(8,128)(2,1)S(1)}, bf16[1,3584,512]{2,1,0:T(8,128)(2,1)}, u32[]{:S(2)}) copy-start(bf16[1,3584,512]{2,1,0:T(8,128)(2,1)} %param.12) | copy-start | bytes 11010052
  121.6 33.0 %all-to-all-start.1 = ((bf16[8,24,896]{2,1,0:T(8,128)(2,1)}), bf16[8,24,896]{2,1,0:T(8,128)(2,1)}, u32[]{:S(2)}, u32[]{:S(2)}) async-start(bf16[8,24,896]{2,1,0:T(8,128)(2,1)} %copy.15), calls=%async_computation.1 | async-start | bytes 688128 | tf_op jit(solution)/shard_map/all_to_all | solution.py:80
  154.6 16.2 %all-to-all-start.4 = ((bf16[8,24,896]{2,1,0:T(8,128)(2,1)}), bf16[8,24,896]{2,1,0:T(8,128)(2,1)S(1)}, u32[]{:S(2)}, u32[]{:S(2)}) async-start(bf16[8,24,896]{2,1,0:T(8,128)(2,1)} %copy.17), calls=%async_computation.4 | async-start | bytes 688128 | tf_op jit(solution)/shard_map/all_to_all | solution.py:93
  160.1 4.0 %copy-start.8 = (bf16[192,512]{1,0:T(8,128)(2,1)S(1)}, bf16[192,512]{1,0:T(8,128)(2,1)}, u32[]{:S(2)}) copy-start(bf16[192,512]{1,0:T(8,128)(2,1)} %copy-done.7) | copy-start | bytes 589828
  164.1 3.0 %copy-start.5 = (bf16[128,896]{1,0:T(8,128)(2,1)S(1)}, bf16[128,896]{1,0:T(8,128)(2,1)}, u32[]{:S(2)}) copy-start(bf16[128,896]{1,0:T(8,128)(2,1)} %param.8) | copy-start | bytes 688132
Sparse Core Ops, SparseCore 0:
  28.5 17.0 all-gather.2
  47.1 18.5 all-gather.4
  86.8 29.7 reduce-scatter.6
  119.8 29.8 reduce-scatter.8
where the time goes:
time: 186 us; the launch traced here: 185 us
  blocking collectives  48.1 us (26%)
  local copies, waits for them, and re-layouts  42.5 us (23%)
  waiting for transfers between devices  40.5 us (22%)
  matrix products  25.9 us (14%)
  between operations  13.9 us (7%)
  starting transfers between devices  11.2 us (6%)
  other arithmetic  2.59 us (1%)
    unnamed x28, local copies, waits for them, and re-layouts  42.3 us
    unnamed x6, waiting for transfers between devices  31.6 us
    all_to_all x1, blocking collectives, shards(): lax.all_to_all(sent_inputs, 'ep', split_axis=0, concat_axis=0, tiled=True)  18.3 us
    all_to_all x1, blocking collectives, shards(): lax.all_to_all(sent_grads, 'ep', split_axis=0, concat_axis=0, tiled=True)  14 us
    all_to_all x1, blocking collectives, shards(): lax.all_to_all(slot_gates.astype(jnp.bfloat16), 'ep', split_axis=0, conca...  9.28 us
    all_gather x1, waiting for transfers between devices, shards(): lax.all_gather(got_grads, 'ctx', axis=2, tiled=True)  7.28 us
    psum x1, blocking collectives, shards(): gate_grad = lax.psum(jnp.stack(gate_terms, axis=1), 'ctx')  6.42 us
    all_to_all x1, starting transfers between devices, shards(): lax.all_to_all(expert_out, 'ep', split_axis=0, concat_axis=0, tiled=True)  5.51 us
  transfers between devices with their start and end apart: 6, of which 4 were waited for; matrix products, arithmetic and copies ran while one was open for 25% of the time, Pallas kernels for 0%

commit v1 on v0

v1 whole, which is shorter than its diff:
```python
import jax
import jax.numpy as jnp
from jax import lax
from jax.sharding import PartitionSpec as P


def route_onehot(expert_ids, experts, capacity):
    tok_rows, routes = expert_ids.shape
    flat_ids = expert_ids.reshape(-1)
    labels = jnp.arange(experts, dtype=jnp.int32)
    onehot = (flat_ids[:, None] == labels[None, :]).astype(jnp.int32)
    earlier = jnp.cumsum(onehot, axis=0) - onehot
    slot_rank = jnp.sum(earlier * onehot, axis=1)
    slot_ids = (flat_ids * capacity + slot_rank).reshape(tok_rows, routes)
    positions = jnp.arange(experts * capacity, dtype=jnp.int32)
    return [slot_ids[:, r][:, None] == positions[None, :] for r in range(routes)]


def split_f32(values):
    hi = values.astype(jnp.bfloat16)
    lo = (values - hi.astype(jnp.float32)).astype(jnp.bfloat16)
    return hi, lo


def join_f32(hi, lo):
    return hi.astype(jnp.float32) + lo.astype(jnp.float32)


def ctx_bits(n_ctx):
    bits = n_ctx.bit_length() - 1
    assert 1 << bits == n_ctx
    return bits


def xor_pairs(n_ctx, bit):
    return [(i, i ^ (1 << bit)) for i in range(n_ctx)]


def gather_blocks(block, n_ctx, me):
    held = block[None]
    for bit in reversed(range(ctx_bits(n_ctx))):
        other = lax.ppermute(held, "ctx", xor_pairs(n_ctx, bit))
        mine_first = ((me >> bit) & 1) == 0
        pair = jnp.where(
            mine_first, jnp.stack([held, other], axis=1), jnp.stack([other, held], axis=1)
        )
        held = pair.reshape((-1,) + block.shape)
    return held


def scatter_sum(blocks, n_ctx, me):
    acc = blocks
    for bit in range(ctx_bits(n_ctx)):
        halves = acc.reshape((-1, 2) + acc.shape[1:])
        keep_first = ((me >> bit) & 1) == 0
        keep = jnp.where(keep_first, halves[:, 0], halves[:, 1])
        send = jnp.where(keep_first, halves[:, 1], halves[:, 0]).astype(jnp.bfloat16)
        got = lax.ppermute(send, "ctx", xor_pairs(n_ctx, bit))
        acc = keep + got.astype(jnp.float32)
    return acc[0]


def shards(tokens, cotangent, expert_ids, route_gates, w_gate, w_up, w_down):
    tok_rows, routes = expert_ids.shape
    experts = lax.axis_size("ep")
    n_ctx = lax.axis_size("ctx")
    me = lax.axis_index("ctx")
    capacity = 3 * tok_rows * routes // (2 * experts)
    slot_count = experts * capacity
    col_width = tokens.shape[1]
    pad = 128
    route_maps = route_onehot(expert_ids, experts, capacity)

    slot_gates = jnp.zeros((slot_count,), jnp.float32)
    placed = jnp.zeros((slot_count, 2 * col_width), jnp.float32)
    both = jnp.concatenate([tokens, cotangent], axis=1)
    for r, chosen in enumerate(route_maps):
        slot_gates = slot_gates + jnp.sum(jnp.where(chosen, route_gates[:, r][:, None], 0.0), axis=0)
        placed = placed + jnp.einsum(
            "ts,tc->sc", chosen.astype(jnp.bfloat16), both, preferred_element_type=jnp.float32
        )
    gate_hi, gate_lo = split_f32(slot_gates)
    gate_cols = jnp.zeros((slot_count, pad), jnp.bfloat16)
    gate_cols = gate_cols.at[:, 0].set(gate_hi).at[:, 1].set(gate_lo)
    sent = jnp.concatenate([placed.astype(jnp.bfloat16), gate_cols], axis=1)
    sent = sent.reshape(experts, capacity, 2 * col_width + pad)
    got = lax.all_to_all(sent, "ep", split_axis=0, concat_axis=0, tiled=True)
    got = got.reshape(slot_count, 2 * col_width + pad)
    gate_column = join_f32(got[:, 2 * col_width], got[:, 2 * col_width + 1])[:, None]

    full = gather_blocks(got[:, : 2 * col_width], n_ctx, me)
    rows_in = full[:, :, :col_width]
    grads_in = full[:, :, col_width:]

    group = w_gate.shape[2]
    gate_w = w_gate[0].reshape(n_ctx, col_width, group)
    up_w = w_up[0].reshape(n_ctx, col_width, group)
    down_w = w_down[0].reshape(group, n_ctx, col_width)

    pre_gate = jnp.einsum("nsd,ndf->sf", rows_in, gate_w, preferred_element_type=jnp.float32)
    pre_up = jnp.einsum("nsd,ndf->sf", rows_in, up_w, preferred_element_type=jnp.float32)
    sigma = jax.nn.sigmoid(pre_gate)
    activated = pre_gate * sigma
    hidden = (activated * pre_up).astype(jnp.bfloat16)
    partial_out = jnp.einsum(
        "sf,fnd->nsd", hidden, down_w, preferred_element_type=jnp.float32
    ).astype(jnp.bfloat16)
    gate_part = jnp.einsum(
        "nsd,nsd->s", partial_out.astype(jnp.float32), grads_in.astype(jnp.float32)
    )
    gate_sum = lax.psum(gate_part, "ctx")
    expert_out = scatter_sum(partial_out.astype(jnp.float32), n_ctx, me).astype(jnp.bfloat16)

    hidden_grad = gate_column * jnp.einsum(
        "nsd,fnd->sf", grads_in, down_w, preferred_element_type=jnp.float32
    )
    grad_gate = (hidden_grad * pre_up * sigma * (1.0 + pre_gate * (1.0 - sigma))).astype(
        jnp.bfloat16
    )
    grad_up = (hidden_grad * activated).astype(jnp.bfloat16)
    back_terms = jnp.einsum(
        "sf,ndf->nsd", grad_gate, gate_w, preferred_element_type=jnp.float32
    ) + jnp.einsum("sf,ndf->nsd", grad_up, up_w, preferred_element_type=jnp.float32)
    back_terms = back_terms.astype(jnp.bfloat16).astype(jnp.float32)
    slot_grad = scatter_sum(back_terms, n_ctx, me).astype(jnp.bfloat16)

    w_gate_grad = jnp.einsum(
        "nsd,sf->ndf", rows_in, grad_gate, preferred_element_type=jnp.float32
    ).astype(jnp.bfloat16).reshape(1, n_ctx * col_width, group)
    w_up_grad = jnp.einsum(
        "nsd,sf->ndf", rows_in, grad_up, preferred_element_type=jnp.float32
    ).astype(jnp.bfloat16).reshape(1, n_ctx * col_width, group)

    gg_hi, gg_lo = split_f32(gate_sum)
    gg_cols = jnp.zeros((slot_count, pad), jnp.bfloat16)
    gg_cols = gg_cols.at[:, 0].set(gg_hi).at[:, 1].set(gg_lo)
    back = jnp.concatenate([expert_out, slot_grad, gg_cols], axis=1)
    back = back.reshape(experts, capacity, 2 * col_width + pad)
    back = lax.all_to_all(back, "ep", split_axis=0, concat_axis=0, tiled=True)
    back = back.reshape(slot_count, 2 * col_width + pad)
    slot_gg = join_f32(back[:, 2 * col_width], back[:, 2 * col_width + 1])

    picked = jnp.zeros((tok_rows, 2 * col_width), jnp.float32)
    layer_out = jnp.zeros((tok_rows, col_width), jnp.float32)
    gate_terms = []
    for r, chosen in enumerate(route_maps):
        rows_r = jnp.dot(
            chosen.astype(jnp.bfloat16), back[:, : 2 * col_width], preferred_element_type=jnp.float32
        )
        layer_out = layer_out + route_gates[:, r][:, None] * rows_r[:, :col_width]
        picked = picked + rows_r
        gate_terms.append(jnp.sum(jnp.where(chosen, slot_gg[None, :], 0.0), axis=1))
    input_grad = picked[:, col_width:]
    gate_grad = jnp.stack(gate_terms, axis=1)
    return (
        layer_out.astype(jnp.bfloat16),
        input_grad.astype(jnp.bfloat16),
        gate_grad,
        w_gate_grad,
        w_up_grad,
    )


def solution(mesh):
    in_specs = (
        P("ep", "ctx"),
        P("ep", "ctx"),
        P("ep", None),
        P("ep", None),
        P("ep", None, "ctx"),
        P("ep", None, "ctx"),
        P("ep", "ctx", None),
    )
    out_specs = (
        P("ep", "ctx"),
        P("ep", "ctx"),
        P("ep", None),
        P("ep", None, "ctx"),
        P("ep", None, "ctx"),
    )
    return jax.shard_map(shards, mesh=mesh, in_specs=in_specs, out_specs=out_specs, check_vma=False)
```

time: 186 us -> 129 us (0.69)
  local copies, waits for them, and re-layouts: 42.5 us -> 16.5 us
  other arithmetic: 2.59 us -> 18.9 us
  blocking collectives: 48.1 us -> 33.4 us
  between operations: 13.9 us -> 0.96 us
  matrix products: 25.9 us -> 15.7 us
  waiting for transfers between devices: 40.5 us -> 33.9 us
  starting transfers between devices: 11.2 us -> 8.55 us
    unnamed x28 -> x26, local copies, waits for them, and re-layouts: 42.3 us -> 7.72 us
    unnamed x6 -> x0, waiting for transfers between devices: 31.6 us -> none
    ppermute x0 -> x6, waiting for transfers between devices: none -> 24 us  [the longest x2 14.5 us: gather_blocks(): other = lax.ppermute(held, 'ctx', xor_pairs(n_ctx, bit))]
    all_to_all x3 -> x1, blocking collectives: 41.7 us -> 26.2 us  [shards(): got = lax.all_to_all(sent, 'ep', split_axis=0, concat_axis=0, tiled=True)]
    dot_general x12 -> x10, matrix products: 25.9 us -> 15.7 us  [the longest x1 3.95 us: shards(): jnp.einsum('nsd,sf->ndf', rows_in, grad_up, preferred_element_type=jnp.fl...]
    all_to_all x2 -> x1, waiting for transfers between devices: 1.65 us -> 9.82 us  [shards(): back = lax.all_to_all(back, 'ep', split_axis=0, concat_axis=0, tiled=True)]
    another operation x0 -> x4, local copies, waits for them, and re-layouts: none -> 7.35 us  [the longest x1 7.25 us: shards(): down_w = w_down[0].reshape(group, n_ctx, col_width)]
    all_gather x2 -> x0, waiting for transfers between devices: 7.29 us -> none  [the longest x1 7.28 us: shards(): lax.all_gather(got_grads, 'ctx', axis=2, tiled=True)]
  transfers between devices with their start and end apart: 6 -> 7, of which waited for: 4 -> 4; matrix products, arithmetic and copies ran while one was open for 25% -> 19% of each run, Pallas kernels for 0% -> 0%
where the time goes in v1:
time: 129 us; the launch traced here: 128 us
  waiting for transfers between devices  33.9 us (26%)
  blocking collectives  33.4 us (26%)
  other arithmetic  18.9 us (15%)
  local copies, waits for them, and re-layouts  16.5 us (13%)
  matrix products  15.7 us (12%)
  starting transfers between devices  8.55 us (7%)
    all_to_all x1, blocking collectives, shards(): got = lax.all_to_all(sent, 'ep', split_axis=0, concat_axis=0, tiled=True)  26.2 us
    ppermute x2, waiting for transfers between devices, gather_blocks(): other = lax.ppermute(held, 'ctx', xor_pairs(n_ctx, bit))  14.5 us
    all_to_all x1, waiting for transfers between devices, shards(): back = lax.all_to_all(back, 'ep', split_axis=0, concat_axis=0, tiled=True)  9.82 us
    ppermute x4, waiting for transfers between devices, scatter_sum(): got = lax.ppermute(send, 'ctx', xor_pairs(n_ctx, bit))  9.55 us
    unnamed x26, local copies, waits for them, and re-layouts  7.72 us
    psum x1, blocking collectives, shards(): gate_sum = lax.psum(gate_part, 'ctx')  7.26 us
    another operation x1, local copies, waits for them, and re-layouts, shards(): down_w = w_down[0].reshape(group, n_ctx, col_width)  7.25 us
    all_to_all x1, starting transfers between devices, shards(): back = lax.all_to_all(back, 'ep', split_axis=0, concat_axis=0, tiled=True)  4.43 us
  transfers between devices with their start and end apart: 7, of which 4 were waited for; matrix products, arithmetic and copies ran while one was open for 19% of the time, Pallas kernels for 0%

profile of v1, /device:TPU:0, one launch (start us, length us, event | category | flops | bytes accessed | tf_op | source)
XLA Modules:
  0.0 128.0 jit_solution(1649686845066031923)
XLA Ops:
  5.3 1.3 %fusion.51 = (bf16[192,1]{1,0:T(8,128)(2,1)S(1)}, bf16[192,1]{1,0:T(8,128)(2,1)S(1)}) fusion(f32[192,1]{1,0:T(8,128)S(1)} %copy.46, pred[]{:T(512)} %compare_reduce_fusion, pred[]{:T(512)} %compare_reduce_fusion.1), kind=kLoop, calls=%fused_computation.77 | loop fusion | flops 1152 | bytes 1538 | tf_op jit(solution)/shard_map/select.20
  6.7 1.4 %convolution_convert_fusion = bf16[192,1792]{1,0:T(8,128)(2,1)S(1)} fusion(bf16[128,896]{1,0:T(8,128)(2,1)} %param.16, bf16[128,896]{1,0:T(8,128)(2,1)} %param.15, s32[128]{0:T(128)S(1)} %fusion.54), kind=kOutput, calls=%fused_computation.8 | convolution fusion | flops 89366528 | bytes 1147392 | tf_op jit(solution)/shard_map/ts,tc->sc/dot_general | solution.py:79
  8.3 26.2 %all_to_all.10 = bf16[8,24,1920]{2,1,0:T(8,128)(2,1)S(1)} all-to-all(bf16[8,24,1920]{2,1,0:T(8,128)(2,1)S(1)} %bitcast.154), channel_id=1, replica_groups=mesh['ctx'=4,'ep'=8] {'ep'}, dimensions={0} | all-to-all | bytes 1474560 | tf_op jit(solution)/shard_map/all_to_all | solution.py:87
  34.6 1.6 %collective-permute-start = (bf16[1,192,1792]{2,1,0:T(8,128)(2,1)S(1)}, bf16[1,192,1792]{2,1,0:T(8,128)(2,1)S(1)}, u32[]{:S(2)}, u32[]{:S(2)}) collective-permute-start(bf16[1,192,1792]{2,1,0:T(8,128)(2,1)S(1)} %get-tuple-element.56), channel_id=1, source_target_pairs={{0,16},{8,24},{16,0},{24,8},{1,17},{9,25},{17,1},{25,9},{2,18},{10... | collective-permute-start | bytes 2064392 | tf_op jit(solution)/shard_map/ppermute | solution.py:42
  36.2 14.5 %collective-permute-done = bf16[1,192,1792]{2,1,0:T(8,128)(2,1)S(1)} collective-permute-done((bf16[1,192,1792]{2,1,0:T(8,128)(2,1)S(1)}, bf16[1,192,1792]{2,1,0:T(8,128)(2,1)S(1)}, u32[]{:S(2)}, u32[]{:S(2)}) %collective-permute-start) | collective-permute-done | bytes 688160 | tf_op jit(solution)/shard_map/ppermute | solution.py:42
  50.7 1.3 %maximum_select_fusion.2 = bf16[2,192,1792]{2,1,0:T(8,128)(2,1)} fusion(bf16[1,192,1792]{2,1,0:T(8,128)(2,1)S(1)} %collective-permute-done, bf16[1,192,1792]{2,1,0:T(8,128)(2,1)S(1)} %get-tuple-element.56, pred[]{:T(512)S(6)} %eq.48), kind=kLoop, calls=%fused_computation.16 | loop fusion | flops 2064384 | bytes 2752513 | tf_op jit(solution)/shard_map/jit(_where)/select_n | solution.py:44
  52.0 7.3 %reshape_squeeze.11 = bf16[512,4,896]{2,1,0:T(4,128)(2,1)} reshape(bf16[1,512,3584]{2,1,0:T(8,128)(2,1)} %param.21) | data formatting | bytes 7340032 | tf_op jit(solution)/shard_map/reshape;squeeze | solution.py:98
  60.4 2.8 %copy-done.7 = bf16[1,3584,512]{2,1,0:T(8,128)(2,1)S(1)} copy-done((bf16[1,3584,512]{2,1,0:T(8,128)(2,1)S(1)}, bf16[1,3584,512]{2,1,0:T(8,128)(2,1)}, u32[]{:S(2)}) %copy-start.7) | copy-done | bytes 3670040
  63.2 0.9 convolution_bitcast_fusion
  64.1 1.2 copy-done.6
  66.1 1.2 copy-done.8
  67.3 1.2 fusion.4
  68.4 1.5 %fusion.45 = (bf16[192,512,1]{1,0,2:T(8,128)(2,1)S(1)}, bf16[192,512]{1,0:T(8,128)(2,1)S(1)}) fusion(f32[192,512]{1,0:T(8,128)S(1)} %convolution_bitcast_fusion.1, f32[192,512]{1,0:T(8,128)S(1)} %convolution_bitcast_fusion, bf16[512,4,896]{2,1,0:T(4,128)(2,1)S(1)} %copy-done.8, bf16[4,192,1792]{2,1,0:T(8,128)(2,1)S(1)} %bitcast.140, ...), kind=kOutput, calls=%fused_computation.64 | convolution fusion | flops 706019328 | bytes 6226944 | tf_op jit(solution)/shard_map/nsd,fnd->sf/dot_general | solution.py:114
  70.1 1.5 %copy-done = f32[2,2,192,896]{3,2,1,0:T(8,128)} copy-done((f32[2,2,192,896]{3,2,1,0:T(8,128)}, f32[2,2,192,896]{3,2,1,0:T(8,128)S(1)}, u32[]{:S(2)}) %copy-start) | copy-done | bytes 2752536
  71.6 1.0 fusion.28
  73.1 1.4 %fusion.47 = f32[192,4,896]{2,0,1:T(8,128)S(1)} fusion(bf16[4,896,512]{2,1,0:T(8,128)(2,1)S(1)} %bitcast.144, bf16[192,512]{1,0:T(8,128)(2,1)S(1)} %get-tuple-element.54), kind=kOutput, calls=%fused_computation.66 | convolution fusion | flops 704643072 | bytes 6619136 | tf_op jit(solution)/shard_map/sf,ndf->nsd/dot_general | solution.py:121
  74.5 1.3 %fusion.5 = f32[192,4,896]{2,0,1:T(8,128)S(1)} fusion(f32[192,4,896]{2,0,1:T(8,128)S(1)} %fusion.47, bf16[192,512,1]{1,0,2:T(8,128)(2,1)S(1)} %get-tuple-element.53, bf16[4,896,512]{2,1,0:T(8,128)(2,1)S(1)} %bitcast.146), kind=kOutput, calls=%fused_computation.11 | convolution fusion | flops 706707456 | bytes 9371648 | tf_op jit(solution)/shard_map/sf,ndf->nsd/dot_general | solution.py:123
  75.9 1.0 fusion.29
  76.9 7.3 %psum.7 = f32[192]{0:T(256)S(1)} all-reduce(f32[192]{0:T(256)S(1)} %get-tuple-element.61), channel_id=1, replica_groups=mesh['ctx'=4,'ep'=8] {'ctx'}, use_global_device_ids=true, to_apply=%region_5.6 | all-reduce | flops 192 | bytes 1536 | tf_op jit(solution)/shard_map/psum | solution.py:111
  84.2 2.1 %fusion.11 = f32[1,2,192,896]{3,2,1,0:T(8,128)S(1)} fusion(bf16[2,192,896]{2,1,0:T(8,128)(2,1)} %collective-permute-done.2, f32[2,2,192,896]{3,2,1,0:T(8,128)} %copy-done, pred[]{:T(512)S(6)} %eq.49), kind=kLoop, calls=%fused_computation.20 | loop fusion | flops 1032192 | bytes 4816897 | tf_op jit(solution)/shard_map/reshape | solution.py:54
  86.3 0.9 fusion.39
  88.0 1.0 copy-done.4
  89.0 1.5 %collective-permute-start.5 = (bf16[1,192,896]{2,1,0:T(8,128)(2,1)S(1)}, bf16[1,192,896]{2,1,0:T(8,128)(2,1)S(1)}, u32[]{:S(2)}, u32[]{:S(2)}) collective-permute-start(bf16[1,192,896]{2,1,0:T(8,128)(2,1)S(1)} %fusion.40), channel_id=1, source_target_pairs={{0,16},{8,24},{16,0},{24,8},{1,17},{9,25},{17,1},{25,9},{2,18},{10... | collective-permute-start | bytes 1032200 | tf_op jit(solution)/shard_map/ppermute | solution.py:58
  90.5 1.3 %broadcast_select_fusion.1 = (bf16[192]{0:T(256)(128)(2,1)S(1)}, bf16[192]{0:T(256)(128)(2,1)S(1)}) fusion(pred[]{:T(512)} %compare_reduce_fusion, f32[192]{0:T(256)S(1)} %psum.7, pred[]{:T(512)} %compare_reduce_fusion.1), kind=kLoop, calls=%fused_computation.84 | loop fusion | flops 1152 | bytes 1538 | tf_op jit(solution)/shard_map/select.14
  92.0 6.5 %collective-permute-done.3 = bf16[1,192,896]{2,1,0:T(8,128)(2,1)} collective-permute-done((bf16[1,192,896]{2,1,0:T(8,128)(2,1)}, bf16[1,192,896]{2,1,0:T(8,128)(2,1)}, u32[]{:S(2)}, u32[]{:S(2)}) %collective-permute-start.3) | collective-permute-done | bytes 344096 | tf_op jit(solution)/shard_map/ppermute | solution.py:58
  98.5 1.5 %fusion.41 = bf16[192,896]{1,0:T(8,128)(2,1)S(1)} fusion(bf16[1,192,896]{2,1,0:T(8,128)(2,1)} %collective-permute-done.3, f32[1,2,192,896]{3,2,1,0:T(8,128)} %copy-done.3, pred[]{:T(512)S(6)} %eq.48), kind=kLoop, calls=%fused_computation.61 | loop fusion | flops 688128 | bytes 2064385 | tf_op jit(solution)/shard_map/convert_element_type | solution.py:112
  100.0 3.1 %collective-permute-done.5 = bf16[1,192,896]{2,1,0:T(8,128)(2,1)S(1)} collective-permute-done((bf16[1,192,896]{2,1,0:T(8,128)(2,1)S(1)}, bf16[1,192,896]{2,1,0:T(8,128)(2,1)S(1)}, u32[]{:S(2)}, u32[]{:S(2)}) %collective-permute-start.5) | collective-permute-done | bytes 344096 | tf_op jit(solution)/shard_map/ppermute | solution.py:58
  103.2 0.9 pad_maximum_fusion.1
  104.1 4.4 %all-to-all-start.1 = ((bf16[8,24,1920]{2,1,0:T(8,128)(2,1)}), bf16[8,24,1920]{2,1,0:T(8,128)(2,1)S(1)}, u32[]{:S(2)}, u32[]{:S(2)}) async-start(bf16[8,24,1920]{2,1,0:T(8,128)(2,1)} %bitcast.153), calls=%async_computation.1 | async-start | bytes 1474560 | tf_op jit(solution)/shard_map/all_to_all | solution.py:139
  108.6 4.0 %convolution_convert_fusion.1 = bf16[4,896,512]{2,1,0:T(8,128)(2,1)} fusion(bf16[192,512,1]{1,0,2:T(8,128)(2,1)} %copy-done.11, bf16[4,192,1792]{2,1,0:T(8,128)(2,1)S(1)} %bitcast.141), kind=kOutput, calls=%fused_computation.9 | convolution fusion | flops 706478080 | bytes 5242880 | tf_op jit(solution)/shard_map/nsd,sf->ndf/dot_general | solution.py:130
  112.5 3.0 %convolution_convert_fusion.2 = bf16[4,896,512]{2,1,0:T(8,128)(2,1)} fusion(bf16[4,192,1792]{2,1,0:T(8,128)(2,1)S(1)} %bitcast.142, bf16[192,512]{1,0:T(8,128)(2,1)S(1)} %copy-done.10), kind=kOutput, calls=%fused_computation.10 | convolution fusion | flops 706478080 | bytes 5242880 | tf_op jit(solution)/shard_map/nsd,sf->ndf/dot_general | solution.py:127
  115.5 9.8 %all-to-all-done.1 = bf16[8,24,1920]{2,1,0:T(8,128)(2,1)S(1)} async-done(((bf16[8,24,1920]{2,1,0:T(8,128)(2,1)}), bf16[8,24,1920]{2,1,0:T(8,128)(2,1)S(1)}, u32[]{:S(2)}, u32[]{:S(2)}) %all-to-all-start.1) | async-done | bytes 737312 | tf_op jit(solution)/shard_map/all_to_all | solution.py:139
  (59 shorter events, 11.3 us)
Async XLA Ops:
  34.6 16.1 %collective-permute-start = (bf16[1,192,1792]{2,1,0:T(8,128)(2,1)S(1)}, bf16[1,192,1792]{2,1,0:T(8,128)(2,1)S(1)}, u32[]{:S(2)}, u32[]{:S(2)}) collective-permute-start(bf16[1,192,1792]{2,1,0:T(8,128)(2,1)S(1)} %get-tuple-element.56), channel_id=1, source_target_pairs={{0,16},{8,24},{16,0},{24,8},{1,17},{9,25},{17,1},{25,9},{2,18},{10... | collective-permute-start | bytes 2064392 | tf_op jit(solution)/shard_map/ppermute | solution.py:42
  52.0 7.7 %collective-permute-start.1 = (bf16[2,192,1792]{2,1,0:T(8,128)(2,1)}, bf16[2,192,1792]{2,1,0:T(8,128)(2,1)S(1)}, u32[]{:S(2)}, u32[]{:S(2)}) collective-permute-start(bf16[2,192,1792]{2,1,0:T(8,128)(2,1)} %maximum_select_fusion.2), channel_id=1, source_target_pairs={{0,8},{8,0},{16,24},{24,16},{1,9},{9,1},{17,25},{25,17},{2,10},{10... | collective-permute-start | bytes 4128776 | tf_op jit(solution)/shard_map/ppermute | solution.py:42
  60.2 3.0 %copy-start.7 = (bf16[1,3584,512]{2,1,0:T(8,128)(2,1)S(1)}, bf16[1,3584,512]{2,1,0:T(8,128)(2,1)}, u32[]{:S(2)}) copy-start(bf16[1,3584,512]{2,1,0:T(8,128)(2,1)} %param.20) | copy-start | bytes 11010052
  60.4 8.1 %copy-start.1 = (bf16[2,2,192,1792]{3,2,1,0:T(8,128)(2,1)}, bf16[2,2,192,1792]{3,2,1,0:T(8,128)(2,1)S(1)}, u32[]{:S(2)}) copy-start(bf16[2,2,192,1792]{3,2,1,0:T(8,128)(2,1)S(1)} %copy.48) | copy-start | bytes 8257540
  63.2 2.0 %copy-start.6 = (bf16[1,3584,512]{2,1,0:T(8,128)(2,1)S(1)}, bf16[1,3584,512]{2,1,0:T(8,128)(2,1)}, u32[]{:S(2)}) copy-start(bf16[1,3584,512]{2,1,0:T(8,128)(2,1)} %param.19) | copy-start | bytes 11010052
  65.2 2.0 %copy-start.8 = (bf16[512,4,896]{2,1,0:T(4,128)(2,1)S(1)}, bf16[512,4,896]{2,1,0:T(4,128)(2,1)}, u32[]{:S(2)}) copy-start(bf16[512,4,896]{2,1,0:T(4,128)(2,1)} %reshape_squeeze.11) | copy-start | bytes 11010052
  69.9 3.2 %copy-start.9 = (bf16[192,512]{1,0:T(8,128)(2,1)}, bf16[192,512]{1,0:T(8,128)(2,1)S(1)}, u32[]{:S(2)}) copy-start(bf16[192,512]{1,0:T(8,128)(2,1)S(1)} %get-tuple-element.54) | copy-start | bytes 589828
  69.9 4.6 %copy-start.11 = (bf16[192,512,1]{1,0,2:T(8,128)(2,1)}, bf16[192,512,1]{1,0,2:T(8,128)(2,1)S(1)}, u32[]{:S(2)}) copy-start(bf16[192,512,1]{1,0,2:T(8,128)(2,1)S(1)} %get-tuple-element.53) | copy-start | bytes 589828
  70.1 1.5 %copy-start = (f32[2,2,192,896]{3,2,1,0:T(8,128)}, f32[2,2,192,896]{3,2,1,0:T(8,128)S(1)}, u32[]{:S(2)}) copy-start(f32[2,2,192,896]{3,2,1,0:T(8,128)S(1)} %convert.9) | copy-start | bytes 8257540
  72.6 11.5 %collective-permute-start.2 = (bf16[2,192,896]{2,1,0:T(8,128)(2,1)}, bf16[2,192,896]{2,1,0:T(8,128)(2,1)}, u32[]{:S(2)}, u32[]{:S(2)}) collective-permute-start(bf16[2,192,896]{2,1,0:T(8,128)(2,1)} %fusion.28), channel_id=1, source_target_pairs={{0,8},{8,0},{16,24},{24,16},{1,9},{9,1},{17,25},{25,17},{2,10},{10... | collective-permute-start | bytes 2064392 | tf_op jit(solution)/shard_map/ppermute | solution.py:58
  76.9 10.8 %collective-permute-start.4 = (bf16[2,192,896]{2,1,0:T(8,128)(2,1)}, bf16[2,192,896]{2,1,0:T(8,128)(2,1)S(1)}, u32[]{:S(2)}, u32[]{:S(2)}) collective-permute-start(bf16[2,192,896]{2,1,0:T(8,128)(2,1)} %fusion.29), channel_id=1, source_target_pairs={{0,8},{8,0},{16,24},{24,16},{1,9},{9,1},{17,25},{25,17},{2,10},{10... | collective-permute-start | bytes 2064392 | tf_op jit(solution)/shard_map/ppermute | solution.py:58
  86.3 1.6 %copy-start.3 = (f32[1,2,192,896]{3,2,1,0:T(8,128)}, f32[1,2,192,896]{3,2,1,0:T(8,128)S(1)}, u32[]{:S(2)}) copy-start(f32[1,2,192,896]{3,2,1,0:T(8,128)S(1)} %fusion.11) | copy-start | bytes 4128772
  87.2 11.3 %collective-permute-start.3 = (bf16[1,192,896]{2,1,0:T(8,128)(2,1)}, bf16[1,192,896]{2,1,0:T(8,128)(2,1)}, u32[]{:S(2)}, u32[]{:S(2)}) collective-permute-start(bf16[1,192,896]{2,1,0:T(8,128)(2,1)} %fusion.39), channel_id=1, source_target_pairs={{0,16},{8,24},{16,0},{24,8},{1,17},{9,25},{17,1},{25,9},{2,18},{10... | collective-permute-start | bytes 1032200 | tf_op jit(solution)/shard_map/ppermute | solution.py:58
  87.9 1.1 copy-start.4
  89.0 14.1 %collective-permute-start.5 = (bf16[1,192,896]{2,1,0:T(8,128)(2,1)S(1)}, bf16[1,192,896]{2,1,0:T(8,128)(2,1)S(1)}, u32[]{:S(2)}, u32[]{:S(2)}) collective-permute-start(bf16[1,192,896]{2,1,0:T(8,128)(2,1)S(1)} %fusion.40), channel_id=1, source_target_pairs={{0,16},{8,24},{16,0},{24,8},{1,17},{9,25},{17,1},{25,9},{2,18},{10... | collective-permute-start | bytes 1032200 | tf_op jit(solution)/shard_map/ppermute | solution.py:58
  92.0 11.1 %copy-start.5 = (f32[1,2,192,896]{3,2,1,0:T(8,128)S(1)}, f32[1,2,192,896]{3,2,1,0:T(8,128)}, u32[]{:S(2)}) copy-start(f32[1,2,192,896]{3,2,1,0:T(8,128)} %copy-done.4) | copy-start | bytes 4128772
  100.0 8.5 %copy-start.2 = (bf16[2,2,192,1792]{3,2,1,0:T(8,128)(2,1)S(1)}, bf16[2,2,192,1792]{3,2,1,0:T(8,128)(2,1)}, u32[]{:S(2)}) copy-start(bf16[2,2,192,1792]{3,2,1,0:T(8,128)(2,1)} %copy-done.1) | copy-start | bytes 8257540
  104.1 21.2 %all-to-all-start.1 = ((bf16[8,24,1920]{2,1,0:T(8,128)(2,1)}), bf16[8,24,1920]{2,1,0:T(8,128)(2,1)S(1)}, u32[]{:S(2)}, u32[]{:S(2)}) async-start(bf16[8,24,1920]{2,1,0:T(8,128)(2,1)} %bitcast.153), calls=%async_computation.1 | async-start | bytes 1474560 | tf_op jit(solution)/shard_map/all_to_all | solution.py:139
  108.5 4.0 %copy-start.10 = (bf16[192,512]{1,0:T(8,128)(2,1)S(1)}, bf16[192,512]{1,0:T(8,128)(2,1)}, u32[]{:S(2)}) copy-start(bf16[192,512]{1,0:T(8,128)(2,1)} %copy-done.9) | copy-start | bytes 589828
  112.5 14.0 %copy-start.12 = (f32[128,1]{0,1:T(1,128)S(1)}, f32[128,1]{0,1:T(1,128)}, u32[]{:S(2)}) copy-start(f32[128,1]{0,1:T(1,128)} %param.18) | copy-start | bytes 1540

commit v2 on v1

--- a/solution.py
+++ b/solution.py
@@ -60,6 +60,19 @@
     return acc[0]
 
 
+def all_sum(values, n_ctx):
+    for bit in range(ctx_bits(n_ctx)):
+        values = values + lax.ppermute(values, "ctx", xor_pairs(n_ctx, bit))
+    return values
+
+
+def with_cols(rows, values, pad):
+    hi, lo = split_f32(values)
+    cols = jnp.zeros((rows.shape[0], pad), jnp.bfloat16)
+    cols = cols.at[:, 0].set(hi).at[:, 1].set(lo)
+    return jnp.concatenate([rows, cols], axis=1)
+
+
 def shards(tokens, cotangent, expert_ids, route_gates, w_gate, w_up, w_down):
     tok_rows, routes = expert_ids.shape
     experts = lax.axis_size("ep")
@@ -71,49 +84,55 @@
     pad = 128
     route_maps = route_onehot(expert_ids, experts, capacity)
 
+    def place(values):
+        placed = jnp.zeros((slot_count, values.shape[1]), jnp.float32)
+        for chosen in route_maps:
+            placed = placed + jnp.einsum(
+                "ts,tc->sc", chosen.astype(jnp.bfloat16), values, preferred_element_type=jnp.float32
+            )
+        return placed.astype(jnp.bfloat16)
+
+    def to_experts(rows):
+        sent = rows.reshape(experts, capacity, rows.shape[1])
+        got = lax.all_to_all(sent, "ep", split_axis=0, concat_axis=0, tiled=True)
+        return got.reshape(slot_count, rows.shape[1])
+
     slot_gates = jnp.zeros((slot_count,), jnp.float32)
-    placed = jnp.zeros((slot_count, 2 * col_width), jnp.float32)
-    both = jnp.concatenate([tokens, cotangent], axis=1)
     for r, chosen in enumerate(route_maps):
         slot_gates = slot_gates + jnp.sum(jnp.where(chosen, route_gates[:, r][:, None], 0.0), axis=0)
-        placed = placed + jnp.einsum(
-            "ts,tc->sc", chosen.astype(jnp.bfloat16), both, preferred_element_type=jnp.float32
-        )
-    gate_hi, gate_lo = split_f32(slot_gates)
-    gate_cols = jnp.zeros((slot_count, pad), jnp.bfloat16)
-    gate_cols = gate_cols.at[:, 0].set(gate_hi).at[:, 1].set(gate_lo)
-    sent = jnp.concatenate([placed.astype(jnp.bfloat16), gate_cols], axis=1)
-    sent = sent.reshape(experts, capacity, 2 * col_width + pad)
-    got = lax.all_to_all(sent, "ep", split_axis=0, concat_axis=0, tiled=True)
-    got = got.reshape(slot_count, 2 * col_width + pad)
-    gate_column = join_f32(got[:, 2 * col_width], got[:, 2 * col_width + 1])[:, None]
-
-    full = gather_blocks(got[:, : 2 * col_width], n_ctx, me)
-    rows_in = full[:, :, :col_width]
-    grads_in = full[:, :, col_width:]
+    got_x = to_experts(with_cols(place(tokens), slot_gates, pad))
+    gate_column = join_f32(got_x[:, col_width], got_x[:, col_width + 1])[:, None]
+    rows_in = gather_blocks(got_x[:, :col_width], n_ctx, me)
+    got_dy = to_experts(place(cotangent))
+    grads_in = gather_blocks(got_dy, n_ctx, me)
 
     group = w_gate.shape[2]
     gate_w = w_gate[0].reshape(n_ctx, col_width, group)
     up_w = w_up[0].reshape(n_ctx, col_width, group)
-    down_w = w_down[0].reshape(group, n_ctx, col_width)
+    down_w = w_down[0]
+    down_cols = [down_w[:, q * col_width : (q + 1) * col_width] for q in range(n_ctx)]
 
     pre_gate = jnp.einsum("nsd,ndf->sf", rows_in, gate_w, preferred_element_type=jnp.float32)
     pre_up = jnp.einsum("nsd,ndf->sf", rows_in, up_w, preferred_element_type=jnp.float32)
     sigma = jax.nn.sigmoid(pre_gate)
     activated = pre_gate * sigma
     hidden = (activated * pre_up).astype(jnp.bfloat16)
-    partial_out = jnp.einsum(
-        "sf,fnd->nsd", hidden, down_w, preferred_element_type=jnp.float32
+    partial_out = jnp.stack(
+        [jnp.dot(hidden, cols, preferred_element_type=jnp.float32) for cols in down_cols]
     ).astype(jnp.bfloat16)
     gate_part = jnp.einsum(
         "nsd,nsd->s", partial_out.astype(jnp.float32), grads_in.astype(jnp.float32)
     )
-    gate_sum = lax.psum(gate_part, "ctx")
     expert_out = scatter_sum(partial_out.astype(jnp.float32), n_ctx, me).astype(jnp.bfloat16)
+    gate_sum = all_sum(gate_part, n_ctx)
+    back_out = to_experts(with_cols(expert_out, gate_sum, pad))
 
-    hidden_grad = gate_column * jnp.einsum(
-        "nsd,fnd->sf", grads_in, down_w, preferred_element_type=jnp.float32
+    contract_last = (((1,), (1,)), ((), ()))
+    down_t = sum(
+        lax.dot_general(grads_in[q], down_cols[q], contract_last, preferred_element_type=jnp.float32)
+        for q in range(n_ctx)
     )
+    hidden_grad = gate_column * down_t
     grad_gate = (hidden_grad * pre_up * sigma * (1.0 + pre_gate * (1.0 - sigma))).astype(
         jnp.bfloat16
     )
@@ -123,6 +142,7 @@
     ) + jnp.einsum("sf,ndf->nsd", grad_up, up_w, preferred_element_type=jnp.float32)
     back_terms = back_terms.astype(jnp.bfloat16).astype(jnp.float32)
     slot_grad = scatter_sum(back_terms, n_ctx, me).astype(jnp.bfloat16)
+    back_grad = to_experts(slot_grad)
 
     w_gate_grad = jnp.einsum(
         "nsd,sf->ndf", rows_in, grad_gate, preferred_element_type=jnp.float32
@@ -131,26 +151,17 @@
         "nsd,sf->ndf", rows_in, grad_up, preferred_element_type=jnp.float32
     ).astype(jnp.bfloat16).reshape(1, n_ctx * col_width, group)
 
-    gg_hi, gg_lo = split_f32(gate_sum)
-    gg_cols = jnp.zeros((slot_count, pad), jnp.bfloat16)
-    gg_cols = gg_cols.at[:, 0].set(gg_hi).at[:, 1].set(gg_lo)
-    back = jnp.concatenate([expert_out, slot_grad, gg_cols], axis=1)
-    back = back.reshape(experts, capacity, 2 * col_width + pad)
-    back = lax.all_to_all(back, "ep", split_axis=0, concat_axis=0, tiled=True)
-    back = back.reshape(slot_count, 2 * col_width + pad)
-    slot_gg = join_f32(back[:, 2 * col_width], back[:, 2 * col_width + 1])
-
-    picked = jnp.zeros((tok_rows, 2 * col_width), jnp.float32)
+    slot_gg = join_f32(back_out[:, col_width], back_out[:, col_width + 1])
+    out_rows = back_out[:, :col_width]
     layer_out = jnp.zeros((tok_rows, col_width), jnp.float32)
+    input_grad = jnp.zeros((tok_rows, col_width), jnp.float32)
     gate_terms = []
     for r, chosen in enumerate(route_maps):
-        rows_r = jnp.dot(
-            chosen.astype(jnp.bfloat16), back[:, : 2 * col_width], preferred_element_type=jnp.float32
-        )
-        layer_out = layer_out + route_gates[:, r][:, None] * rows_r[:, :col_width]
-        picked = picked + rows_r
+        pick = chosen.astype(jnp.bfloat16)
+        rows_r = jnp.dot(pick, out_rows, preferred_element_type=jnp.float32)
+        layer_out = layer_out + route_gates[:, r][:, None] * rows_r
+        input_grad = input_grad + jnp.dot(pick, back_grad, preferred_element_type=jnp.float32)
         gate_terms.append(jnp.sum(jnp.where(chosen, slot_gg[None, :], 0.0), axis=1))
-    input_grad = picked[:, col_width:]
     gate_grad = jnp.stack(gate_terms, axis=1)
     return (
         layer_out.astype(jnp.bfloat16),

time: 129 us -> 107 us (0.83)
  blocking collectives: 33.4 us -> 0 us
  starting transfers between devices: 8.55 us -> 28.3 us
  local copies, waits for them, and re-layouts: 16.5 us -> 8.14 us
  other arithmetic: 18.9 us -> 15 us
  waiting for transfers between devices: 33.9 us -> 36.6 us
  matrix products: 15.7 us -> 17.1 us
    all_to_all x1 -> x0, blocking collectives: 26.2 us -> none  [shards(): got = lax.all_to_all(sent, 'ep', split_axis=0, concat_axis=0, tiled=True)]
    all_to_all x1 -> x4, starting transfers between devices: 4.43 us -> 20.4 us  [to_experts(): got = lax.all_to_all(sent, 'ep', split_axis=0, concat_axis=0, tiled=True)]
    psum x1 -> x0, blocking collectives: 7.26 us -> none  [shards(): gate_sum = lax.psum(gate_part, 'ctx')]
    another operation x3 -> x2, local copies, waits for them, and re-layouts: 7.26 us -> 0.01 us  [the longest x1 7.25 us: shards(): down_w = w_down[0].reshape(group, n_ctx, col_width)]
    unnamed x26 -> x18, local copies, waits for them, and re-layouts: 7.72 us -> 4.13 us
    scatter x5, local copies, waits for them, and re-layouts: 0.39 us -> 3.72 us  [with_cols(): cols = cols.at[:, 0].set(hi).at[:, 1].set(lo)]
    dot_general x4 -> x12, matrix products: 4.33 us -> 6.67 us  [the longest x4 1.99 us: shards(): lax.dot_general(grads_in[q], down_cols[q], contract_last, preferred_eleme...]
    all_to_all x1 -> x4, waiting for transfers between devices: 9.82 us -> 12.1 us  [to_experts(): got = lax.all_to_all(sent, 'ep', split_axis=0, concat_axis=0, tiled=True)]
  transfers between devices with their start and end apart: 7 -> 14, of which waited for: 4 -> 8; matrix products, arithmetic and copies ran while one was open for 19% -> 23% of each run, Pallas kernels for 0% -> 0%
where the time goes in v2:
time: 107 us; the launch traced here: 106 us
  waiting for transfers between devices  36.6 us (34%)
  starting transfers between devices  28.3 us (26%)
  matrix products  17.1 us (16%)
  other arithmetic  15 us (14%)
  local copies, waits for them, and re-layouts  8.14 us (8%)
    all_to_all x4, starting transfers between devices, to_experts(): got = lax.all_to_all(sent, 'ep', split_axis=0, concat_axis=0, tiled=True)  20.4 us
    ppermute x4, waiting for transfers between devices, gather_blocks(): other = lax.ppermute(held, 'ctx', xor_pairs(n_ctx, bit))  15 us
    all_to_all x4, waiting for transfers between devices, to_experts(): got = lax.all_to_all(sent, 'ep', split_axis=0, concat_axis=0, tiled=True)  12.1 us
    ppermute x4, waiting for transfers between devices, scatter_sum(): got = lax.ppermute(send, 'ctx', xor_pairs(n_ctx, bit))  7.89 us
    unnamed x18, local copies, waits for them, and re-layouts  4.13 us
    another operation x4, other arithmetic  3.89 us
    scatter x5, local copies, waits for them, and re-layouts, with_cols(): cols = cols.at[:, 0].set(hi).at[:, 1].set(lo)  3.72 us
    ppermute x4, starting transfers between devices, gather_blocks(): other = lax.ppermute(held, 'ctx', xor_pairs(n_ctx, bit))  3.17 us
  transfers between devices with their start and end apart: 14, of which 8 were waited for; matrix products, arithmetic and copies ran while one was open for 23% of the time, Pallas kernels for 0%

profile of v2, /device:TPU:0, one launch (start us, length us, event | category | flops | bytes accessed | tf_op | source)
XLA Modules:
  0.0 106.1 jit_solution(567056300602800814)
XLA Ops:
  3.1 1.0 convolution_convert_fusion.2
  4.1 7.3 %all-to-all-start.1 = ((bf16[8,24,896]{2,1,0:T(8,128)(2,1)}), bf16[8,24,896]{2,1,0:T(8,128)(2,1)S(1)}, u32[]{:S(2)}, u32[]{:S(2)}) async-start(bf16[8,24,896]{2,1,0:T(8,128)(2,1)} %bitcast.35), calls=%async_computation.1 | async-start | bytes 688128 | tf_op jit(solution)/shard_map/all_to_all | solution.py:97
  12.9 1.3 %fusion.31 = (bf16[192,1]{1,0:T(8,128)(2,1)S(1)}, bf16[192,1]{1,0:T(8,128)(2,1)S(1)}) fusion(f32[192,1]{1,0:T(8,128)S(1)} %copy.46, pred[]{:T(512)} %compare_reduce_fusion, pred[]{:T(512)} %compare_reduce_fusion.1), kind=kLoop, calls=%fused_computation.85 | loop fusion | flops 1152 | bytes 1538 | tf_op jit(solution)/shard_map/select.20
  15.5 6.5 %all-to-all-done.1 = bf16[8,24,896]{2,1,0:T(8,128)(2,1)S(1)} async-done(((bf16[8,24,896]{2,1,0:T(8,128)(2,1)}), bf16[8,24,896]{2,1,0:T(8,128)(2,1)S(1)}, u32[]{:S(2)}, u32[]{:S(2)}) %all-to-all-start.1) | async-done | bytes 344096 | tf_op jit(solution)/shard_map/all_to_all | solution.py:97
  22.0 3.6 %all-to-all-start = ((bf16[8,24,1024]{2,1,0:T(8,128)(2,1)}), bf16[8,24,1024]{2,1,0:T(8,128)(2,1)S(1)}, u32[]{:S(2)}, u32[]{:S(2)}) async-start(bf16[8,24,1024]{2,1,0:T(8,128)(2,1)} %bitcast.8), calls=%async_computation | async-start | bytes 786432 | tf_op jit(solution)/shard_map/all_to_all | solution.py:97
  25.6 1.5 %collective-permute-start.4 = (bf16[1,192,896]{2,1,0:T(8,128)(2,1)S(1)}, bf16[1,192,896]{2,1,0:T(8,128)(2,1)S(1)}, u32[]{:S(2)}, u32[]{:S(2)}) collective-permute-start(bf16[1,192,896]{2,1,0:T(8,128)(2,1)S(1)} %bitcast.179), channel_id=1, source_target_pairs={{0,16},{8,24},{16,0},{24,8},{1,17},{9,25},{17,1},{25,9},{2,18},{10... | collective-permute-start | bytes 1032200 | tf_op jit(solution)/shard_map/ppermute | solution.py:42
  27.2 7.5 %collective-permute-done.4 = bf16[1,192,896]{2,1,0:T(8,128)(2,1)S(1)} collective-permute-done((bf16[1,192,896]{2,1,0:T(8,128)(2,1)S(1)}, bf16[1,192,896]{2,1,0:T(8,128)(2,1)S(1)}, u32[]{:S(2)}, u32[]{:S(2)}) %collective-permute-start.4) | collective-permute-done | bytes 344096 | tf_op jit(solution)/shard_map/ppermute | solution.py:42
  34.7 1.0 maximum_select_fusion.4
  35.7 1.2 %all-to-all-done = bf16[8,24,1024]{2,1,0:T(8,128)(2,1)S(1)} async-done(((bf16[8,24,1024]{2,1,0:T(8,128)(2,1)}), bf16[8,24,1024]{2,1,0:T(8,128)(2,1)S(1)}, u32[]{:S(2)}, u32[]{:S(2)}) %all-to-all-start) | async-done | bytes 393248 | tf_op jit(solution)/shard_map/all_to_all | solution.py:97
  37.0 1.6 %collective-permute-start = (bf16[1,192,896]{2,1,0:T(8,128)(2,1)S(1)}, bf16[1,192,896]{2,1,0:T(8,128)(2,1)S(1)}, u32[]{:S(2)}, u32[]{:S(2)}) collective-permute-start(bf16[1,192,896]{2,1,0:T(8,128)(2,1)S(1)} %get-tuple-element.59), channel_id=1, source_target_pairs={{0,16},{8,24},{16,0},{24,8},{1,17},{9,25},{17,1},{25,9},{2,18},{10... | collective-permute-start | bytes 1032200 | tf_op jit(solution)/shard_map/ppermute | solution.py:42
  38.9 7.4 %collective-permute-done = bf16[1,192,896]{2,1,0:T(8,128)(2,1)S(1)} collective-permute-done((bf16[1,192,896]{2,1,0:T(8,128)(2,1)S(1)}, bf16[1,192,896]{2,1,0:T(8,128)(2,1)S(1)}, u32[]{:S(2)}, u32[]{:S(2)}) %collective-permute-start) | collective-permute-done | bytes 344096 | tf_op jit(solution)/shard_map/ppermute | solution.py:42
  47.0 1.6 %copy-done.3 = bf16[1,512,3584]{2,1,0:T(8,128)(2,1)S(1)} copy-done((bf16[1,512,3584]{2,1,0:T(8,128)(2,1)S(1)}, bf16[1,512,3584]{2,1,0:T(8,128)(2,1)}, u32[]{:S(2)}) %copy-start.3) | copy-done | bytes 3670040
  50.3 1.3 %copy-done.2 = bf16[1,3584,512]{2,1,0:T(8,128)(2,1)S(1)} copy-done((bf16[1,3584,512]{2,1,0:T(8,128)(2,1)S(1)}, bf16[1,3584,512]{2,1,0:T(8,128)(2,1)}, u32[]{:S(2)}) %copy-start.2) | copy-done | bytes 3670040
  52.5 1.2 %copy-done.1 = bf16[1,3584,512]{2,1,0:T(8,128)(2,1)S(1)} copy-done((bf16[1,3584,512]{2,1,0:T(8,128)(2,1)S(1)}, bf16[1,3584,512]{2,1,0:T(8,128)(2,1)}, u32[]{:S(2)}) %copy-start.1) | copy-done | bytes 3670040
  56.7 1.3 %fusion.28 = f32[192,4,896]{2,0,1:T(8,128)S(1)} fusion(bf16[4,896,512]{2,1,0:T(8,128)(2,1)S(1)} %bitcast.174, bf16[192,512]{1,0:T(8,128)(2,1)S(1)} %get-tuple-element.56), kind=kOutput, calls=%fused_computation.74 | convolution fusion | flops 704643072 | bytes 6619136 | tf_op jit(solution)/shard_map/sf,ndf->nsd/dot_general | solution.py:140
  58.1 1.3 %fusion.1 = f32[192,4,896]{2,0,1:T(8,128)S(1)} fusion(f32[192,4,896]{2,0,1:T(8,128)S(1)} %fusion.28, bf16[192,512,1]{1,0,2:T(8,128)(2,1)S(1)} %get-tuple-element.55, bf16[4,896,512]{2,1,0:T(8,128)(2,1)S(1)} %bitcast.176), kind=kOutput, calls=%fused_computation.6 | convolution fusion | flops 706707456 | bytes 9371648 | tf_op jit(solution)/shard_map/sf,ndf->nsd/dot_general | solution.py:142
  61.5 1.6 %collective-permute-done.6 = f32[192]{0:T(256)S(1)} collective-permute-done((f32[192]{0:T(256)S(1)}, f32[192]{0:T(256)S(1)}, u32[]{:S(2)}, u32[]{:S(2)}) %collective-permute-start.6) | collective-permute-done | bytes 800 | tf_op jit(solution)/shard_map/ppermute | solution.py:65
  63.1 1.5 %collective-permute-start.7 = (f32[192]{0:T(256)S(1)}, f32[192]{0:T(256)S(1)}, u32[]{:S(2)}, u32[]{:S(2)}) collective-permute-start(f32[192]{0:T(256)S(1)} %add.71), channel_id=1, source_target_pairs={{0,16},{8,24},{16,0},{24,8},{1,17},{9,25},{17,1},{25,9},{2,18},{10... | collective-permute-start | bytes 2312 | tf_op jit(solution)/shard_map/ppermute | solution.py:65
  66.5 1.5 %collective-permute-start.3 = (bf16[1,192,896]{2,1,0:T(8,128)(2,1)}, bf16[1,192,896]{2,1,0:T(8,128)(2,1)}, u32[]{:S(2)}, u32[]{:S(2)}) collective-permute-start(bf16[1,192,896]{2,1,0:T(8,128)(2,1)} %fusion.22), channel_id=1, source_target_pairs={{0,16},{8,24},{16,0},{24,8},{1,17},{9,25},{17,1},{25,9},{2,18},{10... | collective-permute-start | bytes 1032200 | tf_op jit(solution)/shard_map/ppermute | solution.py:58
  68.0 7.9 %collective-permute-done.9 = bf16[1,192,896]{2,1,0:T(8,128)(2,1)S(1)} collective-permute-done((bf16[1,192,896]{2,1,0:T(8,128)(2,1)S(1)}, bf16[1,192,896]{2,1,0:T(8,128)(2,1)S(1)}, u32[]{:S(2)}, u32[]{:S(2)}) %collective-permute-start.9) | collective-permute-done | bytes 344096 | tf_op jit(solution)/shard_map/ppermute | solution.py:58
  76.7 5.7 %all-to-all-start.3 = ((bf16[8,24,896]{2,1,0:T(8,128)(2,1)}), bf16[8,24,896]{2,1,0:T(8,128)(2,1)S(1)}, u32[]{:S(2)}, u32[]{:S(2)}) async-start(bf16[8,24,896]{2,1,0:T(8,128)(2,1)} %bitcast.187), calls=%async_computation.3 | async-start | bytes 688128 | tf_op jit(solution)/shard_map/all_to_all | solution.py:97
  82.5 1.3 %broadcast_select_fusion.1 = (bf16[192]{0:T(256)(128)(2,1)S(1)}, bf16[192]{0:T(256)(128)(2,1)S(1)}) fusion(pred[]{:T(512)} %compare_reduce_fusion, f32[192]{0:T(256)S(1)} %add.71, f32[192]{0:T(256)S(1)} %collective-permute-done.7, pred[]{:T(512)} %compare_reduce_fusion.1), kind=kLoop, calls=%fused_computation.94 | loop fusion | flops 1344 | bytes 2306 | tf_op jit(solution)/shard_map/select.14
  84.4 1.3 %scatter.19 = bf16[192,128]{0,1:T(8,128)(2,1)} dynamic-update-slice(bf16[192,128]{0,1:T(8,128)(2,1)} %scatter.16, bf16[192,1]{0,1:T(2,128)(2,1)S(1)} %reshape.472, s32[]{:T(128)} %constant.104.clone.1, s32[]{:T(128)} %constant.106.clone.1) | dynamic-update-slice | bytes 772 | tf_op jit(solution)/shard_map/scatter | solution.py:72
  85.7 1.6 %copy.55 = bf16[192,128]{1,0:T(8,128)(2,1)} copy(bf16[192,128]{0,1:T(8,128)(2,1)} %scatter.19) | data formatting | bytes 98304 | tf_op jit(solution)/shard_map/scatter | solution.py:72
  87.3 1.1 %fusion.24 = bf16[192,896]{1,0:T(8,128)(2,1)S(1)} fusion(bf16[1,192,896]{2,1,0:T(8,128)(2,1)} %collective-permute-done.3, f32[1,2,192,896]{3,2,1,0:T(8,128)S(1)} %fusion.4, pred[]{:T(512)S(6)} %eq.50), kind=kLoop, calls=%fused_computation.64 | loop fusion | flops 688128 | bytes 2064385 | tf_op jit(solution)/shard_map/convert_element_type | solution.py:126
  89.2 2.1 %all-to-all-done.3 = bf16[8,24,896]{2,1,0:T(8,128)(2,1)S(1)} async-done(((bf16[8,24,896]{2,1,0:T(8,128)(2,1)}), bf16[8,24,896]{2,1,0:T(8,128)(2,1)S(1)}, u32[]{:S(2)}, u32[]{:S(2)}) %all-to-all-start.3) | async-done | bytes 344096 | tf_op jit(solution)/shard_map/all_to_all | solution.py:97
  91.3 3.8 %all-to-all-start.2 = ((bf16[8,24,1024]{2,1,0:T(8,128)(2,1)}), bf16[8,24,1024]{2,1,0:T(8,128)(2,1)S(1)}, u32[]{:S(2)}, u32[]{:S(2)}) async-start(bf16[8,24,1024]{2,1,0:T(8,128)(2,1)} %bitcast.42), calls=%async_computation.2 | async-start | bytes 786432 | tf_op jit(solution)/shard_map/all_to_all | solution.py:97
  95.2 3.0 %convolution_convert_fusion = bf16[4,896,512]{2,1,0:T(8,128)(2,1)} fusion(bf16[4,192,896]{2,1,0:T(8,128)(2,1)S(1)} %bitcast.165, bf16[192,512,1]{1,0,2:T(8,128)(2,1)S(1)} %copy-done.5), kind=kOutput, calls=%fused_computation.4 | convolution fusion | flops 706478080 | bytes 5242880 | tf_op jit(solution)/shard_map/nsd,sf->ndf/dot_general | solution.py:150
  98.2 3.0 %convolution_convert_fusion.1 = bf16[4,896,512]{2,1,0:T(8,128)(2,1)} fusion(bf16[4,192,896]{2,1,0:T(8,128)(2,1)S(1)} %bitcast.166, bf16[192,512]{1,0:T(8,128)(2,1)S(1)} %get-tuple-element.56), kind=kOutput, calls=%fused_computation.5 | convolution fusion | flops 706478080 | bytes 5242880 | tf_op jit(solution)/shard_map/nsd,sf->ndf/dot_general | solution.py:147
  101.2 1.0 convolution_convert_fusion.4
  102.1 2.2 %all-to-all-done.2 = bf16[8,24,1024]{2,1,0:T(8,128)(2,1)S(1)} async-done(((bf16[8,24,1024]{2,1,0:T(8,128)(2,1)}), bf16[8,24,1024]{2,1,0:T(8,128)(2,1)S(1)}, u32[]{:S(2)}, u32[]{:S(2)}) %all-to-all-start.2) | async-done | bytes 393248 | tf_op jit(solution)/shard_map/all_to_all | solution.py:97
  104.5 1.0 fusion.7
  (73 shorter events, 18.8 us)
Async XLA Ops:
  0.6 2.5 %copy-start = (bf16[128,896]{1,0:T(8,128)(2,1)S(1)}, bf16[128,896]{1,0:T(8,128)(2,1)}, u32[]{:S(2)}) copy-start(bf16[128,896]{1,0:T(8,128)(2,1)} %param.16) | copy-start | bytes 688132
  0.6 10.7 %copy-start.8 = (f32[128,1]{0,1:T(1,128)S(1)}, f32[128,1]{0,1:T(1,128)}, u32[]{:S(2)}) copy-start(f32[128,1]{0,1:T(1,128)} %param.18) | copy-start | bytes 1540
  0.7 13.8 %copy-start.6 = (bf16[128,896]{1,0:T(8,128)(2,1)S(1)}, bf16[128,896]{1,0:T(8,128)(2,1)}, u32[]{:S(2)}) copy-start(bf16[128,896]{1,0:T(8,128)(2,1)} %param.15) | copy-start | bytes 688132
  4.1 17.9 %all-to-all-start.1 = ((bf16[8,24,896]{2,1,0:T(8,128)(2,1)}), bf16[8,24,896]{2,1,0:T(8,128)(2,1)S(1)}, u32[]{:S(2)}, u32[]{:S(2)}) async-start(bf16[8,24,896]{2,1,0:T(8,128)(2,1)} %bitcast.35), calls=%async_computation.1 | async-start | bytes 688128 | tf_op jit(solution)/shard_map/all_to_all | solution.py:97
  22.0 14.9 %all-to-all-start = ((bf16[8,24,1024]{2,1,0:T(8,128)(2,1)}), bf16[8,24,1024]{2,1,0:T(8,128)(2,1)S(1)}, u32[]{:S(2)}, u32[]{:S(2)}) async-start(bf16[8,24,1024]{2,1,0:T(8,128)(2,1)} %bitcast.8), calls=%async_computation | async-start | bytes 786432 | tf_op jit(solution)/shard_map/all_to_all | solution.py:97
  25.6 9.1 %collective-permute-start.4 = (bf16[1,192,896]{2,1,0:T(8,128)(2,1)S(1)}, bf16[1,192,896]{2,1,0:T(8,128)(2,1)S(1)}, u32[]{:S(2)}, u32[]{:S(2)}) collective-permute-start(bf16[1,192,896]{2,1,0:T(8,128)(2,1)S(1)} %bitcast.179), channel_id=1, source_target_pairs={{0,16},{8,24},{16,0},{24,8},{1,17},{9,25},{17,1},{25,9},{2,18},{10... | collective-permute-start | bytes 1032200 | tf_op jit(solution)/shard_map/ppermute | solution.py:42
  35.7 10.9 %collective-permute-start.5 = (bf16[2,192,896]{2,1,0:T(8,128)(2,1)}, bf16[2,192,896]{2,1,0:T(8,128)(2,1)S(1)}, u32[]{:S(2)}, u32[]{:S(2)}) collective-permute-start(bf16[2,192,896]{2,1,0:T(8,128)(2,1)} %maximum_select_fusion.4), channel_id=1, source_target_pairs={{0,8},{8,0},{16,24},{24,16},{1,9},{9,1},{17,25},{25,17},{2,10},{10... | collective-permute-start | bytes 2064392 | tf_op jit(solution)/shard_map/ppermute | solution.py:42
  37.0 9.3 %collective-permute-start = (bf16[1,192,896]{2,1,0:T(8,128)(2,1)S(1)}, bf16[1,192,896]{2,1,0:T(8,128)(2,1)S(1)}, u32[]{:S(2)}, u32[]{:S(2)}) collective-permute-start(bf16[1,192,896]{2,1,0:T(8,128)(2,1)S(1)} %get-tuple-element.59), channel_id=1, source_target_pairs={{0,16},{8,24},{16,0},{24,8},{1,17},{9,25},{17,1},{25,9},{2,18},{10... | collective-permute-start | bytes 1032200 | tf_op jit(solution)/shard_map/ppermute | solution.py:42
  46.4 3.7 %collective-permute-start.1 = (bf16[2,192,896]{2,1,0:T(8,128)(2,1)S(1)}, bf16[2,192,896]{2,1,0:T(8,128)(2,1)S(1)}, u32[]{:S(2)}, u32[]{:S(2)}) collective-permute-start(bf16[2,192,896]{2,1,0:T(8,128)(2,1)S(1)} %maximum_select_fusion.2), channel_id=1, source_target_pairs={{0,8},{8,0},{16,24},{24,16},{1,9},{9,1},{17,25},{25,17},{2,10},{10... | collective-permute-start | bytes 2064392 | tf_op jit(solution)/shard_map/ppermute | solution.py:42
  46.6 2.0 %copy-start.3 = (bf16[1,512,3584]{2,1,0:T(8,128)(2,1)S(1)}, bf16[1,512,3584]{2,1,0:T(8,128)(2,1)}, u32[]{:S(2)}) copy-start(bf16[1,512,3584]{2,1,0:T(8,128)(2,1)} %param.21) | copy-start | bytes 11010052
  49.6 2.0 %copy-start.2 = (bf16[1,3584,512]{2,1,0:T(8,128)(2,1)S(1)}, bf16[1,3584,512]{2,1,0:T(8,128)(2,1)}, u32[]{:S(2)}) copy-start(bf16[1,3584,512]{2,1,0:T(8,128)(2,1)} %param.20) | copy-start | bytes 11010052
  51.6 2.0 %copy-start.1 = (bf16[1,3584,512]{2,1,0:T(8,128)(2,1)S(1)}, bf16[1,3584,512]{2,1,0:T(8,128)(2,1)}, u32[]{:S(2)}) copy-start(bf16[1,3584,512]{2,1,0:T(8,128)(2,1)} %param.19) | copy-start | bytes 11010052
  55.2 2.9 %copy-start.4 = (bf16[192,512,1]{1,0,2:T(8,128)(2,1)}, bf16[192,512,1]{1,0,2:T(8,128)(2,1)S(1)}, u32[]{:S(2)}) copy-start(bf16[192,512,1]{1,0,2:T(8,128)(2,1)S(1)} %get-tuple-element.55) | copy-start | bytes 589828
  59.6 5.1 %collective-permute-start.8 = (bf16[2,192,896]{2,1,0:T(8,128)(2,1)S(1)}, bf16[2,192,896]{2,1,0:T(8,128)(2,1)S(1)}, u32[]{:S(2)}, u32[]{:S(2)}) collective-permute-start(bf16[2,192,896]{2,1,0:T(8,128)(2,1)S(1)} %fusion.18), channel_id=1, source_target_pairs={{0,8},{8,0},{16,24},{24,16},{1,9},{9,1},{17,25},{25,17},{2,10},{10... | collective-permute-start | bytes 2064392 | tf_op jit(solution)/shard_map/ppermute | solution.py:58
  60.9 4.6 %collective-permute-start.2 = (bf16[2,192,896]{2,1,0:T(8,128)(2,1)S(1)}, bf16[2,192,896]{2,1,0:T(8,128)(2,1)S(1)}, u32[]{:S(2)}, u32[]{:S(2)}) collective-permute-start(bf16[2,192,896]{2,1,0:T(8,128)(2,1)S(1)} %fusion.17), channel_id=1, source_target_pairs={{0,8},{8,0},{16,24},{24,16},{1,9},{9,1},{17,25},{25,17},{2,10},{10... | collective-permute-start | bytes 2064392 | tf_op jit(solution)/shard_map/ppermute | solution.py:58
  61.0 2.1 %collective-permute-start.6 = (f32[192]{0:T(256)S(1)}, f32[192]{0:T(256)S(1)}, u32[]{:S(2)}, u32[]{:S(2)}) collective-permute-start(f32[192]{0:T(256)S(1)} %get-tuple-element.53), channel_id=1, source_target_pairs={{0,8},{8,0},{16,24},{24,16},{1,9},{9,1},{17,25},{25,17},{2,10},{10... | collective-permute-start | bytes 2312 | tf_op jit(solution)/shard_map/ppermute | solution.py:65
  63.1 19.3 %collective-permute-start.7 = (f32[192]{0:T(256)S(1)}, f32[192]{0:T(256)S(1)}, u32[]{:S(2)}, u32[]{:S(2)}) collective-permute-start(f32[192]{0:T(256)S(1)} %add.71), channel_id=1, source_target_pairs={{0,16},{8,24},{16,0},{24,8},{1,17},{9,25},{17,1},{25,9},{2,18},{10... | collective-permute-start | bytes 2312 | tf_op jit(solution)/shard_map/ppermute | solution.py:65
  64.9 11.0 %collective-permute-start.9 = (bf16[1,192,896]{2,1,0:T(8,128)(2,1)S(1)}, bf16[1,192,896]{2,1,0:T(8,128)(2,1)S(1)}, u32[]{:S(2)}, u32[]{:S(2)}) collective-permute-start(bf16[1,192,896]{2,1,0:T(8,128)(2,1)S(1)} %fusion.23), channel_id=1, source_target_pairs={{0,16},{8,24},{16,0},{24,8},{1,17},{9,25},{17,1},{25,9},{2,18},{10... | collective-permute-start | bytes 1032200 | tf_op jit(solution)/shard_map/ppermute | solution.py:58
  66.5 20.8 %collective-permute-start.3 = (bf16[1,192,896]{2,1,0:T(8,128)(2,1)}, bf16[1,192,896]{2,1,0:T(8,128)(2,1)}, u32[]{:S(2)}, u32[]{:S(2)}) collective-permute-start(bf16[1,192,896]{2,1,0:T(8,128)(2,1)} %fusion.22), channel_id=1, source_target_pairs={{0,16},{8,24},{16,0},{24,8},{1,17},{9,25},{17,1},{25,9},{2,18},{10... | collective-permute-start | bytes 1032200 | tf_op jit(solution)/shard_map/ppermute | solution.py:58
  76.7 14.6 %all-to-all-start.3 = ((bf16[8,24,896]{2,1,0:T(8,128)(2,1)}), bf16[8,24,896]{2,1,0:T(8,128)(2,1)S(1)}, u32[]{:S(2)}, u32[]{:S(2)}) async-start(bf16[8,24,896]{2,1,0:T(8,128)(2,1)} %bitcast.187), calls=%async_computation.3 | async-start | bytes 688128 | tf_op jit(solution)/shard_map/all_to_all | solution.py:97
  87.3 1.1 %copy-start.7 = (bf16[192,128]{1,0:T(8,128)(2,1)S(1)}, bf16[192,128]{1,0:T(8,128)(2,1)}, u32[]{:S(2)}) copy-start(bf16[192,128]{1,0:T(8,128)(2,1)} %copy.55) | copy-start | bytes 147460
  88.4 6.8 %copy-start.5 = (bf16[192,512,1]{1,0,2:T(8,128)(2,1)S(1)}, bf16[192,512,1]{1,0,2:T(8,128)(2,1)}, u32[]{:S(2)}) copy-start(bf16[192,512,1]{1,0,2:T(8,128)(2,1)} %copy-done.4) | copy-start | bytes 589828
  91.3 13.0 %all-to-all-start.2 = ((bf16[8,24,1024]{2,1,0:T(8,128)(2,1)}), bf16[8,24,1024]{2,1,0:T(8,128)(2,1)S(1)}, u32[]{:S(2)}, u32[]{:S(2)}) async-start(bf16[8,24,1024]{2,1,0:T(8,128)(2,1)} %bitcast.42), calls=%async_computation.2 | async-start | bytes 786432 | tf_op jit(solution)/shard_map/all_to_all | solution.py:97

commit v3 on v2

--- a/solution.py
+++ b/solution.py
@@ -4,14 +4,15 @@
 from jax.sharding import PartitionSpec as P
 
 
-def route_onehot(expert_ids, experts, capacity):
+def route_onehot(expert_ids, experts, capacity, me_ep):
     tok_rows, routes = expert_ids.shape
     flat_ids = expert_ids.reshape(-1)
     labels = jnp.arange(experts, dtype=jnp.int32)
     onehot = (flat_ids[:, None] == labels[None, :]).astype(jnp.int32)
     earlier = jnp.cumsum(onehot, axis=0) - onehot
     slot_rank = jnp.sum(earlier * onehot, axis=1)
-    slot_ids = (flat_ids * capacity + slot_rank).reshape(tok_rows, routes)
+    shift = (flat_ids - me_ep) % experts
+    slot_ids = (shift * capacity + slot_rank).reshape(tok_rows, routes)
     positions = jnp.arange(experts * capacity, dtype=jnp.int32)
     return [slot_ids[:, r][:, None] == positions[None, :] for r in range(routes)]
 
@@ -68,9 +69,8 @@
 
 def with_cols(rows, values, pad):
     hi, lo = split_f32(values)
-    cols = jnp.zeros((rows.shape[0], pad), jnp.bfloat16)
-    cols = cols.at[:, 0].set(hi).at[:, 1].set(lo)
-    return jnp.concatenate([rows, cols], axis=1)
+    zeros = jnp.zeros((rows.shape[0], pad - 2), jnp.bfloat16)
+    return jnp.concatenate([rows, hi[:, None], lo[:, None], zeros], axis=1)
 
 
 def shards(tokens, cotangent, expert_ids, route_gates, w_gate, w_up, w_down):
@@ -82,7 +82,8 @@
     slot_count = experts * capacity
     col_width = tokens.shape[1]
     pad = 128
-    route_maps = route_onehot(expert_ids, experts, capacity)
+    me_ep = lax.axis_index("ep")
+    route_maps = route_onehot(expert_ids, experts, capacity, me_ep)
 
     def place(values):
         placed = jnp.zeros((slot_count, values.shape[1]), jnp.float32)
@@ -92,10 +93,19 @@
             )
         return placed.astype(jnp.bfloat16)
 
+    def exchange(rows, sign):
+        blocks = rows.reshape(experts, capacity, rows.shape[1])
+        moved = [blocks[0]]
+        for s in range(1, experts):
+            pairs = [(j, (j + sign * s) % experts) for j in range(experts)]
+            moved.append(lax.ppermute(blocks[s], "ep", pairs))
+        return jnp.stack(moved).reshape(slot_count, rows.shape[1])
+
     def to_experts(rows):
-        sent = rows.reshape(experts, capacity, rows.shape[1])
-        got = lax.all_to_all(sent, "ep", split_axis=0, concat_axis=0, tiled=True)
-        return got.reshape(slot_count, rows.shape[1])
+        return exchange(rows, 1)
+
+    def to_tokens(rows):
+        return exchange(rows, -1)
 
     slot_gates = jnp.zeros((slot_count,), jnp.float32)
     for r, chosen in enumerate(route_maps):
@@ -125,7 +135,7 @@
     )
     expert_out = scatter_sum(partial_out.astype(jnp.float32), n_ctx, me).astype(jnp.bfloat16)
     gate_sum = all_sum(gate_part, n_ctx)
-    back_out = to_experts(with_cols(expert_out, gate_sum, pad))
+    back_out = to_tokens(with_cols(expert_out, gate_sum, pad))
 
     contract_last = (((1,), (1,)), ((), ()))
     down_t = sum(
@@ -142,7 +152,7 @@
     ) + jnp.einsum("sf,ndf->nsd", grad_up, up_w, preferred_element_type=jnp.float32)
     back_terms = back_terms.astype(jnp.bfloat16).astype(jnp.float32)
     slot_grad = scatter_sum(back_terms, n_ctx, me).astype(jnp.bfloat16)
-    back_grad = to_experts(slot_grad)
+    back_grad = to_tokens(slot_grad)
 
     w_gate_grad = jnp.einsum(
         "nsd,sf->ndf", rows_in, grad_gate, preferred_element_type=jnp.float32

time: 107 us -> 171 us (1.60)
  waiting for transfers between devices: 36.6 us -> 91.8 us
  starting transfers between devices: 28.3 us -> 48.2 us
  other arithmetic: 15 us -> 7.31 us
  local copies, waits for them, and re-layouts: 8.14 us -> 6.16 us
    ppermute x0 -> x28, waiting for transfers between devices: none -> 62.7 us  [exchange(): moved.append(lax.ppermute(blocks[s], 'ep', pairs))]
    ppermute x0 -> x28, starting transfers between devices: none -> 40.4 us  [exchange(): moved.append(lax.ppermute(blocks[s], 'ep', pairs))]
    all_to_all x4 -> x0, starting transfers between devices: 20.4 us -> none  [to_experts(): got = lax.all_to_all(sent, 'ep', split_axis=0, concat_axis=0, tiled=True)]
    all_to_all x4 -> x0, waiting for transfers between devices: 12.1 us -> none  [to_experts(): got = lax.all_to_all(sent, 'ep', split_axis=0, concat_axis=0, tiled=True)]
    ppermute x4, waiting for transfers between devices: 7.89 us -> 14 us  [scatter_sum(): got = lax.ppermute(send, 'ctx', xor_pairs(n_ctx, bit))]
    another operation x4 -> x0, other arithmetic: 3.89 us -> none
    scatter x5 -> x0, local copies, waits for them, and re-layouts: 3.72 us -> none  [with_cols(): cols = cols.at[:, 0].set(hi).at[:, 1].set(lo)]
    unnamed x18 -> x41, local copies, waits for them, and re-layouts: 4.13 us -> 4.32 us
  transfers between devices with their start and end apart: 14 -> 38, of which waited for: 8 -> 20; matrix products, arithmetic and copies ran while one was open for 23% -> 10% of each run, Pallas kernels for 0% -> 0%
where the time goes in v3:
time: 171 us
  waiting for transfers between devices  91.8 us (54%)
  starting transfers between devices  48.2 us (28%)
  matrix products  16.4 us (10%)
  other arithmetic  7.31 us (4%)
  local copies, waits for them, and re-layouts  6.16 us (4%)
    ppermute x28, waiting for transfers between devices, exchange(): moved.append(lax.ppermute(blocks[s], 'ep', pairs))  62.7 us
    ppermute x28, starting transfers between devices, exchange(): moved.append(lax.ppermute(blocks[s], 'ep', pairs))  40.4 us
    ppermute x4, waiting for transfers between devices, scatter_sum(): got = lax.ppermute(send, 'ctx', xor_pairs(n_ctx, bit))  14 us
    ppermute x4, waiting for transfers between devices, gather_blocks(): other = lax.ppermute(held, 'ctx', xor_pairs(n_ctx, bit))  13.4 us
    unnamed x41, local copies, waits for them, and re-layouts  4.32 us
  transfers between devices with their start and end apart: 38, of which 20 were waited for; matrix products, arithmetic and copies ran while one was open for 10% of the time, Pallas kernels for 0%

profile of v3, /device:TPU:0, one launch (start us, length us, event | category | flops | bytes accessed | tf_op | source)
XLA Modules:
  0.0 171.1 jit_solution(2243941292559838916)
XLA Ops:
  3.4 6.0 %collective-permute-start.17 = (bf16[24,896]{1,0:T(8,128)(2,1)S(1)}, bf16[24,896]{1,0:T(8,128)(2,1)S(1)}, u32[]{:S(2)}, u32[]{:S(2)}) collective-permute-start(bf16[24,896]{1,0:T(8,128)(2,1)S(1)} %get-tuple-element.34), channel_id=1, source_target_pairs={{0,7},{1,0},{2,1},{3,2},{4,3},{5,4},{6,5},{7,6},{8,15},{9,8},{10,9... | collective-permute-start | bytes 129032 | tf_op jit(solution)/shard_map/ppermute | solution.py:101
  9.9 3.0 %collective-permute-start.14 = (bf16[24,896]{1,0:T(8,128)(2,1)S(1)}, bf16[24,896]{1,0:T(8,128)(2,1)S(1)}, u32[]{:S(2)}, u32[]{:S(2)}) collective-permute-start(bf16[24,896]{1,0:T(8,128)(2,1)S(1)} %get-tuple-element.37), channel_id=1, source_target_pairs={{0,4},{1,5},{2,6},{3,7},{4,0},{5,1},{6,2},{7,3},{8,12},{9,13},{10,... | collective-permute-start | bytes 129032 | tf_op jit(solution)/shard_map/ppermute | solution.py:101
  15.4 4.3 %collective-permute-done.11 = bf16[24,896]{1,0:T(8,128)(2,1)S(1)} collective-permute-done((bf16[24,896]{1,0:T(8,128)(2,1)S(1)}, bf16[24,896]{1,0:T(8,128)(2,1)S(1)}, u32[]{:S(2)}, u32[]{:S(2)}) %collective-permute-start.11) | collective-permute-done | bytes 43040 | tf_op jit(solution)/shard_map/ppermute | solution.py:101
  19.7 6.0 %collective-permute-done.12 = bf16[24,896]{1,0:T(8,128)(2,1)S(1)} collective-permute-done((bf16[24,896]{1,0:T(8,128)(2,1)S(1)}, bf16[24,896]{1,0:T(8,128)(2,1)S(1)}, u32[]{:S(2)}, u32[]{:S(2)}) %collective-permute-start.12) | collective-permute-done | bytes 43040 | tf_op jit(solution)/shard_map/ppermute | solution.py:101
  25.7 5.9 %collective-permute-done.13 = bf16[24,896]{1,0:T(8,128)(2,1)S(1)} collective-permute-done((bf16[24,896]{1,0:T(8,128)(2,1)S(1)}, bf16[24,896]{1,0:T(8,128)(2,1)S(1)}, u32[]{:S(2)}, u32[]{:S(2)}) %collective-permute-start.13) | collective-permute-done | bytes 43040 | tf_op jit(solution)/shard_map/ppermute | solution.py:101
  32.8 3.4 %collective-permute-start.3 = (bf16[24,1024]{1,0:T(8,128)(2,1)S(1)}, bf16[24,1024]{1,0:T(8,128)(2,1)S(1)}, u32[]{:S(2)}, u32[]{:S(2)}) collective-permute-start(bf16[24,1024]{1,0:T(8,128)(2,1)S(1)} %get-tuple-element.22), channel_id=1, source_target_pairs={{0,4},{1,5},{2,6},{3,7},{4,0},{5,1},{6,2},{7,3},{8,12},{9,13},{10,... | collective-permute-start | bytes 147464 | tf_op jit(solution)/shard_map/ppermute | solution.py:101
  36.9 6.2 %collective-permute-done = bf16[24,1024]{1,0:T(8,128)(2,1)S(1)} collective-permute-done((bf16[24,1024]{1,0:T(8,128)(2,1)S(1)}, bf16[24,1024]{1,0:T(8,128)(2,1)S(1)}, u32[]{:S(2)}, u32[]{:S(2)}) %collective-permute-start) | collective-permute-done | bytes 49184 | tf_op jit(solution)/shard_map/ppermute | solution.py:101
  43.7 5.2 %collective-permute-done.1 = bf16[24,1024]{1,0:T(8,128)(2,1)S(1)} collective-permute-done((bf16[24,1024]{1,0:T(8,128)(2,1)S(1)}, bf16[24,1024]{1,0:T(8,128)(2,1)S(1)}, u32[]{:S(2)}, u32[]{:S(2)}) %collective-permute-start.1) | collective-permute-done | bytes 49184 | tf_op jit(solution)/shard_map/ppermute | solution.py:101
  49.0 5.9 %collective-permute-done.2 = bf16[24,1024]{1,0:T(8,128)(2,1)S(1)} collective-permute-done((bf16[24,1024]{1,0:T(8,128)(2,1)S(1)}, bf16[24,1024]{1,0:T(8,128)(2,1)S(1)}, u32[]{:S(2)}, u32[]{:S(2)}) %collective-permute-start.2) | collective-permute-done | bytes 49184 | tf_op jit(solution)/shard_map/ppermute | solution.py:101
  56.5 5.6 %collective-permute-done.18 = bf16[1,192,896]{2,1,0:T(8,128)(2,1)S(1)} collective-permute-done((bf16[1,192,896]{2,1,0:T(8,128)(2,1)S(1)}, bf16[1,192,896]{2,1,0:T(8,128)(2,1)S(1)}, u32[]{:S(2)}, u32[]{:S(2)}) %collective-permute-start.18) | collective-permute-done | bytes 344096 | tf_op jit(solution)/shard_map/ppermute | solution.py:43
  66.1 7.7 %collective-permute-done.7 = bf16[1,192,896]{2,1,0:T(8,128)(2,1)S(1)} collective-permute-done((bf16[1,192,896]{2,1,0:T(8,128)(2,1)S(1)}, bf16[1,192,896]{2,1,0:T(8,128)(2,1)S(1)}, u32[]{:S(2)}, u32[]{:S(2)}) %collective-permute-start.7) | collective-permute-done | bytes 344096 | tf_op jit(solution)/shard_map/ppermute | solution.py:43
  87.1 3.0 %convolution_convert_fusion = bf16[4,896,512]{2,1,0:T(8,128)(2,1)} fusion(bf16[4,192,896]{2,1,0:T(8,128)(2,1)S(1)} %bitcast.244, bf16[192,512,1]{1,0,2:T(8,128)(2,1)S(1)} %get-tuple-element.7), kind=kOutput, calls=%fused_computation.4 | convolution fusion | flops 706478080 | bytes 5242880 | tf_op jit(solution)/shard_map/nsd,sf->ndf/dot_general | solution.py:160
  91.4 3.0 %convolution_convert_fusion.1 = bf16[4,896,512]{2,1,0:T(8,128)(2,1)} fusion(bf16[4,192,896]{2,1,0:T(8,128)(2,1)S(1)} %bitcast.245, bf16[192,512]{1,0:T(8,128)(2,1)S(1)} %get-tuple-element.8), kind=kOutput, calls=%fused_computation.5 | convolution fusion | flops 706478080 | bytes 5242880 | tf_op jit(solution)/shard_map/nsd,sf->ndf/dot_general | solution.py:157
  96.4 1.6 collective-permute-done.21
  101.0 8.6 %collective-permute-done.10 = bf16[1,192,896]{2,1,0:T(8,128)(2,1)S(1)} collective-permute-done((bf16[1,192,896]{2,1,0:T(8,128)(2,1)S(1)}, bf16[1,192,896]{2,1,0:T(8,128)(2,1)S(1)}, u32[]{:S(2)}, u32[]{:S(2)}) %collective-permute-start.10) | collective-permute-done | bytes 344096 | tf_op jit(solution)/shard_map/ppermute | solution.py:59
  109.8 5.4 %collective-permute-done.30 = bf16[1,192,896]{2,1,0:T(8,128)(2,1)S(1)} collective-permute-done((bf16[1,192,896]{2,1,0:T(8,128)(2,1)S(1)}, bf16[1,192,896]{2,1,0:T(8,128)(2,1)S(1)}, u32[]{:S(2)}, u32[]{:S(2)}) %collective-permute-start.30) | collective-permute-done | bytes 344096 | tf_op jit(solution)/shard_map/ppermute | solution.py:59
  115.5 2.0 %collective-permute-start.28 = (bf16[24,1024]{1,0:T(8,128)(2,1)S(1)}, bf16[24,1024]{1,0:T(8,128)(2,1)S(1)}, u32[]{:S(2)}, u32[]{:S(2)}) collective-permute-start(bf16[24,1024]{1,0:T(8,128)(2,1)S(1)} %get-tuple-element.10), channel_id=1, source_target_pairs={{0,1},{1,2},{2,3},{3,4},{4,5},{5,6},{6,7},{7,0},{8,9},{9,10},{10,1... | collective-permute-start | bytes 147464 | tf_op jit(solution)/shard_map/ppermute | solution.py:101
  118.6 3.2 %collective-permute-start.25 = (bf16[24,1024]{1,0:T(8,128)(2,1)S(1)}, bf16[24,1024]{1,0:T(8,128)(2,1)S(1)}, u32[]{:S(2)}, u32[]{:S(2)}) collective-permute-start(bf16[24,1024]{1,0:T(8,128)(2,1)S(1)} %get-tuple-element.13), channel_id=1, source_target_pairs={{0,4},{1,5},{2,6},{3,7},{4,0},{5,1},{6,2},{7,3},{8,12},{9,13},{10,... | collective-permute-start | bytes 147464 | tf_op jit(solution)/shard_map/ppermute | solution.py:101
  121.8 1.9 %collective-permute-start.32 = (bf16[24,896]{1,0:T(8,128)(2,1)S(1)}, bf16[24,896]{1,0:T(8,128)(2,1)S(1)}, u32[]{:S(2)}, u32[]{:S(2)}) collective-permute-start(bf16[24,896]{1,0:T(8,128)(2,1)S(1)} %get-tuple-element.31), channel_id=1, source_target_pairs={{0,6},{1,7},{2,0},{3,1},{4,2},{5,3},{6,4},{7,5},{8,14},{9,15},{10,... | collective-permute-start | bytes 129032 | tf_op jit(solution)/shard_map/ppermute | solution.py:101
  123.7 2.1 %collective-permute-done.32 = bf16[24,896]{1,0:T(8,128)(2,1)S(1)} collective-permute-done((bf16[24,896]{1,0:T(8,128)(2,1)S(1)}, bf16[24,896]{1,0:T(8,128)(2,1)S(1)}, u32[]{:S(2)}, u32[]{:S(2)}) %collective-permute-start.32) | collective-permute-done | bytes 43040 | tf_op jit(solution)/shard_map/ppermute | solution.py:101
  125.8 2.4 %collective-permute-start.33 = (bf16[24,896]{1,0:T(8,128)(2,1)S(1)}, bf16[24,896]{1,0:T(8,128)(2,1)S(1)}, u32[]{:S(2)}, u32[]{:S(2)}) collective-permute-start(bf16[24,896]{1,0:T(8,128)(2,1)S(1)} %get-tuple-element.30), channel_id=1, source_target_pairs={{0,5},{1,6},{2,7},{3,0},{4,1},{5,2},{6,3},{7,4},{8,13},{9,14},{10,... | collective-permute-start | bytes 129032 | tf_op jit(solution)/shard_map/ppermute | solution.py:101
  128.2 2.5 %collective-permute-done.33 = bf16[24,896]{1,0:T(8,128)(2,1)S(1)} collective-permute-done((bf16[24,896]{1,0:T(8,128)(2,1)S(1)}, bf16[24,896]{1,0:T(8,128)(2,1)S(1)}, u32[]{:S(2)}, u32[]{:S(2)}) %collective-permute-start.33) | collective-permute-done | bytes 43040 | tf_op jit(solution)/shard_map/ppermute | solution.py:101
  130.8 3.0 %collective-permute-start.34 = (bf16[24,896]{1,0:T(8,128)(2,1)S(1)}, bf16[24,896]{1,0:T(8,128)(2,1)S(1)}, u32[]{:S(2)}, u32[]{:S(2)}) collective-permute-start(bf16[24,896]{1,0:T(8,128)(2,1)S(1)} %get-tuple-element.29), channel_id=1, source_target_pairs={{0,4},{1,5},{2,6},{3,7},{4,0},{5,1},{6,2},{7,3},{8,12},{9,13},{10,... | collective-permute-start | bytes 129032 | tf_op jit(solution)/shard_map/ppermute | solution.py:101
  133.7 2.0 %collective-permute-done.34 = bf16[24,896]{1,0:T(8,128)(2,1)S(1)} collective-permute-done((bf16[24,896]{1,0:T(8,128)(2,1)S(1)}, bf16[24,896]{1,0:T(8,128)(2,1)S(1)}, u32[]{:S(2)}, u32[]{:S(2)}) %collective-permute-start.34) | collective-permute-done | bytes 43040 | tf_op jit(solution)/shard_map/ppermute | solution.py:101
  135.7 3.6 %collective-permute-start.35 = (bf16[24,896]{1,0:T(8,128)(2,1)S(1)}, bf16[24,896]{1,0:T(8,128)(2,1)S(1)}, u32[]{:S(2)}, u32[]{:S(2)}) collective-permute-start(bf16[24,896]{1,0:T(8,128)(2,1)S(1)} %get-tuple-element.28), channel_id=1, source_target_pairs={{0,3},{1,4},{2,5},{3,6},{4,7},{5,0},{6,1},{7,2},{8,11},{9,12},{10,... | collective-permute-start | bytes 129032 | tf_op jit(solution)/shard_map/ppermute | solution.py:101
  139.3 2.2 %collective-permute-done.35 = bf16[24,896]{1,0:T(8,128)(2,1)S(1)} collective-permute-done((bf16[24,896]{1,0:T(8,128)(2,1)S(1)}, bf16[24,896]{1,0:T(8,128)(2,1)S(1)}, u32[]{:S(2)}, u32[]{:S(2)}) %collective-permute-start.35) | collective-permute-done | bytes 43040 | tf_op jit(solution)/shard_map/ppermute | solution.py:101
  141.5 3.1 %collective-permute-start.36 = (bf16[24,896]{1,0:T(8,128)(2,1)S(1)}, bf16[24,896]{1,0:T(8,128)(2,1)S(1)}, u32[]{:S(2)}, u32[]{:S(2)}) collective-permute-start(bf16[24,896]{1,0:T(8,128)(2,1)S(1)} %get-tuple-element.27), channel_id=1, source_target_pairs={{0,2},{1,3},{2,4},{3,5},{4,6},{5,7},{6,0},{7,1},{8,10},{9,11},{10,... | collective-permute-start | bytes 129032 | tf_op jit(solution)/shard_map/ppermute | solution.py:101
  144.7 4.6 %collective-permute-done.36 = bf16[24,896]{1,0:T(8,128)(2,1)S(1)} collective-permute-done((bf16[24,896]{1,0:T(8,128)(2,1)S(1)}, bf16[24,896]{1,0:T(8,128)(2,1)S(1)}, u32[]{:S(2)}, u32[]{:S(2)}) %collective-permute-start.36) | collective-permute-done | bytes 43040 | tf_op jit(solution)/shard_map/ppermute | solution.py:101
  151.0 5.1 %collective-permute-done.37 = bf16[24,896]{1,0:T(8,128)(2,1)S(1)} collective-permute-done((bf16[24,896]{1,0:T(8,128)(2,1)S(1)}, bf16[24,896]{1,0:T(8,128)(2,1)S(1)}, u32[]{:S(2)}, u32[]{:S(2)}) %collective-permute-start.37) | collective-permute-done | bytes 43040 | tf_op jit(solution)/shard_map/ppermute | solution.py:101
  157.0 3.1 %collective-permute-done.22 = bf16[24,1024]{1,0:T(8,128)(2,1)S(1)} collective-permute-done((bf16[24,1024]{1,0:T(8,128)(2,1)S(1)}, bf16[24,1024]{1,0:T(8,128)(2,1)S(1)}, u32[]{:S(2)}, u32[]{:S(2)}) %collective-permute-start.22) | collective-permute-done | bytes 49184 | tf_op jit(solution)/shard_map/ppermute | solution.py:101
  160.4 3.9 %collective-permute-done.23 = bf16[24,1024]{1,0:T(8,128)(2,1)S(1)} collective-permute-done((bf16[24,1024]{1,0:T(8,128)(2,1)S(1)}, bf16[24,1024]{1,0:T(8,128)(2,1)S(1)}, u32[]{:S(2)}, u32[]{:S(2)}) %collective-permute-start.23) | collective-permute-done | bytes 49184 | tf_op jit(solution)/shard_map/ppermute | solution.py:101
  165.6 3.6 %collective-permute-done.24 = bf16[24,1024]{1,0:T(8,128)(2,1)S(1)} collective-permute-done((bf16[24,1024]{1,0:T(8,128)(2,1)S(1)}, bf16[24,1024]{1,0:T(8,128)(2,1)S(1)}, u32[]{:S(2)}, u32[]{:S(2)}) %collective-permute-start.24) | collective-permute-done | bytes 49184 | tf_op jit(solution)/shard_map/ppermute | solution.py:101
  (149 shorter events, 40.5 us)
Async XLA Ops:
  3.4 32.8 %collective-permute-start.17 = (bf16[24,896]{1,0:T(8,128)(2,1)S(1)}, bf16[24,896]{1,0:T(8,128)(2,1)S(1)}, u32[]{:S(2)}, u32[]{:S(2)}) collective-permute-start(bf16[24,896]{1,0:T(8,128)(2,1)S(1)} %get-tuple-element.34), channel_id=1, source_target_pairs={{0,7},{1,0},{2,1},{3,2},{4,3},{5,4},{6,5},{7,6},{8,15},{9,8},{10,9... | collective-permute-start | bytes 129032 | tf_op jit(solution)/shard_map/ppermute | solution.py:101
  9.5 23.4 %collective-permute-start.16 = (bf16[24,896]{1,0:T(8,128)(2,1)S(1)}, bf16[24,896]{1,0:T(8,128)(2,1)S(1)}, u32[]{:S(2)}, u32[]{:S(2)}) collective-permute-start(bf16[24,896]{1,0:T(8,128)(2,1)S(1)} %get-tuple-element.35), channel_id=1, source_target_pairs={{0,6},{1,7},{2,0},{3,1},{4,2},{5,3},{6,4},{7,5},{8,14},{9,15},{10,... | collective-permute-start | bytes 129032 | tf_op jit(solution)/shard_map/ppermute | solution.py:101
  9.9 22.8 %collective-permute-start.15 = (bf16[24,896]{1,0:T(8,128)(2,1)S(1)}, bf16[24,896]{1,0:T(8,128)(2,1)S(1)}, u32[]{:S(2)}, u32[]{:S(2)}) collective-permute-start(bf16[24,896]{1,0:T(8,128)(2,1)S(1)} %get-tuple-element.36), channel_id=1, source_target_pairs={{0,5},{1,6},{2,7},{3,0},{4,1},{5,2},{6,3},{7,4},{8,13},{9,14},{10,... | collective-permute-start | bytes 129032 | tf_op jit(solution)/shard_map/ppermute | solution.py:101
  9.9 21.7 %collective-permute-start.14 = (bf16[24,896]{1,0:T(8,128)(2,1)S(1)}, bf16[24,896]{1,0:T(8,128)(2,1)S(1)}, u32[]{:S(2)}, u32[]{:S(2)}) collective-permute-start(bf16[24,896]{1,0:T(8,128)(2,1)S(1)} %get-tuple-element.37), channel_id=1, source_target_pairs={{0,4},{1,5},{2,6},{3,7},{4,0},{5,1},{6,2},{7,3},{8,12},{9,13},{10,... | collective-permute-start | bytes 129032 | tf_op jit(solution)/shard_map/ppermute | solution.py:101
  12.9 6.7 %collective-permute-start.11 = (bf16[24,896]{1,0:T(8,128)(2,1)S(1)}, bf16[24,896]{1,0:T(8,128)(2,1)S(1)}, u32[]{:S(2)}, u32[]{:S(2)}) collective-permute-start(bf16[24,896]{1,0:T(8,128)(2,1)S(1)} %get-tuple-element.40), channel_id=1, source_target_pairs={{0,1},{1,2},{2,3},{3,4},{4,5},{5,6},{6,7},{7,0},{8,9},{9,10},{10,1... | collective-permute-start | bytes 129032 | tf_op jit(solution)/shard_map/ppermute | solution.py:101
  19.7 6.0 %collective-permute-start.12 = (bf16[24,896]{1,0:T(8,128)(2,1)S(1)}, bf16[24,896]{1,0:T(8,128)(2,1)S(1)}, u32[]{:S(2)}, u32[]{:S(2)}) collective-permute-start(bf16[24,896]{1,0:T(8,128)(2,1)S(1)} %get-tuple-element.39), channel_id=1, source_target_pairs={{0,2},{1,3},{2,4},{3,5},{4,6},{5,7},{6,0},{7,1},{8,10},{9,11},{10,... | collective-permute-start | bytes 129032 | tf_op jit(solution)/shard_map/ppermute | solution.py:101
  25.7 5.9 %collective-permute-start.13 = (bf16[24,896]{1,0:T(8,128)(2,1)S(1)}, bf16[24,896]{1,0:T(8,128)(2,1)S(1)}, u32[]{:S(2)}, u32[]{:S(2)}) collective-permute-start(bf16[24,896]{1,0:T(8,128)(2,1)S(1)} %get-tuple-element.38), channel_id=1, source_target_pairs={{0,3},{1,4},{2,5},{3,6},{4,7},{5,0},{6,1},{7,2},{8,11},{9,12},{10,... | collective-permute-start | bytes 129032 | tf_op jit(solution)/shard_map/ppermute | solution.py:101
  31.6 24.8 %collective-permute-start.6 = (bf16[24,1024]{1,0:T(8,128)(2,1)S(1)}, bf16[24,1024]{1,0:T(8,128)(2,1)S(1)}, u32[]{:S(2)}, u32[]{:S(2)}) collective-permute-start(bf16[24,1024]{1,0:T(8,128)(2,1)S(1)} %get-tuple-element.19), channel_id=1, source_target_pairs={{0,7},{1,0},{2,1},{3,2},{4,3},{5,4},{6,5},{7,6},{8,15},{9,8},{10,9... | collective-permute-start | bytes 147464 | tf_op jit(solution)/shard_map/ppermute | solution.py:101
  31.6 24.8 %collective-permute-start.5 = (bf16[24,1024]{1,0:T(8,128)(2,1)S(1)}, bf16[24,1024]{1,0:T(8,128)(2,1)S(1)}, u32[]{:S(2)}, u32[]{:S(2)}) collective-permute-start(bf16[24,1024]{1,0:T(8,128)(2,1)S(1)} %get-tuple-element.20), channel_id=1, source_target_pairs={{0,6},{1,7},{2,0},{3,1},{4,2},{5,3},{6,4},{7,5},{8,14},{9,15},{10,... | collective-permute-start | bytes 147464 | tf_op jit(solution)/shard_map/ppermute | solution.py:101
  32.7 23.7 %collective-permute-start.4 = (bf16[24,1024]{1,0:T(8,128)(2,1)S(1)}, bf16[24,1024]{1,0:T(8,128)(2,1)S(1)}, u32[]{:S(2)}, u32[]{:S(2)}) collective-permute-start(bf16[24,1024]{1,0:T(8,128)(2,1)S(1)} %get-tuple-element.21), channel_id=1, source_target_pairs={{0,5},{1,6},{2,7},{3,0},{4,1},{5,2},{6,3},{7,4},{8,13},{9,14},{10,... | collective-permute-start | bytes 147464 | tf_op jit(solution)/shard_map/ppermute | solution.py:101
  32.8 23.6 %collective-permute-start.3 = (bf16[24,1024]{1,0:T(8,128)(2,1)S(1)}, bf16[24,1024]{1,0:T(8,128)(2,1)S(1)}, u32[]{:S(2)}, u32[]{:S(2)}) collective-permute-start(bf16[24,1024]{1,0:T(8,128)(2,1)S(1)} %get-tuple-element.22), channel_id=1, source_target_pairs={{0,4},{1,5},{2,6},{3,7},{4,0},{5,1},{6,2},{7,3},{8,12},{9,13},{10,... | collective-permute-start | bytes 147464 | tf_op jit(solution)/shard_map/ppermute | solution.py:101
  36.2 6.8 %collective-permute-start = (bf16[24,1024]{1,0:T(8,128)(2,1)S(1)}, bf16[24,1024]{1,0:T(8,128)(2,1)S(1)}, u32[]{:S(2)}, u32[]{:S(2)}) collective-permute-start(bf16[24,1024]{1,0:T(8,128)(2,1)S(1)} %get-tuple-element.25), channel_id=1, source_target_pairs={{0,1},{1,2},{2,3},{3,4},{4,5},{5,6},{6,7},{7,0},{8,9},{9,10},{10,1... | collective-permute-start | bytes 147464 | tf_op jit(solution)/shard_map/ppermute | solution.py:101
  43.1 5.9 %collective-permute-start.1 = (bf16[24,1024]{1,0:T(8,128)(2,1)S(1)}, bf16[24,1024]{1,0:T(8,128)(2,1)S(1)}, u32[]{:S(2)}, u32[]{:S(2)}) collective-permute-start(bf16[24,1024]{1,0:T(8,128)(2,1)S(1)} %get-tuple-element.24), channel_id=1, source_target_pairs={{0,2},{1,3},{2,4},{3,5},{4,6},{5,7},{6,0},{7,1},{8,10},{9,11},{10,... | collective-permute-start | bytes 147464 | tf_op jit(solution)/shard_map/ppermute | solution.py:101
  49.0 5.9 %collective-permute-start.2 = (bf16[24,1024]{1,0:T(8,128)(2,1)S(1)}, bf16[24,1024]{1,0:T(8,128)(2,1)S(1)}, u32[]{:S(2)}, u32[]{:S(2)}) collective-permute-start(bf16[24,1024]{1,0:T(8,128)(2,1)S(1)} %get-tuple-element.23), channel_id=1, source_target_pairs={{0,3},{1,4},{2,5},{3,6},{4,7},{5,0},{6,1},{7,2},{8,11},{9,12},{10,... | collective-permute-start | bytes 147464 | tf_op jit(solution)/shard_map/ppermute | solution.py:101
  54.9 7.2 %collective-permute-start.18 = (bf16[1,192,896]{2,1,0:T(8,128)(2,1)S(1)}, bf16[1,192,896]{2,1,0:T(8,128)(2,1)S(1)}, u32[]{:S(2)}, u32[]{:S(2)}) collective-permute-start(bf16[1,192,896]{2,1,0:T(8,128)(2,1)S(1)} %bitcast.258), channel_id=1, source_target_pairs={{0,16},{8,24},{16,0},{24,8},{1,17},{9,25},{17,1},{25,9},{2,18},{10... | collective-permute-start | bytes 1032200 | tf_op jit(solution)/shard_map/ppermute | solution.py:43
  62.2 12.0 %collective-permute-start.19 = (bf16[2,192,896]{2,1,0:T(8,128)(2,1)S(1)}, bf16[2,192,896]{2,1,0:T(8,128)(2,1)S(1)}, u32[]{:S(2)}, u32[]{:S(2)}) collective-permute-start(bf16[2,192,896]{2,1,0:T(8,128)(2,1)S(1)} %maximum_select_fusion.4), channel_id=1, source_target_pairs={{0,8},{8,0},{16,24},{24,16},{1,9},{9,1},{17,25},{25,17},{2,10},{10... | collective-permute-start | bytes 2064392 | tf_op jit(solution)/shard_map/ppermute | solution.py:43
  63.4 10.5 %collective-permute-start.7 = (bf16[1,192,896]{2,1,0:T(8,128)(2,1)S(1)}, bf16[1,192,896]{2,1,0:T(8,128)(2,1)S(1)}, u32[]{:S(2)}, u32[]{:S(2)}) collective-permute-start(bf16[1,192,896]{2,1,0:T(8,128)(2,1)S(1)} %get-tuple-element.18), channel_id=1, source_target_pairs={{0,16},{8,24},{16,0},{24,8},{1,17},{9,25},{17,1},{25,9},{2,18},{10... | collective-permute-start | bytes 1032200 | tf_op jit(solution)/shard_map/ppermute | solution.py:43
  84.8 9.6 %collective-permute-start.20 = (f32[192]{0:T(256)S(1)}, f32[192]{0:T(256)S(1)}, u32[]{:S(2)}, u32[]{:S(2)}) collective-permute-start(f32[192]{0:T(256)S(1)} %get-tuple-element.5), channel_id=1, source_target_pairs={{0,8},{8,0},{16,24},{24,16},{1,9},{9,1},{17,25},{25,17},{2,10},{10... | collective-permute-start | bytes 2312 | tf_op jit(solution)/shard_map/ppermute | solution.py:66
  85.7 12.5 %collective-permute-start.9 = (bf16[2,192,896]{2,1,0:T(8,128)(2,1)S(1)}, bf16[2,192,896]{2,1,0:T(8,128)(2,1)S(1)}, u32[]{:S(2)}, u32[]{:S(2)}) collective-permute-start(bf16[2,192,896]{2,1,0:T(8,128)(2,1)S(1)} %fusion.15), channel_id=1, source_target_pairs={{0,8},{8,0},{16,24},{24,16},{1,9},{9,1},{17,25},{25,17},{2,10},{10... | collective-permute-start | bytes 2064392 | tf_op jit(solution)/shard_map/ppermute | solution.py:59
  98.5 11.1 %collective-permute-start.10 = (bf16[1,192,896]{2,1,0:T(8,128)(2,1)S(1)}, bf16[1,192,896]{2,1,0:T(8,128)(2,1)S(1)}, u32[]{:S(2)}, u32[]{:S(2)}) collective-permute-start(bf16[1,192,896]{2,1,0:T(8,128)(2,1)S(1)} %fusion.20), channel_id=1, source_target_pairs={{0,16},{8,24},{16,0},{24,8},{1,17},{9,25},{17,1},{25,9},{2,18},{10... | collective-permute-start | bytes 1032200 | tf_op jit(solution)/shard_map/ppermute | solution.py:59
  100.4 14.8 %collective-permute-start.30 = (bf16[1,192,896]{2,1,0:T(8,128)(2,1)S(1)}, bf16[1,192,896]{2,1,0:T(8,128)(2,1)S(1)}, u32[]{:S(2)}, u32[]{:S(2)}) collective-permute-start(bf16[1,192,896]{2,1,0:T(8,128)(2,1)S(1)} %fusion.21), channel_id=1, source_target_pairs={{0,16},{8,24},{16,0},{24,8},{1,17},{9,25},{17,1},{25,9},{2,18},{10... | collective-permute-start | bytes 1032200 | tf_op jit(solution)/shard_map/ppermute | solution.py:59
  115.4 6.4 %collective-permute-start.31 = (bf16[24,896]{1,0:T(8,128)(2,1)S(1)}, bf16[24,896]{1,0:T(8,128)(2,1)S(1)}, u32[]{:S(2)}, u32[]{:S(2)}) collective-permute-start(bf16[24,896]{1,0:T(8,128)(2,1)S(1)} %get-tuple-element.32), channel_id=1, source_target_pairs={{0,7},{1,0},{2,1},{3,2},{4,3},{5,4},{6,5},{7,6},{8,15},{9,8},{10,9... | collective-permute-start | bytes 129032 | tf_op jit(solution)/shard_map/ppermute | solution.py:101
  115.5 53.8 %collective-permute-start.28 = (bf16[24,1024]{1,0:T(8,128)(2,1)S(1)}, bf16[24,1024]{1,0:T(8,128)(2,1)S(1)}, u32[]{:S(2)}, u32[]{:S(2)}) collective-permute-start(bf16[24,1024]{1,0:T(8,128)(2,1)S(1)} %get-tuple-element.10), channel_id=1, source_target_pairs={{0,1},{1,2},{2,3},{3,4},{4,5},{5,6},{6,7},{7,0},{8,9},{9,10},{10,1... | collective-permute-start | bytes 147464 | tf_op jit(solution)/shard_map/ppermute | solution.py:101
  117.5 51.8 %collective-permute-start.27 = (bf16[24,1024]{1,0:T(8,128)(2,1)S(1)}, bf16[24,1024]{1,0:T(8,128)(2,1)S(1)}, u32[]{:S(2)}, u32[]{:S(2)}) collective-permute-start(bf16[24,1024]{1,0:T(8,128)(2,1)S(1)} %get-tuple-element.11), channel_id=1, source_target_pairs={{0,2},{1,3},{2,4},{3,5},{4,6},{5,7},{6,0},{7,1},{8,10},{9,11},{10,... | collective-permute-start | bytes 147464 | tf_op jit(solution)/shard_map/ppermute | solution.py:101
  117.5 51.8 %collective-permute-start.26 = (bf16[24,1024]{1,0:T(8,128)(2,1)S(1)}, bf16[24,1024]{1,0:T(8,128)(2,1)S(1)}, u32[]{:S(2)}, u32[]{:S(2)}) collective-permute-start(bf16[24,1024]{1,0:T(8,128)(2,1)S(1)} %get-tuple-element.12), channel_id=1, source_target_pairs={{0,3},{1,4},{2,5},{3,6},{4,7},{5,0},{6,1},{7,2},{8,11},{9,12},{10,... | collective-permute-start | bytes 147464 | tf_op jit(solution)/shard_map/ppermute | solution.py:101
  118.6 50.6 %collective-permute-start.25 = (bf16[24,1024]{1,0:T(8,128)(2,1)S(1)}, bf16[24,1024]{1,0:T(8,128)(2,1)S(1)}, u32[]{:S(2)}, u32[]{:S(2)}) collective-permute-start(bf16[24,1024]{1,0:T(8,128)(2,1)S(1)} %get-tuple-element.13), channel_id=1, source_target_pairs={{0,4},{1,5},{2,6},{3,7},{4,0},{5,1},{6,2},{7,3},{8,12},{9,13},{10,... | collective-permute-start | bytes 147464 | tf_op jit(solution)/shard_map/ppermute | solution.py:101
  125.8 4.9 %collective-permute-start.33 = (bf16[24,896]{1,0:T(8,128)(2,1)S(1)}, bf16[24,896]{1,0:T(8,128)(2,1)S(1)}, u32[]{:S(2)}, u32[]{:S(2)}) collective-permute-start(bf16[24,896]{1,0:T(8,128)(2,1)S(1)} %get-tuple-element.30), channel_id=1, source_target_pairs={{0,5},{1,6},{2,7},{3,0},{4,1},{5,2},{6,3},{7,4},{8,13},{9,14},{10,... | collective-permute-start | bytes 129032 | tf_op jit(solution)/shard_map/ppermute | solution.py:101
  130.8 5.0 %collective-permute-start.34 = (bf16[24,896]{1,0:T(8,128)(2,1)S(1)}, bf16[24,896]{1,0:T(8,128)(2,1)S(1)}, u32[]{:S(2)}, u32[]{:S(2)}) collective-permute-start(bf16[24,896]{1,0:T(8,128)(2,1)S(1)} %get-tuple-element.29), channel_id=1, source_target_pairs={{0,4},{1,5},{2,6},{3,7},{4,0},{5,1},{6,2},{7,3},{8,12},{9,13},{10,... | collective-permute-start | bytes 129032 | tf_op jit(solution)/shard_map/ppermute | solution.py:101
  135.7 5.8 %collective-permute-start.35 = (bf16[24,896]{1,0:T(8,128)(2,1)S(1)}, bf16[24,896]{1,0:T(8,128)(2,1)S(1)}, u32[]{:S(2)}, u32[]{:S(2)}) collective-permute-start(bf16[24,896]{1,0:T(8,128)(2,1)S(1)} %get-tuple-element.28), channel_id=1, source_target_pairs={{0,3},{1,4},{2,5},{3,6},{4,7},{5,0},{6,1},{7,2},{8,11},{9,12},{10,... | collective-permute-start | bytes 129032 | tf_op jit(solution)/shard_map/ppermute | solution.py:101
  141.5 7.8 %collective-permute-start.36 = (bf16[24,896]{1,0:T(8,128)(2,1)S(1)}, bf16[24,896]{1,0:T(8,128)(2,1)S(1)}, u32[]{:S(2)}, u32[]{:S(2)}) collective-permute-start(bf16[24,896]{1,0:T(8,128)(2,1)S(1)} %get-tuple-element.27), channel_id=1, source_target_pairs={{0,2},{1,3},{2,4},{3,5},{4,6},{5,7},{6,0},{7,1},{8,10},{9,11},{10,... | collective-permute-start | bytes 129032 | tf_op jit(solution)/shard_map/ppermute | solution.py:101
  149.3 6.7 %collective-permute-start.37 = (bf16[24,896]{1,0:T(8,128)(2,1)S(1)}, bf16[24,896]{1,0:T(8,128)(2,1)S(1)}, u32[]{:S(2)}, u32[]{:S(2)}) collective-permute-start(bf16[24,896]{1,0:T(8,128)(2,1)S(1)} %get-tuple-element.26), channel_id=1, source_target_pairs={{0,1},{1,2},{2,3},{3,4},{4,5},{5,6},{6,7},{7,0},{8,9},{9,10},{10,1... | collective-permute-start | bytes 129032 | tf_op jit(solution)/shard_map/ppermute | solution.py:101
  164.2 5.0 %collective-permute-start.24 = (bf16[24,1024]{1,0:T(8,128)(2,1)S(1)}, bf16[24,1024]{1,0:T(8,128)(2,1)S(1)}, u32[]{:S(2)}, u32[]{:S(2)}) collective-permute-start(bf16[24,1024]{1,0:T(8,128)(2,1)S(1)} %get-tuple-element.14), channel_id=1, source_target_pairs={{0,5},{1,6},{2,7},{3,0},{4,1},{5,2},{6,3},{7,4},{8,13},{9,14},{10,... | collective-permute-start | bytes 147464 | tf_op jit(solution)/shard_map/ppermute | solution.py:101
  (13 other events, 65.9 us)

commit v4 on v2

--- a/solution.py
+++ b/solution.py
@@ -48,13 +48,15 @@
     return held
 
 
-def scatter_sum(blocks, n_ctx, me):
+def scatter_sum(blocks, n_ctx, me, wait_for=None):
     acc = blocks
     for bit in range(ctx_bits(n_ctx)):
         halves = acc.reshape((-1, 2) + acc.shape[1:])
         keep_first = ((me >> bit) & 1) == 0
         keep = jnp.where(keep_first, halves[:, 0], halves[:, 1])
         send = jnp.where(keep_first, halves[:, 1], halves[:, 0]).astype(jnp.bfloat16)
+        if bit == 1 and wait_for is not None:
+            send, _ = lax.optimization_barrier((send, wait_for))
         got = lax.ppermute(send, "ctx", xor_pairs(n_ctx, bit))
         acc = keep + got.astype(jnp.float32)
     return acc[0]
@@ -68,9 +70,8 @@
 
 def with_cols(rows, values, pad):
     hi, lo = split_f32(values)
-    cols = jnp.zeros((rows.shape[0], pad), jnp.bfloat16)
-    cols = cols.at[:, 0].set(hi).at[:, 1].set(lo)
-    return jnp.concatenate([rows, cols], axis=1)
+    zeros = jnp.zeros((rows.shape[0], pad - 2), jnp.bfloat16)
+    return jnp.concatenate([rows, hi[:, None], lo[:, None], zeros], axis=1)
 
 
 def shards(tokens, cotangent, expert_ids, route_gates, w_gate, w_up, w_down):
@@ -141,7 +142,7 @@
         "sf,ndf->nsd", grad_gate, gate_w, preferred_element_type=jnp.float32
     ) + jnp.einsum("sf,ndf->nsd", grad_up, up_w, preferred_element_type=jnp.float32)
     back_terms = back_terms.astype(jnp.bfloat16).astype(jnp.float32)
-    slot_grad = scatter_sum(back_terms, n_ctx, me).astype(jnp.bfloat16)
+    slot_grad = scatter_sum(back_terms, n_ctx, me, expert_out).astype(jnp.bfloat16)
     back_grad = to_experts(slot_grad)
 
     w_gate_grad = jnp.einsum(

time: 107 us -> 107 us (level)
  waiting for transfers between devices: 36.6 us -> 42.3 us
  other arithmetic: 15 us -> 11.1 us
  local copies, waits for them, and re-layouts: 8.14 us -> 6.46 us
    all_to_all x4, waiting for transfers between devices: 12.1 us -> 17.8 us  [to_experts(): got = lax.all_to_all(sent, 'ep', split_axis=0, concat_axis=0, tiled=True)]
    another operation x4 -> x0, other arithmetic: 3.89 us -> none
    scatter x5 -> x0, local copies, waits for them, and re-layouts: 3.72 us -> none  [with_cols(): cols = cols.at[:, 0].set(hi).at[:, 1].set(lo)]
    concatenate x0 -> x4, local copies, waits for them, and re-layouts: none -> 1.79 us  [with_cols(): return jnp.concatenate([rows, hi[:, None], lo[:, None], zeros], axis=1)]
    unnamed x18 -> x20, local copies, waits for them, and re-layouts: 4.13 us -> 4.13 us
  transfers between devices with their start and end apart: 14 -> 14, of which waited for: 8 -> 8; matrix products, arithmetic and copies ran while one was open for 23% -> 17% of each run, Pallas kernels for 0% -> 0%
where the time goes in v4:
time: 107 us; the launch traced here: 106 us
  waiting for transfers between devices  42.3 us (40%)
  starting transfers between devices  28.1 us (26%)
  matrix products  17 us (16%)
  other arithmetic  11.1 us (10%)
  local copies, waits for them, and re-layouts  6.46 us (6%)
    all_to_all x4, starting transfers between devices, to_experts(): got = lax.all_to_all(sent, 'ep', split_axis=0, concat_axis=0, tiled=True)  20.2 us
    all_to_all x4, waiting for transfers between devices, to_experts(): got = lax.all_to_all(sent, 'ep', split_axis=0, concat_axis=0, tiled=True)  17.8 us
    ppermute x4, waiting for transfers between devices, gather_blocks(): other = lax.ppermute(held, 'ctx', xor_pairs(n_ctx, bit))  15 us
    ppermute x4, waiting for transfers between devices, scatter_sum(): got = lax.ppermute(send, 'ctx', xor_pairs(n_ctx, bit))  7.95 us
    unnamed x20, local copies, waits for them, and re-layouts  4.13 us
    ppermute x4, starting transfers between devices, gather_blocks(): other = lax.ppermute(held, 'ctx', xor_pairs(n_ctx, bit))  3.17 us
    dot_general x1, matrix products, shards(): jnp.einsum('nsd,sf->ndf', rows_in, grad_up, preferred_element_type=jnp.fl...  3 us
    dot_general x1, matrix products, shards(): jnp.einsum('nsd,sf->ndf', rows_in, grad_gate, preferred_element_type=jnp....  3 us
  transfers between devices with their start and end apart: 14, of which 8 were waited for; matrix products, arithmetic and copies ran while one was open for 17% of the time, Pallas kernels for 0%

profile of v4, /device:TPU:0, one launch (start us, length us, event | category | flops | bytes accessed | tf_op | source)
XLA Modules:
  0.0 106.1 jit_solution(3644383721475488655)
XLA Ops:
  3.1 1.0 convolution_convert_fusion.2
  4.1 7.3 %all-to-all-start.1 = ((bf16[8,24,896]{2,1,0:T(8,128)(2,1)}), bf16[8,24,896]{2,1,0:T(8,128)(2,1)S(1)}, u32[]{:S(2)}, u32[]{:S(2)}) async-start(bf16[8,24,896]{2,1,0:T(8,128)(2,1)} %bitcast.34), calls=%async_computation.1 | async-start | bytes 688128 | tf_op jit(solution)/shard_map/all_to_all | solution.py:98
  13.1 9.0 %all-to-all-done.1 = bf16[8,24,896]{2,1,0:T(8,128)(2,1)S(1)} async-done(((bf16[8,24,896]{2,1,0:T(8,128)(2,1)}), bf16[8,24,896]{2,1,0:T(8,128)(2,1)S(1)}, u32[]{:S(2)}, u32[]{:S(2)}) %all-to-all-start.1) | async-done | bytes 344096 | tf_op jit(solution)/shard_map/all_to_all | solution.py:98
  22.0 3.6 %all-to-all-start = ((bf16[8,24,1024]{2,1,0:T(8,128)(2,1)}), bf16[8,24,1024]{2,1,0:T(8,128)(2,1)S(1)}, u32[]{:S(2)}, u32[]{:S(2)}) async-start(bf16[8,24,1024]{2,1,0:T(8,128)(2,1)} %maximum_maximum_fusion), calls=%async_computation | async-start | bytes 786432 | tf_op jit(solution)/shard_map/all_to_all | solution.py:98
  25.6 1.5 %collective-permute-start.4 = (bf16[1,192,896]{2,1,0:T(8,128)(2,1)S(1)}, bf16[1,192,896]{2,1,0:T(8,128)(2,1)S(1)}, u32[]{:S(2)}, u32[]{:S(2)}) collective-permute-start(bf16[1,192,896]{2,1,0:T(8,128)(2,1)S(1)} %bitcast.174), channel_id=1, source_target_pairs={{0,16},{8,24},{16,0},{24,8},{1,17},{9,25},{17,1},{25,9},{2,18},{10... | collective-permute-start | bytes 1032200 | tf_op jit(solution)/shard_map/ppermute | solution.py:42
  27.2 7.5 %collective-permute-done.4 = bf16[1,192,896]{2,1,0:T(8,128)(2,1)S(1)} collective-permute-done((bf16[1,192,896]{2,1,0:T(8,128)(2,1)S(1)}, bf16[1,192,896]{2,1,0:T(8,128)(2,1)S(1)}, u32[]{:S(2)}, u32[]{:S(2)}) %collective-permute-start.4) | collective-permute-done | bytes 344096 | tf_op jit(solution)/shard_map/ppermute | solution.py:42
  34.7 1.0 maximum_select_fusion.4
  35.7 1.2 %all-to-all-done = bf16[8,24,1024]{2,1,0:T(8,128)(2,1)S(1)} async-done(((bf16[8,24,1024]{2,1,0:T(8,128)(2,1)}), bf16[8,24,1024]{2,1,0:T(8,128)(2,1)S(1)}, u32[]{:S(2)}, u32[]{:S(2)}) %all-to-all-start) | async-done | bytes 393248 | tf_op jit(solution)/shard_map/all_to_all | solution.py:98
  37.0 1.6 %collective-permute-start = (bf16[1,192,896]{2,1,0:T(8,128)(2,1)S(1)}, bf16[1,192,896]{2,1,0:T(8,128)(2,1)S(1)}, u32[]{:S(2)}, u32[]{:S(2)}) collective-permute-start(bf16[1,192,896]{2,1,0:T(8,128)(2,1)S(1)} %get-tuple-element.13), channel_id=1, source_target_pairs={{0,16},{8,24},{16,0},{24,8},{1,17},{9,25},{17,1},{25,9},{2,18},{10... | collective-permute-start | bytes 1032200 | tf_op jit(solution)/shard_map/ppermute | solution.py:42
  38.9 7.4 %collective-permute-done = bf16[1,192,896]{2,1,0:T(8,128)(2,1)S(1)} collective-permute-done((bf16[1,192,896]{2,1,0:T(8,128)(2,1)S(1)}, bf16[1,192,896]{2,1,0:T(8,128)(2,1)S(1)}, u32[]{:S(2)}, u32[]{:S(2)}) %collective-permute-start) | collective-permute-done | bytes 344096 | tf_op jit(solution)/shard_map/ppermute | solution.py:42
  47.0 1.6 %copy-done.3 = bf16[1,512,3584]{2,1,0:T(8,128)(2,1)S(1)} copy-done((bf16[1,512,3584]{2,1,0:T(8,128)(2,1)S(1)}, bf16[1,512,3584]{2,1,0:T(8,128)(2,1)}, u32[]{:S(2)}) %copy-start.3) | copy-done | bytes 3670040
  50.3 1.3 %copy-done.2 = bf16[1,3584,512]{2,1,0:T(8,128)(2,1)S(1)} copy-done((bf16[1,3584,512]{2,1,0:T(8,128)(2,1)S(1)}, bf16[1,3584,512]{2,1,0:T(8,128)(2,1)}, u32[]{:S(2)}) %copy-start.2) | copy-done | bytes 3670040
  51.6 0.9 convolution_bitcast_fusion.4
  52.5 1.2 %copy-done.1 = bf16[1,3584,512]{2,1,0:T(8,128)(2,1)S(1)} copy-done((bf16[1,3584,512]{2,1,0:T(8,128)(2,1)S(1)}, bf16[1,3584,512]{2,1,0:T(8,128)(2,1)}, u32[]{:S(2)}) %copy-start.1) | copy-done | bytes 3670040
  53.7 0.9 convolution_bitcast_fusion.5
  56.7 1.3 %fusion.27 = f32[192,4,896]{2,0,1:T(8,128)S(1)} fusion(bf16[4,896,512]{2,1,0:T(8,128)(2,1)S(1)} %bitcast.169, bf16[192,512]{1,0:T(8,128)(2,1)S(1)} %get-tuple-element.10), kind=kOutput, calls=%fused_computation.73 | convolution fusion | flops 704643072 | bytes 6619136 | tf_op jit(solution)/shard_map/sf,ndf->nsd/dot_general | solution.py:141
  58.0 1.3 %fusion.1 = f32[192,4,896]{2,0,1:T(8,128)S(1)} fusion(f32[192,4,896]{2,0,1:T(8,128)S(1)} %fusion.27, bf16[192,512,1]{1,0,2:T(8,128)(2,1)S(1)} %get-tuple-element.9, bf16[4,896,512]{2,1,0:T(8,128)(2,1)S(1)} %bitcast.171), kind=kOutput, calls=%fused_computation.6 | convolution fusion | flops 706707456 | bytes 9371648 | tf_op jit(solution)/shard_map/sf,ndf->nsd/dot_general | solution.py:143
  61.5 1.6 %collective-permute-done.6 = f32[192]{0:T(256)S(1)} collective-permute-done((f32[192]{0:T(256)S(1)}, f32[192]{0:T(256)S(1)}, u32[]{:S(2)}, u32[]{:S(2)}) %collective-permute-start.6) | collective-permute-done | bytes 800 | tf_op jit(solution)/shard_map/ppermute | solution.py:67
  63.1 1.5 %collective-permute-start.7 = (f32[192]{0:T(256)S(1)}, f32[192]{0:T(256)S(1)}, u32[]{:S(2)}, u32[]{:S(2)}) collective-permute-start(f32[192]{0:T(256)S(1)} %add.59), channel_id=1, source_target_pairs={{0,16},{8,24},{16,0},{24,8},{1,17},{9,25},{17,1},{25,9},{2,18},{10... | collective-permute-start | bytes 2312 | tf_op jit(solution)/shard_map/ppermute | solution.py:67
  66.4 1.5 %collective-permute-start.3 = (bf16[1,192,896]{2,1,0:T(8,128)(2,1)}, bf16[1,192,896]{2,1,0:T(8,128)(2,1)}, u32[]{:S(2)}, u32[]{:S(2)}) collective-permute-start(bf16[1,192,896]{2,1,0:T(8,128)(2,1)} %fusion.22), channel_id=1, source_target_pairs={{0,16},{8,24},{16,0},{24,8},{1,17},{9,25},{17,1},{25,9},{2,18},{10... | collective-permute-start | bytes 1032200 | tf_op jit(solution)/shard_map/ppermute | solution.py:60
  68.0 7.9 %collective-permute-done.9 = bf16[1,192,896]{2,1,0:T(8,128)(2,1)S(1)} collective-permute-done((bf16[1,192,896]{2,1,0:T(8,128)(2,1)S(1)}, bf16[1,192,896]{2,1,0:T(8,128)(2,1)S(1)}, u32[]{:S(2)}, u32[]{:S(2)}) %collective-permute-start.9) | collective-permute-done | bytes 344096 | tf_op jit(solution)/shard_map/ppermute | solution.py:60
  76.7 5.7 %all-to-all-start.3 = ((bf16[8,24,896]{2,1,0:T(8,128)(2,1)}), bf16[8,24,896]{2,1,0:T(8,128)(2,1)S(1)}, u32[]{:S(2)}, u32[]{:S(2)}) async-start(bf16[8,24,896]{2,1,0:T(8,128)(2,1)} %bitcast.184), calls=%async_computation.3 | async-start | bytes 688128 | tf_op jit(solution)/shard_map/all_to_all | solution.py:98
  82.4 0.9 concatenate.62
  83.3 0.9 concatenate.63
  84.1 1.1 %fusion.20 = bf16[1,192,896]{2,1,0:T(8,128)(2,1)S(1)} fusion(bf16[1,192,896]{2,1,0:T(8,128)(2,1)} %collective-permute-done.3, f32[1,2,192,896]{3,2,1,0:T(8,128)S(1)} %fusion.4, pred[]{:T(512)S(6)} %eq.50), kind=kLoop, calls=%fused_computation.52 | loop fusion | flops 688128 | bytes 2064385 | tf_op jit(solution)/shard_map/convert_element_type | solution.py:127
  86.1 5.2 %all-to-all-done.3 = bf16[8,24,896]{2,1,0:T(8,128)(2,1)S(1)} async-done(((bf16[8,24,896]{2,1,0:T(8,128)(2,1)}), bf16[8,24,896]{2,1,0:T(8,128)(2,1)S(1)}, u32[]{:S(2)}, u32[]{:S(2)}) %all-to-all-start.3) | async-done | bytes 344096 | tf_op jit(solution)/shard_map/all_to_all | solution.py:98
  91.3 3.6 %all-to-all-start.2 = ((bf16[8,24,1024]{2,1,0:T(8,128)(2,1)}), bf16[8,24,1024]{2,1,0:T(8,128)(2,1)S(1)}, u32[]{:S(2)}, u32[]{:S(2)}) async-start(bf16[8,24,1024]{2,1,0:T(8,128)(2,1)} %maximum_maximum_fusion.1), calls=%async_computation.2 | async-start | bytes 786432 | tf_op jit(solution)/shard_map/all_to_all | solution.py:98
  94.9 3.0 %convolution_convert_fusion = bf16[4,896,512]{2,1,0:T(8,128)(2,1)} fusion(bf16[4,192,896]{2,1,0:T(8,128)(2,1)S(1)} %bitcast.160, bf16[192,512,1]{1,0,2:T(8,128)(2,1)S(1)} %copy-done.5), kind=kOutput, calls=%fused_computation.4 | convolution fusion | flops 706478080 | bytes 5242880 | tf_op jit(solution)/shard_map/nsd,sf->ndf/dot_general | solution.py:151
  97.9 3.0 %convolution_convert_fusion.1 = bf16[4,896,512]{2,1,0:T(8,128)(2,1)} fusion(bf16[4,192,896]{2,1,0:T(8,128)(2,1)S(1)} %bitcast.161, bf16[192,512]{1,0:T(8,128)(2,1)S(1)} %get-tuple-element.10), kind=kOutput, calls=%fused_computation.5 | convolution fusion | flops 706478080 | bytes 5242880 | tf_op jit(solution)/shard_map/nsd,sf->ndf/dot_general | solution.py:148
  100.9 1.0 convolution_convert_fusion.4
  101.9 2.4 %all-to-all-done.2 = bf16[8,24,1024]{2,1,0:T(8,128)(2,1)S(1)} async-done(((bf16[8,24,1024]{2,1,0:T(8,128)(2,1)}), bf16[8,24,1024]{2,1,0:T(8,128)(2,1)S(1)}, u32[]{:S(2)}, u32[]{:S(2)}) %all-to-all-start.2) | async-done | bytes 393248 | tf_op jit(solution)/shard_map/all_to_all | solution.py:98
  104.5 1.0 fusion.7
  (72 shorter events, 15.3 us)
Async XLA Ops:
  0.6 2.5 %copy-start = (bf16[128,896]{1,0:T(8,128)(2,1)S(1)}, bf16[128,896]{1,0:T(8,128)(2,1)}, u32[]{:S(2)}) copy-start(bf16[128,896]{1,0:T(8,128)(2,1)} %param.8) | copy-start | bytes 688132
  0.6 10.7 %copy-start.9 = (f32[128,1]{0,1:T(1,128)S(1)}, f32[128,1]{0,1:T(1,128)}, u32[]{:S(2)}) copy-start(f32[128,1]{0,1:T(1,128)} %param.10) | copy-start | bytes 1540
  0.7 11.3 %copy-start.6 = (bf16[128,896]{1,0:T(8,128)(2,1)S(1)}, bf16[128,896]{1,0:T(8,128)(2,1)}, u32[]{:S(2)}) copy-start(bf16[128,896]{1,0:T(8,128)(2,1)} %param.7) | copy-start | bytes 688132
  4.1 17.9 %all-to-all-start.1 = ((bf16[8,24,896]{2,1,0:T(8,128)(2,1)}), bf16[8,24,896]{2,1,0:T(8,128)(2,1)S(1)}, u32[]{:S(2)}, u32[]{:S(2)}) async-start(bf16[8,24,896]{2,1,0:T(8,128)(2,1)} %bitcast.34), calls=%async_computation.1 | async-start | bytes 688128 | tf_op jit(solution)/shard_map/all_to_all | solution.py:98
  22.0 14.9 %all-to-all-start = ((bf16[8,24,1024]{2,1,0:T(8,128)(2,1)}), bf16[8,24,1024]{2,1,0:T(8,128)(2,1)S(1)}, u32[]{:S(2)}, u32[]{:S(2)}) async-start(bf16[8,24,1024]{2,1,0:T(8,128)(2,1)} %maximum_maximum_fusion), calls=%async_computation | async-start | bytes 786432 | tf_op jit(solution)/shard_map/all_to_all | solution.py:98
  25.6 9.1 %collective-permute-start.4 = (bf16[1,192,896]{2,1,0:T(8,128)(2,1)S(1)}, bf16[1,192,896]{2,1,0:T(8,128)(2,1)S(1)}, u32[]{:S(2)}, u32[]{:S(2)}) collective-permute-start(bf16[1,192,896]{2,1,0:T(8,128)(2,1)S(1)} %bitcast.174), channel_id=1, source_target_pairs={{0,16},{8,24},{16,0},{24,8},{1,17},{9,25},{17,1},{25,9},{2,18},{10... | collective-permute-start | bytes 1032200 | tf_op jit(solution)/shard_map/ppermute | solution.py:42
  35.7 10.9 %collective-permute-start.5 = (bf16[2,192,896]{2,1,0:T(8,128)(2,1)}, bf16[2,192,896]{2,1,0:T(8,128)(2,1)S(1)}, u32[]{:S(2)}, u32[]{:S(2)}) collective-permute-start(bf16[2,192,896]{2,1,0:T(8,128)(2,1)} %maximum_select_fusion.4), channel_id=1, source_target_pairs={{0,8},{8,0},{16,24},{24,16},{1,9},{9,1},{17,25},{25,17},{2,10},{10... | collective-permute-start | bytes 2064392 | tf_op jit(solution)/shard_map/ppermute | solution.py:42
  37.0 9.3 %collective-permute-start = (bf16[1,192,896]{2,1,0:T(8,128)(2,1)S(1)}, bf16[1,192,896]{2,1,0:T(8,128)(2,1)S(1)}, u32[]{:S(2)}, u32[]{:S(2)}) collective-permute-start(bf16[1,192,896]{2,1,0:T(8,128)(2,1)S(1)} %get-tuple-element.13), channel_id=1, source_target_pairs={{0,16},{8,24},{16,0},{24,8},{1,17},{9,25},{17,1},{25,9},{2,18},{10... | collective-permute-start | bytes 1032200 | tf_op jit(solution)/shard_map/ppermute | solution.py:42
  46.4 3.7 %collective-permute-start.1 = (bf16[2,192,896]{2,1,0:T(8,128)(2,1)S(1)}, bf16[2,192,896]{2,1,0:T(8,128)(2,1)S(1)}, u32[]{:S(2)}, u32[]{:S(2)}) collective-permute-start(bf16[2,192,896]{2,1,0:T(8,128)(2,1)S(1)} %maximum_select_fusion.2), channel_id=1, source_target_pairs={{0,8},{8,0},{16,24},{24,16},{1,9},{9,1},{17,25},{25,17},{2,10},{10... | collective-permute-start | bytes 2064392 | tf_op jit(solution)/shard_map/ppermute | solution.py:42
  46.6 2.0 %copy-start.3 = (bf16[1,512,3584]{2,1,0:T(8,128)(2,1)S(1)}, bf16[1,512,3584]{2,1,0:T(8,128)(2,1)}, u32[]{:S(2)}) copy-start(bf16[1,512,3584]{2,1,0:T(8,128)(2,1)} %param.13) | copy-start | bytes 11010052
  49.6 2.0 %copy-start.2 = (bf16[1,3584,512]{2,1,0:T(8,128)(2,1)S(1)}, bf16[1,3584,512]{2,1,0:T(8,128)(2,1)}, u32[]{:S(2)}) copy-start(bf16[1,3584,512]{2,1,0:T(8,128)(2,1)} %param.12) | copy-start | bytes 11010052
  51.6 2.0 %copy-start.1 = (bf16[1,3584,512]{2,1,0:T(8,128)(2,1)S(1)}, bf16[1,3584,512]{2,1,0:T(8,128)(2,1)}, u32[]{:S(2)}) copy-start(bf16[1,3584,512]{2,1,0:T(8,128)(2,1)} %param.11) | copy-start | bytes 11010052
  55.1 2.9 %copy-start.4 = (bf16[192,512,1]{1,0,2:T(8,128)(2,1)}, bf16[192,512,1]{1,0,2:T(8,128)(2,1)S(1)}, u32[]{:S(2)}) copy-start(bf16[192,512,1]{1,0,2:T(8,128)(2,1)S(1)} %get-tuple-element.9) | copy-start | bytes 589828
  59.5 5.1 %collective-permute-start.8 = (bf16[2,192,896]{2,1,0:T(8,128)(2,1)S(1)}, bf16[2,192,896]{2,1,0:T(8,128)(2,1)S(1)}, u32[]{:S(2)}, u32[]{:S(2)}) collective-permute-start(bf16[2,192,896]{2,1,0:T(8,128)(2,1)S(1)} %fusion.18), channel_id=1, source_target_pairs={{0,8},{8,0},{16,24},{24,16},{1,9},{9,1},{17,25},{25,17},{2,10},{10... | collective-permute-start | bytes 2064392 | tf_op jit(solution)/shard_map/ppermute | solution.py:60
  60.9 4.6 %collective-permute-start.2 = (bf16[2,192,896]{2,1,0:T(8,128)(2,1)S(1)}, bf16[2,192,896]{2,1,0:T(8,128)(2,1)S(1)}, u32[]{:S(2)}, u32[]{:S(2)}) collective-permute-start(bf16[2,192,896]{2,1,0:T(8,128)(2,1)S(1)} %fusion.17), channel_id=1, source_target_pairs={{0,8},{8,0},{16,24},{24,16},{1,9},{9,1},{17,25},{25,17},{2,10},{10... | collective-permute-start | bytes 2064392 | tf_op jit(solution)/shard_map/ppermute | solution.py:60
  61.0 2.1 %collective-permute-start.6 = (f32[192]{0:T(256)S(1)}, f32[192]{0:T(256)S(1)}, u32[]{:S(2)}, u32[]{:S(2)}) collective-permute-start(f32[192]{0:T(256)S(1)} %get-tuple-element.5), channel_id=1, source_target_pairs={{0,8},{8,0},{16,24},{24,16},{1,9},{9,1},{17,25},{25,17},{2,10},{10... | collective-permute-start | bytes 2312 | tf_op jit(solution)/shard_map/ppermute | solution.py:67
  63.1 19.3 %collective-permute-start.7 = (f32[192]{0:T(256)S(1)}, f32[192]{0:T(256)S(1)}, u32[]{:S(2)}, u32[]{:S(2)}) collective-permute-start(f32[192]{0:T(256)S(1)} %add.59), channel_id=1, source_target_pairs={{0,16},{8,24},{16,0},{24,8},{1,17},{9,25},{17,1},{25,9},{2,18},{10... | collective-permute-start | bytes 2312 | tf_op jit(solution)/shard_map/ppermute | solution.py:67
  64.9 11.0 %collective-permute-start.9 = (bf16[1,192,896]{2,1,0:T(8,128)(2,1)S(1)}, bf16[1,192,896]{2,1,0:T(8,128)(2,1)S(1)}, u32[]{:S(2)}, u32[]{:S(2)}) collective-permute-start(bf16[1,192,896]{2,1,0:T(8,128)(2,1)S(1)} %fusion.23), channel_id=1, source_target_pairs={{0,16},{8,24},{16,0},{24,8},{1,17},{9,25},{17,1},{25,9},{2,18},{10... | collective-permute-start | bytes 1032200 | tf_op jit(solution)/shard_map/ppermute | solution.py:60
  66.4 17.7 %collective-permute-start.3 = (bf16[1,192,896]{2,1,0:T(8,128)(2,1)}, bf16[1,192,896]{2,1,0:T(8,128)(2,1)}, u32[]{:S(2)}, u32[]{:S(2)}) collective-permute-start(bf16[1,192,896]{2,1,0:T(8,128)(2,1)} %fusion.22), channel_id=1, source_target_pairs={{0,16},{8,24},{16,0},{24,8},{1,17},{9,25},{17,1},{25,9},{2,18},{10... | collective-permute-start | bytes 1032200 | tf_op jit(solution)/shard_map/ppermute | solution.py:60
  76.7 14.6 %all-to-all-start.3 = ((bf16[8,24,896]{2,1,0:T(8,128)(2,1)}), bf16[8,24,896]{2,1,0:T(8,128)(2,1)S(1)}, u32[]{:S(2)}, u32[]{:S(2)}) async-start(bf16[8,24,896]{2,1,0:T(8,128)(2,1)} %bitcast.184), calls=%async_computation.3 | async-start | bytes 688128 | tf_op jit(solution)/shard_map/all_to_all | solution.py:98
  84.1 1.1 %copy-start.7 = (bf16[8,24,1]{2,1,0:T(8,128)(2,1)S(1)}, bf16[8,24,1]{2,1,0:T(8,128)(2,1)}, u32[]{:S(2)}) copy-start(bf16[8,24,1]{2,1,0:T(8,128)(2,1)} %concatenate.62) | copy-start | bytes 1156
  84.1 1.1 %copy-start.8 = (bf16[8,24,1]{2,1,0:T(8,128)(2,1)S(1)}, bf16[8,24,1]{2,1,0:T(8,128)(2,1)}, u32[]{:S(2)}) copy-start(bf16[8,24,1]{2,1,0:T(8,128)(2,1)} %concatenate.63) | copy-start | bytes 1156
  85.2 9.7 %copy-start.5 = (bf16[192,512,1]{1,0,2:T(8,128)(2,1)S(1)}, bf16[192,512,1]{1,0,2:T(8,128)(2,1)}, u32[]{:S(2)}) copy-start(bf16[192,512,1]{1,0,2:T(8,128)(2,1)} %copy-done.4) | copy-start | bytes 589828
  91.3 13.0 %all-to-all-start.2 = ((bf16[8,24,1024]{2,1,0:T(8,128)(2,1)}), bf16[8,24,1024]{2,1,0:T(8,128)(2,1)S(1)}, u32[]{:S(2)}, u32[]{:S(2)}) async-start(bf16[8,24,1024]{2,1,0:T(8,128)(2,1)} %maximum_maximum_fusion.1), calls=%async_computation.2 | async-start | bytes 786432 | tf_op jit(solution)/shard_map/all_to_all | solution.py:98

commit v5 on v4

--- a/solution.py
+++ b/solution.py
@@ -48,7 +48,12 @@
     return held
 
 
-def scatter_sum(blocks, n_ctx, me, wait_for=None):
+def after(values, *needed):
+    zero = sum(jnp.ravel(x)[0].astype(jnp.float32) for x in needed) * 0.0
+    return values + zero.astype(values.dtype)
+
+
+def scatter_sum(blocks, n_ctx, me, wait_for=None, stages=None):
     acc = blocks
     for bit in range(ctx_bits(n_ctx)):
         halves = acc.reshape((-1, 2) + acc.shape[1:])
@@ -56,9 +61,11 @@
         keep = jnp.where(keep_first, halves[:, 0], halves[:, 1])
         send = jnp.where(keep_first, halves[:, 1], halves[:, 0]).astype(jnp.bfloat16)
         if bit == 1 and wait_for is not None:
-            send, _ = lax.optimization_barrier((send, wait_for))
+            send = after(send, wait_for)
         got = lax.ppermute(send, "ctx", xor_pairs(n_ctx, bit))
         acc = keep + got.astype(jnp.float32)
+        if stages is not None:
+            stages.append(acc)
     return acc[0]
 
 
@@ -105,7 +112,7 @@
     gate_column = join_f32(got_x[:, col_width], got_x[:, col_width + 1])[:, None]
     rows_in = gather_blocks(got_x[:, :col_width], n_ctx, me)
     got_dy = to_experts(place(cotangent))
-    grads_in = gather_blocks(got_dy, n_ctx, me)
+    grads_in = gather_blocks(after(got_dy, rows_in), n_ctx, me)
 
     group = w_gate.shape[2]
     gate_w = w_gate[0].reshape(n_ctx, col_width, group)
@@ -124,7 +131,10 @@
     gate_part = jnp.einsum(
         "nsd,nsd->s", partial_out.astype(jnp.float32), grads_in.astype(jnp.float32)
     )
-    expert_out = scatter_sum(partial_out.astype(jnp.float32), n_ctx, me).astype(jnp.bfloat16)
+    out_stages = []
+    expert_out = scatter_sum(
+        partial_out.astype(jnp.float32), n_ctx, me, stages=out_stages
+    ).astype(jnp.bfloat16)
     gate_sum = all_sum(gate_part, n_ctx)
     back_out = to_experts(with_cols(expert_out, gate_sum, pad))
 
@@ -133,7 +143,7 @@
         lax.dot_general(grads_in[q], down_cols[q], contract_last, preferred_element_type=jnp.float32)
         for q in range(n_ctx)
     )
-    hidden_grad = gate_column * down_t
+    hidden_grad = after(gate_column * down_t, out_stages[0])
     grad_gate = (hidden_grad * pre_up * sigma * (1.0 + pre_gate * (1.0 - sigma))).astype(
         jnp.bfloat16
     )

time: 107 us -> 121 us (1.13)
  blocking collectives: 0 us -> 19.1 us
  waiting for transfers between devices: 42.3 us -> 27.4 us
  matrix products: 17 us -> 22.6 us
  starting transfers between devices: 28.1 us -> 22.6 us
  other arithmetic: 11.1 us -> 15.3 us
  local copies, waits for them, and re-layouts: 6.46 us -> 10.1 us
  between operations: 0.99 us -> 2.97 us
    all_to_all x0 -> x1, blocking collectives: none -> 19.1 us  [to_experts(): got = lax.all_to_all(sent, 'ep', split_axis=0, concat_axis=0, tiled=True)]
    all_to_all x4 -> x3, waiting for transfers between devices: 17.8 us -> 12 us  [to_experts(): got = lax.all_to_all(sent, 'ep', split_axis=0, concat_axis=0, tiled=True)]
    ppermute x4, waiting for transfers between devices: 15 us -> 9.77 us  [gather_blocks(): other = lax.ppermute(held, 'ctx', xor_pairs(n_ctx, bit))]
    all_to_all x4 -> x3, starting transfers between devices: 20.2 us -> 15.1 us  [to_experts(): got = lax.all_to_all(sent, 'ep', split_axis=0, concat_axis=0, tiled=True)]
    dot_general x4, matrix products: 1.96 us -> 4.48 us  [shards(): lax.dot_general(grads_in[q], down_cols[q], contract_last, preferred_eleme...]
    ppermute x4, waiting for transfers between devices: 7.95 us -> 5.68 us  [scatter_sum(): got = lax.ppermute(send, 'ctx', xor_pairs(n_ctx, bit))]
    slice x0 -> x3, local copies, waits for them, and re-layouts: none -> 2.22 us  [after(): zero = sum((jnp.ravel(x)[0].astype(jnp.float32) for x in needed)) * 0.0]
    dot_general x1, matrix products: 0.87 us -> 3.06 us  [shards(): jnp.einsum('nsd,ndf->sf', rows_in, gate_w, preferred_element_type=jnp.flo...]
  transfers between devices with their start and end apart: 14 -> 13, of which waited for: 8 -> 6; matrix products, arithmetic and copies ran while one was open for 17% -> 33% of each run, Pallas kernels for 0% -> 0%
where the time goes in v5:
time: 121 us; the launch traced here: 120 us
  waiting for transfers between devices  27.4 us (23%)
  matrix products  22.6 us (19%)
  starting transfers between devices  22.6 us (19%)
  blocking collectives  19.1 us (16%)
  other arithmetic  15.3 us (13%)
  local copies, waits for them, and re-layouts  10.1 us (8%)
  between operations  2.97 us (2%)
    all_to_all x1, blocking collectives, to_experts(): got = lax.all_to_all(sent, 'ep', split_axis=0, concat_axis=0, tiled=True)  19.1 us
    all_to_all x3, starting transfers between devices, to_experts(): got = lax.all_to_all(sent, 'ep', split_axis=0, concat_axis=0, tiled=True)  15.1 us
    all_to_all x3, waiting for transfers between devices, to_experts(): got = lax.all_to_all(sent, 'ep', split_axis=0, concat_axis=0, tiled=True)  12 us
    ppermute x4, waiting for transfers between devices, gather_blocks(): other = lax.ppermute(held, 'ctx', xor_pairs(n_ctx, bit))  9.77 us
    ppermute x4, waiting for transfers between devices, scatter_sum(): got = lax.ppermute(send, 'ctx', xor_pairs(n_ctx, bit))  5.68 us
    dot_general x4, matrix products, shards(): lax.dot_general(grads_in[q], down_cols[q], contract_last, preferred_eleme...  4.48 us
    ppermute x4, starting transfers between devices, gather_blocks(): other = lax.ppermute(held, 'ctx', xor_pairs(n_ctx, bit))  3.31 us
    dot_general x1, matrix products, shards(): jnp.einsum('nsd,ndf->sf', rows_in, gate_w, preferred_element_type=jnp.flo...  3.06 us
  transfers between devices with their start and end apart: 13, of which 6 were waited for; matrix products, arithmetic and copies ran while one was open for 33% of the time, Pallas kernels for 0%

profile of v5, /device:TPU:0, one launch (start us, length us, event | category | flops | bytes accessed | tf_op | source)
XLA Modules:
  0.0 120.1 jit_solution(24221768548688055)
XLA Ops:
  4.7 19.1 %all_to_all.20 = bf16[8,24,1024]{2,1,0:T(8,128)(2,1)S(1)} all-to-all(bf16[8,24,1024]{2,1,0:T(8,128)(2,1)S(1)} %maximum_maximum_fusion), channel_id=1, replica_groups=mesh['ctx'=4,'ep'=8] {'ep'}, dimensions={0} | all-to-all | bytes 786432 | tf_op jit(solution)/shard_map/all_to_all | solution.py:105
  23.9 1.6 %collective-permute-start = (bf16[1,192,896]{2,1,0:T(8,128)(2,1)S(1)}, bf16[1,192,896]{2,1,0:T(8,128)(2,1)S(1)}, u32[]{:S(2)}, u32[]{:S(2)}) collective-permute-start(bf16[1,192,896]{2,1,0:T(8,128)(2,1)S(1)} %get-tuple-element.12), channel_id=1, source_target_pairs={{0,16},{8,24},{16,0},{24,8},{1,17},{9,25},{17,1},{25,9},{2,18},{10... | collective-permute-start | bytes 1032200 | tf_op jit(solution)/shard_map/ppermute | solution.py:42
  25.5 6.3 %collective-permute-done = bf16[1,192,896]{2,1,0:T(8,128)(2,1)S(1)} collective-permute-done((bf16[1,192,896]{2,1,0:T(8,128)(2,1)S(1)}, bf16[1,192,896]{2,1,0:T(8,128)(2,1)S(1)}, u32[]{:S(2)}, u32[]{:S(2)}) %collective-permute-start) | collective-permute-done | bytes 344096 | tf_op jit(solution)/shard_map/ppermute | solution.py:42
  32.0 1.0 convolution_convert_fusion.2
  32.9 5.1 %all-to-all-start.1 = ((bf16[8,24,896]{2,1,0:T(8,128)(2,1)}), bf16[8,24,896]{2,1,0:T(8,128)(2,1)S(1)}, u32[]{:S(2)}, u32[]{:S(2)}) async-start(bf16[8,24,896]{2,1,0:T(8,128)(2,1)} %bitcast.34), calls=%async_computation.1 | async-start | bytes 688128 | tf_op jit(solution)/shard_map/all_to_all | solution.py:105
  38.3 1.6 %maximum_select_fusion = bf16[2,2,192,896]{3,2,1,0:T(8,128)(2,1)S(1)} fusion(bf16[2,1,192,896]{3,2,1,0:T(8,128)(2,1)} %bitcast.12, bf16[2,1,192,896]{3,2,1,0:T(8,128)(2,1)S(1)} %bitcast_select_fusion.1, pred[]{:T(512)S(6)} %eq.51), kind=kLoop, calls=%fused_computation.9 | loop fusion | flops 2064384 | bytes 2752513 | tf_op jit(solution)/shard_map/jit(_where)/select_n | solution.py:44
  39.9 1.3 %select_n.174 = bf16[688128]{0:T(1024)(128)(2,1)S(1)} reshape(bf16[2,2,192,896]{3,2,1,0:T(8,128)(2,1)S(1)} %maximum_select_fusion) | data formatting | bytes 2752512 | tf_op jit(solution)/shard_map/jit(_where)/select_n | solution.py:44
  42.4 6.9 %all-to-all-done.1 = bf16[8,24,896]{2,1,0:T(8,128)(2,1)S(1)} async-done(((bf16[8,24,896]{2,1,0:T(8,128)(2,1)}), bf16[8,24,896]{2,1,0:T(8,128)(2,1)S(1)}, u32[]{:S(2)}, u32[]{:S(2)}) %all-to-all-start.1) | async-done | bytes 344096 | tf_op jit(solution)/shard_map/all_to_all | solution.py:105
  49.3 1.6 %collective-permute-start.4 = (bf16[1,192,896]{2,1,0:T(8,128)(2,1)S(1)}, bf16[1,192,896]{2,1,0:T(8,128)(2,1)S(1)}, u32[]{:S(2)}, u32[]{:S(2)}) collective-permute-start(bf16[1,192,896]{2,1,0:T(8,128)(2,1)S(1)} %bitcast.176), channel_id=1, source_target_pairs={{0,16},{8,24},{16,0},{24,8},{1,17},{9,25},{17,1},{25,9},{2,18},{10... | collective-permute-start | bytes 1032200 | tf_op jit(solution)/shard_map/ppermute | solution.py:42
  50.9 3.1 %convolution_bitcast_fusion.5 = f32[192,512]{1,0:T(8,128)S(1)} fusion(bf16[4,192,896]{2,1,0:T(8,128)(2,1)S(1)} %bitcast.156, bf16[4,896,512]{2,1,0:T(8,128)(2,1)} %bitcast.170), kind=kOutput, calls=%fused_computation.30 | convolution fusion | flops 704643072 | bytes 5439488 | tf_op jit(solution)/shard_map/nsd,ndf->sf/dot_general | solution.py:123
  54.1 1.6 %multiply_convert_fusion.2 = (bf16[192,512]{1,0:T(8,128)(2,1)S(1)}, f32[192,512]{1,0:T(8,128)}) fusion(f32[192,512]{1,0:T(8,128)S(1)} %convolution_bitcast_fusion.5, bf16[4,192,896]{2,1,0:T(8,128)(2,1)S(1)} %bitcast.157, bf16[4,896,512]{2,1,0:T(8,128)(2,1)S(1)} %bitcast.172), kind=kOutput, calls=%fused_computation.59 | convolution fusion | flops 705232896 | bytes 6029312 | tf_op jit(solution)/shard_map/nsd,ndf->sf/dot_general | solution.py:124
  55.7 3.0 %collective-permute-done.4 = bf16[1,192,896]{2,1,0:T(8,128)(2,1)S(1)} collective-permute-done((bf16[1,192,896]{2,1,0:T(8,128)(2,1)S(1)}, bf16[1,192,896]{2,1,0:T(8,128)(2,1)S(1)}, u32[]{:S(2)}, u32[]{:S(2)}) %collective-permute-start.4) | collective-permute-done | bytes 344096 | tf_op jit(solution)/shard_map/ppermute | solution.py:42
  63.9 1.2 %convolution_add_fusion.1 = f32[192,512]{1,0:T(8,128)} fusion(f32[192,512]{1,0:T(8,128)S(1)} %convolution_add_fusion.2, bf16[512,3584]{1,0:T(8,128)(2,1)S(1)} %bitcast.193, bf16[4,192,896]{2,1,0:T(8,128)(2,1)S(1)} %bitcast.167), kind=kOutput, calls=%fused_computation.27 | convolution fusion | flops 176259072 | bytes 2048000 | tf_op jit(solution)/shard_map/dot_general | solution.py:143
  65.1 1.5 %collective-permute-start.7 = (f32[192]{0:T(256)S(1)}, f32[192]{0:T(256)S(1)}, u32[]{:S(2)}, u32[]{:S(2)}) collective-permute-start(f32[192]{0:T(256)S(1)} %add.113), channel_id=1, source_target_pairs={{0,16},{8,24},{16,0},{24,8},{1,17},{9,25},{17,1},{25,9},{2,18},{10... | collective-permute-start | bytes 2312 | tf_op jit(solution)/shard_map/ppermute | solution.py:74
  66.8 1.2 reshape.429
  69.3 1.2 slice.125
  71.1 2.3 %fusion.26 = (bf16[192,512,1]{1,0,2:T(8,128)(2,1)S(1)}, bf16[192,512]{1,0:T(8,128)(2,1)S(1)}) fusion(f32[192,512]{1,0:T(8,128)} %copy-done.11, f32[192,512]{1,0:T(8,128)} %get-tuple-element.16, f32[]{:T(128)} %bitcast.47, f32[192,512]{1,0:T(8,128)} %convolution_add_fusion.1, bf16[512,3584]{1,0:T(8,128)(2,1)} %bitcast.186, ...), kind=kOutput, calls=%fused_computation.72 | convolution fusion | flops 177733632 | bytes 2835712 | tf_op jit(solution)/shard_map/dot_general | solution.py:143
  73.9 1.4 %fusion.28 = f32[192,4,896]{2,0,1:T(8,128)S(1)} fusion(bf16[4,896,512]{2,1,0:T(8,128)(2,1)S(1)} %bitcast.171, bf16[192,512]{1,0:T(8,128)(2,1)S(1)} %get-tuple-element.10), kind=kOutput, calls=%fused_computation.74 | convolution fusion | flops 704643072 | bytes 6619136 | tf_op jit(solution)/shard_map/sf,ndf->nsd/dot_general | solution.py:151
  75.9 1.4 %fusion.1 = f32[192,4,896]{2,0,1:T(8,128)S(1)} fusion(f32[192,4,896]{2,0,1:T(8,128)S(1)} %fusion.28, bf16[192,512,1]{1,0,2:T(8,128)(2,1)S(1)} %get-tuple-element.9, bf16[4,896,512]{2,1,0:T(8,128)(2,1)S(1)} %bitcast.173), kind=kOutput, calls=%fused_computation.6 | convolution fusion | flops 706707456 | bytes 9371648 | tf_op jit(solution)/shard_map/sf,ndf->nsd/dot_general | solution.py:153
  77.4 1.5 %copy-done.1 = f32[192,4,896]{2,0,1:T(8,128)} copy-done((f32[192,4,896]{2,0,1:T(8,128)}, f32[192,4,896]{2,0,1:T(8,128)S(1)}, u32[]{:S(2)}) %copy-start.1) | copy-done | bytes 2752536
  78.9 1.0 fusion.18
  81.6 1.1 fusion.20
  83.0 1.7 %maximum_maximum_fusion.1 = bf16[8,24,1024]{2,1,0:T(8,128)(2,1)} fusion(bf16[8,24,1]{2,1,0:T(8,128)(2,1)} %concatenate.63, bf16[8,24,1]{2,1,0:T(8,128)(2,1)} %concatenate.62, bf16[8,24,896]{2,1,0:T(8,128)(2,1)S(1)} %bitcast.179, bf16[1024]{0:T(1024)(128)(2,1)S(1)} %pad.35.clone), kind=kLoop, calls=%fused_computation.56 | loop fusion | flops 1572864 | bytes 740096 | tf_op jit(solution)/shard_map/concatenate | solution.py:81
  84.7 4.3 %all-to-all-start.2 = ((bf16[8,24,1024]{2,1,0:T(8,128)(2,1)}), bf16[8,24,1024]{2,1,0:T(8,128)(2,1)S(1)}, u32[]{:S(2)}, u32[]{:S(2)}) async-start(bf16[8,24,1024]{2,1,0:T(8,128)(2,1)} %maximum_maximum_fusion.1), calls=%async_computation.2 | async-start | bytes 786432 | tf_op jit(solution)/shard_map/all_to_all | solution.py:105
  90.2 2.2 %fusion.4 = f32[1,2,192,896]{3,2,1,0:T(8,128)S(1)} fusion(bf16[2,192,896]{2,1,0:T(8,128)(2,1)} %collective-permute-done.8, f32[2,2,192,896]{3,2,1,0:T(8,128)} %bitcast.161, pred[]{:T(512)S(6)} %eq.51), kind=kLoop, calls=%fused_computation.15 | loop fusion | flops 1032192 | bytes 4816897 | tf_op jit(solution)/shard_map/reshape | solution.py:59
  92.5 1.6 %collective-permute-start.9 = (bf16[1,192,896]{2,1,0:T(8,128)(2,1)S(1)}, bf16[1,192,896]{2,1,0:T(8,128)(2,1)S(1)}, u32[]{:S(2)}, u32[]{:S(2)}) collective-permute-start(bf16[1,192,896]{2,1,0:T(8,128)(2,1)S(1)} %fusion.24), channel_id=1, source_target_pairs={{0,16},{8,24},{16,0},{24,8},{1,17},{9,25},{17,1},{25,9},{2,18},{10... | collective-permute-start | bytes 1032200 | tf_op jit(solution)/shard_map/ppermute | solution.py:65
  94.1 3.0 %convolution_convert_fusion = bf16[4,896,512]{2,1,0:T(8,128)(2,1)} fusion(bf16[4,192,896]{2,1,0:T(8,128)(2,1)S(1)} %bitcast.158, bf16[192,512,1]{1,0,2:T(8,128)(2,1)S(1)} %copy-done.8), kind=kOutput, calls=%fused_computation.4 | convolution fusion | flops 706478080 | bytes 5242880 | tf_op jit(solution)/shard_map/nsd,sf->ndf/dot_general | solution.py:161
  97.1 5.7 %collective-permute-done.9 = bf16[1,192,896]{2,1,0:T(8,128)(2,1)S(1)} collective-permute-done((bf16[1,192,896]{2,1,0:T(8,128)(2,1)S(1)}, bf16[1,192,896]{2,1,0:T(8,128)(2,1)S(1)}, u32[]{:S(2)}, u32[]{:S(2)}) %collective-permute-start.9) | collective-permute-done | bytes 344096 | tf_op jit(solution)/shard_map/ppermute | solution.py:65
  103.6 5.7 %all-to-all-start.3 = ((bf16[8,24,896]{2,1,0:T(8,128)(2,1)}), bf16[8,24,896]{2,1,0:T(8,128)(2,1)S(1)}, u32[]{:S(2)}, u32[]{:S(2)}) async-start(bf16[8,24,896]{2,1,0:T(8,128)(2,1)} %bitcast.59), calls=%async_computation.3 | async-start | bytes 688128 | tf_op jit(solution)/shard_map/all_to_all | solution.py:105
  109.3 3.0 %convolution_convert_fusion.1 = bf16[4,896,512]{2,1,0:T(8,128)(2,1)} fusion(bf16[4,192,896]{2,1,0:T(8,128)(2,1)S(1)} %bitcast.159, bf16[192,512]{1,0:T(8,128)(2,1)S(1)} %get-tuple-element.10), kind=kOutput, calls=%fused_computation.5 | convolution fusion | flops 706478080 | bytes 5242880 | tf_op jit(solution)/shard_map/nsd,sf->ndf/dot_general | solution.py:158
  113.1 1.0 fusion.7
  114.1 5.1 %all-to-all-done.3 = bf16[8,24,896]{2,1,0:T(8,128)(2,1)S(1)} async-done(((bf16[8,24,896]{2,1,0:T(8,128)(2,1)}), bf16[8,24,896]{2,1,0:T(8,128)(2,1)S(1)}, u32[]{:S(2)}, u32[]{:S(2)}) %all-to-all-start.3) | async-done | bytes 344096 | tf_op jit(solution)/shard_map/all_to_all | solution.py:105
  (82 shorter events, 18.1 us)
Async XLA Ops:
  0.6 3.6 %copy-start = (bf16[128,896]{1,0:T(8,128)(2,1)S(1)}, bf16[128,896]{1,0:T(8,128)(2,1)}, u32[]{:S(2)}) copy-start(bf16[128,896]{1,0:T(8,128)(2,1)} %param.7) | copy-start | bytes 688132
  23.9 8.1 %copy-start.9 = (bf16[128,896]{1,0:T(8,128)(2,1)S(1)}, bf16[128,896]{1,0:T(8,128)(2,1)}, u32[]{:S(2)}) copy-start(bf16[128,896]{1,0:T(8,128)(2,1)} %param.8) | copy-start | bytes 688132
  23.9 7.8 %collective-permute-start = (bf16[1,192,896]{2,1,0:T(8,128)(2,1)S(1)}, bf16[1,192,896]{2,1,0:T(8,128)(2,1)S(1)}, u32[]{:S(2)}, u32[]{:S(2)}) collective-permute-start(bf16[1,192,896]{2,1,0:T(8,128)(2,1)S(1)} %get-tuple-element.12), channel_id=1, source_target_pairs={{0,16},{8,24},{16,0},{24,8},{1,17},{9,25},{17,1},{25,9},{2,18},{10... | collective-permute-start | bytes 1032200 | tf_op jit(solution)/shard_map/ppermute | solution.py:42
  31.9 6.5 %collective-permute-start.1 = (bf16[2,192,896]{2,1,0:T(8,128)(2,1)S(1)}, bf16[2,192,896]{2,1,0:T(8,128)(2,1)}, u32[]{:S(2)}, u32[]{:S(2)}) collective-permute-start(bf16[2,192,896]{2,1,0:T(8,128)(2,1)S(1)} %maximum_select_fusion.2), channel_id=1, source_target_pairs={{0,8},{8,0},{16,24},{24,16},{1,9},{9,1},{17,25},{25,17},{2,10},{10... | collective-permute-start | bytes 2064392 | tf_op jit(solution)/shard_map/ppermute | solution.py:42
  32.9 16.3 %all-to-all-start.1 = ((bf16[8,24,896]{2,1,0:T(8,128)(2,1)}), bf16[8,24,896]{2,1,0:T(8,128)(2,1)S(1)}, u32[]{:S(2)}, u32[]{:S(2)}) async-start(bf16[8,24,896]{2,1,0:T(8,128)(2,1)} %bitcast.34), calls=%async_computation.1 | async-start | bytes 688128 | tf_op jit(solution)/shard_map/all_to_all | solution.py:105
  49.3 9.4 %collective-permute-start.4 = (bf16[1,192,896]{2,1,0:T(8,128)(2,1)S(1)}, bf16[1,192,896]{2,1,0:T(8,128)(2,1)S(1)}, u32[]{:S(2)}, u32[]{:S(2)}) collective-permute-start(bf16[1,192,896]{2,1,0:T(8,128)(2,1)S(1)} %bitcast.176), channel_id=1, source_target_pairs={{0,16},{8,24},{16,0},{24,8},{1,17},{9,25},{17,1},{25,9},{2,18},{10... | collective-permute-start | bytes 1032200 | tf_op jit(solution)/shard_map/ppermute | solution.py:42
  50.9 3.1 %copy-start.4 = (bf16[1,3584,512]{2,1,0:T(8,128)(2,1)S(1)}, bf16[1,3584,512]{2,1,0:T(8,128)(2,1)}, u32[]{:S(2)}) copy-start(bf16[1,3584,512]{2,1,0:T(8,128)(2,1)} %param.12) | copy-start | bytes 11010052
  54.0 1.7 %copy-start.11 = (f32[192,512]{1,0:T(8,128)}, f32[192,512]{1,0:T(8,128)S(1)}, u32[]{:S(2)}) copy-start(f32[192,512]{1,0:T(8,128)S(1)} %convolution_bitcast_fusion.5) | copy-start | bytes 1179652
  54.1 4.9 %copy-start.6 = (bf16[1,512,3584]{2,1,0:T(8,128)(2,1)S(1)}, bf16[1,512,3584]{2,1,0:T(8,128)(2,1)}, u32[]{:S(2)}) copy-start(bf16[1,512,3584]{2,1,0:T(8,128)(2,1)} %param.13) | copy-start | bytes 11010052
  58.9 2.2 %collective-permute-start.5 = (bf16[2,192,896]{2,1,0:T(8,128)(2,1)S(1)}, bf16[2,192,896]{2,1,0:T(8,128)(2,1)S(1)}, u32[]{:S(2)}, u32[]{:S(2)}) collective-permute-start(bf16[2,192,896]{2,1,0:T(8,128)(2,1)S(1)} %maximum_select_fusion.4), channel_id=1, source_target_pairs={{0,8},{8,0},{16,24},{24,16},{1,9},{9,1},{17,25},{25,17},{2,10},{10... | collective-permute-start | bytes 2064392 | tf_op jit(solution)/shard_map/ppermute | solution.py:42
  61.5 2.4 %copy-start.2 = (bf16[2,2,192,896]{3,2,1,0:T(8,128)(2,1)}, bf16[2,2,192,896]{3,2,1,0:T(8,128)(2,1)S(1)}, u32[]{:S(2)}) copy-start(bf16[2,2,192,896]{3,2,1,0:T(8,128)(2,1)S(1)} %copy.55) | copy-start | bytes 4128772
  62.0 3.1 %collective-permute-start.6 = (f32[192]{0:T(256)S(1)}, f32[192]{0:T(256)S(1)}, u32[]{:S(2)}, u32[]{:S(2)}) collective-permute-start(f32[192]{0:T(256)S(1)} %get-tuple-element.5), channel_id=1, source_target_pairs={{0,8},{8,0},{16,24},{24,16},{1,9},{9,1},{17,25},{25,17},{2,10},{10... | collective-permute-start | bytes 2312 | tf_op jit(solution)/shard_map/ppermute | solution.py:74
  62.5 4.1 %collective-permute-start.2 = (bf16[2,192,896]{2,1,0:T(8,128)(2,1)S(1)}, bf16[2,192,896]{2,1,0:T(8,128)(2,1)S(1)}, u32[]{:S(2)}, u32[]{:S(2)}) collective-permute-start(bf16[2,192,896]{2,1,0:T(8,128)(2,1)S(1)} %fusion.17), channel_id=1, source_target_pairs={{0,8},{8,0},{16,24},{24,16},{1,9},{9,1},{17,25},{25,17},{2,10},{10... | collective-permute-start | bytes 2064392 | tf_op jit(solution)/shard_map/ppermute | solution.py:65
  65.1 14.8 %collective-permute-start.7 = (f32[192]{0:T(256)S(1)}, f32[192]{0:T(256)S(1)}, u32[]{:S(2)}, u32[]{:S(2)}) collective-permute-start(f32[192]{0:T(256)S(1)} %add.113), channel_id=1, source_target_pairs={{0,16},{8,24},{16,0},{24,8},{1,17},{9,25},{17,1},{25,9},{2,18},{10... | collective-permute-start | bytes 2312 | tf_op jit(solution)/shard_map/ppermute | solution.py:74
  68.8 12.8 %collective-permute-start.3 = (bf16[1,192,896]{2,1,0:T(8,128)(2,1)}, bf16[1,192,896]{2,1,0:T(8,128)(2,1)}, u32[]{:S(2)}, u32[]{:S(2)}) collective-permute-start(bf16[1,192,896]{2,1,0:T(8,128)(2,1)} %fusion.22), channel_id=1, source_target_pairs={{0,16},{8,24},{16,0},{24,8},{1,17},{9,25},{17,1},{25,9},{2,18},{10... | collective-permute-start | bytes 1032200 | tf_op jit(solution)/shard_map/ppermute | solution.py:65
  71.1 2.8 %copy-start.3 = (bf16[1,3584,512]{2,1,0:T(8,128)(2,1)S(1)}, bf16[1,3584,512]{2,1,0:T(8,128)(2,1)}, u32[]{:S(2)}) copy-start(bf16[1,3584,512]{2,1,0:T(8,128)(2,1)} %param.11) | copy-start | bytes 11010052
  73.5 1.8 %copy-start.7 = (bf16[192,512,1]{1,0,2:T(8,128)(2,1)}, bf16[192,512,1]{1,0,2:T(8,128)(2,1)S(1)}, u32[]{:S(2)}) copy-start(bf16[192,512,1]{1,0,2:T(8,128)(2,1)S(1)} %get-tuple-element.9) | copy-start | bytes 589828
  73.9 2.0 %copy-start.5 = (bf16[1,3584,512]{2,1,0:T(8,128)(2,1)S(1)}, bf16[1,3584,512]{2,1,0:T(8,128)(2,1)}, u32[]{:S(2)}) copy-start(bf16[1,3584,512]{2,1,0:T(8,128)(2,1)} %param.12) | copy-start | bytes 11010052
  77.4 1.5 %copy-start.1 = (f32[192,4,896]{2,0,1:T(8,128)}, f32[192,4,896]{2,0,1:T(8,128)S(1)}, u32[]{:S(2)}) copy-start(f32[192,4,896]{2,0,1:T(8,128)S(1)} %fusion.1) | copy-start | bytes 8257540
  79.9 10.3 %collective-permute-start.8 = (bf16[2,192,896]{2,1,0:T(8,128)(2,1)}, bf16[2,192,896]{2,1,0:T(8,128)(2,1)}, u32[]{:S(2)}, u32[]{:S(2)}) collective-permute-start(bf16[2,192,896]{2,1,0:T(8,128)(2,1)} %fusion.18), channel_id=1, source_target_pairs={{0,8},{8,0},{16,24},{24,16},{1,9},{9,1},{17,25},{25,17},{2,10},{10... | collective-permute-start | bytes 2064392 | tf_op jit(solution)/shard_map/ppermute | solution.py:65
  84.7 18.9 %all-to-all-start.2 = ((bf16[8,24,1024]{2,1,0:T(8,128)(2,1)}), bf16[8,24,1024]{2,1,0:T(8,128)(2,1)S(1)}, u32[]{:S(2)}, u32[]{:S(2)}) async-start(bf16[8,24,1024]{2,1,0:T(8,128)(2,1)} %maximum_maximum_fusion.1), calls=%async_computation.2 | async-start | bytes 786432 | tf_op jit(solution)/shard_map/all_to_all | solution.py:105
  90.2 3.9 %copy-start.8 = (bf16[192,512,1]{1,0,2:T(8,128)(2,1)S(1)}, bf16[192,512,1]{1,0,2:T(8,128)(2,1)}, u32[]{:S(2)}) copy-start(bf16[192,512,1]{1,0,2:T(8,128)(2,1)} %copy-done.7) | copy-start | bytes 589828
  92.5 10.3 %collective-permute-start.9 = (bf16[1,192,896]{2,1,0:T(8,128)(2,1)S(1)}, bf16[1,192,896]{2,1,0:T(8,128)(2,1)S(1)}, u32[]{:S(2)}, u32[]{:S(2)}) collective-permute-start(bf16[1,192,896]{2,1,0:T(8,128)(2,1)S(1)} %fusion.24), channel_id=1, source_target_pairs={{0,16},{8,24},{16,0},{24,8},{1,17},{9,25},{17,1},{25,9},{2,18},{10... | collective-permute-start | bytes 1032200 | tf_op jit(solution)/shard_map/ppermute | solution.py:65
  103.6 15.6 %all-to-all-start.3 = ((bf16[8,24,896]{2,1,0:T(8,128)(2,1)}), bf16[8,24,896]{2,1,0:T(8,128)(2,1)S(1)}, u32[]{:S(2)}, u32[]{:S(2)}) async-start(bf16[8,24,896]{2,1,0:T(8,128)(2,1)} %bitcast.59), calls=%async_computation.3 | async-start | bytes 688128 | tf_op jit(solution)/shard_map/all_to_all | solution.py:105
  109.3 3.8 %copy-start.10 = (f32[128,1]{0,1:T(1,128)S(1)}, f32[128,1]{0,1:T(1,128)}, u32[]{:S(2)}) copy-start(f32[128,1]{0,1:T(1,128)} %param.10) | copy-start | bytes 1540

commit v6 on v4

--- a/solution.py
+++ b/solution.py
@@ -48,6 +48,11 @@
     return held
 
 
+def after(values, *needed):
+    zero = sum(jnp.ravel(x)[0].astype(jnp.float32) for x in needed) * 0.0
+    return values + zero.astype(values.dtype)
+
+
 def scatter_sum(blocks, n_ctx, me, wait_for=None):
     acc = blocks
     for bit in range(ctx_bits(n_ctx)):
@@ -56,7 +61,7 @@
         keep = jnp.where(keep_first, halves[:, 0], halves[:, 1])
         send = jnp.where(keep_first, halves[:, 1], halves[:, 0]).astype(jnp.bfloat16)
         if bit == 1 and wait_for is not None:
-            send, _ = lax.optimization_barrier((send, wait_for))
+            send = after(send, wait_for)
         got = lax.ppermute(send, "ctx", xor_pairs(n_ctx, bit))
         acc = keep + got.astype(jnp.float32)
     return acc[0]

time: 107 us -> 113 us (1.056)
  waiting for transfers between devices: 42.3 us -> 36.7 us
  other arithmetic: 11.1 us -> 15.4 us
  local copies, waits for them, and re-layouts: 6.46 us -> 10.3 us
  matrix products: 17 us -> 19 us
  starting transfers between devices: 28.1 us -> 29.3 us
    all_to_all x4, waiting for transfers between devices: 17.8 us -> 12.4 us  [to_experts(): got = lax.all_to_all(sent, 'ep', split_axis=0, concat_axis=0, tiled=True)]
    reshape x2, other arithmetic: 0.34 us -> 2.62 us  [scatter_sum(): halves = acc.reshape((-1, 2) + acc.shape[1:])]
    all_to_all x4, starting transfers between devices: 20.2 us -> 22.3 us  [to_experts(): got = lax.all_to_all(sent, 'ep', split_axis=0, concat_axis=0, tiled=True)]
    unnamed x20 -> x24, local copies, waits for them, and re-layouts: 4.13 us -> 5.68 us
    ppermute x2, waiting for transfers between devices: 1.64 us -> 0.15 us  [all_sum(): values = values + lax.ppermute(values, 'ctx', xor_pairs(n_ctx, bit))]
    ppermute x4, waiting for transfers between devices: 7.95 us -> 9.2 us  [scatter_sum(): got = lax.ppermute(send, 'ctx', xor_pairs(n_ctx, bit))]
    slice x0 -> x1, local copies, waits for them, and re-layouts: none -> 1.19 us  [after(): zero = sum((jnp.ravel(x)[0].astype(jnp.float32) for x in needed)) * 0.0]
  transfers between devices with their start and end apart: 14 -> 14, of which waited for: 8 -> 8; matrix products, arithmetic and copies ran while one was open for 17% -> 23% of each run, Pallas kernels for 0% -> 0%
where the time goes in v6:
time: 113 us; the launch traced here: 112 us
  waiting for transfers between devices  36.7 us (32%)
  starting transfers between devices  29.3 us (26%)
  matrix products  19 us (17%)
  other arithmetic  15.4 us (14%)
  local copies, waits for them, and re-layouts  10.3 us (9%)
  between operations  1.64 us (1%)
    all_to_all x4, starting transfers between devices, to_experts(): got = lax.all_to_all(sent, 'ep', split_axis=0, concat_axis=0, tiled=True)  22.3 us
    ppermute x4, waiting for transfers between devices, gather_blocks(): other = lax.ppermute(held, 'ctx', xor_pairs(n_ctx, bit))  15 us
    all_to_all x4, waiting for transfers between devices, to_experts(): got = lax.all_to_all(sent, 'ep', split_axis=0, concat_axis=0, tiled=True)  12.4 us
    ppermute x4, waiting for transfers between devices, scatter_sum(): got = lax.ppermute(send, 'ctx', xor_pairs(n_ctx, bit))  9.2 us
    unnamed x24, local copies, waits for them, and re-layouts  5.68 us
    dot_general x1, matrix products, shards(): jnp.einsum('nsd,sf->ndf', rows_in, grad_up, preferred_element_type=jnp.fl...  3.92 us
    ppermute x4, starting transfers between devices, gather_blocks(): other = lax.ppermute(held, 'ctx', xor_pairs(n_ctx, bit))  3.17 us
    dot_general x1, matrix products, shards(): jnp.einsum('nsd,sf->ndf', rows_in, grad_gate, preferred_element_type=jnp....  2.99 us
  transfers between devices with their start and end apart: 14, of which 8 were waited for; matrix products, arithmetic and copies ran while one was open for 23% of the time, Pallas kernels for 0%

profile of v6, /device:TPU:0, one launch (start us, length us, event | category | flops | bytes accessed | tf_op | source)
XLA Modules:
  0.0 112.2 jit_solution(10885027494417340679)
XLA Ops:
  3.1 1.0 convolution_convert_fusion.2
  4.1 7.3 %all-to-all-start.1 = ((bf16[8,24,896]{2,1,0:T(8,128)(2,1)}), bf16[8,24,896]{2,1,0:T(8,128)(2,1)S(1)}, u32[]{:S(2)}, u32[]{:S(2)}) async-start(bf16[8,24,896]{2,1,0:T(8,128)(2,1)} %bitcast.34), calls=%async_computation.1 | async-start | bytes 688128 | tf_op jit(solution)/shard_map/all_to_all | solution.py:103
  13.1 9.0 %all-to-all-done.1 = bf16[8,24,896]{2,1,0:T(8,128)(2,1)S(1)} async-done(((bf16[8,24,896]{2,1,0:T(8,128)(2,1)}), bf16[8,24,896]{2,1,0:T(8,128)(2,1)S(1)}, u32[]{:S(2)}, u32[]{:S(2)}) %all-to-all-start.1) | async-done | bytes 344096 | tf_op jit(solution)/shard_map/all_to_all | solution.py:103
  22.0 3.6 %all-to-all-start = ((bf16[8,24,1024]{2,1,0:T(8,128)(2,1)}), bf16[8,24,1024]{2,1,0:T(8,128)(2,1)S(1)}, u32[]{:S(2)}, u32[]{:S(2)}) async-start(bf16[8,24,1024]{2,1,0:T(8,128)(2,1)} %maximum_maximum_fusion), calls=%async_computation | async-start | bytes 786432 | tf_op jit(solution)/shard_map/all_to_all | solution.py:103
  25.6 1.5 %collective-permute-start.4 = (bf16[1,192,896]{2,1,0:T(8,128)(2,1)S(1)}, bf16[1,192,896]{2,1,0:T(8,128)(2,1)S(1)}, u32[]{:S(2)}, u32[]{:S(2)}) collective-permute-start(bf16[1,192,896]{2,1,0:T(8,128)(2,1)S(1)} %bitcast.175), channel_id=1, source_target_pairs={{0,16},{8,24},{16,0},{24,8},{1,17},{9,25},{17,1},{25,9},{2,18},{10... | collective-permute-start | bytes 1032200 | tf_op jit(solution)/shard_map/ppermute | solution.py:42
  27.2 7.5 %collective-permute-done.4 = bf16[1,192,896]{2,1,0:T(8,128)(2,1)S(1)} collective-permute-done((bf16[1,192,896]{2,1,0:T(8,128)(2,1)S(1)}, bf16[1,192,896]{2,1,0:T(8,128)(2,1)S(1)}, u32[]{:S(2)}, u32[]{:S(2)}) %collective-permute-start.4) | collective-permute-done | bytes 344096 | tf_op jit(solution)/shard_map/ppermute | solution.py:42
  34.7 1.0 maximum_select_fusion.4
  35.7 1.2 %all-to-all-done = bf16[8,24,1024]{2,1,0:T(8,128)(2,1)S(1)} async-done(((bf16[8,24,1024]{2,1,0:T(8,128)(2,1)}), bf16[8,24,1024]{2,1,0:T(8,128)(2,1)S(1)}, u32[]{:S(2)}, u32[]{:S(2)}) %all-to-all-start) | async-done | bytes 393248 | tf_op jit(solution)/shard_map/all_to_all | solution.py:103
  37.0 1.6 %collective-permute-start = (bf16[1,192,896]{2,1,0:T(8,128)(2,1)S(1)}, bf16[1,192,896]{2,1,0:T(8,128)(2,1)S(1)}, u32[]{:S(2)}, u32[]{:S(2)}) collective-permute-start(bf16[1,192,896]{2,1,0:T(8,128)(2,1)S(1)} %get-tuple-element.13), channel_id=1, source_target_pairs={{0,16},{8,24},{16,0},{24,8},{1,17},{9,25},{17,1},{25,9},{2,18},{10... | collective-permute-start | bytes 1032200 | tf_op jit(solution)/shard_map/ppermute | solution.py:42
  38.9 7.4 %collective-permute-done = bf16[1,192,896]{2,1,0:T(8,128)(2,1)S(1)} collective-permute-done((bf16[1,192,896]{2,1,0:T(8,128)(2,1)S(1)}, bf16[1,192,896]{2,1,0:T(8,128)(2,1)S(1)}, u32[]{:S(2)}, u32[]{:S(2)}) %collective-permute-start) | collective-permute-done | bytes 344096 | tf_op jit(solution)/shard_map/ppermute | solution.py:42
  47.0 1.6 %copy-done.8 = bf16[1,512,3584]{2,1,0:T(8,128)(2,1)S(1)} copy-done((bf16[1,512,3584]{2,1,0:T(8,128)(2,1)S(1)}, bf16[1,512,3584]{2,1,0:T(8,128)(2,1)}, u32[]{:S(2)}) %copy-start.8) | copy-done | bytes 3670040
  50.3 1.8 %copy-done.7 = bf16[1,3584,512]{2,1,0:T(8,128)(2,1)S(1)} copy-done((bf16[1,3584,512]{2,1,0:T(8,128)(2,1)S(1)}, bf16[1,3584,512]{2,1,0:T(8,128)(2,1)}, u32[]{:S(2)}) %copy-start.7) | copy-done | bytes 3670040
  53.0 1.1 %copy-done.6 = bf16[1,3584,512]{2,1,0:T(8,128)(2,1)S(1)} copy-done((bf16[1,3584,512]{2,1,0:T(8,128)(2,1)S(1)}, bf16[1,3584,512]{2,1,0:T(8,128)(2,1)}, u32[]{:S(2)}) %copy-start.6) | copy-done | bytes 3670040
  58.7 1.3 %fusion.28 = f32[192,4,896]{2,0,1:T(8,128)S(1)} fusion(bf16[4,896,512]{2,1,0:T(8,128)(2,1)S(1)} %bitcast.170, bf16[192,512]{1,0:T(8,128)(2,1)S(1)} %get-tuple-element.10), kind=kOutput, calls=%fused_computation.74 | convolution fusion | flops 704643072 | bytes 6619136 | tf_op jit(solution)/shard_map/sf,ndf->nsd/dot_general | solution.py:146
  60.0 1.3 %fusion.1 = f32[192,4,896]{2,0,1:T(8,128)S(1)} fusion(f32[192,4,896]{2,0,1:T(8,128)S(1)} %fusion.28, bf16[192,512,1]{1,0,2:T(8,128)(2,1)S(1)} %get-tuple-element.9, bf16[4,896,512]{2,1,0:T(8,128)(2,1)S(1)} %bitcast.172), kind=kOutput, calls=%fused_computation.6 | convolution fusion | flops 706707456 | bytes 9371648 | tf_op jit(solution)/shard_map/sf,ndf->nsd/dot_general | solution.py:148
  61.4 1.0 fusion.18
  62.8 1.5 %collective-permute-start.7 = (f32[192]{0:T(256)S(1)}, f32[192]{0:T(256)S(1)}, u32[]{:S(2)}, u32[]{:S(2)}) collective-permute-start(f32[192]{0:T(256)S(1)} %add.76), channel_id=1, source_target_pairs={{0,16},{8,24},{16,0},{24,8},{1,17},{9,25},{17,1},{25,9},{2,18},{10... | collective-permute-start | bytes 2312 | tf_op jit(solution)/shard_map/ppermute | solution.py:72
  64.5 1.1 copy-done.4
  68.1 2.5 %fusion.5 = f32[1,2,192,896]{3,2,1,0:T(8,128)} fusion(bf16[2,192,896]{2,1,0:T(8,128)(2,1)} %collective-permute-done.8, f32[2,2,192,896]{3,2,1,0:T(8,128)S(1)} %bitcast.158, pred[]{:T(512)S(6)} %eq.51), kind=kLoop, calls=%fused_computation.16 | loop fusion | flops 1032192 | bytes 4816897 | tf_op jit(solution)/shard_map/reshape | solution.py:59
  70.6 5.0 %collective-permute-done.3 = bf16[1,192,896]{2,1,0:T(8,128)(2,1)} collective-permute-done((bf16[1,192,896]{2,1,0:T(8,128)(2,1)S(1)}, bf16[1,192,896]{2,1,0:T(8,128)(2,1)}, u32[]{:S(2)}, u32[]{:S(2)}) %collective-permute-start.3) | collective-permute-done | bytes 344096 | tf_op jit(solution)/shard_map/ppermute | solution.py:65
  75.6 1.1 fusion.20
  76.7 1.1 convert_element_type.236
  77.8 1.8 %maximum_maximum_fusion.1 = bf16[8,24,1024]{2,1,0:T(8,128)(2,1)} fusion(bf16[8,24,1]{2,1,0:T(8,128)(2,1)} %concatenate.63, bf16[8,24,1]{2,1,0:T(8,128)(2,1)} %concatenate.62, bf16[8,24,896]{2,1,0:T(8,128)(2,1)S(1)} %bitcast.178, bf16[1024]{0:T(1024)(128)(2,1)S(1)} %pad.35.clone), kind=kLoop, calls=%fused_computation.56 | loop fusion | flops 1572864 | bytes 740096 | tf_op jit(solution)/shard_map/concatenate | solution.py:79
  79.6 5.7 %all-to-all-start.2 = ((bf16[8,24,1024]{2,1,0:T(8,128)(2,1)}), bf16[8,24,1024]{2,1,0:T(8,128)(2,1)}, u32[]{:S(2)}, u32[]{:S(2)}) async-start(bf16[8,24,1024]{2,1,0:T(8,128)(2,1)} %maximum_maximum_fusion.1), calls=%async_computation.2 | async-start | bytes 786432 | tf_op jit(solution)/shard_map/all_to_all | solution.py:103
  85.3 1.2 %slice.120 = bf16[1]{0:T(256)(128)(2,1)} slice(bf16[172032]{0:T(1024)(128)(2,1)} %convert_element_type.236), slice={[0:1]} | slice | bytes 4 | tf_op jit(solution)/shard_map/slice | solution.py:52
  87.8 3.9 %convolution_convert_fusion = bf16[4,896,512]{2,1,0:T(8,128)(2,1)} fusion(bf16[4,192,896]{2,1,0:T(8,128)(2,1)S(1)} %bitcast.161, bf16[192,512,1]{1,0,2:T(8,128)(2,1)} %copy-done.9), kind=kOutput, calls=%fused_computation.4 | convolution fusion | flops 706478080 | bytes 5242880 | tf_op jit(solution)/shard_map/nsd,sf->ndf/dot_general | solution.py:156
  91.8 4.2 %collective-permute-done.9 = bf16[1,192,896]{2,1,0:T(8,128)(2,1)S(1)} collective-permute-done((bf16[1,192,896]{2,1,0:T(8,128)(2,1)S(1)}, bf16[1,192,896]{2,1,0:T(8,128)(2,1)S(1)}, u32[]{:S(2)}, u32[]{:S(2)}) %collective-permute-start.9) | collective-permute-done | bytes 344096 | tf_op jit(solution)/shard_map/ppermute | solution.py:65
  96.8 5.7 %all-to-all-start.3 = ((bf16[8,24,896]{2,1,0:T(8,128)(2,1)}), bf16[8,24,896]{2,1,0:T(8,128)(2,1)S(1)}, u32[]{:S(2)}, u32[]{:S(2)}) async-start(bf16[8,24,896]{2,1,0:T(8,128)(2,1)} %bitcast.57), calls=%async_computation.3 | async-start | bytes 688128 | tf_op jit(solution)/shard_map/all_to_all | solution.py:103
  102.5 3.0 %convolution_convert_fusion.1 = bf16[4,896,512]{2,1,0:T(8,128)(2,1)} fusion(bf16[4,192,896]{2,1,0:T(8,128)(2,1)S(1)} %bitcast.162, bf16[192,512]{1,0:T(8,128)(2,1)S(1)} %get-tuple-element.10), kind=kOutput, calls=%fused_computation.5 | convolution fusion | flops 706478080 | bytes 5242880 | tf_op jit(solution)/shard_map/nsd,sf->ndf/dot_general | solution.py:153
  105.5 1.0 add_reduce_fusion
  107.2 1.9 %fusion.7 = bf16[128,896]{1,0:T(8,128)(2,1)} fusion(bf16[192,1024]{1,0:T(8,128)(2,1)} %bitcast.41, f32[128]{0:T(128)S(1)} %bitcast.198, s32[128]{0:T(128)S(1)} %fusion.35), kind=kOutput, calls=%fused_computation.33 | convolution fusion | flops 44294144 | bytes 574464 | tf_op jit(solution)/shard_map/dot_general | solution.py:167
  109.1 2.2 %all-to-all-done.3 = bf16[8,24,896]{2,1,0:T(8,128)(2,1)S(1)} async-done(((bf16[8,24,896]{2,1,0:T(8,128)(2,1)}), bf16[8,24,896]{2,1,0:T(8,128)(2,1)S(1)}, u32[]{:S(2)}, u32[]{:S(2)}) %all-to-all-start.3) | async-done | bytes 344096 | tf_op jit(solution)/shard_map/all_to_all | solution.py:103
  (78 shorter events, 18.4 us)
Async XLA Ops:
  0.6 2.5 %copy-start = (bf16[128,896]{1,0:T(8,128)(2,1)S(1)}, bf16[128,896]{1,0:T(8,128)(2,1)}, u32[]{:S(2)}) copy-start(bf16[128,896]{1,0:T(8,128)(2,1)} %param.8) | copy-start | bytes 688132
  0.6 10.7 %copy-start.11 = (f32[128,1]{0,1:T(1,128)S(1)}, f32[128,1]{0,1:T(1,128)}, u32[]{:S(2)}) copy-start(f32[128,1]{0,1:T(1,128)} %param.10) | copy-start | bytes 1540
  0.7 11.3 %copy-start.10 = (bf16[128,896]{1,0:T(8,128)(2,1)S(1)}, bf16[128,896]{1,0:T(8,128)(2,1)}, u32[]{:S(2)}) copy-start(bf16[128,896]{1,0:T(8,128)(2,1)} %param.7) | copy-start | bytes 688132
  4.1 17.9 %all-to-all-start.1 = ((bf16[8,24,896]{2,1,0:T(8,128)(2,1)}), bf16[8,24,896]{2,1,0:T(8,128)(2,1)S(1)}, u32[]{:S(2)}, u32[]{:S(2)}) async-start(bf16[8,24,896]{2,1,0:T(8,128)(2,1)} %bitcast.34), calls=%async_computation.1 | async-start | bytes 688128 | tf_op jit(solution)/shard_map/all_to_all | solution.py:103
  22.0 14.9 %all-to-all-start = ((bf16[8,24,1024]{2,1,0:T(8,128)(2,1)}), bf16[8,24,1024]{2,1,0:T(8,128)(2,1)S(1)}, u32[]{:S(2)}, u32[]{:S(2)}) async-start(bf16[8,24,1024]{2,1,0:T(8,128)(2,1)} %maximum_maximum_fusion), calls=%async_computation | async-start | bytes 786432 | tf_op jit(solution)/shard_map/all_to_all | solution.py:103
  25.6 9.1 %collective-permute-start.4 = (bf16[1,192,896]{2,1,0:T(8,128)(2,1)S(1)}, bf16[1,192,896]{2,1,0:T(8,128)(2,1)S(1)}, u32[]{:S(2)}, u32[]{:S(2)}) collective-permute-start(bf16[1,192,896]{2,1,0:T(8,128)(2,1)S(1)} %bitcast.175), channel_id=1, source_target_pairs={{0,16},{8,24},{16,0},{24,8},{1,17},{9,25},{17,1},{25,9},{2,18},{10... | collective-permute-start | bytes 1032200 | tf_op jit(solution)/shard_map/ppermute | solution.py:42
  35.7 10.9 %collective-permute-start.5 = (bf16[2,192,896]{2,1,0:T(8,128)(2,1)}, bf16[2,192,896]{2,1,0:T(8,128)(2,1)S(1)}, u32[]{:S(2)}, u32[]{:S(2)}) collective-permute-start(bf16[2,192,896]{2,1,0:T(8,128)(2,1)} %maximum_select_fusion.4), channel_id=1, source_target_pairs={{0,8},{8,0},{16,24},{24,16},{1,9},{9,1},{17,25},{25,17},{2,10},{10... | collective-permute-start | bytes 2064392 | tf_op jit(solution)/shard_map/ppermute | solution.py:42
  37.0 9.3 %collective-permute-start = (bf16[1,192,896]{2,1,0:T(8,128)(2,1)S(1)}, bf16[1,192,896]{2,1,0:T(8,128)(2,1)S(1)}, u32[]{:S(2)}, u32[]{:S(2)}) collective-permute-start(bf16[1,192,896]{2,1,0:T(8,128)(2,1)S(1)} %get-tuple-element.13), channel_id=1, source_target_pairs={{0,16},{8,24},{16,0},{24,8},{1,17},{9,25},{17,1},{25,9},{2,18},{10... | collective-permute-start | bytes 1032200 | tf_op jit(solution)/shard_map/ppermute | solution.py:42
  46.4 3.7 %collective-permute-start.1 = (bf16[2,192,896]{2,1,0:T(8,128)(2,1)S(1)}, bf16[2,192,896]{2,1,0:T(8,128)(2,1)S(1)}, u32[]{:S(2)}, u32[]{:S(2)}) collective-permute-start(bf16[2,192,896]{2,1,0:T(8,128)(2,1)S(1)} %maximum_select_fusion.2), channel_id=1, source_target_pairs={{0,8},{8,0},{16,24},{24,16},{1,9},{9,1},{17,25},{25,17},{2,10},{10... | collective-permute-start | bytes 2064392 | tf_op jit(solution)/shard_map/ppermute | solution.py:42
  46.6 2.0 %copy-start.8 = (bf16[1,512,3584]{2,1,0:T(8,128)(2,1)S(1)}, bf16[1,512,3584]{2,1,0:T(8,128)(2,1)}, u32[]{:S(2)}) copy-start(bf16[1,512,3584]{2,1,0:T(8,128)(2,1)} %param.13) | copy-start | bytes 11010052
  49.6 2.5 %copy-start.7 = (bf16[1,3584,512]{2,1,0:T(8,128)(2,1)S(1)}, bf16[1,3584,512]{2,1,0:T(8,128)(2,1)}, u32[]{:S(2)}) copy-start(bf16[1,3584,512]{2,1,0:T(8,128)(2,1)} %param.12) | copy-start | bytes 11010052
  50.3 2.7 %copy-start.1 = (bf16[2,2,192,896]{3,2,1,0:T(8,128)(2,1)}, bf16[2,2,192,896]{3,2,1,0:T(8,128)(2,1)S(1)}, u32[]{:S(2)}) copy-start(bf16[2,2,192,896]{3,2,1,0:T(8,128)(2,1)S(1)} %maximum_select_fusion) | copy-start | bytes 4128772
  52.1 2.0 %copy-start.6 = (bf16[1,3584,512]{2,1,0:T(8,128)(2,1)S(1)}, bf16[1,3584,512]{2,1,0:T(8,128)(2,1)}, u32[]{:S(2)}) copy-start(bf16[1,3584,512]{2,1,0:T(8,128)(2,1)} %param.11) | copy-start | bytes 11010052
  55.7 4.3 %copy-start.9 = (bf16[192,512,1]{1,0,2:T(8,128)(2,1)}, bf16[192,512,1]{1,0,2:T(8,128)(2,1)S(1)}, u32[]{:S(2)}) copy-start(bf16[192,512,1]{1,0,2:T(8,128)(2,1)S(1)} %get-tuple-element.9) | copy-start | bytes 589828
  57.7 5.1 %collective-permute-start.6 = (f32[192]{0:T(256)S(1)}, f32[192]{0:T(256)S(1)}, u32[]{:S(2)}, u32[]{:S(2)}) collective-permute-start(f32[192]{0:T(256)S(1)} %get-tuple-element.5), channel_id=1, source_target_pairs={{0,8},{8,0},{16,24},{24,16},{1,9},{9,1},{17,25},{25,17},{2,10},{10... | collective-permute-start | bytes 2312 | tf_op jit(solution)/shard_map/ppermute | solution.py:72
  58.6 5.8 %collective-permute-start.2 = (bf16[2,192,896]{2,1,0:T(8,128)(2,1)S(1)}, bf16[2,192,896]{2,1,0:T(8,128)(2,1)S(1)}, u32[]{:S(2)}, u32[]{:S(2)}) collective-permute-start(bf16[2,192,896]{2,1,0:T(8,128)(2,1)S(1)} %fusion.17), channel_id=1, source_target_pairs={{0,8},{8,0},{16,24},{24,16},{1,9},{9,1},{17,25},{25,17},{2,10},{10... | collective-permute-start | bytes 2064392 | tf_op jit(solution)/shard_map/ppermute | solution.py:65
  62.3 5.8 %collective-permute-start.8 = (bf16[2,192,896]{2,1,0:T(8,128)(2,1)}, bf16[2,192,896]{2,1,0:T(8,128)(2,1)}, u32[]{:S(2)}, u32[]{:S(2)}) collective-permute-start(bf16[2,192,896]{2,1,0:T(8,128)(2,1)} %fusion.18), channel_id=1, source_target_pairs={{0,8},{8,0},{16,24},{24,16},{1,9},{9,1},{17,25},{25,17},{2,10},{10... | collective-permute-start | bytes 2064392 | tf_op jit(solution)/shard_map/ppermute | solution.py:65
  62.8 3.6 %collective-permute-start.7 = (f32[192]{0:T(256)S(1)}, f32[192]{0:T(256)S(1)}, u32[]{:S(2)}, u32[]{:S(2)}) collective-permute-start(f32[192]{0:T(256)S(1)} %add.76), channel_id=1, source_target_pairs={{0,16},{8,24},{16,0},{24,8},{1,17},{9,25},{17,1},{25,9},{2,18},{10... | collective-permute-start | bytes 2312 | tf_op jit(solution)/shard_map/ppermute | solution.py:72
  64.5 1.1 copy-start.4
  65.7 9.9 %collective-permute-start.3 = (bf16[1,192,896]{2,1,0:T(8,128)(2,1)S(1)}, bf16[1,192,896]{2,1,0:T(8,128)(2,1)}, u32[]{:S(2)}, u32[]{:S(2)}) collective-permute-start(bf16[1,192,896]{2,1,0:T(8,128)(2,1)S(1)} %fusion.22), channel_id=1, source_target_pairs={{0,16},{8,24},{16,0},{24,8},{1,17},{9,25},{17,1},{25,9},{2,18},{10... | collective-permute-start | bytes 1032200 | tf_op jit(solution)/shard_map/ppermute | solution.py:65
  68.1 7.5 %copy-start.5 = (f32[1,2,192,896]{3,2,1,0:T(8,128)S(1)}, f32[1,2,192,896]{3,2,1,0:T(8,128)}, u32[]{:S(2)}) copy-start(f32[1,2,192,896]{3,2,1,0:T(8,128)} %copy-done.4) | copy-start | bytes 4128772
  76.7 10.5 %copy-start.3 = (f32[1,2,192,896]{3,2,1,0:T(8,128)S(1)}, f32[1,2,192,896]{3,2,1,0:T(8,128)}, u32[]{:S(2)}) copy-start(f32[1,2,192,896]{3,2,1,0:T(8,128)} %fusion.5) | copy-start | bytes 4128772
  77.8 10.0 %copy-start.2 = (bf16[2,2,192,896]{3,2,1,0:T(8,128)(2,1)S(1)}, bf16[2,2,192,896]{3,2,1,0:T(8,128)(2,1)}, u32[]{:S(2)}) copy-start(bf16[2,2,192,896]{3,2,1,0:T(8,128)(2,1)} %copy-done.1) | copy-start | bytes 4128772
  79.6 17.2 %all-to-all-start.2 = ((bf16[8,24,1024]{2,1,0:T(8,128)(2,1)}), bf16[8,24,1024]{2,1,0:T(8,128)(2,1)}, u32[]{:S(2)}, u32[]{:S(2)}) async-start(bf16[8,24,1024]{2,1,0:T(8,128)(2,1)} %maximum_maximum_fusion.1), calls=%async_computation.2 | async-start | bytes 786432 | tf_op jit(solution)/shard_map/all_to_all | solution.py:103
  87.3 8.7 %collective-permute-start.9 = (bf16[1,192,896]{2,1,0:T(8,128)(2,1)S(1)}, bf16[1,192,896]{2,1,0:T(8,128)(2,1)S(1)}, u32[]{:S(2)}, u32[]{:S(2)}) collective-permute-start(bf16[1,192,896]{2,1,0:T(8,128)(2,1)S(1)} %fusion.24), channel_id=1, source_target_pairs={{0,16},{8,24},{16,0},{24,8},{1,17},{9,25},{17,1},{25,9},{2,18},{10... | collective-permute-start | bytes 1032200 | tf_op jit(solution)/shard_map/ppermute | solution.py:65
  96.8 14.5 %all-to-all-start.3 = ((bf16[8,24,896]{2,1,0:T(8,128)(2,1)}), bf16[8,24,896]{2,1,0:T(8,128)(2,1)S(1)}, u32[]{:S(2)}, u32[]{:S(2)}) async-start(bf16[8,24,896]{2,1,0:T(8,128)(2,1)} %bitcast.57), calls=%async_computation.3 | async-start | bytes 688128 | tf_op jit(solution)/shard_map/all_to_all | solution.py:103

commit v7 on v6

--- a/solution.py
+++ b/solution.py
@@ -129,9 +129,7 @@
     gate_part = jnp.einsum(
         "nsd,nsd->s", partial_out.astype(jnp.float32), grads_in.astype(jnp.float32)
     )
-    expert_out = scatter_sum(partial_out.astype(jnp.float32), n_ctx, me).astype(jnp.bfloat16)
     gate_sum = all_sum(gate_part, n_ctx)
-    back_out = to_experts(with_cols(expert_out, gate_sum, pad))
 
     contract_last = (((1,), (1,)), ((), ()))
     down_t = sum(
@@ -147,8 +145,12 @@
         "sf,ndf->nsd", grad_gate, gate_w, preferred_element_type=jnp.float32
     ) + jnp.einsum("sf,ndf->nsd", grad_up, up_w, preferred_element_type=jnp.float32)
     back_terms = back_terms.astype(jnp.bfloat16).astype(jnp.float32)
-    slot_grad = scatter_sum(back_terms, n_ctx, me, expert_out).astype(jnp.bfloat16)
+    slot_grad = scatter_sum(back_terms, n_ctx, me).astype(jnp.bfloat16)
     back_grad = to_experts(slot_grad)
+    expert_out = scatter_sum(
+        partial_out.astype(jnp.float32), n_ctx, me, slot_grad
+    ).astype(jnp.bfloat16)
+    back_out = to_experts(with_cols(expert_out, gate_sum, pad))
 
     w_gate_grad = jnp.einsum(
         "nsd,sf->ndf", rows_in, grad_gate, preferred_element_type=jnp.float32

time: 113 us -> 114 us (level)
  waiting for transfers between devices: 36.7 us -> 47.1 us
  other arithmetic: 15.4 us -> 11.2 us
  local copies, waits for them, and re-layouts: 10.3 us -> 8.26 us
  matrix products: 19 us -> 17.1 us
  starting transfers between devices: 29.3 us -> 27.6 us
    all_to_all x4, waiting for transfers between devices: 12.4 us -> 20.5 us  [to_experts(): got = lax.all_to_all(sent, 'ep', split_axis=0, concat_axis=0, tiled=True)]
    reshape x2, other arithmetic: 2.62 us -> 0.4 us  [scatter_sum(): halves = acc.reshape((-1, 2) + acc.shape[1:])]
    all_to_all x4, starting transfers between devices: 22.3 us -> 20.2 us  [to_experts(): got = lax.all_to_all(sent, 'ep', split_axis=0, concat_axis=0, tiled=True)]
    ppermute x4, starting transfers between devices: 1.73 us -> 3.74 us  [scatter_sum(): got = lax.ppermute(send, 'ctx', xor_pairs(n_ctx, bit))]
    ppermute x2, waiting for transfers between devices: 0.15 us -> 2.1 us  [all_sum(): values = values + lax.ppermute(values, 'ctx', xor_pairs(n_ctx, bit))]
    unnamed x24 -> x20, local copies, waits for them, and re-layouts: 5.68 us -> 4.1 us
    ppermute x2, starting transfers between devices: 2.07 us -> 0.52 us  [all_sum(): values = values + lax.ppermute(values, 'ctx', xor_pairs(n_ctx, bit))]
  transfers between devices with their start and end apart: 14 -> 14, of which waited for: 8 -> 10; matrix products, arithmetic and copies ran while one was open for 23% -> 15% of each run, Pallas kernels for 0% -> 0%
where the time goes in v7:
time: 114 us; the launch traced here: 113 us
  waiting for transfers between devices  47.1 us (41%)
  starting transfers between devices  27.6 us (24%)
  matrix products  17.1 us (15%)
  other arithmetic  11.2 us (10%)
  local copies, waits for them, and re-layouts  8.26 us (7%)
  between operations  1.63 us (1%)
    all_to_all x4, waiting for transfers between devices, to_experts(): got = lax.all_to_all(sent, 'ep', split_axis=0, concat_axis=0, tiled=True)  20.5 us
    all_to_all x4, starting transfers between devices, to_experts(): got = lax.all_to_all(sent, 'ep', split_axis=0, concat_axis=0, tiled=True)  20.2 us
    ppermute x4, waiting for transfers between devices, gather_blocks(): other = lax.ppermute(held, 'ctx', xor_pairs(n_ctx, bit))  15 us
    ppermute x4, waiting for transfers between devices, scatter_sum(): got = lax.ppermute(send, 'ctx', xor_pairs(n_ctx, bit))  9.47 us
    unnamed x20, local copies, waits for them, and re-layouts  4.1 us
    ppermute x4, starting transfers between devices, scatter_sum(): got = lax.ppermute(send, 'ctx', xor_pairs(n_ctx, bit))  3.74 us
    ppermute x4, starting transfers between devices, gather_blocks(): other = lax.ppermute(held, 'ctx', xor_pairs(n_ctx, bit))  3.17 us
    dot_general x1, matrix products, shards(): jnp.einsum('nsd,sf->ndf', rows_in, grad_up, preferred_element_type=jnp.fl...  3 us
  transfers between devices with their start and end apart: 14, of which 10 were waited for; matrix products, arithmetic and copies ran while one was open for 15% of the time, Pallas kernels for 0%

profile of v7, /device:TPU:0, one launch (start us, length us, event | category | flops | bytes accessed | tf_op | source)
XLA Modules:
  0.0 113.0 jit_solution(17726800047021789172)
XLA Ops:
  3.1 1.0 convolution_convert_fusion.2
  4.1 7.3 %all-to-all-start.1 = ((bf16[8,24,896]{2,1,0:T(8,128)(2,1)}), bf16[8,24,896]{2,1,0:T(8,128)(2,1)S(1)}, u32[]{:S(2)}, u32[]{:S(2)}) async-start(bf16[8,24,896]{2,1,0:T(8,128)(2,1)} %bitcast.32), calls=%async_computation.1 | async-start | bytes 688128 | tf_op jit(solution)/shard_map/all_to_all | solution.py:103
  13.1 9.0 %all-to-all-done.1 = bf16[8,24,896]{2,1,0:T(8,128)(2,1)S(1)} async-done(((bf16[8,24,896]{2,1,0:T(8,128)(2,1)}), bf16[8,24,896]{2,1,0:T(8,128)(2,1)S(1)}, u32[]{:S(2)}, u32[]{:S(2)}) %all-to-all-start.1) | async-done | bytes 344096 | tf_op jit(solution)/shard_map/all_to_all | solution.py:103
  22.0 3.6 %all-to-all-start = ((bf16[8,24,1024]{2,1,0:T(8,128)(2,1)}), bf16[8,24,1024]{2,1,0:T(8,128)(2,1)S(1)}, u32[]{:S(2)}, u32[]{:S(2)}) async-start(bf16[8,24,1024]{2,1,0:T(8,128)(2,1)} %maximum_maximum_fusion), calls=%async_computation | async-start | bytes 786432 | tf_op jit(solution)/shard_map/all_to_all | solution.py:103
  25.6 1.5 %collective-permute-start.3 = (bf16[1,192,896]{2,1,0:T(8,128)(2,1)S(1)}, bf16[1,192,896]{2,1,0:T(8,128)(2,1)S(1)}, u32[]{:S(2)}, u32[]{:S(2)}) collective-permute-start(bf16[1,192,896]{2,1,0:T(8,128)(2,1)S(1)} %bitcast.175), channel_id=1, source_target_pairs={{0,16},{8,24},{16,0},{24,8},{1,17},{9,25},{17,1},{25,9},{2,18},{10... | collective-permute-start | bytes 1032200 | tf_op jit(solution)/shard_map/ppermute | solution.py:42
  27.2 7.5 %collective-permute-done.3 = bf16[1,192,896]{2,1,0:T(8,128)(2,1)S(1)} collective-permute-done((bf16[1,192,896]{2,1,0:T(8,128)(2,1)S(1)}, bf16[1,192,896]{2,1,0:T(8,128)(2,1)S(1)}, u32[]{:S(2)}, u32[]{:S(2)}) %collective-permute-start.3) | collective-permute-done | bytes 344096 | tf_op jit(solution)/shard_map/ppermute | solution.py:42
  34.7 1.0 maximum_select_fusion.4
  35.7 1.2 %all-to-all-done = bf16[8,24,1024]{2,1,0:T(8,128)(2,1)S(1)} async-done(((bf16[8,24,1024]{2,1,0:T(8,128)(2,1)}), bf16[8,24,1024]{2,1,0:T(8,128)(2,1)S(1)}, u32[]{:S(2)}, u32[]{:S(2)}) %all-to-all-start) | async-done | bytes 393248 | tf_op jit(solution)/shard_map/all_to_all | solution.py:103
  37.0 1.6 %collective-permute-start = (bf16[1,192,896]{2,1,0:T(8,128)(2,1)S(1)}, bf16[1,192,896]{2,1,0:T(8,128)(2,1)S(1)}, u32[]{:S(2)}, u32[]{:S(2)}) collective-permute-start(bf16[1,192,896]{2,1,0:T(8,128)(2,1)S(1)} %get-tuple-element.13), channel_id=1, source_target_pairs={{0,16},{8,24},{16,0},{24,8},{1,17},{9,25},{17,1},{25,9},{2,18},{10... | collective-permute-start | bytes 1032200 | tf_op jit(solution)/shard_map/ppermute | solution.py:42
  38.9 7.4 %collective-permute-done = bf16[1,192,896]{2,1,0:T(8,128)(2,1)S(1)} collective-permute-done((bf16[1,192,896]{2,1,0:T(8,128)(2,1)S(1)}, bf16[1,192,896]{2,1,0:T(8,128)(2,1)S(1)}, u32[]{:S(2)}, u32[]{:S(2)}) %collective-permute-start) | collective-permute-done | bytes 344096 | tf_op jit(solution)/shard_map/ppermute | solution.py:42
  47.0 1.6 %copy-done.3 = bf16[1,512,3584]{2,1,0:T(8,128)(2,1)S(1)} copy-done((bf16[1,512,3584]{2,1,0:T(8,128)(2,1)S(1)}, bf16[1,512,3584]{2,1,0:T(8,128)(2,1)}, u32[]{:S(2)}) %copy-start.3) | copy-done | bytes 3670040
  50.4 1.3 %copy-done.2 = bf16[1,3584,512]{2,1,0:T(8,128)(2,1)S(1)} copy-done((bf16[1,3584,512]{2,1,0:T(8,128)(2,1)S(1)}, bf16[1,3584,512]{2,1,0:T(8,128)(2,1)}, u32[]{:S(2)}) %copy-start.2) | copy-done | bytes 3670040
  51.6 0.9 convolution_bitcast_fusion.4
  52.5 1.2 %copy-done.1 = bf16[1,3584,512]{2,1,0:T(8,128)(2,1)S(1)} copy-done((bf16[1,3584,512]{2,1,0:T(8,128)(2,1)S(1)}, bf16[1,3584,512]{2,1,0:T(8,128)(2,1)}, u32[]{:S(2)}) %copy-start.1) | copy-done | bytes 3670040
  56.7 1.4 %fusion.28 = f32[192,4,896]{2,0,1:T(8,128)S(1)} fusion(bf16[4,896,512]{2,1,0:T(8,128)(2,1)S(1)} %bitcast.170, bf16[192,512]{1,0:T(8,128)(2,1)S(1)} %get-tuple-element.10), kind=kOutput, calls=%fused_computation.74 | convolution fusion | flops 704643072 | bytes 6619136 | tf_op jit(solution)/shard_map/sf,ndf->nsd/dot_general | solution.py:144
  58.1 1.3 %fusion.1 = f32[192,4,896]{2,0,1:T(8,128)S(1)} fusion(f32[192,4,896]{2,0,1:T(8,128)S(1)} %fusion.28, bf16[192,512,1]{1,0,2:T(8,128)(2,1)S(1)} %get-tuple-element.9, bf16[4,896,512]{2,1,0:T(8,128)(2,1)S(1)} %bitcast.172), kind=kOutput, calls=%fused_computation.6 | convolution fusion | flops 706707456 | bytes 9371648 | tf_op jit(solution)/shard_map/sf,ndf->nsd/dot_general | solution.py:146
  61.1 0.9 collective-permute-done.5
  62.2 1.6 %collective-permute-start.6 = (bf16[1,192,896]{2,1,0:T(8,128)(2,1)S(1)}, bf16[1,192,896]{2,1,0:T(8,128)(2,1)S(1)}, u32[]{:S(2)}, u32[]{:S(2)}) collective-permute-start(bf16[1,192,896]{2,1,0:T(8,128)(2,1)S(1)} %fusion.24), channel_id=1, source_target_pairs={{0,16},{8,24},{16,0},{24,8},{1,17},{9,25},{17,1},{25,9},{2,18},{10... | collective-permute-start | bytes 1032200 | tf_op jit(solution)/shard_map/ppermute | solution.py:65
  64.0 8.6 %collective-permute-done.6 = bf16[1,192,896]{2,1,0:T(8,128)(2,1)S(1)} collective-permute-done((bf16[1,192,896]{2,1,0:T(8,128)(2,1)S(1)}, bf16[1,192,896]{2,1,0:T(8,128)(2,1)S(1)}, u32[]{:S(2)}, u32[]{:S(2)}) %collective-permute-start.6) | collective-permute-done | bytes 344096 | tf_op jit(solution)/shard_map/ppermute | solution.py:65
  73.4 1.3 %convert_element_type.231 = bf16[172032]{0:T(1024)(128)(2,1)S(1)} reshape(bf16[1,192,896]{2,1,0:T(8,128)(2,1)} %fusion.19) | data formatting | bytes 688128 | tf_op jit(solution)/shard_map/convert_element_type | solution.py:148
  76.7 1.5 %collective-permute-start.7 = (bf16[1,192,896]{2,1,0:T(8,128)(2,1)}, bf16[1,192,896]{2,1,0:T(8,128)(2,1)}, u32[]{:S(2)}, u32[]{:S(2)}) collective-permute-start(bf16[1,192,896]{2,1,0:T(8,128)(2,1)} %fusion.23), channel_id=1, source_target_pairs={{0,16},{8,24},{16,0},{24,8},{1,17},{9,25},{17,1},{25,9},{2,18},{10... | collective-permute-start | bytes 1032200 | tf_op jit(solution)/shard_map/ppermute | solution.py:65
  78.2 1.1 %collective-permute-done.8 = f32[192]{0:T(256)S(1)} collective-permute-done((f32[192]{0:T(256)S(1)}, f32[192]{0:T(256)S(1)}, u32[]{:S(2)}, u32[]{:S(2)}) %collective-permute-start.8) | collective-permute-done | bytes 800 | tf_op jit(solution)/shard_map/ppermute | solution.py:72
  79.9 5.7 %all-to-all-start.3 = ((bf16[8,24,896]{2,1,0:T(8,128)(2,1)}), bf16[8,24,896]{2,1,0:T(8,128)(2,1)S(1)}, u32[]{:S(2)}, u32[]{:S(2)}) async-start(bf16[8,24,896]{2,1,0:T(8,128)(2,1)} %bitcast.57), calls=%async_computation.3 | async-start | bytes 688128 | tf_op jit(solution)/shard_map/all_to_all | solution.py:103
  85.6 1.0 collective-permute-done.9
  88.3 1.1 fusion.20
  90.3 6.0 %all-to-all-done.3 = bf16[8,24,896]{2,1,0:T(8,128)(2,1)S(1)} async-done(((bf16[8,24,896]{2,1,0:T(8,128)(2,1)}), bf16[8,24,896]{2,1,0:T(8,128)(2,1)S(1)}, u32[]{:S(2)}, u32[]{:S(2)}) %all-to-all-start.3) | async-done | bytes 344096 | tf_op jit(solution)/shard_map/all_to_all | solution.py:103
  96.3 3.6 %all-to-all-start.2 = ((bf16[8,24,1024]{2,1,0:T(8,128)(2,1)}), bf16[8,24,1024]{2,1,0:T(8,128)(2,1)S(1)}, u32[]{:S(2)}, u32[]{:S(2)}) async-start(bf16[8,24,1024]{2,1,0:T(8,128)(2,1)} %maximum_maximum_fusion.1), calls=%async_computation.2 | async-start | bytes 786432 | tf_op jit(solution)/shard_map/all_to_all | solution.py:103
  100.0 3.0 %convolution_convert_fusion = bf16[4,896,512]{2,1,0:T(8,128)(2,1)} fusion(bf16[4,192,896]{2,1,0:T(8,128)(2,1)S(1)} %bitcast.161, bf16[192,512,1]{1,0,2:T(8,128)(2,1)S(1)} %copy-done.5), kind=kOutput, calls=%fused_computation.4 | convolution fusion | flops 706478080 | bytes 5242880 | tf_op jit(solution)/shard_map/nsd,sf->ndf/dot_general | solution.py:158
  103.0 3.0 %convolution_convert_fusion.1 = bf16[4,896,512]{2,1,0:T(8,128)(2,1)} fusion(bf16[4,192,896]{2,1,0:T(8,128)(2,1)S(1)} %bitcast.162, bf16[192,512]{1,0:T(8,128)(2,1)S(1)} %get-tuple-element.10), kind=kOutput, calls=%fused_computation.5 | convolution fusion | flops 706478080 | bytes 5242880 | tf_op jit(solution)/shard_map/nsd,sf->ndf/dot_general | solution.py:155
  106.0 1.0 convolution_convert_fusion.4
  106.9 4.3 %all-to-all-done.2 = bf16[8,24,1024]{2,1,0:T(8,128)(2,1)S(1)} async-done(((bf16[8,24,1024]{2,1,0:T(8,128)(2,1)}), bf16[8,24,1024]{2,1,0:T(8,128)(2,1)S(1)}, u32[]{:S(2)}, u32[]{:S(2)}) %all-to-all-start.2) | async-done | bytes 393248 | tf_op jit(solution)/shard_map/all_to_all | solution.py:103
  111.4 1.0 fusion.7
  (74 shorter events, 18.0 us)
Async XLA Ops:
  0.6 2.5 %copy-start = (bf16[128,896]{1,0:T(8,128)(2,1)S(1)}, bf16[128,896]{1,0:T(8,128)(2,1)}, u32[]{:S(2)}) copy-start(bf16[128,896]{1,0:T(8,128)(2,1)} %param.8) | copy-start | bytes 688132
  0.6 10.7 %copy-start.9 = (f32[128,1]{0,1:T(1,128)S(1)}, f32[128,1]{0,1:T(1,128)}, u32[]{:S(2)}) copy-start(f32[128,1]{0,1:T(1,128)} %param.10) | copy-start | bytes 1540
  0.7 11.3 %copy-start.6 = (bf16[128,896]{1,0:T(8,128)(2,1)S(1)}, bf16[128,896]{1,0:T(8,128)(2,1)}, u32[]{:S(2)}) copy-start(bf16[128,896]{1,0:T(8,128)(2,1)} %param.7) | copy-start | bytes 688132
  4.1 17.9 %all-to-all-start.1 = ((bf16[8,24,896]{2,1,0:T(8,128)(2,1)}), bf16[8,24,896]{2,1,0:T(8,128)(2,1)S(1)}, u32[]{:S(2)}, u32[]{:S(2)}) async-start(bf16[8,24,896]{2,1,0:T(8,128)(2,1)} %bitcast.32), calls=%async_computation.1 | async-start | bytes 688128 | tf_op jit(solution)/shard_map/all_to_all | solution.py:103
  22.0 14.9 %all-to-all-start = ((bf16[8,24,1024]{2,1,0:T(8,128)(2,1)}), bf16[8,24,1024]{2,1,0:T(8,128)(2,1)S(1)}, u32[]{:S(2)}, u32[]{:S(2)}) async-start(bf16[8,24,1024]{2,1,0:T(8,128)(2,1)} %maximum_maximum_fusion), calls=%async_computation | async-start | bytes 786432 | tf_op jit(solution)/shard_map/all_to_all | solution.py:103
  25.6 9.1 %collective-permute-start.3 = (bf16[1,192,896]{2,1,0:T(8,128)(2,1)S(1)}, bf16[1,192,896]{2,1,0:T(8,128)(2,1)S(1)}, u32[]{:S(2)}, u32[]{:S(2)}) collective-permute-start(bf16[1,192,896]{2,1,0:T(8,128)(2,1)S(1)} %bitcast.175), channel_id=1, source_target_pairs={{0,16},{8,24},{16,0},{24,8},{1,17},{9,25},{17,1},{25,9},{2,18},{10... | collective-permute-start | bytes 1032200 | tf_op jit(solution)/shard_map/ppermute | solution.py:42
  35.7 10.9 %collective-permute-start.4 = (bf16[2,192,896]{2,1,0:T(8,128)(2,1)}, bf16[2,192,896]{2,1,0:T(8,128)(2,1)S(1)}, u32[]{:S(2)}, u32[]{:S(2)}) collective-permute-start(bf16[2,192,896]{2,1,0:T(8,128)(2,1)} %maximum_select_fusion.4), channel_id=1, source_target_pairs={{0,8},{8,0},{16,24},{24,16},{1,9},{9,1},{17,25},{25,17},{2,10},{10... | collective-permute-start | bytes 2064392 | tf_op jit(solution)/shard_map/ppermute | solution.py:42
  37.0 9.3 %collective-permute-start = (bf16[1,192,896]{2,1,0:T(8,128)(2,1)S(1)}, bf16[1,192,896]{2,1,0:T(8,128)(2,1)S(1)}, u32[]{:S(2)}, u32[]{:S(2)}) collective-permute-start(bf16[1,192,896]{2,1,0:T(8,128)(2,1)S(1)} %get-tuple-element.13), channel_id=1, source_target_pairs={{0,16},{8,24},{16,0},{24,8},{1,17},{9,25},{17,1},{25,9},{2,18},{10... | collective-permute-start | bytes 1032200 | tf_op jit(solution)/shard_map/ppermute | solution.py:42
  46.4 3.7 %collective-permute-start.1 = (bf16[2,192,896]{2,1,0:T(8,128)(2,1)S(1)}, bf16[2,192,896]{2,1,0:T(8,128)(2,1)S(1)}, u32[]{:S(2)}, u32[]{:S(2)}) collective-permute-start(bf16[2,192,896]{2,1,0:T(8,128)(2,1)S(1)} %maximum_select_fusion.2), channel_id=1, source_target_pairs={{0,8},{8,0},{16,24},{24,16},{1,9},{9,1},{17,25},{25,17},{2,10},{10... | collective-permute-start | bytes 2064392 | tf_op jit(solution)/shard_map/ppermute | solution.py:42
  46.6 2.0 %copy-start.3 = (bf16[1,512,3584]{2,1,0:T(8,128)(2,1)S(1)}, bf16[1,512,3584]{2,1,0:T(8,128)(2,1)}, u32[]{:S(2)}) copy-start(bf16[1,512,3584]{2,1,0:T(8,128)(2,1)} %param.13) | copy-start | bytes 11010052
  49.6 2.0 %copy-start.2 = (bf16[1,3584,512]{2,1,0:T(8,128)(2,1)S(1)}, bf16[1,3584,512]{2,1,0:T(8,128)(2,1)}, u32[]{:S(2)}) copy-start(bf16[1,3584,512]{2,1,0:T(8,128)(2,1)} %param.12) | copy-start | bytes 11010052
  51.6 2.0 %copy-start.1 = (bf16[1,3584,512]{2,1,0:T(8,128)(2,1)S(1)}, bf16[1,3584,512]{2,1,0:T(8,128)(2,1)}, u32[]{:S(2)}) copy-start(bf16[1,3584,512]{2,1,0:T(8,128)(2,1)} %param.11) | copy-start | bytes 11010052
  55.2 2.9 %copy-start.4 = (bf16[192,512,1]{1,0,2:T(8,128)(2,1)}, bf16[192,512,1]{1,0,2:T(8,128)(2,1)S(1)}, u32[]{:S(2)}) copy-start(bf16[192,512,1]{1,0,2:T(8,128)(2,1)S(1)} %get-tuple-element.9) | copy-start | bytes 589828
  59.6 2.3 %collective-permute-start.5 = (bf16[2,192,896]{2,1,0:T(8,128)(2,1)S(1)}, bf16[2,192,896]{2,1,0:T(8,128)(2,1)S(1)}, u32[]{:S(2)}, u32[]{:S(2)}) collective-permute-start(bf16[2,192,896]{2,1,0:T(8,128)(2,1)S(1)} %fusion.18), channel_id=1, source_target_pairs={{0,8},{8,0},{16,24},{24,16},{1,9},{9,1},{17,25},{25,17},{2,10},{10... | collective-permute-start | bytes 2064392 | tf_op jit(solution)/shard_map/ppermute | solution.py:65
  61.0 2.8 %collective-permute-start.2 = (bf16[2,192,896]{2,1,0:T(8,128)(2,1)S(1)}, bf16[2,192,896]{2,1,0:T(8,128)(2,1)S(1)}, u32[]{:S(2)}, u32[]{:S(2)}) collective-permute-start(bf16[2,192,896]{2,1,0:T(8,128)(2,1)S(1)} %fusion.17), channel_id=1, source_target_pairs={{0,8},{8,0},{16,24},{24,16},{1,9},{9,1},{17,25},{25,17},{2,10},{10... | collective-permute-start | bytes 2064392 | tf_op jit(solution)/shard_map/ppermute | solution.py:65
  62.2 10.4 %collective-permute-start.6 = (bf16[1,192,896]{2,1,0:T(8,128)(2,1)S(1)}, bf16[1,192,896]{2,1,0:T(8,128)(2,1)S(1)}, u32[]{:S(2)}, u32[]{:S(2)}) collective-permute-start(bf16[1,192,896]{2,1,0:T(8,128)(2,1)S(1)} %fusion.24), channel_id=1, source_target_pairs={{0,16},{8,24},{16,0},{24,8},{1,17},{9,25},{17,1},{25,9},{2,18},{10... | collective-permute-start | bytes 1032200 | tf_op jit(solution)/shard_map/ppermute | solution.py:65
  76.7 11.6 %collective-permute-start.7 = (bf16[1,192,896]{2,1,0:T(8,128)(2,1)}, bf16[1,192,896]{2,1,0:T(8,128)(2,1)}, u32[]{:S(2)}, u32[]{:S(2)}) collective-permute-start(bf16[1,192,896]{2,1,0:T(8,128)(2,1)} %fusion.23), channel_id=1, source_target_pairs={{0,16},{8,24},{16,0},{24,8},{1,17},{9,25},{17,1},{25,9},{2,18},{10... | collective-permute-start | bytes 1032200 | tf_op jit(solution)/shard_map/ppermute | solution.py:65
  78.2 1.1 %collective-permute-start.8 = (f32[192]{0:T(256)S(1)}, f32[192]{0:T(256)S(1)}, u32[]{:S(2)}, u32[]{:S(2)}) collective-permute-start(f32[192]{0:T(256)S(1)} %get-tuple-element.5), channel_id=1, source_target_pairs={{0,8},{8,0},{16,24},{24,16},{1,9},{9,1},{17,25},{25,17},{2,10},{10... | collective-permute-start | bytes 2312 | tf_op jit(solution)/shard_map/ppermute | solution.py:72
  79.4 7.2 %collective-permute-start.9 = (f32[192]{0:T(256)S(1)}, f32[192]{0:T(256)S(1)}, u32[]{:S(2)}, u32[]{:S(2)}) collective-permute-start(f32[192]{0:T(256)S(1)} %add.87), channel_id=1, source_target_pairs={{0,16},{8,24},{16,0},{24,8},{1,17},{9,25},{17,1},{25,9},{2,18},{10... | collective-permute-start | bytes 2312 | tf_op jit(solution)/shard_map/ppermute | solution.py:72
  79.9 16.4 %all-to-all-start.3 = ((bf16[8,24,896]{2,1,0:T(8,128)(2,1)}), bf16[8,24,896]{2,1,0:T(8,128)(2,1)S(1)}, u32[]{:S(2)}, u32[]{:S(2)}) async-start(bf16[8,24,896]{2,1,0:T(8,128)(2,1)} %bitcast.57), calls=%async_computation.3 | async-start | bytes 688128 | tf_op jit(solution)/shard_map/all_to_all | solution.py:103
  88.3 1.1 copy-start.7
  88.3 1.1 copy-start.8
  89.4 10.6 %copy-start.5 = (bf16[192,512,1]{1,0,2:T(8,128)(2,1)S(1)}, bf16[192,512,1]{1,0,2:T(8,128)(2,1)}, u32[]{:S(2)}) copy-start(bf16[192,512,1]{1,0,2:T(8,128)(2,1)} %copy-done.4) | copy-start | bytes 589828
  96.3 14.9 %all-to-all-start.2 = ((bf16[8,24,1024]{2,1,0:T(8,128)(2,1)}), bf16[8,24,1024]{2,1,0:T(8,128)(2,1)S(1)}, u32[]{:S(2)}, u32[]{:S(2)}) async-start(bf16[8,24,1024]{2,1,0:T(8,128)(2,1)} %maximum_maximum_fusion.1), calls=%async_computation.2 | async-start | bytes 786432 | tf_op jit(solution)/shard_map/all_to_all | solution.py:103

commit v8 on v2

--- a/solution.py
+++ b/solution.py
@@ -8,9 +8,11 @@
     tok_rows, routes = expert_ids.shape
     flat_ids = expert_ids.reshape(-1)
     labels = jnp.arange(experts, dtype=jnp.int32)
-    onehot = (flat_ids[:, None] == labels[None, :]).astype(jnp.int32)
-    earlier = jnp.cumsum(onehot, axis=0) - onehot
-    slot_rank = jnp.sum(earlier * onehot, axis=1)
+    onehot = (flat_ids[:, None] == labels[None, :]).astype(jnp.bfloat16)
+    pairs = jnp.arange(flat_ids.shape[0], dtype=jnp.int32)
+    before = (pairs[:, None] > pairs[None, :]).astype(jnp.bfloat16)
+    earlier = jnp.dot(before, onehot, preferred_element_type=jnp.float32)
+    slot_rank = jnp.sum(earlier * onehot.astype(jnp.float32), axis=1).astype(jnp.int32)
     slot_ids = (flat_ids * capacity + slot_rank).reshape(tok_rows, routes)
     positions = jnp.arange(experts * capacity, dtype=jnp.int32)
     return [slot_ids[:, r][:, None] == positions[None, :] for r in range(routes)]
@@ -68,9 +70,8 @@
 
 def with_cols(rows, values, pad):
     hi, lo = split_f32(values)
-    cols = jnp.zeros((rows.shape[0], pad), jnp.bfloat16)
-    cols = cols.at[:, 0].set(hi).at[:, 1].set(lo)
-    return jnp.concatenate([rows, cols], axis=1)
+    zeros = jnp.zeros((rows.shape[0], pad - 2), jnp.bfloat16)
+    return jnp.concatenate([rows, hi[:, None], lo[:, None], zeros], axis=1)
 
 
 def shards(tokens, cotangent, expert_ids, route_gates, w_gate, w_up, w_down):

time: 107 us -> 106 us (level)
  waiting for transfers between devices: 36.6 us -> 41.7 us
  other arithmetic: 15 us -> 10 us
  local copies, waits for them, and re-layouts: 8.14 us -> 6.45 us
    all_to_all x4, waiting for transfers between devices: 12.1 us -> 17.1 us  [to_experts(): got = lax.all_to_all(sent, 'ep', split_axis=0, concat_axis=0, tiled=True)]
    another operation x5 -> x0, other arithmetic: 4.07 us -> none
    scatter x5 -> x0, local copies, waits for them, and re-layouts: 3.72 us -> none  [with_cols(): cols = cols.at[:, 0].set(hi).at[:, 1].set(lo)]
    concatenate x0 -> x4, local copies, waits for them, and re-layouts: none -> 1.79 us  [with_cols(): return jnp.concatenate([rows, hi[:, None], lo[:, None], zeros], axis=1)]
    unnamed x18 -> x20, local copies, waits for them, and re-layouts: 4.13 us -> 4.13 us
  transfers between devices with their start and end apart: 14 -> 14, of which waited for: 8 -> 8; matrix products, arithmetic and copies ran while one was open for 23% -> 18% of each run, Pallas kernels for 0% -> 0%
where the time goes in v8:
time: 106 us; the launch traced here: 105 us
  waiting for transfers between devices  41.7 us (39%)
  starting transfers between devices  28.1 us (27%)
  matrix products  17.9 us (17%)
  other arithmetic  10 us (9%)
  local copies, waits for them, and re-layouts  6.45 us (6%)
    all_to_all x4, starting transfers between devices, to_experts(): got = lax.all_to_all(sent, 'ep', split_axis=0, concat_axis=0, tiled=True)  20.2 us
    all_to_all x4, waiting for transfers between devices, to_experts(): got = lax.all_to_all(sent, 'ep', split_axis=0, concat_axis=0, tiled=True)  17.1 us
    ppermute x4, waiting for transfers between devices, gather_blocks(): other = lax.ppermute(held, 'ctx', xor_pairs(n_ctx, bit))  15 us
    ppermute x4, waiting for transfers between devices, scatter_sum(): got = lax.ppermute(send, 'ctx', xor_pairs(n_ctx, bit))  7.95 us
    unnamed x20, local copies, waits for them, and re-layouts  4.13 us
    ppermute x4, starting transfers between devices, gather_blocks(): other = lax.ppermute(held, 'ctx', xor_pairs(n_ctx, bit))  3.18 us
    dot_general x1, matrix products, shards(): jnp.einsum('nsd,sf->ndf', rows_in, grad_up, preferred_element_type=jnp.fl...  3 us
    dot_general x1, matrix products, shards(): jnp.einsum('nsd,sf->ndf', rows_in, grad_gate, preferred_element_type=jnp....  3 us
  transfers between devices with their start and end apart: 14, of which 8 were waited for; matrix products, arithmetic and copies ran while one was open for 18% of the time, Pallas kernels for 0%

profile of v8, /device:TPU:0, one launch (start us, length us, event | category | flops | bytes accessed | tf_op | source)
XLA Modules:
  0.0 105.2 jit_solution(5119150277767369664)
XLA Ops:
  0.7 0.9 fusion.8
  2.2 1.0 convolution_convert_fusion.2
  3.2 7.3 %all-to-all-start.1 = ((bf16[8,24,896]{2,1,0:T(8,128)(2,1)}), bf16[8,24,896]{2,1,0:T(8,128)(2,1)S(1)}, u32[]{:S(2)}, u32[]{:S(2)}) async-start(bf16[8,24,896]{2,1,0:T(8,128)(2,1)} %bitcast.34), calls=%async_computation.1 | async-start | bytes 688128 | tf_op jit(solution)/shard_map/all_to_all | solution.py:98
  12.8 8.3 %all-to-all-done.1 = bf16[8,24,896]{2,1,0:T(8,128)(2,1)S(1)} async-done(((bf16[8,24,896]{2,1,0:T(8,128)(2,1)}), bf16[8,24,896]{2,1,0:T(8,128)(2,1)S(1)}, u32[]{:S(2)}, u32[]{:S(2)}) %all-to-all-start.1) | async-done | bytes 344096 | tf_op jit(solution)/shard_map/all_to_all | solution.py:98
  21.1 3.6 %all-to-all-start = ((bf16[8,24,1024]{2,1,0:T(8,128)(2,1)}), bf16[8,24,1024]{2,1,0:T(8,128)(2,1)S(1)}, u32[]{:S(2)}, u32[]{:S(2)}) async-start(bf16[8,24,1024]{2,1,0:T(8,128)(2,1)} %maximum_maximum_fusion), calls=%async_computation | async-start | bytes 786432 | tf_op jit(solution)/shard_map/all_to_all | solution.py:98
  24.7 1.5 %collective-permute-start.4 = (bf16[1,192,896]{2,1,0:T(8,128)(2,1)S(1)}, bf16[1,192,896]{2,1,0:T(8,128)(2,1)S(1)}, u32[]{:S(2)}, u32[]{:S(2)}) collective-permute-start(bf16[1,192,896]{2,1,0:T(8,128)(2,1)S(1)} %bitcast.174), channel_id=1, source_target_pairs={{0,16},{8,24},{16,0},{24,8},{1,17},{9,25},{17,1},{25,9},{2,18},{10... | collective-permute-start | bytes 1032200 | tf_op jit(solution)/shard_map/ppermute | solution.py:44
  26.2 7.5 %collective-permute-done.4 = bf16[1,192,896]{2,1,0:T(8,128)(2,1)S(1)} collective-permute-done((bf16[1,192,896]{2,1,0:T(8,128)(2,1)S(1)}, bf16[1,192,896]{2,1,0:T(8,128)(2,1)S(1)}, u32[]{:S(2)}, u32[]{:S(2)}) %collective-permute-start.4) | collective-permute-done | bytes 344096 | tf_op jit(solution)/shard_map/ppermute | solution.py:44
  33.8 1.0 maximum_select_fusion.4
  34.7 1.2 %all-to-all-done = bf16[8,24,1024]{2,1,0:T(8,128)(2,1)S(1)} async-done(((bf16[8,24,1024]{2,1,0:T(8,128)(2,1)}), bf16[8,24,1024]{2,1,0:T(8,128)(2,1)S(1)}, u32[]{:S(2)}, u32[]{:S(2)}) %all-to-all-start) | async-done | bytes 393248 | tf_op jit(solution)/shard_map/all_to_all | solution.py:98
  36.0 1.6 %collective-permute-start = (bf16[1,192,896]{2,1,0:T(8,128)(2,1)S(1)}, bf16[1,192,896]{2,1,0:T(8,128)(2,1)S(1)}, u32[]{:S(2)}, u32[]{:S(2)}) collective-permute-start(bf16[1,192,896]{2,1,0:T(8,128)(2,1)S(1)} %get-tuple-element.13), channel_id=1, source_target_pairs={{0,16},{8,24},{16,0},{24,8},{1,17},{9,25},{17,1},{25,9},{2,18},{10... | collective-permute-start | bytes 1032200 | tf_op jit(solution)/shard_map/ppermute | solution.py:44
  37.9 7.4 %collective-permute-done = bf16[1,192,896]{2,1,0:T(8,128)(2,1)S(1)} collective-permute-done((bf16[1,192,896]{2,1,0:T(8,128)(2,1)S(1)}, bf16[1,192,896]{2,1,0:T(8,128)(2,1)S(1)}, u32[]{:S(2)}, u32[]{:S(2)}) %collective-permute-start) | collective-permute-done | bytes 344096 | tf_op jit(solution)/shard_map/ppermute | solution.py:44
  46.1 1.6 %copy-done.3 = bf16[1,512,3584]{2,1,0:T(8,128)(2,1)S(1)} copy-done((bf16[1,512,3584]{2,1,0:T(8,128)(2,1)S(1)}, bf16[1,512,3584]{2,1,0:T(8,128)(2,1)}, u32[]{:S(2)}) %copy-start.3) | copy-done | bytes 3670040
  49.4 1.3 %copy-done.2 = bf16[1,3584,512]{2,1,0:T(8,128)(2,1)S(1)} copy-done((bf16[1,3584,512]{2,1,0:T(8,128)(2,1)S(1)}, bf16[1,3584,512]{2,1,0:T(8,128)(2,1)}, u32[]{:S(2)}) %copy-start.2) | copy-done | bytes 3670040
  50.7 0.9 convolution_bitcast_fusion.4
  51.6 1.2 %copy-done.1 = bf16[1,3584,512]{2,1,0:T(8,128)(2,1)S(1)} copy-done((bf16[1,3584,512]{2,1,0:T(8,128)(2,1)S(1)}, bf16[1,3584,512]{2,1,0:T(8,128)(2,1)}, u32[]{:S(2)}) %copy-start.1) | copy-done | bytes 3670040
  52.7 0.9 convolution_bitcast_fusion.5
  55.7 1.3 %fusion.28 = f32[192,4,896]{2,0,1:T(8,128)S(1)} fusion(bf16[4,896,512]{2,1,0:T(8,128)(2,1)S(1)} %bitcast.169, bf16[192,512]{1,0:T(8,128)(2,1)S(1)} %get-tuple-element.10), kind=kOutput, calls=%fused_computation.75 | convolution fusion | flops 704643072 | bytes 6619136 | tf_op jit(solution)/shard_map/sf,ndf->nsd/dot_general | solution.py:141
  57.1 1.3 %fusion.1 = f32[192,4,896]{2,0,1:T(8,128)S(1)} fusion(f32[192,4,896]{2,0,1:T(8,128)S(1)} %fusion.28, bf16[192,512,1]{1,0,2:T(8,128)(2,1)S(1)} %get-tuple-element.9, bf16[4,896,512]{2,1,0:T(8,128)(2,1)S(1)} %bitcast.171), kind=kOutput, calls=%fused_computation.6 | convolution fusion | flops 706707456 | bytes 9371648 | tf_op jit(solution)/shard_map/sf,ndf->nsd/dot_general | solution.py:143
  60.5 1.6 %collective-permute-done.6 = f32[192]{0:T(256)S(1)} collective-permute-done((f32[192]{0:T(256)S(1)}, f32[192]{0:T(256)S(1)}, u32[]{:S(2)}, u32[]{:S(2)}) %collective-permute-start.6) | collective-permute-done | bytes 800 | tf_op jit(solution)/shard_map/ppermute | solution.py:67
  62.2 1.5 %collective-permute-start.7 = (f32[192]{0:T(256)S(1)}, f32[192]{0:T(256)S(1)}, u32[]{:S(2)}, u32[]{:S(2)}) collective-permute-start(f32[192]{0:T(256)S(1)} %add.59), channel_id=1, source_target_pairs={{0,16},{8,24},{16,0},{24,8},{1,17},{9,25},{17,1},{25,9},{2,18},{10... | collective-permute-start | bytes 2312 | tf_op jit(solution)/shard_map/ppermute | solution.py:67
  65.5 1.5 %collective-permute-start.3 = (bf16[1,192,896]{2,1,0:T(8,128)(2,1)}, bf16[1,192,896]{2,1,0:T(8,128)(2,1)}, u32[]{:S(2)}, u32[]{:S(2)}) collective-permute-start(bf16[1,192,896]{2,1,0:T(8,128)(2,1)} %fusion.23), channel_id=1, source_target_pairs={{0,16},{8,24},{16,0},{24,8},{1,17},{9,25},{17,1},{25,9},{2,18},{10... | collective-permute-start | bytes 1032200 | tf_op jit(solution)/shard_map/ppermute | solution.py:60
  67.0 7.9 %collective-permute-done.9 = bf16[1,192,896]{2,1,0:T(8,128)(2,1)S(1)} collective-permute-done((bf16[1,192,896]{2,1,0:T(8,128)(2,1)S(1)}, bf16[1,192,896]{2,1,0:T(8,128)(2,1)S(1)}, u32[]{:S(2)}, u32[]{:S(2)}) %collective-permute-start.9) | collective-permute-done | bytes 344096 | tf_op jit(solution)/shard_map/ppermute | solution.py:60
  75.8 5.7 %all-to-all-start.3 = ((bf16[8,24,896]{2,1,0:T(8,128)(2,1)}), bf16[8,24,896]{2,1,0:T(8,128)(2,1)S(1)}, u32[]{:S(2)}, u32[]{:S(2)}) async-start(bf16[8,24,896]{2,1,0:T(8,128)(2,1)} %bitcast.184), calls=%async_computation.3 | async-start | bytes 688128 | tf_op jit(solution)/shard_map/all_to_all | solution.py:98
  82.4 0.9 concatenate.63
  83.2 1.1 %fusion.21 = bf16[1,192,896]{2,1,0:T(8,128)(2,1)S(1)} fusion(bf16[1,192,896]{2,1,0:T(8,128)(2,1)} %collective-permute-done.3, f32[1,2,192,896]{3,2,1,0:T(8,128)S(1)} %fusion.4, pred[]{:T(512)S(6)} %eq.50), kind=kLoop, calls=%fused_computation.54 | loop fusion | flops 688128 | bytes 2064385 | tf_op jit(solution)/shard_map/convert_element_type | solution.py:127
  85.2 5.2 %all-to-all-done.3 = bf16[8,24,896]{2,1,0:T(8,128)(2,1)S(1)} async-done(((bf16[8,24,896]{2,1,0:T(8,128)(2,1)}), bf16[8,24,896]{2,1,0:T(8,128)(2,1)S(1)}, u32[]{:S(2)}, u32[]{:S(2)}) %all-to-all-start.3) | async-done | bytes 344096 | tf_op jit(solution)/shard_map/all_to_all | solution.py:98
  90.3 3.6 %all-to-all-start.2 = ((bf16[8,24,1024]{2,1,0:T(8,128)(2,1)}), bf16[8,24,1024]{2,1,0:T(8,128)(2,1)S(1)}, u32[]{:S(2)}, u32[]{:S(2)}) async-start(bf16[8,24,1024]{2,1,0:T(8,128)(2,1)} %maximum_maximum_fusion.1), calls=%async_computation.2 | async-start | bytes 786432 | tf_op jit(solution)/shard_map/all_to_all | solution.py:98
  94.0 3.0 %convolution_convert_fusion = bf16[4,896,512]{2,1,0:T(8,128)(2,1)} fusion(bf16[4,192,896]{2,1,0:T(8,128)(2,1)S(1)} %bitcast.160, bf16[192,512,1]{1,0,2:T(8,128)(2,1)S(1)} %copy-done.5), kind=kOutput, calls=%fused_computation.4 | convolution fusion | flops 706478080 | bytes 5242880 | tf_op jit(solution)/shard_map/nsd,sf->ndf/dot_general | solution.py:151
  97.0 3.0 %convolution_convert_fusion.1 = bf16[4,896,512]{2,1,0:T(8,128)(2,1)} fusion(bf16[4,192,896]{2,1,0:T(8,128)(2,1)S(1)} %bitcast.161, bf16[192,512]{1,0:T(8,128)(2,1)S(1)} %get-tuple-element.10), kind=kOutput, calls=%fused_computation.5 | convolution fusion | flops 706478080 | bytes 5242880 | tf_op jit(solution)/shard_map/nsd,sf->ndf/dot_general | solution.py:148
  100.0 1.0 convolution_convert_fusion.4
  101.0 2.4 %all-to-all-done.2 = bf16[8,24,1024]{2,1,0:T(8,128)(2,1)S(1)} async-done(((bf16[8,24,1024]{2,1,0:T(8,128)(2,1)}), bf16[8,24,1024]{2,1,0:T(8,128)(2,1)S(1)}, u32[]{:S(2)}, u32[]{:S(2)}) %all-to-all-start.2) | async-done | bytes 393248 | tf_op jit(solution)/shard_map/all_to_all | solution.py:98
  103.6 1.0 fusion.7
  (70 shorter events, 15.0 us)
Async XLA Ops:
  0.6 1.6 %copy-start = (bf16[128,896]{1,0:T(8,128)(2,1)S(1)}, bf16[128,896]{1,0:T(8,128)(2,1)}, u32[]{:S(2)}) copy-start(bf16[128,896]{1,0:T(8,128)(2,1)} %param.8) | copy-start | bytes 688132
  0.6 11.0 %copy-start.6 = (bf16[128,896]{1,0:T(8,128)(2,1)S(1)}, bf16[128,896]{1,0:T(8,128)(2,1)}, u32[]{:S(2)}) copy-start(bf16[128,896]{1,0:T(8,128)(2,1)} %param.7) | copy-start | bytes 688132
  3.2 17.9 %all-to-all-start.1 = ((bf16[8,24,896]{2,1,0:T(8,128)(2,1)}), bf16[8,24,896]{2,1,0:T(8,128)(2,1)S(1)}, u32[]{:S(2)}, u32[]{:S(2)}) async-start(bf16[8,24,896]{2,1,0:T(8,128)(2,1)} %bitcast.34), calls=%async_computation.1 | async-start | bytes 688128 | tf_op jit(solution)/shard_map/all_to_all | solution.py:98
  21.1 14.9 %all-to-all-start = ((bf16[8,24,1024]{2,1,0:T(8,128)(2,1)}), bf16[8,24,1024]{2,1,0:T(8,128)(2,1)S(1)}, u32[]{:S(2)}, u32[]{:S(2)}) async-start(bf16[8,24,1024]{2,1,0:T(8,128)(2,1)} %maximum_maximum_fusion), calls=%async_computation | async-start | bytes 786432 | tf_op jit(solution)/shard_map/all_to_all | solution.py:98
  24.7 9.1 %collective-permute-start.4 = (bf16[1,192,896]{2,1,0:T(8,128)(2,1)S(1)}, bf16[1,192,896]{2,1,0:T(8,128)(2,1)S(1)}, u32[]{:S(2)}, u32[]{:S(2)}) collective-permute-start(bf16[1,192,896]{2,1,0:T(8,128)(2,1)S(1)} %bitcast.174), channel_id=1, source_target_pairs={{0,16},{8,24},{16,0},{24,8},{1,17},{9,25},{17,1},{25,9},{2,18},{10... | collective-permute-start | bytes 1032200 | tf_op jit(solution)/shard_map/ppermute | solution.py:44
  34.7 10.9 %collective-permute-start.5 = (bf16[2,192,896]{2,1,0:T(8,128)(2,1)}, bf16[2,192,896]{2,1,0:T(8,128)(2,1)S(1)}, u32[]{:S(2)}, u32[]{:S(2)}) collective-permute-start(bf16[2,192,896]{2,1,0:T(8,128)(2,1)} %maximum_select_fusion.4), channel_id=1, source_target_pairs={{0,8},{8,0},{16,24},{24,16},{1,9},{9,1},{17,25},{25,17},{2,10},{10... | collective-permute-start | bytes 2064392 | tf_op jit(solution)/shard_map/ppermute | solution.py:44
  36.0 9.3 %collective-permute-start = (bf16[1,192,896]{2,1,0:T(8,128)(2,1)S(1)}, bf16[1,192,896]{2,1,0:T(8,128)(2,1)S(1)}, u32[]{:S(2)}, u32[]{:S(2)}) collective-permute-start(bf16[1,192,896]{2,1,0:T(8,128)(2,1)S(1)} %get-tuple-element.13), channel_id=1, source_target_pairs={{0,16},{8,24},{16,0},{24,8},{1,17},{9,25},{17,1},{25,9},{2,18},{10... | collective-permute-start | bytes 1032200 | tf_op jit(solution)/shard_map/ppermute | solution.py:44
  45.5 3.7 %collective-permute-start.1 = (bf16[2,192,896]{2,1,0:T(8,128)(2,1)S(1)}, bf16[2,192,896]{2,1,0:T(8,128)(2,1)S(1)}, u32[]{:S(2)}, u32[]{:S(2)}) collective-permute-start(bf16[2,192,896]{2,1,0:T(8,128)(2,1)S(1)} %maximum_select_fusion.2), channel_id=1, source_target_pairs={{0,8},{8,0},{16,24},{24,16},{1,9},{9,1},{17,25},{25,17},{2,10},{10... | collective-permute-start | bytes 2064392 | tf_op jit(solution)/shard_map/ppermute | solution.py:44
  45.7 2.0 %copy-start.3 = (bf16[1,512,3584]{2,1,0:T(8,128)(2,1)S(1)}, bf16[1,512,3584]{2,1,0:T(8,128)(2,1)}, u32[]{:S(2)}) copy-start(bf16[1,512,3584]{2,1,0:T(8,128)(2,1)} %param.13) | copy-start | bytes 11010052
  48.7 2.0 %copy-start.2 = (bf16[1,3584,512]{2,1,0:T(8,128)(2,1)S(1)}, bf16[1,3584,512]{2,1,0:T(8,128)(2,1)}, u32[]{:S(2)}) copy-start(bf16[1,3584,512]{2,1,0:T(8,128)(2,1)} %param.12) | copy-start | bytes 11010052
  50.7 2.0 %copy-start.1 = (bf16[1,3584,512]{2,1,0:T(8,128)(2,1)S(1)}, bf16[1,3584,512]{2,1,0:T(8,128)(2,1)}, u32[]{:S(2)}) copy-start(bf16[1,3584,512]{2,1,0:T(8,128)(2,1)} %param.11) | copy-start | bytes 11010052
  54.2 2.9 %copy-start.4 = (bf16[192,512,1]{1,0,2:T(8,128)(2,1)}, bf16[192,512,1]{1,0,2:T(8,128)(2,1)S(1)}, u32[]{:S(2)}) copy-start(bf16[192,512,1]{1,0,2:T(8,128)(2,1)S(1)} %get-tuple-element.9) | copy-start | bytes 589828
  58.6 5.1 %collective-permute-start.8 = (bf16[2,192,896]{2,1,0:T(8,128)(2,1)S(1)}, bf16[2,192,896]{2,1,0:T(8,128)(2,1)S(1)}, u32[]{:S(2)}, u32[]{:S(2)}) collective-permute-start(bf16[2,192,896]{2,1,0:T(8,128)(2,1)S(1)} %fusion.19), channel_id=1, source_target_pairs={{0,8},{8,0},{16,24},{24,16},{1,9},{9,1},{17,25},{25,17},{2,10},{10... | collective-permute-start | bytes 2064392 | tf_op jit(solution)/shard_map/ppermute | solution.py:60
  59.9 4.6 %collective-permute-start.2 = (bf16[2,192,896]{2,1,0:T(8,128)(2,1)S(1)}, bf16[2,192,896]{2,1,0:T(8,128)(2,1)S(1)}, u32[]{:S(2)}, u32[]{:S(2)}) collective-permute-start(bf16[2,192,896]{2,1,0:T(8,128)(2,1)S(1)} %fusion.18), channel_id=1, source_target_pairs={{0,8},{8,0},{16,24},{24,16},{1,9},{9,1},{17,25},{25,17},{2,10},{10... | collective-permute-start | bytes 2064392 | tf_op jit(solution)/shard_map/ppermute | solution.py:60
  60.0 2.1 %collective-permute-start.6 = (f32[192]{0:T(256)S(1)}, f32[192]{0:T(256)S(1)}, u32[]{:S(2)}, u32[]{:S(2)}) collective-permute-start(f32[192]{0:T(256)S(1)} %get-tuple-element.5), channel_id=1, source_target_pairs={{0,8},{8,0},{16,24},{24,16},{1,9},{9,1},{17,25},{25,17},{2,10},{10... | collective-permute-start | bytes 2312 | tf_op jit(solution)/shard_map/ppermute | solution.py:67
  62.2 19.3 %collective-permute-start.7 = (f32[192]{0:T(256)S(1)}, f32[192]{0:T(256)S(1)}, u32[]{:S(2)}, u32[]{:S(2)}) collective-permute-start(f32[192]{0:T(256)S(1)} %add.59), channel_id=1, source_target_pairs={{0,16},{8,24},{16,0},{24,8},{1,17},{9,25},{17,1},{25,9},{2,18},{10... | collective-permute-start | bytes 2312 | tf_op jit(solution)/shard_map/ppermute | solution.py:67
  63.9 11.0 %collective-permute-start.9 = (bf16[1,192,896]{2,1,0:T(8,128)(2,1)S(1)}, bf16[1,192,896]{2,1,0:T(8,128)(2,1)S(1)}, u32[]{:S(2)}, u32[]{:S(2)}) collective-permute-start(bf16[1,192,896]{2,1,0:T(8,128)(2,1)S(1)} %fusion.24), channel_id=1, source_target_pairs={{0,16},{8,24},{16,0},{24,8},{1,17},{9,25},{17,1},{25,9},{2,18},{10... | collective-permute-start | bytes 1032200 | tf_op jit(solution)/shard_map/ppermute | solution.py:60
  65.5 17.7 %collective-permute-start.3 = (bf16[1,192,896]{2,1,0:T(8,128)(2,1)}, bf16[1,192,896]{2,1,0:T(8,128)(2,1)}, u32[]{:S(2)}, u32[]{:S(2)}) collective-permute-start(bf16[1,192,896]{2,1,0:T(8,128)(2,1)} %fusion.23), channel_id=1, source_target_pairs={{0,16},{8,24},{16,0},{24,8},{1,17},{9,25},{17,1},{25,9},{2,18},{10... | collective-permute-start | bytes 1032200 | tf_op jit(solution)/shard_map/ppermute | solution.py:60
  75.8 14.6 %all-to-all-start.3 = ((bf16[8,24,896]{2,1,0:T(8,128)(2,1)}), bf16[8,24,896]{2,1,0:T(8,128)(2,1)S(1)}, u32[]{:S(2)}, u32[]{:S(2)}) async-start(bf16[8,24,896]{2,1,0:T(8,128)(2,1)} %bitcast.184), calls=%async_computation.3 | async-start | bytes 688128 | tf_op jit(solution)/shard_map/all_to_all | solution.py:98
  83.2 1.1 %copy-start.7 = (bf16[8,24,1]{2,1,0:T(8,128)(2,1)S(1)}, bf16[8,24,1]{2,1,0:T(8,128)(2,1)}, u32[]{:S(2)}) copy-start(bf16[8,24,1]{2,1,0:T(8,128)(2,1)} %concatenate.62) | copy-start | bytes 1156
  83.2 1.1 %copy-start.8 = (bf16[8,24,1]{2,1,0:T(8,128)(2,1)S(1)}, bf16[8,24,1]{2,1,0:T(8,128)(2,1)}, u32[]{:S(2)}) copy-start(bf16[8,24,1]{2,1,0:T(8,128)(2,1)} %concatenate.63) | copy-start | bytes 1156
  84.3 9.7 %copy-start.5 = (bf16[192,512,1]{1,0,2:T(8,128)(2,1)S(1)}, bf16[192,512,1]{1,0,2:T(8,128)(2,1)}, u32[]{:S(2)}) copy-start(bf16[192,512,1]{1,0,2:T(8,128)(2,1)} %copy-done.4) | copy-start | bytes 589828
  90.3 13.0 %all-to-all-start.2 = ((bf16[8,24,1024]{2,1,0:T(8,128)(2,1)}), bf16[8,24,1024]{2,1,0:T(8,128)(2,1)S(1)}, u32[]{:S(2)}, u32[]{:S(2)}) async-start(bf16[8,24,1024]{2,1,0:T(8,128)(2,1)} %maximum_maximum_fusion.1), calls=%async_computation.2 | async-start | bytes 786432 | tf_op jit(solution)/shard_map/all_to_all | solution.py:98
  97.0 6.6 %copy-start.9 = (f32[128,1]{0,1:T(1,128)S(1)}, f32[128,1]{0,1:T(1,128)}, u32[]{:S(2)}) copy-start(f32[128,1]{0,1:T(1,128)} %param.10) | copy-start | bytes 1540

commit v9 on v8

--- a/solution.py
+++ b/solution.py
@@ -124,9 +124,7 @@
     gate_part = jnp.einsum(
         "nsd,nsd->s", partial_out.astype(jnp.float32), grads_in.astype(jnp.float32)
     )
-    expert_out = scatter_sum(partial_out.astype(jnp.float32), n_ctx, me).astype(jnp.bfloat16)
     gate_sum = all_sum(gate_part, n_ctx)
-    back_out = to_experts(with_cols(expert_out, gate_sum, pad))
 
     contract_last = (((1,), (1,)), ((), ()))
     down_t = sum(
@@ -141,9 +139,11 @@
     back_terms = jnp.einsum(
         "sf,ndf->nsd", grad_gate, gate_w, preferred_element_type=jnp.float32
     ) + jnp.einsum("sf,ndf->nsd", grad_up, up_w, preferred_element_type=jnp.float32)
-    back_terms = back_terms.astype(jnp.bfloat16).astype(jnp.float32)
-    slot_grad = scatter_sum(back_terms, n_ctx, me).astype(jnp.bfloat16)
-    back_grad = to_experts(slot_grad)
+    back_terms = back_terms.astype(jnp.bfloat16)
+    both_parts = jnp.concatenate([partial_out, back_terms], axis=2).astype(jnp.float32)
+    both_sums = scatter_sum(both_parts, n_ctx, me).astype(jnp.bfloat16)
+    back = to_experts(with_cols(both_sums, gate_sum, pad))
+    back_grad = back[:, col_width : 2 * col_width]
 
     w_gate_grad = jnp.einsum(
         "nsd,sf->ndf", rows_in, grad_gate, preferred_element_type=jnp.float32
@@ -152,8 +152,8 @@
         "nsd,sf->ndf", rows_in, grad_up, preferred_element_type=jnp.float32
     ).astype(jnp.bfloat16).reshape(1, n_ctx * col_width, group)
 
-    slot_gg = join_f32(back_out[:, col_width], back_out[:, col_width + 1])
-    out_rows = back_out[:, :col_width]
+    slot_gg = join_f32(back[:, 2 * col_width], back[:, 2 * col_width + 1])
+    out_rows = back[:, :col_width]
     layer_out = jnp.zeros((tok_rows, col_width), jnp.float32)
     input_grad = jnp.zeros((tok_rows, col_width), jnp.float32)
     gate_terms = []

time: 106 us -> 116 us (1.094)
  waiting for transfers between devices: 41.7 us -> 55.2 us
  starting transfers between devices: 28.1 us -> 22.4 us
  local copies, waits for them, and re-layouts: 6.45 us -> 7.63 us
    ppermute x2, waiting for transfers between devices: 1.64 us -> 15.9 us  [all_sum(): values = values + lax.ppermute(values, 'ctx', xor_pairs(n_ctx, bit))]
    ppermute x4 -> x2, waiting for transfers between devices: 7.95 us -> 2.76 us  [scatter_sum(): got = lax.ppermute(send, 'ctx', xor_pairs(n_ctx, bit))]
    all_to_all x4 -> x3, waiting for transfers between devices: 17.1 us -> 21.5 us  [to_experts(): got = lax.all_to_all(sent, 'ep', split_axis=0, concat_axis=0, tiled=True)]
    all_to_all x4 -> x3, starting transfers between devices: 20.2 us -> 16.6 us  [to_experts(): got = lax.all_to_all(sent, 'ep', split_axis=0, concat_axis=0, tiled=True)]
    ppermute x2, starting transfers between devices: 2 us -> 0.58 us  [all_sum(): values = values + lax.ppermute(values, 'ctx', xor_pairs(n_ctx, bit))]
    ppermute x4 -> x2, starting transfers between devices: 2.73 us -> 2.09 us  [scatter_sum(): got = lax.ppermute(send, 'ctx', xor_pairs(n_ctx, bit))]
    convert_element_type x4 -> x2, other arithmetic: 2.08 us -> 2.58 us  [the longest x1 2.13 us: shards(): both_sums = scatter_sum(both_parts, n_ctx, me).astype(jnp.bfloat16)]
    unnamed x20 -> x14, local copies, waits for them, and re-layouts: 4.13 us -> 4.57 us
  transfers between devices with their start and end apart: 14 -> 11, of which waited for: 8 -> 8; matrix products, arithmetic and copies ran while one was open for 18% -> 12% of each run, Pallas kernels for 0% -> 0%
where the time goes in v9:
time: 116 us; the launch traced here: 115 us
  waiting for transfers between devices  55.2 us (48%)
  starting transfers between devices  22.4 us (19%)
  matrix products  18.9 us (16%)
  other arithmetic  9.94 us (9%)
  local copies, waits for them, and re-layouts  7.63 us (7%)
    all_to_all x3, waiting for transfers between devices, to_experts(): got = lax.all_to_all(sent, 'ep', split_axis=0, concat_axis=0, tiled=True)  21.5 us
    all_to_all x3, starting transfers between devices, to_experts(): got = lax.all_to_all(sent, 'ep', split_axis=0, concat_axis=0, tiled=True)  16.6 us
    ppermute x2, waiting for transfers between devices, all_sum(): values = values + lax.ppermute(values, 'ctx', xor_pairs(n_ctx, bit))  15.9 us
    ppermute x4, waiting for transfers between devices, gather_blocks(): other = lax.ppermute(held, 'ctx', xor_pairs(n_ctx, bit))  15 us
    unnamed x14, local copies, waits for them, and re-layouts  4.57 us
    ppermute x4, starting transfers between devices, gather_blocks(): other = lax.ppermute(held, 'ctx', xor_pairs(n_ctx, bit))  3.17 us
    dot_general x1, matrix products, shards(): jnp.einsum('nsd,sf->ndf', rows_in, grad_gate, preferred_element_type=jnp....  3 us
    dot_general x1, matrix products, shards(): jnp.einsum('nsd,sf->ndf', rows_in, grad_up, preferred_element_type=jnp.fl...  3 us
  transfers between devices with their start and end apart: 11, of which 8 were waited for; matrix products, arithmetic and copies ran while one was open for 12% of the time, Pallas kernels for 0%

profile of v9, /device:TPU:0, one launch (start us, length us, event | category | flops | bytes accessed | tf_op | source)
XLA Modules:
  0.0 114.9 jit_solution(10972204607516025964)
XLA Ops:
  0.6 0.9 fusion.8
  2.2 1.0 convolution_convert_fusion.2
  3.2 7.2 %all-to-all-start.1 = ((bf16[8,24,896]{2,1,0:T(8,128)(2,1)}), bf16[8,24,896]{2,1,0:T(8,128)(2,1)S(1)}, u32[]{:S(2)}, u32[]{:S(2)}) async-start(bf16[8,24,896]{2,1,0:T(8,128)(2,1)} %bitcast.24), calls=%async_computation.1 | async-start | bytes 688128 | tf_op jit(solution)/shard_map/all_to_all | solution.py:98
  11.6 1.2 %convolution_convert_fusion.3 = bf16[192,896]{1,0:T(8,128)(2,1)S(1)} fusion(bf16[128,896]{1,0:T(8,128)(2,1)} %param.7, s32[128]{0:T(128)S(1)} %fusion.32), kind=kOutput, calls=%fused_computation.24 | convolution fusion | flops 44236800 | bytes 573952 | tf_op jit(solution)/shard_map/ts,tc->sc/dot_general | solution.py:91
  13.7 7.4 %all-to-all-done.1 = bf16[8,24,896]{2,1,0:T(8,128)(2,1)S(1)} async-done(((bf16[8,24,896]{2,1,0:T(8,128)(2,1)}), bf16[8,24,896]{2,1,0:T(8,128)(2,1)S(1)}, u32[]{:S(2)}, u32[]{:S(2)}) %all-to-all-start.1) | async-done | bytes 344096 | tf_op jit(solution)/shard_map/all_to_all | solution.py:98
  21.1 3.6 %all-to-all-start = ((bf16[8,24,1024]{2,1,0:T(8,128)(2,1)}), bf16[8,24,1024]{2,1,0:T(8,128)(2,1)S(1)}, u32[]{:S(2)}, u32[]{:S(2)}) async-start(bf16[8,24,1024]{2,1,0:T(8,128)(2,1)} %pad_maximum_fusion), calls=%async_computation | async-start | bytes 786432 | tf_op jit(solution)/shard_map/all_to_all | solution.py:98
  24.7 1.5 %collective-permute-start.2 = (bf16[1,192,896]{2,1,0:T(8,128)(2,1)S(1)}, bf16[1,192,896]{2,1,0:T(8,128)(2,1)S(1)}, u32[]{:S(2)}, u32[]{:S(2)}) collective-permute-start(bf16[1,192,896]{2,1,0:T(8,128)(2,1)S(1)} %bitcast.139), channel_id=1, source_target_pairs={{0,16},{8,24},{16,0},{24,8},{1,17},{9,25},{17,1},{25,9},{2,18},{10... | collective-permute-start | bytes 1032200 | tf_op jit(solution)/shard_map/ppermute | solution.py:44
  26.2 7.5 %collective-permute-done.2 = bf16[1,192,896]{2,1,0:T(8,128)(2,1)S(1)} collective-permute-done((bf16[1,192,896]{2,1,0:T(8,128)(2,1)S(1)}, bf16[1,192,896]{2,1,0:T(8,128)(2,1)S(1)}, u32[]{:S(2)}, u32[]{:S(2)}) %collective-permute-start.2) | collective-permute-done | bytes 344096 | tf_op jit(solution)/shard_map/ppermute | solution.py:44
  33.8 1.0 maximum_select_fusion.4
  34.7 1.2 %all-to-all-done = bf16[8,24,1024]{2,1,0:T(8,128)(2,1)S(1)} async-done(((bf16[8,24,1024]{2,1,0:T(8,128)(2,1)}), bf16[8,24,1024]{2,1,0:T(8,128)(2,1)S(1)}, u32[]{:S(2)}, u32[]{:S(2)}) %all-to-all-start) | async-done | bytes 393248 | tf_op jit(solution)/shard_map/all_to_all | solution.py:98
  36.0 1.6 %collective-permute-start = (bf16[1,192,896]{2,1,0:T(8,128)(2,1)S(1)}, bf16[1,192,896]{2,1,0:T(8,128)(2,1)S(1)}, u32[]{:S(2)}, u32[]{:S(2)}) collective-permute-start(bf16[1,192,896]{2,1,0:T(8,128)(2,1)S(1)} %get-tuple-element.13), channel_id=1, source_target_pairs={{0,16},{8,24},{16,0},{24,8},{1,17},{9,25},{17,1},{25,9},{2,18},{10... | collective-permute-start | bytes 1032200 | tf_op jit(solution)/shard_map/ppermute | solution.py:44
  37.9 7.4 %collective-permute-done = bf16[1,192,896]{2,1,0:T(8,128)(2,1)S(1)} collective-permute-done((bf16[1,192,896]{2,1,0:T(8,128)(2,1)S(1)}, bf16[1,192,896]{2,1,0:T(8,128)(2,1)S(1)}, u32[]{:S(2)}, u32[]{:S(2)}) %collective-permute-start) | collective-permute-done | bytes 344096 | tf_op jit(solution)/shard_map/ppermute | solution.py:44
  46.1 1.6 %copy-done.5 = bf16[1,512,3584]{2,1,0:T(8,128)(2,1)S(1)} copy-done((bf16[1,512,3584]{2,1,0:T(8,128)(2,1)S(1)}, bf16[1,512,3584]{2,1,0:T(8,128)(2,1)}, u32[]{:S(2)}) %copy-start.5) | copy-done | bytes 3670040
  49.9 1.8 %copy-done.3 = bf16[1,3584,512]{2,1,0:T(8,128)(2,1)S(1)} copy-done((bf16[1,3584,512]{2,1,0:T(8,128)(2,1)S(1)}, bf16[1,3584,512]{2,1,0:T(8,128)(2,1)}, u32[]{:S(2)}) %copy-start.3) | copy-done | bytes 3670040
  51.7 0.9 convolution_bitcast_fusion.5
  52.6 1.1 copy-done.4
  53.7 1.0 multiply_convert_fusion.2
  56.2 1.4 %fusion.24 = f32[192,4,896]{2,0,1:T(8,128)S(1)} fusion(bf16[4,896,512]{2,1,0:T(8,128)(2,1)S(1)} %bitcast.134, bf16[192,512]{1,0:T(8,128)(2,1)S(1)} %get-tuple-element.10), kind=kOutput, calls=%fused_computation.65 | convolution fusion | flops 704643072 | bytes 6619136 | tf_op jit(solution)/shard_map/sf,ndf->nsd/dot_general | solution.py:139
  57.6 1.4 %add_convert_fusion = bf16[192,4,896]{2,0,1:T(8,128)(2,1)S(1)} fusion(f32[192,4,896]{2,0,1:T(8,128)S(1)} %fusion.24, bf16[192,512,1]{1,0,2:T(8,128)(2,1)S(1)} %get-tuple-element.11, bf16[4,896,512]{2,1,0:T(8,128)(2,1)S(1)} %bitcast.138), kind=kOutput, calls=%fused_computation.9 | convolution fusion | flops 706019328 | bytes 7995392 | tf_op jit(solution)/shard_map/sf,ndf->nsd/dot_general | solution.py:141
  60.7 2.8 %collective-permute-done.4 = bf16[2,192,1792]{2,1,0:T(8,128)(2,1)S(1)} collective-permute-done((bf16[2,192,1792]{2,1,0:T(8,128)(2,1)S(1)}, bf16[2,192,1792]{2,1,0:T(8,128)(2,1)S(1)}, u32[]{:S(2)}, u32[]{:S(2)}) %collective-permute-start.4) | collective-permute-done | bytes 1376288 | tf_op jit(solution)/shard_map/ppermute | solution.py:60
  63.9 1.0 fusion.18
  64.9 1.5 %collective-permute-start.5 = (bf16[1,192,1792]{2,1,0:T(8,128)(2,1)}, bf16[1,192,1792]{2,1,0:T(8,128)(2,1)}, u32[]{:S(2)}, u32[]{:S(2)}) collective-permute-start(bf16[1,192,1792]{2,1,0:T(8,128)(2,1)} %fusion.18), channel_id=1, source_target_pairs={{0,16},{8,24},{16,0},{24,8},{1,17},{9,25},{17,1},{25,9},{2,18},{10... | collective-permute-start | bytes 2064392 | tf_op jit(solution)/shard_map/ppermute | solution.py:60
  66.5 1.1 collective-permute-done.6
  68.1 14.9 %collective-permute-done.7 = f32[192]{0:T(256)S(1)} collective-permute-done((f32[192]{0:T(256)S(1)}, f32[192]{0:T(256)S(1)}, u32[]{:S(2)}, u32[]{:S(2)}) %collective-permute-start.7) | collective-permute-done | bytes 800 | tf_op jit(solution)/shard_map/ppermute | solution.py:67
  83.4 2.1 %fusion.5 = bf16[1,192,1792]{2,1,0:T(8,128)(2,1)} fusion(bf16[1,192,1792]{2,1,0:T(8,128)(2,1)} %collective-permute-done.5, f32[1,2,192,1792]{3,2,1,0:T(8,128)S(1)} %fusion.2, pred[]{:T(512)S(6)} %eq.48), kind=kLoop, calls=%fused_computation.16 | loop fusion | flops 1376256 | bytes 4128769 | tf_op jit(solution)/shard_map/convert_element_type | solution.py:144
  85.6 2.1 %concatenate.69 = bf16[8,24,1920]{2,1,0:T(8,128)(2,1)} concatenate(bf16[8,24,1792]{2,1,0:T(8,128)(2,1)} %bitcast.142, bf16[8,24,1]{2,1,0:T(8,128)(2,1)S(1)} %concatenate.70, bf16[8,24,1]{2,1,0:T(8,128)(2,1)S(1)} %concatenate.71, bf16[8,24,126]{2,1,0:T(8,128)(2,1)S(1)} %concatenate.63), dimensions={2} | concatenate | bytes 1474560 | tf_op jit(solution)/shard_map/concatenate | solution.py:74
  87.6 5.7 %all-to-all-start.2 = ((bf16[8,24,1920]{2,1,0:T(8,128)(2,1)}), bf16[8,24,1920]{2,1,0:T(8,128)(2,1)S(1)}, u32[]{:S(2)}, u32[]{:S(2)}) async-start(bf16[8,24,1920]{2,1,0:T(8,128)(2,1)} %concatenate.69), calls=%async_computation.2 | async-start | bytes 1474560 | tf_op jit(solution)/shard_map/all_to_all | solution.py:98
  93.3 3.0 %convolution_convert_fusion.1 = bf16[4,896,512]{2,1,0:T(8,128)(2,1)} fusion(bf16[4,192,896]{2,1,0:T(8,128)(2,1)S(1)} %bitcast.124, bf16[192,512]{1,0:T(8,128)(2,1)S(1)} %get-tuple-element.10), kind=kOutput, calls=%fused_computation.11 | convolution fusion | flops 706478080 | bytes 5242880 | tf_op jit(solution)/shard_map/nsd,sf->ndf/dot_general | solution.py:148
  96.3 3.0 %convolution_convert_fusion = bf16[4,896,512]{2,1,0:T(8,128)(2,1)} fusion(bf16[4,192,896]{2,1,0:T(8,128)(2,1)S(1)} %bitcast.125, bf16[192,512,1]{1,0,2:T(8,128)(2,1)S(1)} %get-tuple-element.11), kind=kOutput, calls=%fused_computation.10 | convolution fusion | flops 706478080 | bytes 5242880 | tf_op jit(solution)/shard_map/nsd,sf->ndf/dot_general | solution.py:151
  99.3 12.8 %all-to-all-done.2 = bf16[8,24,1920]{2,1,0:T(8,128)(2,1)S(1)} async-done(((bf16[8,24,1920]{2,1,0:T(8,128)(2,1)}), bf16[8,24,1920]{2,1,0:T(8,128)(2,1)S(1)}, u32[]{:S(2)}, u32[]{:S(2)}) %all-to-all-start.2) | async-done | bytes 737312 | tf_op jit(solution)/shard_map/all_to_all | solution.py:98
  112.2 1.0 fusion.7
  113.2 1.0 convolution_convert_fusion.4
  (53 shorter events, 11.5 us)
Async XLA Ops:
  0.6 1.6 %copy-start = (bf16[128,896]{1,0:T(8,128)(2,1)S(1)}, bf16[128,896]{1,0:T(8,128)(2,1)}, u32[]{:S(2)}) copy-start(bf16[128,896]{1,0:T(8,128)(2,1)} %param.8) | copy-start | bytes 688132
  3.2 17.9 %all-to-all-start.1 = ((bf16[8,24,896]{2,1,0:T(8,128)(2,1)}), bf16[8,24,896]{2,1,0:T(8,128)(2,1)S(1)}, u32[]{:S(2)}, u32[]{:S(2)}) async-start(bf16[8,24,896]{2,1,0:T(8,128)(2,1)} %bitcast.24), calls=%async_computation.1 | async-start | bytes 688128 | tf_op jit(solution)/shard_map/all_to_all | solution.py:98
  21.1 14.9 %all-to-all-start = ((bf16[8,24,1024]{2,1,0:T(8,128)(2,1)}), bf16[8,24,1024]{2,1,0:T(8,128)(2,1)S(1)}, u32[]{:S(2)}, u32[]{:S(2)}) async-start(bf16[8,24,1024]{2,1,0:T(8,128)(2,1)} %pad_maximum_fusion), calls=%async_computation | async-start | bytes 786432 | tf_op jit(solution)/shard_map/all_to_all | solution.py:98
  24.7 9.1 %collective-permute-start.2 = (bf16[1,192,896]{2,1,0:T(8,128)(2,1)S(1)}, bf16[1,192,896]{2,1,0:T(8,128)(2,1)S(1)}, u32[]{:S(2)}, u32[]{:S(2)}) collective-permute-start(bf16[1,192,896]{2,1,0:T(8,128)(2,1)S(1)} %bitcast.139), channel_id=1, source_target_pairs={{0,16},{8,24},{16,0},{24,8},{1,17},{9,25},{17,1},{25,9},{2,18},{10... | collective-permute-start | bytes 1032200 | tf_op jit(solution)/shard_map/ppermute | solution.py:44
  34.7 10.9 %collective-permute-start.3 = (bf16[2,192,896]{2,1,0:T(8,128)(2,1)}, bf16[2,192,896]{2,1,0:T(8,128)(2,1)S(1)}, u32[]{:S(2)}, u32[]{:S(2)}) collective-permute-start(bf16[2,192,896]{2,1,0:T(8,128)(2,1)} %maximum_select_fusion.4), channel_id=1, source_target_pairs={{0,8},{8,0},{16,24},{24,16},{1,9},{9,1},{17,25},{25,17},{2,10},{10... | collective-permute-start | bytes 2064392 | tf_op jit(solution)/shard_map/ppermute | solution.py:44
  36.0 9.3 %collective-permute-start = (bf16[1,192,896]{2,1,0:T(8,128)(2,1)S(1)}, bf16[1,192,896]{2,1,0:T(8,128)(2,1)S(1)}, u32[]{:S(2)}, u32[]{:S(2)}) collective-permute-start(bf16[1,192,896]{2,1,0:T(8,128)(2,1)S(1)} %get-tuple-element.13), channel_id=1, source_target_pairs={{0,16},{8,24},{16,0},{24,8},{1,17},{9,25},{17,1},{25,9},{2,18},{10... | collective-permute-start | bytes 1032200 | tf_op jit(solution)/shard_map/ppermute | solution.py:44
  45.5 4.2 %collective-permute-start.1 = (bf16[2,192,896]{2,1,0:T(8,128)(2,1)S(1)}, bf16[2,192,896]{2,1,0:T(8,128)(2,1)S(1)}, u32[]{:S(2)}, u32[]{:S(2)}) collective-permute-start(bf16[2,192,896]{2,1,0:T(8,128)(2,1)S(1)} %maximum_select_fusion.2), channel_id=1, source_target_pairs={{0,8},{8,0},{16,24},{24,16},{1,9},{9,1},{17,25},{25,17},{2,10},{10... | collective-permute-start | bytes 2064392 | tf_op jit(solution)/shard_map/ppermute | solution.py:44
  45.7 2.0 %copy-start.5 = (bf16[1,512,3584]{2,1,0:T(8,128)(2,1)S(1)}, bf16[1,512,3584]{2,1,0:T(8,128)(2,1)}, u32[]{:S(2)}) copy-start(bf16[1,512,3584]{2,1,0:T(8,128)(2,1)} %param.13) | copy-start | bytes 11010052
  49.1 2.5 %copy-start.3 = (bf16[1,3584,512]{2,1,0:T(8,128)(2,1)S(1)}, bf16[1,3584,512]{2,1,0:T(8,128)(2,1)}, u32[]{:S(2)}) copy-start(bf16[1,3584,512]{2,1,0:T(8,128)(2,1)} %param.11) | copy-start | bytes 11010052
  49.9 2.7 %copy-start.1 = (bf16[2,2,192,896]{3,2,1,0:T(8,128)(2,1)}, bf16[2,2,192,896]{3,2,1,0:T(8,128)(2,1)S(1)}, u32[]{:S(2)}) copy-start(bf16[2,2,192,896]{3,2,1,0:T(8,128)(2,1)S(1)} %maximum_select_fusion) | copy-start | bytes 4128772
  51.7 2.0 %copy-start.4 = (bf16[1,3584,512]{2,1,0:T(8,128)(2,1)S(1)}, bf16[1,3584,512]{2,1,0:T(8,128)(2,1)}, u32[]{:S(2)}) copy-start(bf16[1,3584,512]{2,1,0:T(8,128)(2,1)} %param.12) | copy-start | bytes 11010052
  60.1 3.3 %collective-permute-start.4 = (bf16[2,192,1792]{2,1,0:T(8,128)(2,1)S(1)}, bf16[2,192,1792]{2,1,0:T(8,128)(2,1)S(1)}, u32[]{:S(2)}, u32[]{:S(2)}) collective-permute-start(bf16[2,192,1792]{2,1,0:T(8,128)(2,1)S(1)} %fusion.4), channel_id=1, source_target_pairs={{0,8},{8,0},{16,24},{24,16},{1,9},{9,1},{17,25},{25,17},{2,10},{10... | collective-permute-start | bytes 4128776 | tf_op jit(solution)/shard_map/ppermute | solution.py:60
  64.9 18.5 %collective-permute-start.5 = (bf16[1,192,1792]{2,1,0:T(8,128)(2,1)}, bf16[1,192,1792]{2,1,0:T(8,128)(2,1)}, u32[]{:S(2)}, u32[]{:S(2)}) collective-permute-start(bf16[1,192,1792]{2,1,0:T(8,128)(2,1)} %fusion.18), channel_id=1, source_target_pairs={{0,16},{8,24},{16,0},{24,8},{1,17},{9,25},{17,1},{25,9},{2,18},{10... | collective-permute-start | bytes 2064392 | tf_op jit(solution)/shard_map/ppermute | solution.py:60
  66.4 1.1 collective-permute-start.6
  67.6 15.4 %collective-permute-start.7 = (f32[192]{0:T(256)S(1)}, f32[192]{0:T(256)S(1)}, u32[]{:S(2)}, u32[]{:S(2)}) collective-permute-start(f32[192]{0:T(256)S(1)} %add.59), channel_id=1, source_target_pairs={{0,16},{8,24},{16,0},{24,8},{1,17},{9,25},{17,1},{25,9},{2,18},{10... | collective-permute-start | bytes 2312 | tf_op jit(solution)/shard_map/ppermute | solution.py:67
  85.6 7.8 %copy-start.2 = (bf16[2,2,192,896]{3,2,1,0:T(8,128)(2,1)S(1)}, bf16[2,2,192,896]{3,2,1,0:T(8,128)(2,1)}, u32[]{:S(2)}) copy-start(bf16[2,2,192,896]{3,2,1,0:T(8,128)(2,1)} %copy-done.1) | copy-start | bytes 4128772
  87.6 24.6 %all-to-all-start.2 = ((bf16[8,24,1920]{2,1,0:T(8,128)(2,1)}), bf16[8,24,1920]{2,1,0:T(8,128)(2,1)S(1)}, u32[]{:S(2)}, u32[]{:S(2)}) async-start(bf16[8,24,1920]{2,1,0:T(8,128)(2,1)} %concatenate.69), calls=%async_computation.2 | async-start | bytes 1474560 | tf_op jit(solution)/shard_map/all_to_all | solution.py:98
  96.3 15.8 %copy-start.6 = (f32[128,1]{0,1:T(1,128)S(1)}, f32[128,1]{0,1:T(1,128)}, u32[]{:S(2)}) copy-start(f32[128,1]{0,1:T(1,128)} %param.10) | copy-start | bytes 1540

commit v10 on v8

--- a/solution.py
+++ b/solution.py
@@ -70,8 +70,10 @@
 
 def with_cols(rows, values, pad):
     hi, lo = split_f32(values)
-    zeros = jnp.zeros((rows.shape[0], pad - 2), jnp.bfloat16)
-    return jnp.concatenate([rows, hi[:, None], lo[:, None], zeros], axis=1)
+    lane = lax.broadcasted_iota(jnp.int32, (rows.shape[0], pad), 1)
+    zero = jnp.zeros((), jnp.bfloat16)
+    cols = jnp.where(lane == 0, hi[:, None], jnp.where(lane == 1, lo[:, None], zero))
+    return jnp.concatenate([rows, cols], axis=1)
 
 
 def shards(tokens, cotangent, expert_ids, route_gates, w_gate, w_up, w_down):

time: 106 us -> 109 us (1.028)
  other arithmetic: 10 us -> 14.4 us
  local copies, waits for them, and re-layouts: 6.45 us -> 4.92 us
    reshape x2, other arithmetic: 0.34 us -> 2.76 us  [scatter_sum(): halves = acc.reshape((-1, 2) + acc.shape[1:])]
    concatenate x4 -> x0, local copies, waits for them, and re-layouts: 1.79 us -> none  [with_cols(): return jnp.concatenate([rows, hi[:, None], lo[:, None], zeros], axis=1)]
    convert_element_type x4, other arithmetic: 1.15 us -> 2.87 us  [scatter_sum(): jnp.where(keep_first, halves[:, 1], halves[:, 0]).astype(jnp.bfloat16)]
    ppermute x4, waiting for transfers between devices: 7.95 us -> 6.84 us  [scatter_sum(): got = lax.ppermute(send, 'ctx', xor_pairs(n_ctx, bit))]
    unnamed x20 -> x22, local copies, waits for them, and re-layouts: 4.13 us -> 4.58 us
  transfers between devices with their start and end apart: 14 -> 14, of which waited for: 8 -> 9; matrix products, arithmetic and copies ran while one was open for 18% -> 20% of each run, Pallas kernels for 0% -> 0%
where the time goes in v10:
time: 109 us; the launch traced here: 108 us
  waiting for transfers between devices  41.5 us (38%)
  starting transfers between devices  27.6 us (25%)
  matrix products  18.9 us (17%)
  other arithmetic  14.4 us (13%)
  local copies, waits for them, and re-layouts  4.92 us (5%)
    all_to_all x4, starting transfers between devices, to_experts(): got = lax.all_to_all(sent, 'ep', split_axis=0, concat_axis=0, tiled=True)  20.2 us
    all_to_all x4, waiting for transfers between devices, to_experts(): got = lax.all_to_all(sent, 'ep', split_axis=0, concat_axis=0, tiled=True)  17.7 us
    ppermute x4, waiting for transfers between devices, gather_blocks(): other = lax.ppermute(held, 'ctx', xor_pairs(n_ctx, bit))  15 us
    ppermute x4, waiting for transfers between devices, scatter_sum(): got = lax.ppermute(send, 'ctx', xor_pairs(n_ctx, bit))  6.84 us
    unnamed x22, local copies, waits for them, and re-layouts  4.58 us
    dot_general x1, matrix products, shards(): jnp.einsum('nsd,sf->ndf', rows_in, grad_up, preferred_element_type=jnp.fl...  3.91 us
    ppermute x4, starting transfers between devices, gather_blocks(): other = lax.ppermute(held, 'ctx', xor_pairs(n_ctx, bit))  3.18 us
    dot_general x1, matrix products, shards(): jnp.einsum('nsd,sf->ndf', rows_in, grad_gate, preferred_element_type=jnp....  3 us
  transfers between devices with their start and end apart: 14, of which 9 were waited for; matrix products, arithmetic and copies ran while one was open for 20% of the time, Pallas kernels for 0%

profile of v10, /device:TPU:0, one launch (start us, length us, event | category | flops | bytes accessed | tf_op | source)
XLA Modules:
  0.0 108.3 jit_solution(11580023158875627779)
XLA Ops:
  2.2 1.0 convolution_convert_fusion.2
  3.2 7.3 %all-to-all-start.1 = ((bf16[8,24,896]{2,1,0:T(8,128)(2,1)}), bf16[8,24,896]{2,1,0:T(8,128)(2,1)S(1)}, u32[]{:S(2)}, u32[]{:S(2)}) async-start(bf16[8,24,896]{2,1,0:T(8,128)(2,1)} %bitcast.34), calls=%async_computation.1 | async-start | bytes 688128 | tf_op jit(solution)/shard_map/all_to_all | solution.py:100
  12.4 8.7 %all-to-all-done.1 = bf16[8,24,896]{2,1,0:T(8,128)(2,1)S(1)} async-done(((bf16[8,24,896]{2,1,0:T(8,128)(2,1)}), bf16[8,24,896]{2,1,0:T(8,128)(2,1)S(1)}, u32[]{:S(2)}, u32[]{:S(2)}) %all-to-all-start.1) | async-done | bytes 344096 | tf_op jit(solution)/shard_map/all_to_all | solution.py:100
  21.1 3.6 %all-to-all-start = ((bf16[8,24,1024]{2,1,0:T(8,128)(2,1)}), bf16[8,24,1024]{2,1,0:T(8,128)(2,1)S(1)}, u32[]{:S(2)}, u32[]{:S(2)}) async-start(bf16[8,24,1024]{2,1,0:T(8,128)(2,1)} %bitcast.7), calls=%async_computation | async-start | bytes 786432 | tf_op jit(solution)/shard_map/all_to_all | solution.py:100
  24.7 1.5 %collective-permute-start.4 = (bf16[1,192,896]{2,1,0:T(8,128)(2,1)S(1)}, bf16[1,192,896]{2,1,0:T(8,128)(2,1)S(1)}, u32[]{:S(2)}, u32[]{:S(2)}) collective-permute-start(bf16[1,192,896]{2,1,0:T(8,128)(2,1)S(1)} %bitcast.174), channel_id=1, source_target_pairs={{0,16},{8,24},{16,0},{24,8},{1,17},{9,25},{17,1},{25,9},{2,18},{10... | collective-permute-start | bytes 1032200 | tf_op jit(solution)/shard_map/ppermute | solution.py:44
  26.2 7.5 %collective-permute-done.4 = bf16[1,192,896]{2,1,0:T(8,128)(2,1)S(1)} collective-permute-done((bf16[1,192,896]{2,1,0:T(8,128)(2,1)S(1)}, bf16[1,192,896]{2,1,0:T(8,128)(2,1)S(1)}, u32[]{:S(2)}, u32[]{:S(2)}) %collective-permute-start.4) | collective-permute-done | bytes 344096 | tf_op jit(solution)/shard_map/ppermute | solution.py:44
  33.8 1.0 maximum_select_fusion.4
  34.7 1.2 %all-to-all-done = bf16[8,24,1024]{2,1,0:T(8,128)(2,1)S(1)} async-done(((bf16[8,24,1024]{2,1,0:T(8,128)(2,1)}), bf16[8,24,1024]{2,1,0:T(8,128)(2,1)S(1)}, u32[]{:S(2)}, u32[]{:S(2)}) %all-to-all-start) | async-done | bytes 393248 | tf_op jit(solution)/shard_map/all_to_all | solution.py:100
  36.0 1.6 %collective-permute-start = (bf16[1,192,896]{2,1,0:T(8,128)(2,1)S(1)}, bf16[1,192,896]{2,1,0:T(8,128)(2,1)S(1)}, u32[]{:S(2)}, u32[]{:S(2)}) collective-permute-start(bf16[1,192,896]{2,1,0:T(8,128)(2,1)S(1)} %get-tuple-element.13), channel_id=1, source_target_pairs={{0,16},{8,24},{16,0},{24,8},{1,17},{9,25},{17,1},{25,9},{2,18},{10... | collective-permute-start | bytes 1032200 | tf_op jit(solution)/shard_map/ppermute | solution.py:44
  37.9 7.4 %collective-permute-done = bf16[1,192,896]{2,1,0:T(8,128)(2,1)S(1)} collective-permute-done((bf16[1,192,896]{2,1,0:T(8,128)(2,1)S(1)}, bf16[1,192,896]{2,1,0:T(8,128)(2,1)S(1)}, u32[]{:S(2)}, u32[]{:S(2)}) %collective-permute-start) | collective-permute-done | bytes 344096 | tf_op jit(solution)/shard_map/ppermute | solution.py:44
  46.1 1.6 %copy-done.7 = bf16[1,512,3584]{2,1,0:T(8,128)(2,1)S(1)} copy-done((bf16[1,512,3584]{2,1,0:T(8,128)(2,1)S(1)}, bf16[1,512,3584]{2,1,0:T(8,128)(2,1)}, u32[]{:S(2)}) %copy-start.7) | copy-done | bytes 3670040
  49.5 1.8 %copy-done.6 = bf16[1,3584,512]{2,1,0:T(8,128)(2,1)S(1)} copy-done((bf16[1,3584,512]{2,1,0:T(8,128)(2,1)S(1)}, bf16[1,3584,512]{2,1,0:T(8,128)(2,1)}, u32[]{:S(2)}) %copy-start.6) | copy-done | bytes 3670040
  52.1 1.1 %copy-done.5 = bf16[1,3584,512]{2,1,0:T(8,128)(2,1)S(1)} copy-done((bf16[1,3584,512]{2,1,0:T(8,128)(2,1)S(1)}, bf16[1,3584,512]{2,1,0:T(8,128)(2,1)}, u32[]{:S(2)}) %copy-start.5) | copy-done | bytes 3670040
  56.3 1.3 %fusion.28 = f32[192,4,896]{2,0,1:T(8,128)S(1)} fusion(bf16[4,896,512]{2,1,0:T(8,128)(2,1)S(1)} %bitcast.169, bf16[192,512]{1,0:T(8,128)(2,1)S(1)} %get-tuple-element.10), kind=kOutput, calls=%fused_computation.75 | convolution fusion | flops 704643072 | bytes 6619136 | tf_op jit(solution)/shard_map/sf,ndf->nsd/dot_general | solution.py:143
  57.6 1.3 %fusion.1 = f32[192,4,896]{2,0,1:T(8,128)S(1)} fusion(f32[192,4,896]{2,0,1:T(8,128)S(1)} %fusion.28, bf16[192,512,1]{1,0,2:T(8,128)(2,1)S(1)} %get-tuple-element.9, bf16[4,896,512]{2,1,0:T(8,128)(2,1)S(1)} %bitcast.171), kind=kOutput, calls=%fused_computation.6 | convolution fusion | flops 706707456 | bytes 9371648 | tf_op jit(solution)/shard_map/sf,ndf->nsd/dot_general | solution.py:145
  59.0 1.0 fusion.19
  61.2 1.0 collective-permute-done.6
  62.3 1.5 %collective-permute-start.7 = (f32[192]{0:T(256)S(1)}, f32[192]{0:T(256)S(1)}, u32[]{:S(2)}, u32[]{:S(2)}) collective-permute-start(f32[192]{0:T(256)S(1)} %add.59), channel_id=1, source_target_pairs={{0,16},{8,24},{16,0},{24,8},{1,17},{9,25},{17,1},{25,9},{2,18},{10... | collective-permute-start | bytes 2312 | tf_op jit(solution)/shard_map/ppermute | solution.py:67
  63.8 1.0 fusion.18
  64.8 1.0 collective-permute-done.7
  66.0 1.4 %fusion.5 = f32[1,2,192,896]{3,2,1,0:T(8,128)S(1)} fusion(bf16[2,192,896]{2,1,0:T(8,128)(2,1)} %collective-permute-done.8, f32[2,2,192,896]{3,2,1,0:T(8,128)S(1)} %bitcast.157, pred[]{:T(512)S(6)} %eq.65), kind=kLoop, calls=%fused_computation.16 | loop fusion | flops 1032192 | bytes 4816897 | tf_op jit(solution)/shard_map/reshape | solution.py:56
  67.5 1.6 %collective-permute-start.9 = (bf16[1,192,896]{2,1,0:T(8,128)(2,1)S(1)}, bf16[1,192,896]{2,1,0:T(8,128)(2,1)S(1)}, u32[]{:S(2)}, u32[]{:S(2)}) collective-permute-start(bf16[1,192,896]{2,1,0:T(8,128)(2,1)S(1)} %fusion.24), channel_id=1, source_target_pairs={{0,16},{8,24},{16,0},{24,8},{1,17},{9,25},{17,1},{25,9},{2,18},{10... | collective-permute-start | bytes 1032200 | tf_op jit(solution)/shard_map/ppermute | solution.py:60
  69.1 1.3 %fusion.4 = f32[1,2,192,896]{3,2,1,0:T(8,128)S(1)} fusion(bf16[2,192,896]{2,1,0:T(8,128)(2,1)} %collective-permute-done.2, f32[2,2,192,896]{3,2,1,0:T(8,128)S(1)} %copy-done.2, pred[]{:T(512)S(6)} %eq.65), kind=kLoop, calls=%fused_computation.14 | loop fusion | flops 1032192 | bytes 4816897 | tf_op jit(solution)/shard_map/reshape | solution.py:56
  71.8 6.8 %collective-permute-done.9 = bf16[1,192,896]{2,1,0:T(8,128)(2,1)S(1)} collective-permute-done((bf16[1,192,896]{2,1,0:T(8,128)(2,1)S(1)}, bf16[1,192,896]{2,1,0:T(8,128)(2,1)S(1)}, u32[]{:S(2)}, u32[]{:S(2)}) %collective-permute-start.9) | collective-permute-done | bytes 344096 | tf_op jit(solution)/shard_map/ppermute | solution.py:60
  79.4 5.7 %all-to-all-start.3 = ((bf16[8,24,896]{2,1,0:T(8,128)(2,1)}), bf16[8,24,896]{2,1,0:T(8,128)(2,1)S(1)}, u32[]{:S(2)}, u32[]{:S(2)}) async-start(bf16[8,24,896]{2,1,0:T(8,128)(2,1)} %bitcast.56), calls=%async_computation.3 | async-start | bytes 688128 | tf_op jit(solution)/shard_map/all_to_all | solution.py:100
  85.3 1.2 %fusion.21 = bf16[1,192,896]{2,1,0:T(8,128)(2,1)S(1)} fusion(bf16[1,192,896]{2,1,0:T(8,128)(2,1)} %collective-permute-done.3, f32[1,2,192,896]{3,2,1,0:T(8,128)S(1)} %fusion.4, pred[]{:T(512)S(6)} %eq.64), kind=kLoop, calls=%fused_computation.54 | loop fusion | flops 688128 | bytes 2064385 | tf_op jit(solution)/shard_map/convert_element_type | solution.py:129
  87.3 6.7 %all-to-all-done.3 = bf16[8,24,896]{2,1,0:T(8,128)(2,1)S(1)} async-done(((bf16[8,24,896]{2,1,0:T(8,128)(2,1)}), bf16[8,24,896]{2,1,0:T(8,128)(2,1)S(1)}, u32[]{:S(2)}, u32[]{:S(2)}) %all-to-all-start.3) | async-done | bytes 344096 | tf_op jit(solution)/shard_map/all_to_all | solution.py:100
  93.9 3.6 %all-to-all-start.2 = ((bf16[8,24,1024]{2,1,0:T(8,128)(2,1)}), bf16[8,24,1024]{2,1,0:T(8,128)(2,1)S(1)}, u32[]{:S(2)}, u32[]{:S(2)}) async-start(bf16[8,24,1024]{2,1,0:T(8,128)(2,1)} %pad_maximum_fusion.1), calls=%async_computation.2 | async-start | bytes 786432 | tf_op jit(solution)/shard_map/all_to_all | solution.py:100
  97.6 3.9 %convolution_convert_fusion = bf16[4,896,512]{2,1,0:T(8,128)(2,1)} fusion(bf16[4,192,896]{2,1,0:T(8,128)(2,1)S(1)} %bitcast.160, bf16[192,512,1]{1,0,2:T(8,128)(2,1)} %copy-done.8), kind=kOutput, calls=%fused_computation.4 | convolution fusion | flops 706478080 | bytes 5242880 | tf_op jit(solution)/shard_map/nsd,sf->ndf/dot_general | solution.py:153
  101.5 3.0 %convolution_convert_fusion.1 = bf16[4,896,512]{2,1,0:T(8,128)(2,1)} fusion(bf16[4,192,896]{2,1,0:T(8,128)(2,1)S(1)} %bitcast.161, bf16[192,512]{1,0:T(8,128)(2,1)S(1)} %get-tuple-element.10), kind=kOutput, calls=%fused_computation.5 | convolution fusion | flops 706478080 | bytes 5242880 | tf_op jit(solution)/shard_map/nsd,sf->ndf/dot_general | solution.py:150
  105.5 1.1 all-to-all-done.2
  106.7 1.0 fusion.7
  (70 shorter events, 16.5 us)
Async XLA Ops:
  0.6 1.6 %copy-start = (bf16[128,896]{1,0:T(8,128)(2,1)S(1)}, bf16[128,896]{1,0:T(8,128)(2,1)}, u32[]{:S(2)}) copy-start(bf16[128,896]{1,0:T(8,128)(2,1)} %param.8) | copy-start | bytes 688132
  0.6 10.7 %copy-start.9 = (bf16[128,896]{1,0:T(8,128)(2,1)S(1)}, bf16[128,896]{1,0:T(8,128)(2,1)}, u32[]{:S(2)}) copy-start(bf16[128,896]{1,0:T(8,128)(2,1)} %param.7) | copy-start | bytes 688132
  3.2 17.9 %all-to-all-start.1 = ((bf16[8,24,896]{2,1,0:T(8,128)(2,1)}), bf16[8,24,896]{2,1,0:T(8,128)(2,1)S(1)}, u32[]{:S(2)}, u32[]{:S(2)}) async-start(bf16[8,24,896]{2,1,0:T(8,128)(2,1)} %bitcast.34), calls=%async_computation.1 | async-start | bytes 688128 | tf_op jit(solution)/shard_map/all_to_all | solution.py:100
  21.1 14.9 %all-to-all-start = ((bf16[8,24,1024]{2,1,0:T(8,128)(2,1)}), bf16[8,24,1024]{2,1,0:T(8,128)(2,1)S(1)}, u32[]{:S(2)}, u32[]{:S(2)}) async-start(bf16[8,24,1024]{2,1,0:T(8,128)(2,1)} %bitcast.7), calls=%async_computation | async-start | bytes 786432 | tf_op jit(solution)/shard_map/all_to_all | solution.py:100
  24.7 9.1 %collective-permute-start.4 = (bf16[1,192,896]{2,1,0:T(8,128)(2,1)S(1)}, bf16[1,192,896]{2,1,0:T(8,128)(2,1)S(1)}, u32[]{:S(2)}, u32[]{:S(2)}) collective-permute-start(bf16[1,192,896]{2,1,0:T(8,128)(2,1)S(1)} %bitcast.174), channel_id=1, source_target_pairs={{0,16},{8,24},{16,0},{24,8},{1,17},{9,25},{17,1},{25,9},{2,18},{10... | collective-permute-start | bytes 1032200 | tf_op jit(solution)/shard_map/ppermute | solution.py:44
  34.7 10.9 %collective-permute-start.5 = (bf16[2,192,896]{2,1,0:T(8,128)(2,1)}, bf16[2,192,896]{2,1,0:T(8,128)(2,1)S(1)}, u32[]{:S(2)}, u32[]{:S(2)}) collective-permute-start(bf16[2,192,896]{2,1,0:T(8,128)(2,1)} %maximum_select_fusion.4), channel_id=1, source_target_pairs={{0,8},{8,0},{16,24},{24,16},{1,9},{9,1},{17,25},{25,17},{2,10},{10... | collective-permute-start | bytes 2064392 | tf_op jit(solution)/shard_map/ppermute | solution.py:44
  36.0 9.3 %collective-permute-start = (bf16[1,192,896]{2,1,0:T(8,128)(2,1)S(1)}, bf16[1,192,896]{2,1,0:T(8,128)(2,1)S(1)}, u32[]{:S(2)}, u32[]{:S(2)}) collective-permute-start(bf16[1,192,896]{2,1,0:T(8,128)(2,1)S(1)} %get-tuple-element.13), channel_id=1, source_target_pairs={{0,16},{8,24},{16,0},{24,8},{1,17},{9,25},{17,1},{25,9},{2,18},{10... | collective-permute-start | bytes 1032200 | tf_op jit(solution)/shard_map/ppermute | solution.py:44
  45.5 3.7 %collective-permute-start.1 = (bf16[2,192,896]{2,1,0:T(8,128)(2,1)S(1)}, bf16[2,192,896]{2,1,0:T(8,128)(2,1)S(1)}, u32[]{:S(2)}, u32[]{:S(2)}) collective-permute-start(bf16[2,192,896]{2,1,0:T(8,128)(2,1)S(1)} %maximum_select_fusion.2), channel_id=1, source_target_pairs={{0,8},{8,0},{16,24},{24,16},{1,9},{9,1},{17,25},{25,17},{2,10},{10... | collective-permute-start | bytes 2064392 | tf_op jit(solution)/shard_map/ppermute | solution.py:44
  45.7 2.0 %copy-start.7 = (bf16[1,512,3584]{2,1,0:T(8,128)(2,1)S(1)}, bf16[1,512,3584]{2,1,0:T(8,128)(2,1)}, u32[]{:S(2)}) copy-start(bf16[1,512,3584]{2,1,0:T(8,128)(2,1)} %param.13) | copy-start | bytes 11010052
  48.7 2.5 %copy-start.6 = (bf16[1,3584,512]{2,1,0:T(8,128)(2,1)S(1)}, bf16[1,3584,512]{2,1,0:T(8,128)(2,1)}, u32[]{:S(2)}) copy-start(bf16[1,3584,512]{2,1,0:T(8,128)(2,1)} %param.12) | copy-start | bytes 11010052
  49.4 2.7 %copy-start.3 = (bf16[2,2,192,896]{3,2,1,0:T(8,128)(2,1)}, bf16[2,2,192,896]{3,2,1,0:T(8,128)(2,1)S(1)}, u32[]{:S(2)}) copy-start(bf16[2,2,192,896]{3,2,1,0:T(8,128)(2,1)S(1)} %maximum_select_fusion) | copy-start | bytes 4128772
  51.2 2.0 %copy-start.5 = (bf16[1,3584,512]{2,1,0:T(8,128)(2,1)S(1)}, bf16[1,3584,512]{2,1,0:T(8,128)(2,1)}, u32[]{:S(2)}) copy-start(bf16[1,3584,512]{2,1,0:T(8,128)(2,1)} %param.11) | copy-start | bytes 11010052
  54.7 2.9 %copy-start.8 = (bf16[192,512,1]{1,0,2:T(8,128)(2,1)}, bf16[192,512,1]{1,0,2:T(8,128)(2,1)S(1)}, u32[]{:S(2)}) copy-start(bf16[192,512,1]{1,0,2:T(8,128)(2,1)S(1)} %get-tuple-element.9) | copy-start | bytes 589828
  60.0 6.0 %collective-permute-start.8 = (bf16[2,192,896]{2,1,0:T(8,128)(2,1)}, bf16[2,192,896]{2,1,0:T(8,128)(2,1)}, u32[]{:S(2)}, u32[]{:S(2)}) collective-permute-start(bf16[2,192,896]{2,1,0:T(8,128)(2,1)} %fusion.19), channel_id=1, source_target_pairs={{0,8},{8,0},{16,24},{24,16},{1,9},{9,1},{17,25},{25,17},{2,10},{10... | collective-permute-start | bytes 2064392 | tf_op jit(solution)/shard_map/ppermute | solution.py:60
  60.9 1.3 %collective-permute-start.6 = (f32[192]{0:T(256)S(1)}, f32[192]{0:T(256)S(1)}, u32[]{:S(2)}, u32[]{:S(2)}) collective-permute-start(f32[192]{0:T(256)S(1)} %get-tuple-element.5), channel_id=1, source_target_pairs={{0,8},{8,0},{16,24},{24,16},{1,9},{9,1},{17,25},{25,17},{2,10},{10... | collective-permute-start | bytes 2312 | tf_op jit(solution)/shard_map/ppermute | solution.py:67
  61.2 2.6 %copy-start.1 = (f32[2,2,192,896]{3,2,1,0:T(8,128)}, f32[2,2,192,896]{3,2,1,0:T(8,128)S(1)}, u32[]{:S(2)}) copy-start(f32[2,2,192,896]{3,2,1,0:T(8,128)S(1)} %convert.5) | copy-start | bytes 8257540
  62.3 3.6 %collective-permute-start.7 = (f32[192]{0:T(256)S(1)}, f32[192]{0:T(256)S(1)}, u32[]{:S(2)}, u32[]{:S(2)}) collective-permute-start(f32[192]{0:T(256)S(1)} %add.59), channel_id=1, source_target_pairs={{0,16},{8,24},{16,0},{24,8},{1,17},{9,25},{17,1},{25,9},{2,18},{10... | collective-permute-start | bytes 2312 | tf_op jit(solution)/shard_map/ppermute | solution.py:67
  64.8 4.3 %collective-permute-start.2 = (bf16[2,192,896]{2,1,0:T(8,128)(2,1)}, bf16[2,192,896]{2,1,0:T(8,128)(2,1)}, u32[]{:S(2)}, u32[]{:S(2)}) collective-permute-start(bf16[2,192,896]{2,1,0:T(8,128)(2,1)} %fusion.18), channel_id=1, source_target_pairs={{0,8},{8,0},{16,24},{24,16},{1,9},{9,1},{17,25},{25,17},{2,10},{10... | collective-permute-start | bytes 2064392 | tf_op jit(solution)/shard_map/ppermute | solution.py:60
  66.0 3.1 %copy-start.2 = (f32[2,2,192,896]{3,2,1,0:T(8,128)S(1)}, f32[2,2,192,896]{3,2,1,0:T(8,128)}, u32[]{:S(2)}) copy-start(f32[2,2,192,896]{3,2,1,0:T(8,128)} %copy-done.1) | copy-start | bytes 8257540
  67.5 11.1 %collective-permute-start.9 = (bf16[1,192,896]{2,1,0:T(8,128)(2,1)S(1)}, bf16[1,192,896]{2,1,0:T(8,128)(2,1)S(1)}, u32[]{:S(2)}, u32[]{:S(2)}) collective-permute-start(bf16[1,192,896]{2,1,0:T(8,128)(2,1)S(1)} %fusion.24), channel_id=1, source_target_pairs={{0,16},{8,24},{16,0},{24,8},{1,17},{9,25},{17,1},{25,9},{2,18},{10... | collective-permute-start | bytes 1032200 | tf_op jit(solution)/shard_map/ppermute | solution.py:60
  71.3 14.0 %collective-permute-start.3 = (bf16[1,192,896]{2,1,0:T(8,128)(2,1)}, bf16[1,192,896]{2,1,0:T(8,128)(2,1)}, u32[]{:S(2)}, u32[]{:S(2)}) collective-permute-start(bf16[1,192,896]{2,1,0:T(8,128)(2,1)} %fusion.23), channel_id=1, source_target_pairs={{0,16},{8,24},{16,0},{24,8},{1,17},{9,25},{17,1},{25,9},{2,18},{10... | collective-permute-start | bytes 1032200 | tf_op jit(solution)/shard_map/ppermute | solution.py:60
  79.4 14.5 %all-to-all-start.3 = ((bf16[8,24,896]{2,1,0:T(8,128)(2,1)}), bf16[8,24,896]{2,1,0:T(8,128)(2,1)S(1)}, u32[]{:S(2)}, u32[]{:S(2)}) async-start(bf16[8,24,896]{2,1,0:T(8,128)(2,1)} %bitcast.56), calls=%async_computation.3 | async-start | bytes 688128 | tf_op jit(solution)/shard_map/all_to_all | solution.py:100
  85.3 12.3 %copy-start.4 = (bf16[2,2,192,896]{3,2,1,0:T(8,128)(2,1)S(1)}, bf16[2,2,192,896]{3,2,1,0:T(8,128)(2,1)}, u32[]{:S(2)}) copy-start(bf16[2,2,192,896]{3,2,1,0:T(8,128)(2,1)} %copy-done.3) | copy-start | bytes 4128772
  93.9 12.6 %all-to-all-start.2 = ((bf16[8,24,1024]{2,1,0:T(8,128)(2,1)}), bf16[8,24,1024]{2,1,0:T(8,128)(2,1)S(1)}, u32[]{:S(2)}, u32[]{:S(2)}) async-start(bf16[8,24,1024]{2,1,0:T(8,128)(2,1)} %pad_maximum_fusion.1), calls=%async_computation.2 | async-start | bytes 786432 | tf_op jit(solution)/shard_map/all_to_all | solution.py:100
  101.5 5.2 %copy-start.10 = (f32[128,1]{0,1:T(1,128)S(1)}, f32[128,1]{0,1:T(1,128)}, u32[]{:S(2)}) copy-start(f32[128,1]{0,1:T(1,128)} %param.10) | copy-start | bytes 1540

commit v11 on v7

--- a/solution.py
+++ b/solution.py
@@ -8,9 +8,11 @@
     tok_rows, routes = expert_ids.shape
     flat_ids = expert_ids.reshape(-1)
     labels = jnp.arange(experts, dtype=jnp.int32)
-    onehot = (flat_ids[:, None] == labels[None, :]).astype(jnp.int32)
-    earlier = jnp.cumsum(onehot, axis=0) - onehot
-    slot_rank = jnp.sum(earlier * onehot, axis=1)
+    onehot = (flat_ids[:, None] == labels[None, :]).astype(jnp.bfloat16)
+    pairs = jnp.arange(flat_ids.shape[0], dtype=jnp.int32)
+    before = (pairs[:, None] > pairs[None, :]).astype(jnp.bfloat16)
+    earlier = jnp.dot(before, onehot, preferred_element_type=jnp.float32)
+    slot_rank = jnp.sum(earlier * onehot.astype(jnp.float32), axis=1).astype(jnp.int32)
     slot_ids = (flat_ids * capacity + slot_rank).reshape(tok_rows, routes)
     positions = jnp.arange(experts * capacity, dtype=jnp.int32)
     return [slot_ids[:, r][:, None] == positions[None, :] for r in range(routes)]
@@ -48,8 +50,8 @@
     return held
 
 
-def after(values, *needed):
-    zero = sum(jnp.ravel(x)[0].astype(jnp.float32) for x in needed) * 0.0
+def after(values, needed):
+    zero = needed[(0,) * needed.ndim].astype(jnp.float32) * 0.0
     return values + zero.astype(values.dtype)
 
 

time: 114 us -> 111 us (0.974)
  other arithmetic: 11.2 us -> 9.3 us
  local copies, waits for them, and re-layouts: 8.26 us -> 7 us
    convert_element_type x1 -> x0, local copies, waits for them, and re-layouts: 1.32 us -> none  [shards(): slot_grad = scatter_sum(back_terms, n_ctx, me).astype(jnp.bfloat16)]
    unnamed x20 -> x22, local copies, waits for them, and re-layouts: 4.1 us -> 4.14 us
  transfers between devices with their start and end apart: 14 -> 14, of which waited for: 10 -> 10; matrix products, arithmetic and copies ran while one was open for 15% -> 16% of each run, Pallas kernels for 0% -> 0%
where the time goes in v11:
time: 111 us; the launch traced here: 110 us
  waiting for transfers between devices  46.5 us (42%)
  starting transfers between devices  27.7 us (25%)
  matrix products  17.9 us (16%)
  other arithmetic  9.3 us (8%)
  local copies, waits for them, and re-layouts  7 us (6%)
  between operations  1.64 us (1%)
    all_to_all x4, starting transfers between devices, to_experts(): got = lax.all_to_all(sent, 'ep', split_axis=0, concat_axis=0, tiled=True)  20.2 us
    all_to_all x4, waiting for transfers between devices, to_experts(): got = lax.all_to_all(sent, 'ep', split_axis=0, concat_axis=0, tiled=True)  19.9 us
    ppermute x4, waiting for transfers between devices, gather_blocks(): other = lax.ppermute(held, 'ctx', xor_pairs(n_ctx, bit))  15 us
    ppermute x4, waiting for transfers between devices, scatter_sum(): got = lax.ppermute(send, 'ctx', xor_pairs(n_ctx, bit))  9.52 us
    unnamed x22, local copies, waits for them, and re-layouts  4.14 us
    ppermute x4, starting transfers between devices, scatter_sum(): got = lax.ppermute(send, 'ctx', xor_pairs(n_ctx, bit))  3.76 us
    ppermute x4, starting transfers between devices, gather_blocks(): other = lax.ppermute(held, 'ctx', xor_pairs(n_ctx, bit))  3.18 us
    dot_general x1, matrix products, shards(): jnp.einsum('nsd,sf->ndf', rows_in, grad_up, preferred_element_type=jnp.fl...  3 us
  transfers between devices with their start and end apart: 14, of which 10 were waited for; matrix products, arithmetic and copies ran while one was open for 16% of the time, Pallas kernels for 0%

profile of v11, /device:TPU:0, one launch (start us, length us, event | category | flops | bytes accessed | tf_op | source)
XLA Modules:
  0.0 110.0 jit_solution(174662550614882597)
XLA Ops:
  0.7 0.9 fusion.8
  2.2 1.0 convolution_convert_fusion.2
  3.2 7.3 %all-to-all-start.1 = ((bf16[8,24,896]{2,1,0:T(8,128)(2,1)}), bf16[8,24,896]{2,1,0:T(8,128)(2,1)S(1)}, u32[]{:S(2)}, u32[]{:S(2)}) async-start(bf16[8,24,896]{2,1,0:T(8,128)(2,1)} %bitcast.32), calls=%async_computation.1 | async-start | bytes 688128 | tf_op jit(solution)/shard_map/all_to_all | solution.py:105
  12.8 8.3 %all-to-all-done.1 = bf16[8,24,896]{2,1,0:T(8,128)(2,1)S(1)} async-done(((bf16[8,24,896]{2,1,0:T(8,128)(2,1)}), bf16[8,24,896]{2,1,0:T(8,128)(2,1)S(1)}, u32[]{:S(2)}, u32[]{:S(2)}) %all-to-all-start.1) | async-done | bytes 344096 | tf_op jit(solution)/shard_map/all_to_all | solution.py:105
  21.1 3.6 %all-to-all-start = ((bf16[8,24,1024]{2,1,0:T(8,128)(2,1)}), bf16[8,24,1024]{2,1,0:T(8,128)(2,1)S(1)}, u32[]{:S(2)}, u32[]{:S(2)}) async-start(bf16[8,24,1024]{2,1,0:T(8,128)(2,1)} %maximum_maximum_fusion), calls=%async_computation | async-start | bytes 786432 | tf_op jit(solution)/shard_map/all_to_all | solution.py:105
  24.7 1.5 %collective-permute-start.3 = (bf16[1,192,896]{2,1,0:T(8,128)(2,1)S(1)}, bf16[1,192,896]{2,1,0:T(8,128)(2,1)S(1)}, u32[]{:S(2)}, u32[]{:S(2)}) collective-permute-start(bf16[1,192,896]{2,1,0:T(8,128)(2,1)S(1)} %bitcast.176), channel_id=1, source_target_pairs={{0,16},{8,24},{16,0},{24,8},{1,17},{9,25},{17,1},{25,9},{2,18},{10... | collective-permute-start | bytes 1032200 | tf_op jit(solution)/shard_map/ppermute | solution.py:44
  26.2 7.5 %collective-permute-done.3 = bf16[1,192,896]{2,1,0:T(8,128)(2,1)S(1)} collective-permute-done((bf16[1,192,896]{2,1,0:T(8,128)(2,1)S(1)}, bf16[1,192,896]{2,1,0:T(8,128)(2,1)S(1)}, u32[]{:S(2)}, u32[]{:S(2)}) %collective-permute-start.3) | collective-permute-done | bytes 344096 | tf_op jit(solution)/shard_map/ppermute | solution.py:44
  33.8 1.0 maximum_select_fusion.4
  34.7 1.2 %all-to-all-done = bf16[8,24,1024]{2,1,0:T(8,128)(2,1)S(1)} async-done(((bf16[8,24,1024]{2,1,0:T(8,128)(2,1)}), bf16[8,24,1024]{2,1,0:T(8,128)(2,1)S(1)}, u32[]{:S(2)}, u32[]{:S(2)}) %all-to-all-start) | async-done | bytes 393248 | tf_op jit(solution)/shard_map/all_to_all | solution.py:105
  36.0 1.6 %collective-permute-start = (bf16[1,192,896]{2,1,0:T(8,128)(2,1)S(1)}, bf16[1,192,896]{2,1,0:T(8,128)(2,1)S(1)}, u32[]{:S(2)}, u32[]{:S(2)}) collective-permute-start(bf16[1,192,896]{2,1,0:T(8,128)(2,1)S(1)} %get-tuple-element.13), channel_id=1, source_target_pairs={{0,16},{8,24},{16,0},{24,8},{1,17},{9,25},{17,1},{25,9},{2,18},{10... | collective-permute-start | bytes 1032200 | tf_op jit(solution)/shard_map/ppermute | solution.py:44
  37.9 7.4 %collective-permute-done = bf16[1,192,896]{2,1,0:T(8,128)(2,1)S(1)} collective-permute-done((bf16[1,192,896]{2,1,0:T(8,128)(2,1)S(1)}, bf16[1,192,896]{2,1,0:T(8,128)(2,1)S(1)}, u32[]{:S(2)}, u32[]{:S(2)}) %collective-permute-start) | collective-permute-done | bytes 344096 | tf_op jit(solution)/shard_map/ppermute | solution.py:44
  46.1 1.6 %copy-done.4 = bf16[1,512,3584]{2,1,0:T(8,128)(2,1)S(1)} copy-done((bf16[1,512,3584]{2,1,0:T(8,128)(2,1)S(1)}, bf16[1,512,3584]{2,1,0:T(8,128)(2,1)}, u32[]{:S(2)}) %copy-start.4) | copy-done | bytes 3670040
  49.4 1.3 %copy-done.2 = bf16[1,3584,512]{2,1,0:T(8,128)(2,1)S(1)} copy-done((bf16[1,3584,512]{2,1,0:T(8,128)(2,1)S(1)}, bf16[1,3584,512]{2,1,0:T(8,128)(2,1)}, u32[]{:S(2)}) %copy-start.2) | copy-done | bytes 3670040
  50.7 0.9 convolution_bitcast_fusion.4
  51.6 1.2 %copy-done.1 = bf16[1,3584,512]{2,1,0:T(8,128)(2,1)S(1)} copy-done((bf16[1,3584,512]{2,1,0:T(8,128)(2,1)S(1)}, bf16[1,3584,512]{2,1,0:T(8,128)(2,1)}, u32[]{:S(2)}) %copy-start.1) | copy-done | bytes 3670040
  55.7 1.3 %fusion.29 = f32[192,4,896]{2,0,1:T(8,128)S(1)} fusion(bf16[4,896,512]{2,1,0:T(8,128)(2,1)S(1)} %bitcast.171, bf16[192,512]{1,0:T(8,128)(2,1)S(1)} %get-tuple-element.10), kind=kOutput, calls=%fused_computation.76 | convolution fusion | flops 704643072 | bytes 6619136 | tf_op jit(solution)/shard_map/sf,ndf->nsd/dot_general | solution.py:146
  57.1 1.3 %fusion.1 = f32[192,4,896]{2,0,1:T(8,128)S(1)} fusion(f32[192,4,896]{2,0,1:T(8,128)S(1)} %fusion.29, bf16[192,512,1]{1,0,2:T(8,128)(2,1)S(1)} %get-tuple-element.9, bf16[4,896,512]{2,1,0:T(8,128)(2,1)S(1)} %bitcast.173), kind=kOutput, calls=%fused_computation.6 | convolution fusion | flops 706707456 | bytes 9371648 | tf_op jit(solution)/shard_map/sf,ndf->nsd/dot_general | solution.py:148
  60.0 0.9 collective-permute-done.5
  61.2 1.6 %collective-permute-start.6 = (bf16[1,192,896]{2,1,0:T(8,128)(2,1)S(1)}, bf16[1,192,896]{2,1,0:T(8,128)(2,1)S(1)}, u32[]{:S(2)}, u32[]{:S(2)}) collective-permute-start(bf16[1,192,896]{2,1,0:T(8,128)(2,1)S(1)} %fusion.25), channel_id=1, source_target_pairs={{0,16},{8,24},{16,0},{24,8},{1,17},{9,25},{17,1},{25,9},{2,18},{10... | collective-permute-start | bytes 1032200 | tf_op jit(solution)/shard_map/ppermute | solution.py:67
  62.9 8.6 %collective-permute-done.6 = bf16[1,192,896]{2,1,0:T(8,128)(2,1)S(1)} collective-permute-done((bf16[1,192,896]{2,1,0:T(8,128)(2,1)S(1)}, bf16[1,192,896]{2,1,0:T(8,128)(2,1)S(1)}, u32[]{:S(2)}, u32[]{:S(2)}) %collective-permute-start.6) | collective-permute-done | bytes 344096 | tf_op jit(solution)/shard_map/ppermute | solution.py:67
  73.7 1.5 %collective-permute-start.7 = (bf16[1,192,896]{2,1,0:T(8,128)(2,1)}, bf16[1,192,896]{2,1,0:T(8,128)(2,1)}, u32[]{:S(2)}, u32[]{:S(2)}) collective-permute-start(bf16[1,192,896]{2,1,0:T(8,128)(2,1)} %fusion.24), channel_id=1, source_target_pairs={{0,16},{8,24},{16,0},{24,8},{1,17},{9,25},{17,1},{25,9},{2,18},{10... | collective-permute-start | bytes 1032200 | tf_op jit(solution)/shard_map/ppermute | solution.py:67
  75.2 1.1 %collective-permute-done.8 = f32[192]{0:T(256)S(1)} collective-permute-done((f32[192]{0:T(256)S(1)}, f32[192]{0:T(256)S(1)}, u32[]{:S(2)}, u32[]{:S(2)}) %collective-permute-start.8) | collective-permute-done | bytes 800 | tf_op jit(solution)/shard_map/ppermute | solution.py:74
  76.9 5.7 %all-to-all-start.3 = ((bf16[8,24,896]{2,1,0:T(8,128)(2,1)}), bf16[8,24,896]{2,1,0:T(8,128)(2,1)S(1)}, u32[]{:S(2)}, u32[]{:S(2)}) async-start(bf16[8,24,896]{2,1,0:T(8,128)(2,1)} %bitcast.187), calls=%async_computation.3 | async-start | bytes 688128 | tf_op jit(solution)/shard_map/all_to_all | solution.py:105
  82.6 1.0 collective-permute-done.9
  85.3 1.1 fusion.21
  87.2 6.0 %all-to-all-done.3 = bf16[8,24,896]{2,1,0:T(8,128)(2,1)S(1)} async-done(((bf16[8,24,896]{2,1,0:T(8,128)(2,1)}), bf16[8,24,896]{2,1,0:T(8,128)(2,1)S(1)}, u32[]{:S(2)}, u32[]{:S(2)}) %all-to-all-start.3) | async-done | bytes 344096 | tf_op jit(solution)/shard_map/all_to_all | solution.py:105
  93.3 3.6 %all-to-all-start.2 = ((bf16[8,24,1024]{2,1,0:T(8,128)(2,1)}), bf16[8,24,1024]{2,1,0:T(8,128)(2,1)S(1)}, u32[]{:S(2)}, u32[]{:S(2)}) async-start(bf16[8,24,1024]{2,1,0:T(8,128)(2,1)} %maximum_maximum_fusion.1), calls=%async_computation.2 | async-start | bytes 786432 | tf_op jit(solution)/shard_map/all_to_all | solution.py:105
  96.9 3.0 %convolution_convert_fusion = bf16[4,896,512]{2,1,0:T(8,128)(2,1)} fusion(bf16[4,192,896]{2,1,0:T(8,128)(2,1)S(1)} %bitcast.162, bf16[192,512,1]{1,0,2:T(8,128)(2,1)S(1)} %copy-done.6), kind=kOutput, calls=%fused_computation.4 | convolution fusion | flops 706478080 | bytes 5242880 | tf_op jit(solution)/shard_map/nsd,sf->ndf/dot_general | solution.py:160
  99.9 3.0 %convolution_convert_fusion.1 = bf16[4,896,512]{2,1,0:T(8,128)(2,1)} fusion(bf16[4,192,896]{2,1,0:T(8,128)(2,1)S(1)} %bitcast.163, bf16[192,512]{1,0:T(8,128)(2,1)S(1)} %get-tuple-element.10), kind=kOutput, calls=%fused_computation.5 | convolution fusion | flops 706478080 | bytes 5242880 | tf_op jit(solution)/shard_map/nsd,sf->ndf/dot_general | solution.py:157
  102.9 1.0 convolution_convert_fusion.4
  103.9 4.3 %all-to-all-done.2 = bf16[8,24,1024]{2,1,0:T(8,128)(2,1)S(1)} async-done(((bf16[8,24,1024]{2,1,0:T(8,128)(2,1)}), bf16[8,24,1024]{2,1,0:T(8,128)(2,1)S(1)}, u32[]{:S(2)}, u32[]{:S(2)}) %all-to-all-start.2) | async-done | bytes 393248 | tf_op jit(solution)/shard_map/all_to_all | solution.py:105
  108.4 1.0 fusion.7
  (73 shorter events, 16.0 us)
Async XLA Ops:
  0.6 1.6 %copy-start = (bf16[128,896]{1,0:T(8,128)(2,1)S(1)}, bf16[128,896]{1,0:T(8,128)(2,1)}, u32[]{:S(2)}) copy-start(bf16[128,896]{1,0:T(8,128)(2,1)} %param.8) | copy-start | bytes 688132
  0.6 11.0 %copy-start.7 = (bf16[128,896]{1,0:T(8,128)(2,1)S(1)}, bf16[128,896]{1,0:T(8,128)(2,1)}, u32[]{:S(2)}) copy-start(bf16[128,896]{1,0:T(8,128)(2,1)} %param.7) | copy-start | bytes 688132
  3.2 17.9 %all-to-all-start.1 = ((bf16[8,24,896]{2,1,0:T(8,128)(2,1)}), bf16[8,24,896]{2,1,0:T(8,128)(2,1)S(1)}, u32[]{:S(2)}, u32[]{:S(2)}) async-start(bf16[8,24,896]{2,1,0:T(8,128)(2,1)} %bitcast.32), calls=%async_computation.1 | async-start | bytes 688128 | tf_op jit(solution)/shard_map/all_to_all | solution.py:105
  21.1 14.9 %all-to-all-start = ((bf16[8,24,1024]{2,1,0:T(8,128)(2,1)}), bf16[8,24,1024]{2,1,0:T(8,128)(2,1)S(1)}, u32[]{:S(2)}, u32[]{:S(2)}) async-start(bf16[8,24,1024]{2,1,0:T(8,128)(2,1)} %maximum_maximum_fusion), calls=%async_computation | async-start | bytes 786432 | tf_op jit(solution)/shard_map/all_to_all | solution.py:105
  24.7 9.1 %collective-permute-start.3 = (bf16[1,192,896]{2,1,0:T(8,128)(2,1)S(1)}, bf16[1,192,896]{2,1,0:T(8,128)(2,1)S(1)}, u32[]{:S(2)}, u32[]{:S(2)}) collective-permute-start(bf16[1,192,896]{2,1,0:T(8,128)(2,1)S(1)} %bitcast.176), channel_id=1, source_target_pairs={{0,16},{8,24},{16,0},{24,8},{1,17},{9,25},{17,1},{25,9},{2,18},{10... | collective-permute-start | bytes 1032200 | tf_op jit(solution)/shard_map/ppermute | solution.py:44
  34.7 10.9 %collective-permute-start.4 = (bf16[2,192,896]{2,1,0:T(8,128)(2,1)}, bf16[2,192,896]{2,1,0:T(8,128)(2,1)S(1)}, u32[]{:S(2)}, u32[]{:S(2)}) collective-permute-start(bf16[2,192,896]{2,1,0:T(8,128)(2,1)} %maximum_select_fusion.4), channel_id=1, source_target_pairs={{0,8},{8,0},{16,24},{24,16},{1,9},{9,1},{17,25},{25,17},{2,10},{10... | collective-permute-start | bytes 2064392 | tf_op jit(solution)/shard_map/ppermute | solution.py:44
  36.0 9.3 %collective-permute-start = (bf16[1,192,896]{2,1,0:T(8,128)(2,1)S(1)}, bf16[1,192,896]{2,1,0:T(8,128)(2,1)S(1)}, u32[]{:S(2)}, u32[]{:S(2)}) collective-permute-start(bf16[1,192,896]{2,1,0:T(8,128)(2,1)S(1)} %get-tuple-element.13), channel_id=1, source_target_pairs={{0,16},{8,24},{16,0},{24,8},{1,17},{9,25},{17,1},{25,9},{2,18},{10... | collective-permute-start | bytes 1032200 | tf_op jit(solution)/shard_map/ppermute | solution.py:44
  45.5 3.7 %collective-permute-start.1 = (bf16[2,192,896]{2,1,0:T(8,128)(2,1)S(1)}, bf16[2,192,896]{2,1,0:T(8,128)(2,1)S(1)}, u32[]{:S(2)}, u32[]{:S(2)}) collective-permute-start(bf16[2,192,896]{2,1,0:T(8,128)(2,1)S(1)} %maximum_select_fusion.2), channel_id=1, source_target_pairs={{0,8},{8,0},{16,24},{24,16},{1,9},{9,1},{17,25},{25,17},{2,10},{10... | collective-permute-start | bytes 2064392 | tf_op jit(solution)/shard_map/ppermute | solution.py:44
  45.7 2.0 %copy-start.4 = (bf16[1,512,3584]{2,1,0:T(8,128)(2,1)S(1)}, bf16[1,512,3584]{2,1,0:T(8,128)(2,1)}, u32[]{:S(2)}) copy-start(bf16[1,512,3584]{2,1,0:T(8,128)(2,1)} %param.13) | copy-start | bytes 11010052
  48.7 2.0 %copy-start.2 = (bf16[1,3584,512]{2,1,0:T(8,128)(2,1)S(1)}, bf16[1,3584,512]{2,1,0:T(8,128)(2,1)}, u32[]{:S(2)}) copy-start(bf16[1,3584,512]{2,1,0:T(8,128)(2,1)} %param.12) | copy-start | bytes 11010052
  50.7 2.0 %copy-start.1 = (bf16[1,3584,512]{2,1,0:T(8,128)(2,1)S(1)}, bf16[1,3584,512]{2,1,0:T(8,128)(2,1)}, u32[]{:S(2)}) copy-start(bf16[1,3584,512]{2,1,0:T(8,128)(2,1)} %param.11) | copy-start | bytes 11010052
  54.2 2.9 %copy-start.5 = (bf16[192,512,1]{1,0,2:T(8,128)(2,1)}, bf16[192,512,1]{1,0,2:T(8,128)(2,1)S(1)}, u32[]{:S(2)}) copy-start(bf16[192,512,1]{1,0,2:T(8,128)(2,1)S(1)} %get-tuple-element.9) | copy-start | bytes 589828
  58.6 2.3 %collective-permute-start.5 = (bf16[2,192,896]{2,1,0:T(8,128)(2,1)S(1)}, bf16[2,192,896]{2,1,0:T(8,128)(2,1)S(1)}, u32[]{:S(2)}, u32[]{:S(2)}) collective-permute-start(bf16[2,192,896]{2,1,0:T(8,128)(2,1)S(1)} %fusion.19), channel_id=1, source_target_pairs={{0,8},{8,0},{16,24},{24,16},{1,9},{9,1},{17,25},{25,17},{2,10},{10... | collective-permute-start | bytes 2064392 | tf_op jit(solution)/shard_map/ppermute | solution.py:67
  59.9 2.8 %collective-permute-start.2 = (bf16[2,192,896]{2,1,0:T(8,128)(2,1)S(1)}, bf16[2,192,896]{2,1,0:T(8,128)(2,1)S(1)}, u32[]{:S(2)}, u32[]{:S(2)}) collective-permute-start(bf16[2,192,896]{2,1,0:T(8,128)(2,1)S(1)} %fusion.18), channel_id=1, source_target_pairs={{0,8},{8,0},{16,24},{24,16},{1,9},{9,1},{17,25},{25,17},{2,10},{10... | collective-permute-start | bytes 2064392 | tf_op jit(solution)/shard_map/ppermute | solution.py:67
  61.2 10.4 %collective-permute-start.6 = (bf16[1,192,896]{2,1,0:T(8,128)(2,1)S(1)}, bf16[1,192,896]{2,1,0:T(8,128)(2,1)S(1)}, u32[]{:S(2)}, u32[]{:S(2)}) collective-permute-start(bf16[1,192,896]{2,1,0:T(8,128)(2,1)S(1)} %fusion.25), channel_id=1, source_target_pairs={{0,16},{8,24},{16,0},{24,8},{1,17},{9,25},{17,1},{25,9},{2,18},{10... | collective-permute-start | bytes 1032200 | tf_op jit(solution)/shard_map/ppermute | solution.py:67
  71.7 5.2 %copy-start.3 = (bf16[1,192,896]{2,1,0:T(8,128)(2,1)}, bf16[1,192,896]{2,1,0:T(8,128)(2,1)S(1)}, u32[]{:S(2)}) copy-start(bf16[1,192,896]{2,1,0:T(8,128)(2,1)S(1)} %fusion.20) | copy-start | bytes 1032196
  73.7 11.6 %collective-permute-start.7 = (bf16[1,192,896]{2,1,0:T(8,128)(2,1)}, bf16[1,192,896]{2,1,0:T(8,128)(2,1)}, u32[]{:S(2)}, u32[]{:S(2)}) collective-permute-start(bf16[1,192,896]{2,1,0:T(8,128)(2,1)} %fusion.24), channel_id=1, source_target_pairs={{0,16},{8,24},{16,0},{24,8},{1,17},{9,25},{17,1},{25,9},{2,18},{10... | collective-permute-start | bytes 1032200 | tf_op jit(solution)/shard_map/ppermute | solution.py:67
  75.2 1.1 %collective-permute-start.8 = (f32[192]{0:T(256)S(1)}, f32[192]{0:T(256)S(1)}, u32[]{:S(2)}, u32[]{:S(2)}) collective-permute-start(f32[192]{0:T(256)S(1)} %get-tuple-element.5), channel_id=1, source_target_pairs={{0,8},{8,0},{16,24},{24,16},{1,9},{9,1},{17,25},{25,17},{2,10},{10... | collective-permute-start | bytes 2312 | tf_op jit(solution)/shard_map/ppermute | solution.py:74
  76.3 7.2 %collective-permute-start.9 = (f32[192]{0:T(256)S(1)}, f32[192]{0:T(256)S(1)}, u32[]{:S(2)}, u32[]{:S(2)}) collective-permute-start(f32[192]{0:T(256)S(1)} %add.87), channel_id=1, source_target_pairs={{0,16},{8,24},{16,0},{24,8},{1,17},{9,25},{17,1},{25,9},{2,18},{10... | collective-permute-start | bytes 2312 | tf_op jit(solution)/shard_map/ppermute | solution.py:74
  76.9 16.4 %all-to-all-start.3 = ((bf16[8,24,896]{2,1,0:T(8,128)(2,1)}), bf16[8,24,896]{2,1,0:T(8,128)(2,1)S(1)}, u32[]{:S(2)}, u32[]{:S(2)}) async-start(bf16[8,24,896]{2,1,0:T(8,128)(2,1)} %bitcast.187), calls=%async_computation.3 | async-start | bytes 688128 | tf_op jit(solution)/shard_map/all_to_all | solution.py:105
  85.3 1.1 %copy-start.8 = (bf16[8,24,1]{2,1,0:T(8,128)(2,1)S(1)}, bf16[8,24,1]{2,1,0:T(8,128)(2,1)}, u32[]{:S(2)}) copy-start(bf16[8,24,1]{2,1,0:T(8,128)(2,1)} %concatenate.62) | copy-start | bytes 1156
  85.3 1.1 %copy-start.9 = (bf16[8,24,1]{2,1,0:T(8,128)(2,1)S(1)}, bf16[8,24,1]{2,1,0:T(8,128)(2,1)}, u32[]{:S(2)}) copy-start(bf16[8,24,1]{2,1,0:T(8,128)(2,1)} %concatenate.63) | copy-start | bytes 1156
  86.3 10.6 %copy-start.6 = (bf16[192,512,1]{1,0,2:T(8,128)(2,1)S(1)}, bf16[192,512,1]{1,0,2:T(8,128)(2,1)}, u32[]{:S(2)}) copy-start(bf16[192,512,1]{1,0,2:T(8,128)(2,1)} %copy-done.5) | copy-start | bytes 589828
  93.3 14.9 %all-to-all-start.2 = ((bf16[8,24,1024]{2,1,0:T(8,128)(2,1)}), bf16[8,24,1024]{2,1,0:T(8,128)(2,1)S(1)}, u32[]{:S(2)}, u32[]{:S(2)}) async-start(bf16[8,24,1024]{2,1,0:T(8,128)(2,1)} %maximum_maximum_fusion.1), calls=%async_computation.2 | async-start | bytes 786432 | tf_op jit(solution)/shard_map/all_to_all | solution.py:105
  99.9 8.4 %copy-start.10 = (f32[128,1]{0,1:T(1,128)S(1)}, f32[128,1]{0,1:T(1,128)}, u32[]{:S(2)}) copy-start(f32[128,1]{0,1:T(1,128)} %param.10) | copy-start | bytes 1540

commit v12 on v8

--- a/solution.py
+++ b/solution.py
@@ -124,8 +124,13 @@
     gate_part = jnp.einsum(
         "nsd,nsd->s", partial_out.astype(jnp.float32), grads_in.astype(jnp.float32)
     )
-    expert_out = scatter_sum(partial_out.astype(jnp.float32), n_ctx, me).astype(jnp.bfloat16)
-    gate_sum = all_sum(gate_part, n_ctx)
+    gate_cols = with_cols(jnp.zeros((slot_count, 0), jnp.bfloat16), gate_part, pad)
+    out_parts = jnp.concatenate(
+        [partial_out, jnp.broadcast_to(gate_cols[None], (n_ctx, slot_count, pad))], axis=2
+    )
+    out_sums = scatter_sum(out_parts.astype(jnp.float32), n_ctx, me)
+    expert_out = out_sums[:, :col_width].astype(jnp.bfloat16)
+    gate_sum = out_sums[:, col_width] + out_sums[:, col_width + 1]
     back_out = to_experts(with_cols(expert_out, gate_sum, pad))
 
     contract_last = (((1,), (1,)), ((), ()))

time: 106 us -> 106 us (level)
  waiting for transfers between devices: 41.7 us -> 44.4 us
  starting transfers between devices: 28.1 us -> 26.5 us
  local copies, waits for them, and re-layouts: 6.45 us -> 5.07 us
    all_to_all x4, waiting for transfers between devices: 17.1 us -> 19.8 us  [to_experts(): got = lax.all_to_all(sent, 'ep', split_axis=0, concat_axis=0, tiled=True)]
    ppermute x2 -> x0, starting transfers between devices: 2 us -> none  [all_sum(): values = values + lax.ppermute(values, 'ctx', xor_pairs(n_ctx, bit))]
    ppermute x4, waiting for transfers between devices: 7.95 us -> 9.73 us  [scatter_sum(): got = lax.ppermute(send, 'ctx', xor_pairs(n_ctx, bit))]
    concatenate x4 -> x3, local copies, waits for them, and re-layouts: 1.79 us -> 0.15 us  [with_cols(): return jnp.concatenate([rows, hi[:, None], lo[:, None], zeros], axis=1)]
    ppermute x2 -> x0, waiting for transfers between devices: 1.64 us -> none  [all_sum(): values = values + lax.ppermute(values, 'ctx', xor_pairs(n_ctx, bit))]
    squeeze x0 -> x1, other arithmetic: none -> 1.16 us  [scatter_sum(): return acc[0]]
  transfers between devices with their start and end apart: 14 -> 12, of which waited for: 8 -> 9; matrix products, arithmetic and copies ran while one was open for 18% -> 17% of each run, Pallas kernels for 0% -> 0%
where the time goes in v12:
time: 106 us
  waiting for transfers between devices  44.4 us (42%)
  starting transfers between devices  26.5 us (25%)
  matrix products  18 us (17%)
  other arithmetic  10.7 us (10%)
  local copies, waits for them, and re-layouts  5.07 us (5%)
    all_to_all x4, starting transfers between devices, to_experts(): got = lax.all_to_all(sent, 'ep', split_axis=0, concat_axis=0, tiled=True)  20.2 us
    all_to_all x4, waiting for transfers between devices, to_experts(): got = lax.all_to_all(sent, 'ep', split_axis=0, concat_axis=0, tiled=True)  19.8 us
    ppermute x4, waiting for transfers between devices, gather_blocks(): other = lax.ppermute(held, 'ctx', xor_pairs(n_ctx, bit))  14.9 us
    ppermute x4, waiting for transfers between devices, scatter_sum(): got = lax.ppermute(send, 'ctx', xor_pairs(n_ctx, bit))  9.73 us
    unnamed x20, local copies, waits for them, and re-layouts  4.14 us
    ppermute x4, starting transfers between devices, gather_blocks(): other = lax.ppermute(held, 'ctx', xor_pairs(n_ctx, bit))  3.18 us
    ppermute x4, starting transfers between devices, scatter_sum(): got = lax.ppermute(send, 'ctx', xor_pairs(n_ctx, bit))  3.12 us
    dot_general x1, matrix products, shards(): jnp.einsum('nsd,sf->ndf', rows_in, grad_gate, preferred_element_type=jnp....  3 us
  transfers between devices with their start and end apart: 12, of which 9 were waited for; matrix products, arithmetic and copies ran while one was open for 17% of the time, Pallas kernels for 0%

profile of v12, /device:TPU:0, one launch (start us, length us, event | category | flops | bytes accessed | tf_op | source)
XLA Modules:
  0.0 105.7 jit_solution(11409167237963813758)
XLA Ops:
  0.7 0.9 fusion.8
  2.2 1.0 convolution_convert_fusion.2
  3.2 7.3 %all-to-all-start.1 = ((bf16[8,24,896]{2,1,0:T(8,128)(2,1)}), bf16[8,24,896]{2,1,0:T(8,128)(2,1)S(1)}, u32[]{:S(2)}, u32[]{:S(2)}) async-start(bf16[8,24,896]{2,1,0:T(8,128)(2,1)} %bitcast.24), calls=%async_computation.1 | async-start | bytes 688128 | tf_op jit(solution)/shard_map/all_to_all | solution.py:98
  12.8 8.3 %all-to-all-done.1 = bf16[8,24,896]{2,1,0:T(8,128)(2,1)S(1)} async-done(((bf16[8,24,896]{2,1,0:T(8,128)(2,1)}), bf16[8,24,896]{2,1,0:T(8,128)(2,1)S(1)}, u32[]{:S(2)}, u32[]{:S(2)}) %all-to-all-start.1) | async-done | bytes 344096 | tf_op jit(solution)/shard_map/all_to_all | solution.py:98
  21.1 3.6 %all-to-all-start = ((bf16[8,24,1024]{2,1,0:T(8,128)(2,1)}), bf16[8,24,1024]{2,1,0:T(8,128)(2,1)S(1)}, u32[]{:S(2)}, u32[]{:S(2)}) async-start(bf16[8,24,1024]{2,1,0:T(8,128)(2,1)} %maximum_maximum_fusion), calls=%async_computation | async-start | bytes 786432 | tf_op jit(solution)/shard_map/all_to_all | solution.py:98
  24.7 1.5 %collective-permute-start.2 = (bf16[1,192,896]{2,1,0:T(8,128)(2,1)S(1)}, bf16[1,192,896]{2,1,0:T(8,128)(2,1)S(1)}, u32[]{:S(2)}, u32[]{:S(2)}) collective-permute-start(bf16[1,192,896]{2,1,0:T(8,128)(2,1)S(1)} %bitcast.161), channel_id=1, source_target_pairs={{0,16},{8,24},{16,0},{24,8},{1,17},{9,25},{17,1},{25,9},{2,18},{10... | collective-permute-start | bytes 1032200 | tf_op jit(solution)/shard_map/ppermute | solution.py:44
  26.2 7.5 %collective-permute-done.2 = bf16[1,192,896]{2,1,0:T(8,128)(2,1)S(1)} collective-permute-done((bf16[1,192,896]{2,1,0:T(8,128)(2,1)S(1)}, bf16[1,192,896]{2,1,0:T(8,128)(2,1)S(1)}, u32[]{:S(2)}, u32[]{:S(2)}) %collective-permute-start.2) | collective-permute-done | bytes 344096 | tf_op jit(solution)/shard_map/ppermute | solution.py:44
  33.8 1.0 maximum_select_fusion.4
  34.7 1.2 %all-to-all-done = bf16[8,24,1024]{2,1,0:T(8,128)(2,1)S(1)} async-done(((bf16[8,24,1024]{2,1,0:T(8,128)(2,1)}), bf16[8,24,1024]{2,1,0:T(8,128)(2,1)S(1)}, u32[]{:S(2)}, u32[]{:S(2)}) %all-to-all-start) | async-done | bytes 393248 | tf_op jit(solution)/shard_map/all_to_all | solution.py:98
  36.0 1.6 %collective-permute-start = (bf16[1,192,896]{2,1,0:T(8,128)(2,1)S(1)}, bf16[1,192,896]{2,1,0:T(8,128)(2,1)S(1)}, u32[]{:S(2)}, u32[]{:S(2)}) collective-permute-start(bf16[1,192,896]{2,1,0:T(8,128)(2,1)S(1)} %get-tuple-element.17), channel_id=1, source_target_pairs={{0,16},{8,24},{16,0},{24,8},{1,17},{9,25},{17,1},{25,9},{2,18},{10... | collective-permute-start | bytes 1032200 | tf_op jit(solution)/shard_map/ppermute | solution.py:44
  38.0 7.3 %collective-permute-done = bf16[1,192,896]{2,1,0:T(8,128)(2,1)S(1)} collective-permute-done((bf16[1,192,896]{2,1,0:T(8,128)(2,1)S(1)}, bf16[1,192,896]{2,1,0:T(8,128)(2,1)S(1)}, u32[]{:S(2)}, u32[]{:S(2)}) %collective-permute-start) | collective-permute-done | bytes 344096 | tf_op jit(solution)/shard_map/ppermute | solution.py:44
  46.1 1.6 %copy-done.3 = bf16[1,512,3584]{2,1,0:T(8,128)(2,1)S(1)} copy-done((bf16[1,512,3584]{2,1,0:T(8,128)(2,1)S(1)}, bf16[1,512,3584]{2,1,0:T(8,128)(2,1)}, u32[]{:S(2)}) %copy-start.3) | copy-done | bytes 3670040
  49.4 1.3 %copy-done.2 = bf16[1,3584,512]{2,1,0:T(8,128)(2,1)S(1)} copy-done((bf16[1,3584,512]{2,1,0:T(8,128)(2,1)S(1)}, bf16[1,3584,512]{2,1,0:T(8,128)(2,1)}, u32[]{:S(2)}) %copy-start.2) | copy-done | bytes 3670040
  50.7 0.9 convolution_bitcast_fusion.4
  51.6 1.2 %copy-done.1 = bf16[1,3584,512]{2,1,0:T(8,128)(2,1)S(1)} copy-done((bf16[1,3584,512]{2,1,0:T(8,128)(2,1)S(1)}, bf16[1,3584,512]{2,1,0:T(8,128)(2,1)}, u32[]{:S(2)}) %copy-start.1) | copy-done | bytes 3670040
  52.7 0.9 convolution_bitcast_fusion.5
  56.5 1.4 %fusion.28 = f32[192,4,896]{2,0,1:T(8,128)S(1)} fusion(bf16[4,896,512]{2,1,0:T(8,128)(2,1)S(1)} %bitcast.156, bf16[192,512]{1,0:T(8,128)(2,1)S(1)} %get-tuple-element.14), kind=kOutput, calls=%fused_computation.75 | convolution fusion | flops 704643072 | bytes 6619136 | tf_op jit(solution)/shard_map/sf,ndf->nsd/dot_general | solution.py:146
  57.9 1.3 %fusion.1 = f32[192,4,896]{2,0,1:T(8,128)S(1)} fusion(f32[192,4,896]{2,0,1:T(8,128)S(1)} %fusion.28, bf16[192,512,1]{1,0,2:T(8,128)(2,1)S(1)} %get-tuple-element.13, bf16[4,896,512]{2,1,0:T(8,128)(2,1)S(1)} %bitcast.158), kind=kOutput, calls=%fused_computation.6 | convolution fusion | flops 706707456 | bytes 9371648 | tf_op jit(solution)/shard_map/sf,ndf->nsd/dot_general | solution.py:148
  60.7 1.0 collective-permute-done.6
  62.0 1.6 %collective-permute-start.7 = (bf16[1,192,896]{2,1,0:T(8,128)(2,1)S(1)}, bf16[1,192,896]{2,1,0:T(8,128)(2,1)S(1)}, u32[]{:S(2)}, u32[]{:S(2)}) collective-permute-start(bf16[1,192,896]{2,1,0:T(8,128)(2,1)S(1)} %fusion.24), channel_id=1, source_target_pairs={{0,16},{8,24},{16,0},{24,8},{1,17},{9,25},{17,1},{25,9},{2,18},{10... | collective-permute-start | bytes 1032200 | tf_op jit(solution)/shard_map/ppermute | solution.py:60
  64.8 0.9 collective-permute-start.5
  65.7 7.2 %collective-permute-done.7 = bf16[1,192,896]{2,1,0:T(8,128)(2,1)S(1)} collective-permute-done((bf16[1,192,896]{2,1,0:T(8,128)(2,1)S(1)}, bf16[1,192,896]{2,1,0:T(8,128)(2,1)S(1)}, u32[]{:S(2)}, u32[]{:S(2)}) %collective-permute-start.7) | collective-permute-done | bytes 344096 | tf_op jit(solution)/shard_map/ppermute | solution.py:60
  73.8 5.7 %all-to-all-start.3 = ((bf16[8,24,896]{2,1,0:T(8,128)(2,1)}), bf16[8,24,896]{2,1,0:T(8,128)(2,1)S(1)}, u32[]{:S(2)}, u32[]{:S(2)}) async-start(bf16[8,24,896]{2,1,0:T(8,128)(2,1)} %bitcast.171), calls=%async_computation.3 | async-start | bytes 688128 | tf_op jit(solution)/shard_map/all_to_all | solution.py:98
  79.5 1.4 %collective-permute-done.5 = bf16[1,192,1024]{2,1,0:T(8,128)(2,1)} collective-permute-done((bf16[1,192,1024]{2,1,0:T(8,128)(2,1)}, bf16[1,192,1024]{2,1,0:T(8,128)(2,1)}, u32[]{:S(2)}, u32[]{:S(2)}) %collective-permute-start.5) | collective-permute-done | bytes 393248 | tf_op jit(solution)/shard_map/ppermute | solution.py:60
  80.9 1.2 %fusion.19 = f32[192,1024]{1,0:T(8,128)S(1)} fusion(bf16[1,192,1024]{2,1,0:T(8,128)(2,1)} %collective-permute-done.5, f32[1,2,192,1024]{3,2,1,0:T(8,128)S(1)} %fusion.2, pred[]{:T(512)S(6)} %eq.50), kind=kLoop, calls=%fused_computation.47 | loop fusion | flops 589824 | bytes 2752513 | tf_op jit(solution)/shard_map/squeeze | solution.py:62
  83.1 6.2 %all-to-all-done.3 = bf16[8,24,896]{2,1,0:T(8,128)(2,1)S(1)} async-done(((bf16[8,24,896]{2,1,0:T(8,128)(2,1)}), bf16[8,24,896]{2,1,0:T(8,128)(2,1)S(1)}, u32[]{:S(2)}, u32[]{:S(2)}) %all-to-all-start.3) | async-done | bytes 344096 | tf_op jit(solution)/shard_map/all_to_all | solution.py:98
  89.3 3.6 %all-to-all-start.2 = ((bf16[8,24,1024]{2,1,0:T(8,128)(2,1)}), bf16[8,24,1024]{2,1,0:T(8,128)(2,1)S(1)}, u32[]{:S(2)}, u32[]{:S(2)}) async-start(bf16[8,24,1024]{2,1,0:T(8,128)(2,1)} %maximum_maximum_fusion.1), calls=%async_computation.2 | async-start | bytes 786432 | tf_op jit(solution)/shard_map/all_to_all | solution.py:98
  92.9 3.0 %convolution_convert_fusion = bf16[4,896,512]{2,1,0:T(8,128)(2,1)} fusion(bf16[4,192,896]{2,1,0:T(8,128)(2,1)S(1)} %bitcast.147, bf16[192,512,1]{1,0,2:T(8,128)(2,1)S(1)} %copy-done.7), kind=kOutput, calls=%fused_computation.4 | convolution fusion | flops 706478080 | bytes 5242880 | tf_op jit(solution)/shard_map/nsd,sf->ndf/dot_general | solution.py:156
  95.9 3.0 %convolution_convert_fusion.1 = bf16[4,896,512]{2,1,0:T(8,128)(2,1)} fusion(bf16[4,192,896]{2,1,0:T(8,128)(2,1)S(1)} %bitcast.148, bf16[192,512]{1,0:T(8,128)(2,1)S(1)} %copy-done.5), kind=kOutput, calls=%fused_computation.5 | convolution fusion | flops 706478080 | bytes 5242880 | tf_op jit(solution)/shard_map/nsd,sf->ndf/dot_general | solution.py:153
  98.9 1.0 convolution_convert_fusion.4
  99.9 4.0 %all-to-all-done.2 = bf16[8,24,1024]{2,1,0:T(8,128)(2,1)S(1)} async-done(((bf16[8,24,1024]{2,1,0:T(8,128)(2,1)}), bf16[8,24,1024]{2,1,0:T(8,128)(2,1)S(1)}, u32[]{:S(2)}, u32[]{:S(2)}) %all-to-all-start.2) | async-done | bytes 393248 | tf_op jit(solution)/shard_map/all_to_all | solution.py:98
  104.1 1.0 fusion.7
  (70 shorter events, 14.1 us)
Async XLA Ops:
  0.6 1.6 %copy-start = (bf16[128,896]{1,0:T(8,128)(2,1)S(1)}, bf16[128,896]{1,0:T(8,128)(2,1)}, u32[]{:S(2)}) copy-start(bf16[128,896]{1,0:T(8,128)(2,1)} %param.8) | copy-start | bytes 688132
  0.6 11.0 %copy-start.8 = (bf16[128,896]{1,0:T(8,128)(2,1)S(1)}, bf16[128,896]{1,0:T(8,128)(2,1)}, u32[]{:S(2)}) copy-start(bf16[128,896]{1,0:T(8,128)(2,1)} %param.7) | copy-start | bytes 688132
  3.2 17.9 %all-to-all-start.1 = ((bf16[8,24,896]{2,1,0:T(8,128)(2,1)}), bf16[8,24,896]{2,1,0:T(8,128)(2,1)S(1)}, u32[]{:S(2)}, u32[]{:S(2)}) async-start(bf16[8,24,896]{2,1,0:T(8,128)(2,1)} %bitcast.24), calls=%async_computation.1 | async-start | bytes 688128 | tf_op jit(solution)/shard_map/all_to_all | solution.py:98
  21.1 14.9 %all-to-all-start = ((bf16[8,24,1024]{2,1,0:T(8,128)(2,1)}), bf16[8,24,1024]{2,1,0:T(8,128)(2,1)S(1)}, u32[]{:S(2)}, u32[]{:S(2)}) async-start(bf16[8,24,1024]{2,1,0:T(8,128)(2,1)} %maximum_maximum_fusion), calls=%async_computation | async-start | bytes 786432 | tf_op jit(solution)/shard_map/all_to_all | solution.py:98
  24.7 9.1 %collective-permute-start.2 = (bf16[1,192,896]{2,1,0:T(8,128)(2,1)S(1)}, bf16[1,192,896]{2,1,0:T(8,128)(2,1)S(1)}, u32[]{:S(2)}, u32[]{:S(2)}) collective-permute-start(bf16[1,192,896]{2,1,0:T(8,128)(2,1)S(1)} %bitcast.161), channel_id=1, source_target_pairs={{0,16},{8,24},{16,0},{24,8},{1,17},{9,25},{17,1},{25,9},{2,18},{10... | collective-permute-start | bytes 1032200 | tf_op jit(solution)/shard_map/ppermute | solution.py:44
  34.7 10.9 %collective-permute-start.3 = (bf16[2,192,896]{2,1,0:T(8,128)(2,1)}, bf16[2,192,896]{2,1,0:T(8,128)(2,1)S(1)}, u32[]{:S(2)}, u32[]{:S(2)}) collective-permute-start(bf16[2,192,896]{2,1,0:T(8,128)(2,1)} %maximum_select_fusion.4), channel_id=1, source_target_pairs={{0,8},{8,0},{16,24},{24,16},{1,9},{9,1},{17,25},{25,17},{2,10},{10... | collective-permute-start | bytes 2064392 | tf_op jit(solution)/shard_map/ppermute | solution.py:44
  36.0 9.3 %collective-permute-start = (bf16[1,192,896]{2,1,0:T(8,128)(2,1)S(1)}, bf16[1,192,896]{2,1,0:T(8,128)(2,1)S(1)}, u32[]{:S(2)}, u32[]{:S(2)}) collective-permute-start(bf16[1,192,896]{2,1,0:T(8,128)(2,1)S(1)} %get-tuple-element.17), channel_id=1, source_target_pairs={{0,16},{8,24},{16,0},{24,8},{1,17},{9,25},{17,1},{25,9},{2,18},{10... | collective-permute-start | bytes 1032200 | tf_op jit(solution)/shard_map/ppermute | solution.py:44
  45.5 3.7 %collective-permute-start.1 = (bf16[2,192,896]{2,1,0:T(8,128)(2,1)S(1)}, bf16[2,192,896]{2,1,0:T(8,128)(2,1)S(1)}, u32[]{:S(2)}, u32[]{:S(2)}) collective-permute-start(bf16[2,192,896]{2,1,0:T(8,128)(2,1)S(1)} %maximum_select_fusion.2), channel_id=1, source_target_pairs={{0,8},{8,0},{16,24},{24,16},{1,9},{9,1},{17,25},{25,17},{2,10},{10... | collective-permute-start | bytes 2064392 | tf_op jit(solution)/shard_map/ppermute | solution.py:44
  45.7 2.0 %copy-start.3 = (bf16[1,512,3584]{2,1,0:T(8,128)(2,1)S(1)}, bf16[1,512,3584]{2,1,0:T(8,128)(2,1)}, u32[]{:S(2)}) copy-start(bf16[1,512,3584]{2,1,0:T(8,128)(2,1)} %param.13) | copy-start | bytes 11010052
  48.7 2.0 %copy-start.2 = (bf16[1,3584,512]{2,1,0:T(8,128)(2,1)S(1)}, bf16[1,3584,512]{2,1,0:T(8,128)(2,1)}, u32[]{:S(2)}) copy-start(bf16[1,3584,512]{2,1,0:T(8,128)(2,1)} %param.12) | copy-start | bytes 11010052
  50.7 2.0 %copy-start.1 = (bf16[1,3584,512]{2,1,0:T(8,128)(2,1)S(1)}, bf16[1,3584,512]{2,1,0:T(8,128)(2,1)}, u32[]{:S(2)}) copy-start(bf16[1,3584,512]{2,1,0:T(8,128)(2,1)} %param.11) | copy-start | bytes 11010052
  54.2 2.3 %copy-start.4 = (bf16[192,512]{1,0:T(8,128)(2,1)}, bf16[192,512]{1,0:T(8,128)(2,1)S(1)}, u32[]{:S(2)}) copy-start(bf16[192,512]{1,0:T(8,128)(2,1)S(1)} %get-tuple-element.14) | copy-start | bytes 589828
  54.2 3.7 %copy-start.6 = (bf16[192,512,1]{1,0,2:T(8,128)(2,1)}, bf16[192,512,1]{1,0,2:T(8,128)(2,1)S(1)}, u32[]{:S(2)}) copy-start(bf16[192,512,1]{1,0,2:T(8,128)(2,1)S(1)} %get-tuple-element.13) | copy-start | bytes 589828
  59.4 2.3 %collective-permute-start.6 = (bf16[2,192,896]{2,1,0:T(8,128)(2,1)S(1)}, bf16[2,192,896]{2,1,0:T(8,128)(2,1)S(1)}, u32[]{:S(2)}, u32[]{:S(2)}) collective-permute-start(bf16[2,192,896]{2,1,0:T(8,128)(2,1)S(1)} %fusion.20), channel_id=1, source_target_pairs={{0,8},{8,0},{16,24},{24,16},{1,9},{9,1},{17,25},{25,17},{2,10},{10... | collective-permute-start | bytes 2064392 | tf_op jit(solution)/shard_map/ppermute | solution.py:60
  60.6 3.0 %collective-permute-start.4 = (bf16[2,192,1024]{2,1,0:T(8,128)(2,1)S(1)}, bf16[2,192,1024]{2,1,0:T(8,128)(2,1)S(1)}, u32[]{:S(2)}, u32[]{:S(2)}) collective-permute-start(bf16[2,192,1024]{2,1,0:T(8,128)(2,1)S(1)} %fusion.18), channel_id=1, source_target_pairs={{0,8},{8,0},{16,24},{24,16},{1,9},{9,1},{17,25},{25,17},{2,10},{10... | collective-permute-start | bytes 2359304 | tf_op jit(solution)/shard_map/ppermute | solution.py:60
  62.0 11.0 %collective-permute-start.7 = (bf16[1,192,896]{2,1,0:T(8,128)(2,1)S(1)}, bf16[1,192,896]{2,1,0:T(8,128)(2,1)S(1)}, u32[]{:S(2)}, u32[]{:S(2)}) collective-permute-start(bf16[1,192,896]{2,1,0:T(8,128)(2,1)S(1)} %fusion.24), channel_id=1, source_target_pairs={{0,16},{8,24},{16,0},{24,8},{1,17},{9,25},{17,1},{25,9},{2,18},{10... | collective-permute-start | bytes 1032200 | tf_op jit(solution)/shard_map/ppermute | solution.py:60
  64.8 16.1 %collective-permute-start.5 = (bf16[1,192,1024]{2,1,0:T(8,128)(2,1)}, bf16[1,192,1024]{2,1,0:T(8,128)(2,1)}, u32[]{:S(2)}, u32[]{:S(2)}) collective-permute-start(bf16[1,192,1024]{2,1,0:T(8,128)(2,1)} %fusion.22), channel_id=1, source_target_pairs={{0,16},{8,24},{16,0},{24,8},{1,17},{9,25},{17,1},{25,9},{2,18},{10... | collective-permute-start | bytes 1179656 | tf_op jit(solution)/shard_map/ppermute | solution.py:60
  73.8 15.5 %all-to-all-start.3 = ((bf16[8,24,896]{2,1,0:T(8,128)(2,1)}), bf16[8,24,896]{2,1,0:T(8,128)(2,1)S(1)}, u32[]{:S(2)}, u32[]{:S(2)}) async-start(bf16[8,24,896]{2,1,0:T(8,128)(2,1)} %bitcast.171), calls=%async_computation.3 | async-start | bytes 688128 | tf_op jit(solution)/shard_map/all_to_all | solution.py:98
  82.1 10.8 %copy-start.7 = (bf16[192,512,1]{1,0,2:T(8,128)(2,1)S(1)}, bf16[192,512,1]{1,0,2:T(8,128)(2,1)}, u32[]{:S(2)}) copy-start(bf16[192,512,1]{1,0,2:T(8,128)(2,1)} %copy-done.6) | copy-start | bytes 589828
  89.3 14.7 %all-to-all-start.2 = ((bf16[8,24,1024]{2,1,0:T(8,128)(2,1)}), bf16[8,24,1024]{2,1,0:T(8,128)(2,1)S(1)}, u32[]{:S(2)}, u32[]{:S(2)}) async-start(bf16[8,24,1024]{2,1,0:T(8,128)(2,1)} %maximum_maximum_fusion.1), calls=%async_computation.2 | async-start | bytes 786432 | tf_op jit(solution)/shard_map/all_to_all | solution.py:98
  92.9 3.0 %copy-start.5 = (bf16[192,512]{1,0:T(8,128)(2,1)S(1)}, bf16[192,512]{1,0:T(8,128)(2,1)}, u32[]{:S(2)}) copy-start(bf16[192,512]{1,0:T(8,128)(2,1)} %copy-done.4) | copy-start | bytes 589828
  95.9 8.2 %copy-start.9 = (f32[128,1]{0,1:T(1,128)S(1)}, f32[128,1]{0,1:T(1,128)}, u32[]{:S(2)}) copy-start(f32[128,1]{0,1:T(1,128)} %param.10) | copy-start | bytes 1540

commit v13 on v8

--- a/solution.py
+++ b/solution.py
@@ -152,17 +152,15 @@
         "nsd,sf->ndf", rows_in, grad_up, preferred_element_type=jnp.float32
     ).astype(jnp.bfloat16).reshape(1, n_ctx * col_width, group)
 
-    slot_gg = join_f32(back_out[:, col_width], back_out[:, col_width + 1])
-    out_rows = back_out[:, :col_width]
     layer_out = jnp.zeros((tok_rows, col_width), jnp.float32)
     input_grad = jnp.zeros((tok_rows, col_width), jnp.float32)
     gate_terms = []
     for r, chosen in enumerate(route_maps):
         pick = chosen.astype(jnp.bfloat16)
-        rows_r = jnp.dot(pick, out_rows, preferred_element_type=jnp.float32)
-        layer_out = layer_out + route_gates[:, r][:, None] * rows_r
+        rows_r = jnp.dot(pick, back_out, preferred_element_type=jnp.float32)
+        layer_out = layer_out + route_gates[:, r][:, None] * rows_r[:, :col_width]
         input_grad = input_grad + jnp.dot(pick, back_grad, preferred_element_type=jnp.float32)
-        gate_terms.append(jnp.sum(jnp.where(chosen, slot_gg[None, :], 0.0), axis=1))
+        gate_terms.append(rows_r[:, col_width] + rows_r[:, col_width + 1])
     gate_grad = jnp.stack(gate_terms, axis=1)
     return (
         layer_out.astype(jnp.bfloat16),

time: 106 us -> 106 us (level)
    unnamed x20 -> x21, local copies, waits for them, and re-layouts: 4.13 us -> 4.71 us
where the time goes in v13:
time: 106 us; the launch traced here: 105 us
  waiting for transfers between devices  41.7 us (39%)
  starting transfers between devices  28.1 us (27%)
  matrix products  17.2 us (16%)
  other arithmetic  10.1 us (10%)
  local copies, waits for them, and re-layouts  7.04 us (7%)
    all_to_all x4, starting transfers between devices, to_experts(): got = lax.all_to_all(sent, 'ep', split_axis=0, concat_axis=0, tiled=True)  20.2 us
    all_to_all x4, waiting for transfers between devices, to_experts(): got = lax.all_to_all(sent, 'ep', split_axis=0, concat_axis=0, tiled=True)  17.1 us
    ppermute x4, waiting for transfers between devices, gather_blocks(): other = lax.ppermute(held, 'ctx', xor_pairs(n_ctx, bit))  15 us
    ppermute x4, waiting for transfers between devices, scatter_sum(): got = lax.ppermute(send, 'ctx', xor_pairs(n_ctx, bit))  7.95 us
    unnamed x21, local copies, waits for them, and re-layouts  4.71 us
    ppermute x4, starting transfers between devices, gather_blocks(): other = lax.ppermute(held, 'ctx', xor_pairs(n_ctx, bit))  3.18 us
    dot_general x1, matrix products, shards(): jnp.einsum('nsd,sf->ndf', rows_in, grad_up, preferred_element_type=jnp.fl...  3 us
    dot_general x1, matrix products, shards(): jnp.einsum('nsd,sf->ndf', rows_in, grad_gate, preferred_element_type=jnp....  3 us
  transfers between devices with their start and end apart: 14, of which 8 were waited for; matrix products, arithmetic and copies ran while one was open for 18% of the time, Pallas kernels for 0%

profile of v13, /device:TPU:0, one launch (start us, length us, event | category | flops | bytes accessed | tf_op | source)
XLA Modules:
  0.0 105.1 jit_solution(2697727353516576229)
XLA Ops:
  0.7 0.9 fusion.7
  2.2 1.0 convolution_convert_fusion.2
  3.2 7.3 %all-to-all-start.1 = ((bf16[8,24,896]{2,1,0:T(8,128)(2,1)}), bf16[8,24,896]{2,1,0:T(8,128)(2,1)S(1)}, u32[]{:S(2)}, u32[]{:S(2)}) async-start(bf16[8,24,896]{2,1,0:T(8,128)(2,1)} %bitcast.34), calls=%async_computation.1 | async-start | bytes 688128 | tf_op jit(solution)/shard_map/all_to_all | solution.py:98
  12.8 8.3 %all-to-all-done.1 = bf16[8,24,896]{2,1,0:T(8,128)(2,1)S(1)} async-done(((bf16[8,24,896]{2,1,0:T(8,128)(2,1)}), bf16[8,24,896]{2,1,0:T(8,128)(2,1)S(1)}, u32[]{:S(2)}, u32[]{:S(2)}) %all-to-all-start.1) | async-done | bytes 344096 | tf_op jit(solution)/shard_map/all_to_all | solution.py:98
  21.1 3.6 %all-to-all-start = ((bf16[8,24,1024]{2,1,0:T(8,128)(2,1)}), bf16[8,24,1024]{2,1,0:T(8,128)(2,1)S(1)}, u32[]{:S(2)}, u32[]{:S(2)}) async-start(bf16[8,24,1024]{2,1,0:T(8,128)(2,1)} %maximum_maximum_fusion), calls=%async_computation | async-start | bytes 786432 | tf_op jit(solution)/shard_map/all_to_all | solution.py:98
  24.7 1.5 %collective-permute-start.4 = (bf16[1,192,896]{2,1,0:T(8,128)(2,1)S(1)}, bf16[1,192,896]{2,1,0:T(8,128)(2,1)S(1)}, u32[]{:S(2)}, u32[]{:S(2)}) collective-permute-start(bf16[1,192,896]{2,1,0:T(8,128)(2,1)S(1)} %bitcast.174), channel_id=1, source_target_pairs={{0,16},{8,24},{16,0},{24,8},{1,17},{9,25},{17,1},{25,9},{2,18},{10... | collective-permute-start | bytes 1032200 | tf_op jit(solution)/shard_map/ppermute | solution.py:44
  26.2 7.5 %collective-permute-done.4 = bf16[1,192,896]{2,1,0:T(8,128)(2,1)S(1)} collective-permute-done((bf16[1,192,896]{2,1,0:T(8,128)(2,1)S(1)}, bf16[1,192,896]{2,1,0:T(8,128)(2,1)S(1)}, u32[]{:S(2)}, u32[]{:S(2)}) %collective-permute-start.4) | collective-permute-done | bytes 344096 | tf_op jit(solution)/shard_map/ppermute | solution.py:44
  33.8 1.0 maximum_select_fusion.4
  34.7 1.2 %all-to-all-done = bf16[8,24,1024]{2,1,0:T(8,128)(2,1)S(1)} async-done(((bf16[8,24,1024]{2,1,0:T(8,128)(2,1)}), bf16[8,24,1024]{2,1,0:T(8,128)(2,1)S(1)}, u32[]{:S(2)}, u32[]{:S(2)}) %all-to-all-start) | async-done | bytes 393248 | tf_op jit(solution)/shard_map/all_to_all | solution.py:98
  36.0 1.6 %collective-permute-start = (bf16[1,192,896]{2,1,0:T(8,128)(2,1)S(1)}, bf16[1,192,896]{2,1,0:T(8,128)(2,1)S(1)}, u32[]{:S(2)}, u32[]{:S(2)}) collective-permute-start(bf16[1,192,896]{2,1,0:T(8,128)(2,1)S(1)} %get-tuple-element.33), channel_id=1, source_target_pairs={{0,16},{8,24},{16,0},{24,8},{1,17},{9,25},{17,1},{25,9},{2,18},{10... | collective-permute-start | bytes 1032200 | tf_op jit(solution)/shard_map/ppermute | solution.py:44
  37.9 7.4 %collective-permute-done = bf16[1,192,896]{2,1,0:T(8,128)(2,1)S(1)} collective-permute-done((bf16[1,192,896]{2,1,0:T(8,128)(2,1)S(1)}, bf16[1,192,896]{2,1,0:T(8,128)(2,1)S(1)}, u32[]{:S(2)}, u32[]{:S(2)}) %collective-permute-start) | collective-permute-done | bytes 344096 | tf_op jit(solution)/shard_map/ppermute | solution.py:44
  46.1 1.6 %copy-done.3 = bf16[1,512,3584]{2,1,0:T(8,128)(2,1)S(1)} copy-done((bf16[1,512,3584]{2,1,0:T(8,128)(2,1)S(1)}, bf16[1,512,3584]{2,1,0:T(8,128)(2,1)}, u32[]{:S(2)}) %copy-start.3) | copy-done | bytes 3670040
  49.4 1.3 %copy-done.2 = bf16[1,3584,512]{2,1,0:T(8,128)(2,1)S(1)} copy-done((bf16[1,3584,512]{2,1,0:T(8,128)(2,1)S(1)}, bf16[1,3584,512]{2,1,0:T(8,128)(2,1)}, u32[]{:S(2)}) %copy-start.2) | copy-done | bytes 3670040
  50.7 0.9 convolution_bitcast_fusion.4
  51.6 1.2 %copy-done.1 = bf16[1,3584,512]{2,1,0:T(8,128)(2,1)S(1)} copy-done((bf16[1,3584,512]{2,1,0:T(8,128)(2,1)S(1)}, bf16[1,3584,512]{2,1,0:T(8,128)(2,1)}, u32[]{:S(2)}) %copy-start.1) | copy-done | bytes 3670040
  52.7 0.9 convolution_bitcast_fusion.5
  55.7 1.3 %fusion.27 = f32[192,4,896]{2,0,1:T(8,128)S(1)} fusion(bf16[4,896,512]{2,1,0:T(8,128)(2,1)S(1)} %bitcast.169, bf16[192,512]{1,0:T(8,128)(2,1)S(1)} %get-tuple-element.30), kind=kOutput, calls=%fused_computation.74 | convolution fusion | flops 704643072 | bytes 6619136 | tf_op jit(solution)/shard_map/sf,ndf->nsd/dot_general | solution.py:141
  57.1 1.3 %fusion.1 = f32[192,4,896]{2,0,1:T(8,128)S(1)} fusion(f32[192,4,896]{2,0,1:T(8,128)S(1)} %fusion.27, bf16[192,512,1]{1,0,2:T(8,128)(2,1)S(1)} %get-tuple-element.29, bf16[4,896,512]{2,1,0:T(8,128)(2,1)S(1)} %bitcast.171), kind=kOutput, calls=%fused_computation.6 | convolution fusion | flops 706707456 | bytes 9371648 | tf_op jit(solution)/shard_map/sf,ndf->nsd/dot_general | solution.py:143
  60.5 1.6 %collective-permute-done.6 = f32[192]{0:T(256)S(1)} collective-permute-done((f32[192]{0:T(256)S(1)}, f32[192]{0:T(256)S(1)}, u32[]{:S(2)}, u32[]{:S(2)}) %collective-permute-start.6) | collective-permute-done | bytes 800 | tf_op jit(solution)/shard_map/ppermute | solution.py:67
  62.2 1.5 %collective-permute-start.7 = (f32[192]{0:T(256)S(1)}, f32[192]{0:T(256)S(1)}, u32[]{:S(2)}, u32[]{:S(2)}) collective-permute-start(f32[192]{0:T(256)S(1)} %add.53), channel_id=1, source_target_pairs={{0,16},{8,24},{16,0},{24,8},{1,17},{9,25},{17,1},{25,9},{2,18},{10... | collective-permute-start | bytes 2312 | tf_op jit(solution)/shard_map/ppermute | solution.py:67
  65.5 1.5 %collective-permute-start.3 = (bf16[1,192,896]{2,1,0:T(8,128)(2,1)}, bf16[1,192,896]{2,1,0:T(8,128)(2,1)}, u32[]{:S(2)}, u32[]{:S(2)}) collective-permute-start(bf16[1,192,896]{2,1,0:T(8,128)(2,1)} %fusion.23), channel_id=1, source_target_pairs={{0,16},{8,24},{16,0},{24,8},{1,17},{9,25},{17,1},{25,9},{2,18},{10... | collective-permute-start | bytes 1032200 | tf_op jit(solution)/shard_map/ppermute | solution.py:60
  67.0 7.9 %collective-permute-done.9 = bf16[1,192,896]{2,1,0:T(8,128)(2,1)S(1)} collective-permute-done((bf16[1,192,896]{2,1,0:T(8,128)(2,1)S(1)}, bf16[1,192,896]{2,1,0:T(8,128)(2,1)S(1)}, u32[]{:S(2)}, u32[]{:S(2)}) %collective-permute-start.9) | collective-permute-done | bytes 344096 | tf_op jit(solution)/shard_map/ppermute | solution.py:60
  75.8 5.7 %all-to-all-start.3 = ((bf16[8,24,896]{2,1,0:T(8,128)(2,1)}), bf16[8,24,896]{2,1,0:T(8,128)(2,1)S(1)}, u32[]{:S(2)}, u32[]{:S(2)}) async-start(bf16[8,24,896]{2,1,0:T(8,128)(2,1)} %bitcast.185), calls=%async_computation.3 | async-start | bytes 688128 | tf_op jit(solution)/shard_map/all_to_all | solution.py:98
  81.5 0.9 concatenate.62
  82.4 0.9 concatenate.63
  83.2 1.1 %fusion.20 = bf16[1,192,896]{2,1,0:T(8,128)(2,1)S(1)} fusion(bf16[1,192,896]{2,1,0:T(8,128)(2,1)} %collective-permute-done.3, f32[1,2,192,896]{3,2,1,0:T(8,128)S(1)} %fusion.4, pred[]{:T(512)S(6)} %eq.50), kind=kLoop, calls=%fused_computation.52 | loop fusion | flops 688128 | bytes 2064385 | tf_op jit(solution)/shard_map/convert_element_type | solution.py:127
  85.2 5.2 %all-to-all-done.3 = bf16[8,24,896]{2,1,0:T(8,128)(2,1)S(1)} async-done(((bf16[8,24,896]{2,1,0:T(8,128)(2,1)}), bf16[8,24,896]{2,1,0:T(8,128)(2,1)S(1)}, u32[]{:S(2)}, u32[]{:S(2)}) %all-to-all-start.3) | async-done | bytes 344096 | tf_op jit(solution)/shard_map/all_to_all | solution.py:98
  90.3 3.6 %all-to-all-start.2 = ((bf16[8,24,1024]{2,1,0:T(8,128)(2,1)}), bf16[8,24,1024]{2,1,0:T(8,128)(2,1)S(1)}, u32[]{:S(2)}, u32[]{:S(2)}) async-start(bf16[8,24,1024]{2,1,0:T(8,128)(2,1)} %maximum_maximum_fusion.1), calls=%async_computation.2 | async-start | bytes 786432 | tf_op jit(solution)/shard_map/all_to_all | solution.py:98
  94.0 3.0 %convolution_convert_fusion = bf16[4,896,512]{2,1,0:T(8,128)(2,1)} fusion(bf16[4,192,896]{2,1,0:T(8,128)(2,1)S(1)} %bitcast.160, bf16[192,512,1]{1,0,2:T(8,128)(2,1)S(1)} %copy-done.5), kind=kOutput, calls=%fused_computation.4 | convolution fusion | flops 706478080 | bytes 5242880 | tf_op jit(solution)/shard_map/nsd,sf->ndf/dot_general | solution.py:151
  97.0 3.0 %convolution_convert_fusion.1 = bf16[4,896,512]{2,1,0:T(8,128)(2,1)} fusion(bf16[4,192,896]{2,1,0:T(8,128)(2,1)S(1)} %bitcast.161, bf16[192,512]{1,0:T(8,128)(2,1)S(1)} %get-tuple-element.30), kind=kOutput, calls=%fused_computation.5 | convolution fusion | flops 706478080 | bytes 5242880 | tf_op jit(solution)/shard_map/nsd,sf->ndf/dot_general | solution.py:148
  100.0 1.0 convolution_convert_fusion.4
  101.0 2.4 %all-to-all-done.2 = bf16[8,24,1024]{2,1,0:T(8,128)(2,1)S(1)} async-done(((bf16[8,24,1024]{2,1,0:T(8,128)(2,1)}), bf16[8,24,1024]{2,1,0:T(8,128)(2,1)S(1)}, u32[]{:S(2)}, u32[]{:S(2)}) %all-to-all-start.2) | async-done | bytes 393248 | tf_op jit(solution)/shard_map/all_to_all | solution.py:98
  (71 shorter events, 15.0 us)
Async XLA Ops:
  0.6 1.6 %copy-start = (bf16[128,896]{1,0:T(8,128)(2,1)S(1)}, bf16[128,896]{1,0:T(8,128)(2,1)}, u32[]{:S(2)}) copy-start(bf16[128,896]{1,0:T(8,128)(2,1)} %param.8) | copy-start | bytes 688132
  0.6 11.0 %copy-start.6 = (bf16[128,896]{1,0:T(8,128)(2,1)S(1)}, bf16[128,896]{1,0:T(8,128)(2,1)}, u32[]{:S(2)}) copy-start(bf16[128,896]{1,0:T(8,128)(2,1)} %param.7) | copy-start | bytes 688132
  3.2 17.9 %all-to-all-start.1 = ((bf16[8,24,896]{2,1,0:T(8,128)(2,1)}), bf16[8,24,896]{2,1,0:T(8,128)(2,1)S(1)}, u32[]{:S(2)}, u32[]{:S(2)}) async-start(bf16[8,24,896]{2,1,0:T(8,128)(2,1)} %bitcast.34), calls=%async_computation.1 | async-start | bytes 688128 | tf_op jit(solution)/shard_map/all_to_all | solution.py:98
  21.1 14.9 %all-to-all-start = ((bf16[8,24,1024]{2,1,0:T(8,128)(2,1)}), bf16[8,24,1024]{2,1,0:T(8,128)(2,1)S(1)}, u32[]{:S(2)}, u32[]{:S(2)}) async-start(bf16[8,24,1024]{2,1,0:T(8,128)(2,1)} %maximum_maximum_fusion), calls=%async_computation | async-start | bytes 786432 | tf_op jit(solution)/shard_map/all_to_all | solution.py:98
  24.7 9.1 %collective-permute-start.4 = (bf16[1,192,896]{2,1,0:T(8,128)(2,1)S(1)}, bf16[1,192,896]{2,1,0:T(8,128)(2,1)S(1)}, u32[]{:S(2)}, u32[]{:S(2)}) collective-permute-start(bf16[1,192,896]{2,1,0:T(8,128)(2,1)S(1)} %bitcast.174), channel_id=1, source_target_pairs={{0,16},{8,24},{16,0},{24,8},{1,17},{9,25},{17,1},{25,9},{2,18},{10... | collective-permute-start | bytes 1032200 | tf_op jit(solution)/shard_map/ppermute | solution.py:44
  34.7 10.9 %collective-permute-start.5 = (bf16[2,192,896]{2,1,0:T(8,128)(2,1)}, bf16[2,192,896]{2,1,0:T(8,128)(2,1)S(1)}, u32[]{:S(2)}, u32[]{:S(2)}) collective-permute-start(bf16[2,192,896]{2,1,0:T(8,128)(2,1)} %maximum_select_fusion.4), channel_id=1, source_target_pairs={{0,8},{8,0},{16,24},{24,16},{1,9},{9,1},{17,25},{25,17},{2,10},{10... | collective-permute-start | bytes 2064392 | tf_op jit(solution)/shard_map/ppermute | solution.py:44
  36.0 9.3 %collective-permute-start = (bf16[1,192,896]{2,1,0:T(8,128)(2,1)S(1)}, bf16[1,192,896]{2,1,0:T(8,128)(2,1)S(1)}, u32[]{:S(2)}, u32[]{:S(2)}) collective-permute-start(bf16[1,192,896]{2,1,0:T(8,128)(2,1)S(1)} %get-tuple-element.33), channel_id=1, source_target_pairs={{0,16},{8,24},{16,0},{24,8},{1,17},{9,25},{17,1},{25,9},{2,18},{10... | collective-permute-start | bytes 1032200 | tf_op jit(solution)/shard_map/ppermute | solution.py:44
  45.5 3.7 %collective-permute-start.1 = (bf16[2,192,896]{2,1,0:T(8,128)(2,1)S(1)}, bf16[2,192,896]{2,1,0:T(8,128)(2,1)S(1)}, u32[]{:S(2)}, u32[]{:S(2)}) collective-permute-start(bf16[2,192,896]{2,1,0:T(8,128)(2,1)S(1)} %maximum_select_fusion.2), channel_id=1, source_target_pairs={{0,8},{8,0},{16,24},{24,16},{1,9},{9,1},{17,25},{25,17},{2,10},{10... | collective-permute-start | bytes 2064392 | tf_op jit(solution)/shard_map/ppermute | solution.py:44
  45.7 2.0 %copy-start.3 = (bf16[1,512,3584]{2,1,0:T(8,128)(2,1)S(1)}, bf16[1,512,3584]{2,1,0:T(8,128)(2,1)}, u32[]{:S(2)}) copy-start(bf16[1,512,3584]{2,1,0:T(8,128)(2,1)} %param.13) | copy-start | bytes 11010052
  48.7 2.0 %copy-start.2 = (bf16[1,3584,512]{2,1,0:T(8,128)(2,1)S(1)}, bf16[1,3584,512]{2,1,0:T(8,128)(2,1)}, u32[]{:S(2)}) copy-start(bf16[1,3584,512]{2,1,0:T(8,128)(2,1)} %param.12) | copy-start | bytes 11010052
  50.7 2.0 %copy-start.1 = (bf16[1,3584,512]{2,1,0:T(8,128)(2,1)S(1)}, bf16[1,3584,512]{2,1,0:T(8,128)(2,1)}, u32[]{:S(2)}) copy-start(bf16[1,3584,512]{2,1,0:T(8,128)(2,1)} %param.11) | copy-start | bytes 11010052
  54.2 2.9 %copy-start.4 = (bf16[192,512,1]{1,0,2:T(8,128)(2,1)}, bf16[192,512,1]{1,0,2:T(8,128)(2,1)S(1)}, u32[]{:S(2)}) copy-start(bf16[192,512,1]{1,0,2:T(8,128)(2,1)S(1)} %get-tuple-element.29) | copy-start | bytes 589828
  58.6 5.1 %collective-permute-start.8 = (bf16[2,192,896]{2,1,0:T(8,128)(2,1)S(1)}, bf16[2,192,896]{2,1,0:T(8,128)(2,1)S(1)}, u32[]{:S(2)}, u32[]{:S(2)}) collective-permute-start(bf16[2,192,896]{2,1,0:T(8,128)(2,1)S(1)} %fusion.18), channel_id=1, source_target_pairs={{0,8},{8,0},{16,24},{24,16},{1,9},{9,1},{17,25},{25,17},{2,10},{10... | collective-permute-start | bytes 2064392 | tf_op jit(solution)/shard_map/ppermute | solution.py:60
  59.9 4.6 %collective-permute-start.2 = (bf16[2,192,896]{2,1,0:T(8,128)(2,1)S(1)}, bf16[2,192,896]{2,1,0:T(8,128)(2,1)S(1)}, u32[]{:S(2)}, u32[]{:S(2)}) collective-permute-start(bf16[2,192,896]{2,1,0:T(8,128)(2,1)S(1)} %fusion.17), channel_id=1, source_target_pairs={{0,8},{8,0},{16,24},{24,16},{1,9},{9,1},{17,25},{25,17},{2,10},{10... | collective-permute-start | bytes 2064392 | tf_op jit(solution)/shard_map/ppermute | solution.py:60
  60.0 2.1 %collective-permute-start.6 = (f32[192]{0:T(256)S(1)}, f32[192]{0:T(256)S(1)}, u32[]{:S(2)}, u32[]{:S(2)}) collective-permute-start(f32[192]{0:T(256)S(1)} %get-tuple-element.25), channel_id=1, source_target_pairs={{0,8},{8,0},{16,24},{24,16},{1,9},{9,1},{17,25},{25,17},{2,10},{10... | collective-permute-start | bytes 2312 | tf_op jit(solution)/shard_map/ppermute | solution.py:67
  62.2 19.3 %collective-permute-start.7 = (f32[192]{0:T(256)S(1)}, f32[192]{0:T(256)S(1)}, u32[]{:S(2)}, u32[]{:S(2)}) collective-permute-start(f32[192]{0:T(256)S(1)} %add.53), channel_id=1, source_target_pairs={{0,16},{8,24},{16,0},{24,8},{1,17},{9,25},{17,1},{25,9},{2,18},{10... | collective-permute-start | bytes 2312 | tf_op jit(solution)/shard_map/ppermute | solution.py:67
  63.9 11.0 %collective-permute-start.9 = (bf16[1,192,896]{2,1,0:T(8,128)(2,1)S(1)}, bf16[1,192,896]{2,1,0:T(8,128)(2,1)S(1)}, u32[]{:S(2)}, u32[]{:S(2)}) collective-permute-start(bf16[1,192,896]{2,1,0:T(8,128)(2,1)S(1)} %fusion.24), channel_id=1, source_target_pairs={{0,16},{8,24},{16,0},{24,8},{1,17},{9,25},{17,1},{25,9},{2,18},{10... | collective-permute-start | bytes 1032200 | tf_op jit(solution)/shard_map/ppermute | solution.py:60
  65.5 17.7 %collective-permute-start.3 = (bf16[1,192,896]{2,1,0:T(8,128)(2,1)}, bf16[1,192,896]{2,1,0:T(8,128)(2,1)}, u32[]{:S(2)}, u32[]{:S(2)}) collective-permute-start(bf16[1,192,896]{2,1,0:T(8,128)(2,1)} %fusion.23), channel_id=1, source_target_pairs={{0,16},{8,24},{16,0},{24,8},{1,17},{9,25},{17,1},{25,9},{2,18},{10... | collective-permute-start | bytes 1032200 | tf_op jit(solution)/shard_map/ppermute | solution.py:60
  75.8 14.6 %all-to-all-start.3 = ((bf16[8,24,896]{2,1,0:T(8,128)(2,1)}), bf16[8,24,896]{2,1,0:T(8,128)(2,1)S(1)}, u32[]{:S(2)}, u32[]{:S(2)}) async-start(bf16[8,24,896]{2,1,0:T(8,128)(2,1)} %bitcast.185), calls=%async_computation.3 | async-start | bytes 688128 | tf_op jit(solution)/shard_map/all_to_all | solution.py:98
  83.2 1.1 %copy-start.7 = (bf16[8,24,1]{2,1,0:T(8,128)(2,1)S(1)}, bf16[8,24,1]{2,1,0:T(8,128)(2,1)}, u32[]{:S(2)}) copy-start(bf16[8,24,1]{2,1,0:T(8,128)(2,1)} %concatenate.62) | copy-start | bytes 1156
  83.2 1.1 %copy-start.8 = (bf16[8,24,1]{2,1,0:T(8,128)(2,1)S(1)}, bf16[8,24,1]{2,1,0:T(8,128)(2,1)}, u32[]{:S(2)}) copy-start(bf16[8,24,1]{2,1,0:T(8,128)(2,1)} %concatenate.63) | copy-start | bytes 1156
  84.3 9.7 %copy-start.5 = (bf16[192,512,1]{1,0,2:T(8,128)(2,1)S(1)}, bf16[192,512,1]{1,0,2:T(8,128)(2,1)}, u32[]{:S(2)}) copy-start(bf16[192,512,1]{1,0,2:T(8,128)(2,1)} %copy-done.4) | copy-start | bytes 589828
  90.3 13.0 %all-to-all-start.2 = ((bf16[8,24,1024]{2,1,0:T(8,128)(2,1)}), bf16[8,24,1024]{2,1,0:T(8,128)(2,1)S(1)}, u32[]{:S(2)}, u32[]{:S(2)}) async-start(bf16[8,24,1024]{2,1,0:T(8,128)(2,1)} %maximum_maximum_fusion.1), calls=%async_computation.2 | async-start | bytes 786432 | tf_op jit(solution)/shard_map/all_to_all | solution.py:98
  100.0 3.7 %copy-start.9 = (f32[128,1]{0,1:T(1,128)S(1)}, f32[128,1]{0,1:T(1,128)}, u32[]{:S(2)}) copy-start(f32[128,1]{0,1:T(1,128)} %param.10) | copy-start | bytes 1540

commit v14 on v12

--- a/solution.py
+++ b/solution.py
@@ -60,12 +60,6 @@
         got = lax.ppermute(send, "ctx", xor_pairs(n_ctx, bit))
         acc = keep + got.astype(jnp.float32)
     return acc[0]
-
-
-def all_sum(values, n_ctx):
-    for bit in range(ctx_bits(n_ctx)):
-        values = values + lax.ppermute(values, "ctx", xor_pairs(n_ctx, bit))
-    return values
 
 
 def with_cols(rows, values, pad):
@@ -157,17 +151,15 @@
         "nsd,sf->ndf", rows_in, grad_up, preferred_element_type=jnp.float32
     ).astype(jnp.bfloat16).reshape(1, n_ctx * col_width, group)
 
-    slot_gg = join_f32(back_out[:, col_width], back_out[:, col_width + 1])
-    out_rows = back_out[:, :col_width]
     layer_out = jnp.zeros((tok_rows, col_width), jnp.float32)
     input_grad = jnp.zeros((tok_rows, col_width), jnp.float32)
     gate_terms = []
     for r, chosen in enumerate(route_maps):
         pick = chosen.astype(jnp.bfloat16)
-        rows_r = jnp.dot(pick, out_rows, preferred_element_type=jnp.float32)
-        layer_out = layer_out + route_gates[:, r][:, None] * rows_r
+        rows_r = jnp.dot(pick, back_out, preferred_element_type=jnp.float32)
+        layer_out = layer_out + route_gates[:, r][:, None] * rows_r[:, :col_width]
         input_grad = input_grad + jnp.dot(pick, back_grad, preferred_element_type=jnp.float32)
-        gate_terms.append(jnp.sum(jnp.where(chosen, slot_gg[None, :], 0.0), axis=1))
+        gate_terms.append(rows_r[:, col_width] + rows_r[:, col_width + 1])
     gate_grad = jnp.stack(gate_terms, axis=1)
     return (
         layer_out.astype(jnp.bfloat16),

time: 106 us -> 106 us (level)
    unnamed x20 -> x21, local copies, waits for them, and re-layouts: 4.14 us -> 4.72 us
where the time goes in v14:
time: 106 us
  waiting for transfers between devices  44.4 us (42%)
  starting transfers between devices  26.5 us (25%)
  matrix products  17.3 us (16%)
  other arithmetic  10.8 us (10%)
  local copies, waits for them, and re-layouts  5.65 us (5%)
    all_to_all x4, starting transfers between devices, to_experts(): got = lax.all_to_all(sent, 'ep', split_axis=0, concat_axis=0, tiled=True)  20.2 us
    all_to_all x4, waiting for transfers between devices, to_experts(): got = lax.all_to_all(sent, 'ep', split_axis=0, concat_axis=0, tiled=True)  19.8 us
    ppermute x4, waiting for transfers between devices, gather_blocks(): other = lax.ppermute(held, 'ctx', xor_pairs(n_ctx, bit))  14.9 us
    ppermute x4, waiting for transfers between devices, scatter_sum(): got = lax.ppermute(send, 'ctx', xor_pairs(n_ctx, bit))  9.73 us
    unnamed x21, local copies, waits for them, and re-layouts  4.72 us
    ppermute x4, starting transfers between devices, gather_blocks(): other = lax.ppermute(held, 'ctx', xor_pairs(n_ctx, bit))  3.18 us
    ppermute x4, starting transfers between devices, scatter_sum(): got = lax.ppermute(send, 'ctx', xor_pairs(n_ctx, bit))  3.12 us
    dot_general x1, matrix products, shards(): jnp.einsum('nsd,sf->ndf', rows_in, grad_gate, preferred_element_type=jnp....  3 us
  transfers between devices with their start and end apart: 12, of which 9 were waited for; matrix products, arithmetic and copies ran while one was open for 17% of the time, Pallas kernels for 0%

profile of v14, /device:TPU:0, one launch (start us, length us, event | category | flops | bytes accessed | tf_op | source)
XLA Modules:
  0.0 105.7 jit_solution(820099891917406253)
XLA Ops:
  0.7 0.9 fusion.7
  2.2 1.0 convolution_convert_fusion.2
  3.2 7.3 %all-to-all-start.1 = ((bf16[8,24,896]{2,1,0:T(8,128)(2,1)}), bf16[8,24,896]{2,1,0:T(8,128)(2,1)S(1)}, u32[]{:S(2)}, u32[]{:S(2)}) async-start(bf16[8,24,896]{2,1,0:T(8,128)(2,1)} %bitcast.24), calls=%async_computation.1 | async-start | bytes 688128 | tf_op jit(solution)/shard_map/all_to_all | solution.py:92
  12.8 8.3 %all-to-all-done.1 = bf16[8,24,896]{2,1,0:T(8,128)(2,1)S(1)} async-done(((bf16[8,24,896]{2,1,0:T(8,128)(2,1)}), bf16[8,24,896]{2,1,0:T(8,128)(2,1)S(1)}, u32[]{:S(2)}, u32[]{:S(2)}) %all-to-all-start.1) | async-done | bytes 344096 | tf_op jit(solution)/shard_map/all_to_all | solution.py:92
  21.1 3.6 %all-to-all-start = ((bf16[8,24,1024]{2,1,0:T(8,128)(2,1)}), bf16[8,24,1024]{2,1,0:T(8,128)(2,1)S(1)}, u32[]{:S(2)}, u32[]{:S(2)}) async-start(bf16[8,24,1024]{2,1,0:T(8,128)(2,1)} %maximum_maximum_fusion), calls=%async_computation | async-start | bytes 786432 | tf_op jit(solution)/shard_map/all_to_all | solution.py:92
  24.7 1.5 %collective-permute-start.2 = (bf16[1,192,896]{2,1,0:T(8,128)(2,1)S(1)}, bf16[1,192,896]{2,1,0:T(8,128)(2,1)S(1)}, u32[]{:S(2)}, u32[]{:S(2)}) collective-permute-start(bf16[1,192,896]{2,1,0:T(8,128)(2,1)S(1)} %bitcast.161), channel_id=1, source_target_pairs={{0,16},{8,24},{16,0},{24,8},{1,17},{9,25},{17,1},{25,9},{2,18},{10... | collective-permute-start | bytes 1032200 | tf_op jit(solution)/shard_map/ppermute | solution.py:44
  26.2 7.5 %collective-permute-done.2 = bf16[1,192,896]{2,1,0:T(8,128)(2,1)S(1)} collective-permute-done((bf16[1,192,896]{2,1,0:T(8,128)(2,1)S(1)}, bf16[1,192,896]{2,1,0:T(8,128)(2,1)S(1)}, u32[]{:S(2)}, u32[]{:S(2)}) %collective-permute-start.2) | collective-permute-done | bytes 344096 | tf_op jit(solution)/shard_map/ppermute | solution.py:44
  33.8 1.0 maximum_select_fusion.4
  34.7 1.2 %all-to-all-done = bf16[8,24,1024]{2,1,0:T(8,128)(2,1)S(1)} async-done(((bf16[8,24,1024]{2,1,0:T(8,128)(2,1)}), bf16[8,24,1024]{2,1,0:T(8,128)(2,1)S(1)}, u32[]{:S(2)}, u32[]{:S(2)}) %all-to-all-start) | async-done | bytes 393248 | tf_op jit(solution)/shard_map/all_to_all | solution.py:92
  36.0 1.6 %collective-permute-start = (bf16[1,192,896]{2,1,0:T(8,128)(2,1)S(1)}, bf16[1,192,896]{2,1,0:T(8,128)(2,1)S(1)}, u32[]{:S(2)}, u32[]{:S(2)}) collective-permute-start(bf16[1,192,896]{2,1,0:T(8,128)(2,1)S(1)} %get-tuple-element.37), channel_id=1, source_target_pairs={{0,16},{8,24},{16,0},{24,8},{1,17},{9,25},{17,1},{25,9},{2,18},{10... | collective-permute-start | bytes 1032200 | tf_op jit(solution)/shard_map/ppermute | solution.py:44
  38.0 7.3 %collective-permute-done = bf16[1,192,896]{2,1,0:T(8,128)(2,1)S(1)} collective-permute-done((bf16[1,192,896]{2,1,0:T(8,128)(2,1)S(1)}, bf16[1,192,896]{2,1,0:T(8,128)(2,1)S(1)}, u32[]{:S(2)}, u32[]{:S(2)}) %collective-permute-start) | collective-permute-done | bytes 344096 | tf_op jit(solution)/shard_map/ppermute | solution.py:44
  46.1 1.6 %copy-done.3 = bf16[1,512,3584]{2,1,0:T(8,128)(2,1)S(1)} copy-done((bf16[1,512,3584]{2,1,0:T(8,128)(2,1)S(1)}, bf16[1,512,3584]{2,1,0:T(8,128)(2,1)}, u32[]{:S(2)}) %copy-start.3) | copy-done | bytes 3670040
  49.4 1.3 %copy-done.2 = bf16[1,3584,512]{2,1,0:T(8,128)(2,1)S(1)} copy-done((bf16[1,3584,512]{2,1,0:T(8,128)(2,1)S(1)}, bf16[1,3584,512]{2,1,0:T(8,128)(2,1)}, u32[]{:S(2)}) %copy-start.2) | copy-done | bytes 3670040
  50.7 0.9 convolution_bitcast_fusion.4
  51.6 1.2 %copy-done.1 = bf16[1,3584,512]{2,1,0:T(8,128)(2,1)S(1)} copy-done((bf16[1,3584,512]{2,1,0:T(8,128)(2,1)S(1)}, bf16[1,3584,512]{2,1,0:T(8,128)(2,1)}, u32[]{:S(2)}) %copy-start.1) | copy-done | bytes 3670040
  52.7 0.9 convolution_bitcast_fusion.5
  56.5 1.4 %fusion.27 = f32[192,4,896]{2,0,1:T(8,128)S(1)} fusion(bf16[4,896,512]{2,1,0:T(8,128)(2,1)S(1)} %bitcast.156, bf16[192,512]{1,0:T(8,128)(2,1)S(1)} %get-tuple-element.34), kind=kOutput, calls=%fused_computation.74 | convolution fusion | flops 704643072 | bytes 6619136 | tf_op jit(solution)/shard_map/sf,ndf->nsd/dot_general | solution.py:140
  57.9 1.3 %fusion.1 = f32[192,4,896]{2,0,1:T(8,128)S(1)} fusion(f32[192,4,896]{2,0,1:T(8,128)S(1)} %fusion.27, bf16[192,512,1]{1,0,2:T(8,128)(2,1)S(1)} %get-tuple-element.33, bf16[4,896,512]{2,1,0:T(8,128)(2,1)S(1)} %bitcast.158), kind=kOutput, calls=%fused_computation.6 | convolution fusion | flops 706707456 | bytes 9371648 | tf_op jit(solution)/shard_map/sf,ndf->nsd/dot_general | solution.py:142
  60.7 1.0 collective-permute-done.6
  62.0 1.6 %collective-permute-start.7 = (bf16[1,192,896]{2,1,0:T(8,128)(2,1)S(1)}, bf16[1,192,896]{2,1,0:T(8,128)(2,1)S(1)}, u32[]{:S(2)}, u32[]{:S(2)}) collective-permute-start(bf16[1,192,896]{2,1,0:T(8,128)(2,1)S(1)} %fusion.24), channel_id=1, source_target_pairs={{0,16},{8,24},{16,0},{24,8},{1,17},{9,25},{17,1},{25,9},{2,18},{10... | collective-permute-start | bytes 1032200 | tf_op jit(solution)/shard_map/ppermute | solution.py:60
  64.8 0.9 collective-permute-start.5
  65.7 7.2 %collective-permute-done.7 = bf16[1,192,896]{2,1,0:T(8,128)(2,1)S(1)} collective-permute-done((bf16[1,192,896]{2,1,0:T(8,128)(2,1)S(1)}, bf16[1,192,896]{2,1,0:T(8,128)(2,1)S(1)}, u32[]{:S(2)}, u32[]{:S(2)}) %collective-permute-start.7) | collective-permute-done | bytes 344096 | tf_op jit(solution)/shard_map/ppermute | solution.py:60
  73.8 5.7 %all-to-all-start.3 = ((bf16[8,24,896]{2,1,0:T(8,128)(2,1)}), bf16[8,24,896]{2,1,0:T(8,128)(2,1)S(1)}, u32[]{:S(2)}, u32[]{:S(2)}) async-start(bf16[8,24,896]{2,1,0:T(8,128)(2,1)} %bitcast.172), calls=%async_computation.3 | async-start | bytes 688128 | tf_op jit(solution)/shard_map/all_to_all | solution.py:92
  79.5 1.4 %collective-permute-done.5 = bf16[1,192,1024]{2,1,0:T(8,128)(2,1)} collective-permute-done((bf16[1,192,1024]{2,1,0:T(8,128)(2,1)}, bf16[1,192,1024]{2,1,0:T(8,128)(2,1)}, u32[]{:S(2)}, u32[]{:S(2)}) %collective-permute-start.5) | collective-permute-done | bytes 393248 | tf_op jit(solution)/shard_map/ppermute | solution.py:60
  80.9 1.2 %fusion.18 = f32[192,1024]{1,0:T(8,128)S(1)} fusion(bf16[1,192,1024]{2,1,0:T(8,128)(2,1)} %collective-permute-done.5, f32[1,2,192,1024]{3,2,1,0:T(8,128)S(1)} %fusion.2, pred[]{:T(512)S(6)} %eq.50), kind=kLoop, calls=%fused_computation.45 | loop fusion | flops 589824 | bytes 2752513 | tf_op jit(solution)/shard_map/squeeze | solution.py:62
  82.2 0.9 maximum_maximum_fusion.1
  83.1 6.2 %all-to-all-done.3 = bf16[8,24,896]{2,1,0:T(8,128)(2,1)S(1)} async-done(((bf16[8,24,896]{2,1,0:T(8,128)(2,1)}), bf16[8,24,896]{2,1,0:T(8,128)(2,1)S(1)}, u32[]{:S(2)}, u32[]{:S(2)}) %all-to-all-start.3) | async-done | bytes 344096 | tf_op jit(solution)/shard_map/all_to_all | solution.py:92
  89.3 3.6 %all-to-all-start.2 = ((bf16[8,24,1024]{2,1,0:T(8,128)(2,1)}), bf16[8,24,1024]{2,1,0:T(8,128)(2,1)S(1)}, u32[]{:S(2)}, u32[]{:S(2)}) async-start(bf16[8,24,1024]{2,1,0:T(8,128)(2,1)} %maximum_maximum_fusion.1), calls=%async_computation.2 | async-start | bytes 786432 | tf_op jit(solution)/shard_map/all_to_all | solution.py:92
  92.9 3.0 %convolution_convert_fusion = bf16[4,896,512]{2,1,0:T(8,128)(2,1)} fusion(bf16[4,192,896]{2,1,0:T(8,128)(2,1)S(1)} %bitcast.147, bf16[192,512,1]{1,0,2:T(8,128)(2,1)S(1)} %copy-done.7), kind=kOutput, calls=%fused_computation.4 | convolution fusion | flops 706478080 | bytes 5242880 | tf_op jit(solution)/shard_map/nsd,sf->ndf/dot_general | solution.py:150
  95.9 3.0 %convolution_convert_fusion.1 = bf16[4,896,512]{2,1,0:T(8,128)(2,1)} fusion(bf16[4,192,896]{2,1,0:T(8,128)(2,1)S(1)} %bitcast.148, bf16[192,512]{1,0:T(8,128)(2,1)S(1)} %copy-done.5), kind=kOutput, calls=%fused_computation.5 | convolution fusion | flops 706478080 | bytes 5242880 | tf_op jit(solution)/shard_map/nsd,sf->ndf/dot_general | solution.py:147
  98.9 1.0 convolution_convert_fusion.4
  99.9 4.0 %all-to-all-done.2 = bf16[8,24,1024]{2,1,0:T(8,128)(2,1)S(1)} async-done(((bf16[8,24,1024]{2,1,0:T(8,128)(2,1)}), bf16[8,24,1024]{2,1,0:T(8,128)(2,1)S(1)}, u32[]{:S(2)}, u32[]{:S(2)}) %all-to-all-start.2) | async-done | bytes 393248 | tf_op jit(solution)/shard_map/all_to_all | solution.py:92
  (71 shorter events, 14.2 us)
Async XLA Ops:
  0.6 1.6 %copy-start = (bf16[128,896]{1,0:T(8,128)(2,1)S(1)}, bf16[128,896]{1,0:T(8,128)(2,1)}, u32[]{:S(2)}) copy-start(bf16[128,896]{1,0:T(8,128)(2,1)} %param.8) | copy-start | bytes 688132
  0.6 11.0 %copy-start.8 = (bf16[128,896]{1,0:T(8,128)(2,1)S(1)}, bf16[128,896]{1,0:T(8,128)(2,1)}, u32[]{:S(2)}) copy-start(bf16[128,896]{1,0:T(8,128)(2,1)} %param.7) | copy-start | bytes 688132
  3.2 17.9 %all-to-all-start.1 = ((bf16[8,24,896]{2,1,0:T(8,128)(2,1)}), bf16[8,24,896]{2,1,0:T(8,128)(2,1)S(1)}, u32[]{:S(2)}, u32[]{:S(2)}) async-start(bf16[8,24,896]{2,1,0:T(8,128)(2,1)} %bitcast.24), calls=%async_computation.1 | async-start | bytes 688128 | tf_op jit(solution)/shard_map/all_to_all | solution.py:92
  21.1 14.9 %all-to-all-start = ((bf16[8,24,1024]{2,1,0:T(8,128)(2,1)}), bf16[8,24,1024]{2,1,0:T(8,128)(2,1)S(1)}, u32[]{:S(2)}, u32[]{:S(2)}) async-start(bf16[8,24,1024]{2,1,0:T(8,128)(2,1)} %maximum_maximum_fusion), calls=%async_computation | async-start | bytes 786432 | tf_op jit(solution)/shard_map/all_to_all | solution.py:92
  24.7 9.1 %collective-permute-start.2 = (bf16[1,192,896]{2,1,0:T(8,128)(2,1)S(1)}, bf16[1,192,896]{2,1,0:T(8,128)(2,1)S(1)}, u32[]{:S(2)}, u32[]{:S(2)}) collective-permute-start(bf16[1,192,896]{2,1,0:T(8,128)(2,1)S(1)} %bitcast.161), channel_id=1, source_target_pairs={{0,16},{8,24},{16,0},{24,8},{1,17},{9,25},{17,1},{25,9},{2,18},{10... | collective-permute-start | bytes 1032200 | tf_op jit(solution)/shard_map/ppermute | solution.py:44
  34.7 10.9 %collective-permute-start.3 = (bf16[2,192,896]{2,1,0:T(8,128)(2,1)}, bf16[2,192,896]{2,1,0:T(8,128)(2,1)S(1)}, u32[]{:S(2)}, u32[]{:S(2)}) collective-permute-start(bf16[2,192,896]{2,1,0:T(8,128)(2,1)} %maximum_select_fusion.4), channel_id=1, source_target_pairs={{0,8},{8,0},{16,24},{24,16},{1,9},{9,1},{17,25},{25,17},{2,10},{10... | collective-permute-start | bytes 2064392 | tf_op jit(solution)/shard_map/ppermute | solution.py:44
  36.0 9.3 %collective-permute-start = (bf16[1,192,896]{2,1,0:T(8,128)(2,1)S(1)}, bf16[1,192,896]{2,1,0:T(8,128)(2,1)S(1)}, u32[]{:S(2)}, u32[]{:S(2)}) collective-permute-start(bf16[1,192,896]{2,1,0:T(8,128)(2,1)S(1)} %get-tuple-element.37), channel_id=1, source_target_pairs={{0,16},{8,24},{16,0},{24,8},{1,17},{9,25},{17,1},{25,9},{2,18},{10... | collective-permute-start | bytes 1032200 | tf_op jit(solution)/shard_map/ppermute | solution.py:44
  45.5 3.7 %collective-permute-start.1 = (bf16[2,192,896]{2,1,0:T(8,128)(2,1)S(1)}, bf16[2,192,896]{2,1,0:T(8,128)(2,1)S(1)}, u32[]{:S(2)}, u32[]{:S(2)}) collective-permute-start(bf16[2,192,896]{2,1,0:T(8,128)(2,1)S(1)} %maximum_select_fusion.2), channel_id=1, source_target_pairs={{0,8},{8,0},{16,24},{24,16},{1,9},{9,1},{17,25},{25,17},{2,10},{10... | collective-permute-start | bytes 2064392 | tf_op jit(solution)/shard_map/ppermute | solution.py:44
  45.7 2.0 %copy-start.3 = (bf16[1,512,3584]{2,1,0:T(8,128)(2,1)S(1)}, bf16[1,512,3584]{2,1,0:T(8,128)(2,1)}, u32[]{:S(2)}) copy-start(bf16[1,512,3584]{2,1,0:T(8,128)(2,1)} %param.13) | copy-start | bytes 11010052
  48.7 2.0 %copy-start.2 = (bf16[1,3584,512]{2,1,0:T(8,128)(2,1)S(1)}, bf16[1,3584,512]{2,1,0:T(8,128)(2,1)}, u32[]{:S(2)}) copy-start(bf16[1,3584,512]{2,1,0:T(8,128)(2,1)} %param.12) | copy-start | bytes 11010052
  50.7 2.0 %copy-start.1 = (bf16[1,3584,512]{2,1,0:T(8,128)(2,1)S(1)}, bf16[1,3584,512]{2,1,0:T(8,128)(2,1)}, u32[]{:S(2)}) copy-start(bf16[1,3584,512]{2,1,0:T(8,128)(2,1)} %param.11) | copy-start | bytes 11010052
  54.2 2.3 %copy-start.4 = (bf16[192,512]{1,0:T(8,128)(2,1)}, bf16[192,512]{1,0:T(8,128)(2,1)S(1)}, u32[]{:S(2)}) copy-start(bf16[192,512]{1,0:T(8,128)(2,1)S(1)} %get-tuple-element.34) | copy-start | bytes 589828
  54.2 3.7 %copy-start.6 = (bf16[192,512,1]{1,0,2:T(8,128)(2,1)}, bf16[192,512,1]{1,0,2:T(8,128)(2,1)S(1)}, u32[]{:S(2)}) copy-start(bf16[192,512,1]{1,0,2:T(8,128)(2,1)S(1)} %get-tuple-element.33) | copy-start | bytes 589828
  59.4 2.3 %collective-permute-start.6 = (bf16[2,192,896]{2,1,0:T(8,128)(2,1)S(1)}, bf16[2,192,896]{2,1,0:T(8,128)(2,1)S(1)}, u32[]{:S(2)}, u32[]{:S(2)}) collective-permute-start(bf16[2,192,896]{2,1,0:T(8,128)(2,1)S(1)} %fusion.19), channel_id=1, source_target_pairs={{0,8},{8,0},{16,24},{24,16},{1,9},{9,1},{17,25},{25,17},{2,10},{10... | collective-permute-start | bytes 2064392 | tf_op jit(solution)/shard_map/ppermute | solution.py:60
  60.6 3.0 %collective-permute-start.4 = (bf16[2,192,1024]{2,1,0:T(8,128)(2,1)S(1)}, bf16[2,192,1024]{2,1,0:T(8,128)(2,1)S(1)}, u32[]{:S(2)}, u32[]{:S(2)}) collective-permute-start(bf16[2,192,1024]{2,1,0:T(8,128)(2,1)S(1)} %fusion.17), channel_id=1, source_target_pairs={{0,8},{8,0},{16,24},{24,16},{1,9},{9,1},{17,25},{25,17},{2,10},{10... | collective-permute-start | bytes 2359304 | tf_op jit(solution)/shard_map/ppermute | solution.py:60
  62.0 11.0 %collective-permute-start.7 = (bf16[1,192,896]{2,1,0:T(8,128)(2,1)S(1)}, bf16[1,192,896]{2,1,0:T(8,128)(2,1)S(1)}, u32[]{:S(2)}, u32[]{:S(2)}) collective-permute-start(bf16[1,192,896]{2,1,0:T(8,128)(2,1)S(1)} %fusion.24), channel_id=1, source_target_pairs={{0,16},{8,24},{16,0},{24,8},{1,17},{9,25},{17,1},{25,9},{2,18},{10... | collective-permute-start | bytes 1032200 | tf_op jit(solution)/shard_map/ppermute | solution.py:60
  64.8 16.1 %collective-permute-start.5 = (bf16[1,192,1024]{2,1,0:T(8,128)(2,1)}, bf16[1,192,1024]{2,1,0:T(8,128)(2,1)}, u32[]{:S(2)}, u32[]{:S(2)}) collective-permute-start(bf16[1,192,1024]{2,1,0:T(8,128)(2,1)} %fusion.22), channel_id=1, source_target_pairs={{0,16},{8,24},{16,0},{24,8},{1,17},{9,25},{17,1},{25,9},{2,18},{10... | collective-permute-start | bytes 1179656 | tf_op jit(solution)/shard_map/ppermute | solution.py:60
  73.8 15.5 %all-to-all-start.3 = ((bf16[8,24,896]{2,1,0:T(8,128)(2,1)}), bf16[8,24,896]{2,1,0:T(8,128)(2,1)S(1)}, u32[]{:S(2)}, u32[]{:S(2)}) async-start(bf16[8,24,896]{2,1,0:T(8,128)(2,1)} %bitcast.172), calls=%async_computation.3 | async-start | bytes 688128 | tf_op jit(solution)/shard_map/all_to_all | solution.py:92
  82.1 10.8 %copy-start.7 = (bf16[192,512,1]{1,0,2:T(8,128)(2,1)S(1)}, bf16[192,512,1]{1,0,2:T(8,128)(2,1)}, u32[]{:S(2)}) copy-start(bf16[192,512,1]{1,0,2:T(8,128)(2,1)} %copy-done.6) | copy-start | bytes 589828
  89.3 14.7 %all-to-all-start.2 = ((bf16[8,24,1024]{2,1,0:T(8,128)(2,1)}), bf16[8,24,1024]{2,1,0:T(8,128)(2,1)S(1)}, u32[]{:S(2)}, u32[]{:S(2)}) async-start(bf16[8,24,1024]{2,1,0:T(8,128)(2,1)} %maximum_maximum_fusion.1), calls=%async_computation.2 | async-start | bytes 786432 | tf_op jit(solution)/shard_map/all_to_all | solution.py:92
  92.9 3.0 %copy-start.5 = (bf16[192,512]{1,0:T(8,128)(2,1)S(1)}, bf16[192,512]{1,0:T(8,128)(2,1)}, u32[]{:S(2)}) copy-start(bf16[192,512]{1,0:T(8,128)(2,1)} %copy-done.4) | copy-start | bytes 589828
  98.9 5.4 %copy-start.9 = (f32[128,1]{0,1:T(1,128)S(1)}, f32[128,1]{0,1:T(1,128)}, u32[]{:S(2)}) copy-start(f32[128,1]{0,1:T(1,128)} %param.10) | copy-start | bytes 1540

commit v15 on v13

--- a/solution.py
+++ b/solution.py
@@ -1,6 +1,7 @@
 import jax
 import jax.numpy as jnp
 from jax import lax
+from jax.experimental import pallas as pl
 from jax.sharding import PartitionSpec as P
 
 
@@ -74,6 +75,37 @@
     return jnp.concatenate([rows, hi[:, None], lo[:, None], zeros], axis=1)
 
 
+def pre_kernel(x_ref, wg_ref, wu_ref, pg_ref, pu_ref):
+    @pl.when(pl.program_id(0) == 0)
+    def _():
+        pg_ref[...] = jnp.zeros_like(pg_ref)
+        pu_ref[...] = jnp.zeros_like(pu_ref)
+
+    x = x_ref[0]
+    pg_ref[...] += jnp.dot(x, wg_ref[...], preferred_element_type=jnp.float32)
+    pu_ref[...] += jnp.dot(x, wu_ref[...], preferred_element_type=jnp.float32)
+
+
+def pre_projections(rows_in, gate_w, up_w):
+    n, slots, width = rows_in.shape
+    group = gate_w.shape[1]
+    out = jax.ShapeDtypeStruct((slots, group), jnp.float32)
+    return pl.pallas_call(
+        pre_kernel,
+        grid=(n,),
+        in_specs=[
+            pl.BlockSpec((1, slots, width), lambda q: (q, 0, 0)),
+            pl.BlockSpec((width, group), lambda q: (q, 0)),
+            pl.BlockSpec((width, group), lambda q: (q, 0)),
+        ],
+        out_specs=[
+            pl.BlockSpec((slots, group), lambda q: (0, 0)),
+            pl.BlockSpec((slots, group), lambda q: (0, 0)),
+        ],
+        out_shape=[out, out],
+    )(rows_in, gate_w, up_w)
+
+
 def shards(tokens, cotangent, expert_ids, route_gates, w_gate, w_up, w_down):
     tok_rows, routes = expert_ids.shape
     experts = lax.axis_size("ep")
@@ -113,8 +145,7 @@
     down_w = w_down[0]
     down_cols = [down_w[:, q * col_width : (q + 1) * col_width] for q in range(n_ctx)]
 
-    pre_gate = jnp.einsum("nsd,ndf->sf", rows_in, gate_w, preferred_element_type=jnp.float32)
-    pre_up = jnp.einsum("nsd,ndf->sf", rows_in, up_w, preferred_element_type=jnp.float32)
+    pre_gate, pre_up = pre_projections(rows_in, w_gate[0], w_up[0])
     sigma = jax.nn.sigmoid(pre_gate)
     activated = pre_gate * sigma
     hidden = (activated * pre_up).astype(jnp.bfloat16)

time: 106 us -> 112 us (1.057)
  Pallas kernels: 0 us -> 5.91 us
    pallas_call x0 -> x1, Pallas kernels: none -> 5.91 us  [pre_projections(): pl.pallas_call(pre_kernel, grid=(n,), in_specs=[pl.BlockSpec((1, slots, w...]
    dot_general x2 -> x0, matrix products: 1.74 us -> none  [the longest x1 0.87 us: shards(): jnp.einsum('nsd,ndf->sf', rows_in, up_w, preferred_element_type=jnp.float32)]
    dot_general x4, matrix products: 1.97 us -> 3.5 us  [shards(): lax.dot_general(grads_in[q], down_cols[q], contract_last, preferred_eleme...]
    unnamed x21 -> x23, local copies, waits for them, and re-layouts: 4.71 us -> 4.2 us
where the time goes in v15:
time: 112 us; the launch traced here: 111 us
  waiting for transfers between devices  40.7 us (36%)
  starting transfers between devices  28.1 us (25%)
  matrix products  18 us (16%)
  other arithmetic  10.2 us (9%)
  local copies, waits for them, and re-layouts  7.6 us (7%)
  Pallas kernels  5.91 us (5%)
    all_to_all x4, starting transfers between devices, to_experts(): got = lax.all_to_all(sent, 'ep', split_axis=0, concat_axis=0, tiled=True)  20.2 us
    all_to_all x4, waiting for transfers between devices, to_experts(): got = lax.all_to_all(sent, 'ep', split_axis=0, concat_axis=0, tiled=True)  16.1 us
    ppermute x4, waiting for transfers between devices, gather_blocks(): other = lax.ppermute(held, 'ctx', xor_pairs(n_ctx, bit))  15 us
    ppermute x4, waiting for transfers between devices, scatter_sum(): got = lax.ppermute(send, 'ctx', xor_pairs(n_ctx, bit))  7.95 us
    pallas_call x1, Pallas kernels, pre_projections(): pl.pallas_call(pre_kernel, grid=(n,), in_specs=[pl.BlockSpec((1, slots, w...  5.91 us
    unnamed x23, local copies, waits for them, and re-layouts  4.2 us
    dot_general x1, matrix products, shards(): jnp.einsum('nsd,sf->ndf', rows_in, grad_up, preferred_element_type=jnp.fl...  3.93 us
    dot_general x4, matrix products, shards(): lax.dot_general(grads_in[q], down_cols[q], contract_last, preferred_eleme...  3.5 us
  transfers between devices with their start and end apart: 14, of which 8 were waited for; matrix products, arithmetic and copies ran while one was open for 18% of the time, Pallas kernels for 0%

profile of v15, /device:TPU:0, one launch (start us, length us, event | category | flops | bytes accessed | tf_op | source)
XLA Modules:
  0.0 111.5 jit_solution(1245699999967633781)
XLA Ops:
  0.7 0.9 fusion.7
  2.2 1.0 convolution_convert_fusion.2
  3.2 7.3 %all-to-all-start.1 = ((bf16[8,24,896]{2,1,0:T(8,128)(2,1)}), bf16[8,24,896]{2,1,0:T(8,128)(2,1)S(1)}, u32[]{:S(2)}, u32[]{:S(2)}) async-start(bf16[8,24,896]{2,1,0:T(8,128)(2,1)} %bitcast.32), calls=%async_computation.1 | async-start | bytes 688128 | tf_op jit(solution)/shard_map/all_to_all | solution.py:130
  12.8 8.3 %all-to-all-done.1 = bf16[8,24,896]{2,1,0:T(8,128)(2,1)S(1)} async-done(((bf16[8,24,896]{2,1,0:T(8,128)(2,1)}), bf16[8,24,896]{2,1,0:T(8,128)(2,1)S(1)}, u32[]{:S(2)}, u32[]{:S(2)}) %all-to-all-start.1) | async-done | bytes 344096 | tf_op jit(solution)/shard_map/all_to_all | solution.py:130
  21.1 3.6 %all-to-all-start = ((bf16[8,24,1024]{2,1,0:T(8,128)(2,1)}), bf16[8,24,1024]{2,1,0:T(8,128)(2,1)S(1)}, u32[]{:S(2)}, u32[]{:S(2)}) async-start(bf16[8,24,1024]{2,1,0:T(8,128)(2,1)} %maximum_maximum_fusion), calls=%async_computation | async-start | bytes 786432 | tf_op jit(solution)/shard_map/all_to_all | solution.py:130
  24.7 1.5 %collective-permute-start.4 = (bf16[1,192,896]{2,1,0:T(8,128)(2,1)S(1)}, bf16[1,192,896]{2,1,0:T(8,128)(2,1)S(1)}, u32[]{:S(2)}, u32[]{:S(2)}) collective-permute-start(bf16[1,192,896]{2,1,0:T(8,128)(2,1)S(1)} %bitcast.167), channel_id=1, source_target_pairs={{0,16},{8,24},{16,0},{24,8},{1,17},{9,25},{17,1},{25,9},{2,18},{10... | collective-permute-start | bytes 1032200 | tf_op jit(solution)/shard_map/ppermute | solution.py:45
  26.2 7.5 %collective-permute-done.4 = bf16[1,192,896]{2,1,0:T(8,128)(2,1)S(1)} collective-permute-done((bf16[1,192,896]{2,1,0:T(8,128)(2,1)S(1)}, bf16[1,192,896]{2,1,0:T(8,128)(2,1)S(1)}, u32[]{:S(2)}, u32[]{:S(2)}) %collective-permute-start.4) | collective-permute-done | bytes 344096 | tf_op jit(solution)/shard_map/ppermute | solution.py:45
  33.8 1.0 maximum_select_fusion.4
  34.7 1.2 %all-to-all-done = bf16[8,24,1024]{2,1,0:T(8,128)(2,1)S(1)} async-done(((bf16[8,24,1024]{2,1,0:T(8,128)(2,1)}), bf16[8,24,1024]{2,1,0:T(8,128)(2,1)S(1)}, u32[]{:S(2)}, u32[]{:S(2)}) %all-to-all-start) | async-done | bytes 393248 | tf_op jit(solution)/shard_map/all_to_all | solution.py:130
  36.0 1.6 %collective-permute-start = (bf16[1,192,896]{2,1,0:T(8,128)(2,1)S(1)}, bf16[1,192,896]{2,1,0:T(8,128)(2,1)S(1)}, u32[]{:S(2)}, u32[]{:S(2)}) collective-permute-start(bf16[1,192,896]{2,1,0:T(8,128)(2,1)S(1)} %get-tuple-element.32), channel_id=1, source_target_pairs={{0,16},{8,24},{16,0},{24,8},{1,17},{9,25},{17,1},{25,9},{2,18},{10... | collective-permute-start | bytes 1032200 | tf_op jit(solution)/shard_map/ppermute | solution.py:45
  37.9 7.4 %collective-permute-done = bf16[1,192,896]{2,1,0:T(8,128)(2,1)S(1)} collective-permute-done((bf16[1,192,896]{2,1,0:T(8,128)(2,1)S(1)}, bf16[1,192,896]{2,1,0:T(8,128)(2,1)S(1)}, u32[]{:S(2)}, u32[]{:S(2)}) %collective-permute-start) | collective-permute-done | bytes 344096 | tf_op jit(solution)/shard_map/ppermute | solution.py:45
  46.0 1.6 %copy-done.4 = bf16[1,512,3584]{2,1,0:T(8,128)(2,1)S(1)} copy-done((bf16[1,512,3584]{2,1,0:T(8,128)(2,1)S(1)}, bf16[1,512,3584]{2,1,0:T(8,128)(2,1)}, u32[]{:S(2)}) %copy-start.4) | copy-done | bytes 3670040
  49.3 1.2 %copy.37 = bf16[2,2,192,896]{3,2,1,0:T(8,128)(2,1)} copy(bf16[2,2,192,896]{3,2,0,1:T(8,128)(2,1)S(1)} %maximum_select_fusion) | data formatting | bytes 2752512 | tf_op jit(solution)/shard_map/jit(_where)/select_n | solution.py:47
  50.4 5.9 %shard_map.110 = (f32[192,512]{1,0:T(8,128)}, f32[192,512]{1,0:T(8,128)}) custom-call(bf16[4,192,896]{2,1,0:T(8,128)(2,1)} %bitcast.150, bf16[3584,512]{1,0:T(8,128)(2,1)} %bitcast.155, bf16[3584,512]{1,0:T(8,128)(2,1)} %bitcast.157), custom_call_target="tpu_custom_call" | custom-call | tf_op jit(solution)/shard_map/pallas_call | solution.py:93
  56.4 2.1 %fusion.25 = (bf16[192,512,1]{1,0,2:T(8,128)(2,1)S(1)}, bf16[192,512]{1,0:T(8,128)(2,1)S(1)}, bf16[192,512]{1,0:T(8,128)(2,1)S(1)}) fusion(f32[192,512]{1,0:T(8,128)} %get-tuple-element.7, f32[192,512]{1,0:T(8,128)} %get-tuple-element.8, f32[192,512]{1,0:T(8,128)S(1)} %convolution_add_fusion.1, bf16[512,3584]{1,0:T(8,128)(2,1)} %bitcast.178, ...), kind=kOutput, calls=%fused_computation.70 | convolution fusion | flops 177831936 | bytes 3032064 | tf_op jit(solution)/shard_map/dot_general | solution.py:164
  60.4 0.9 copy-done.2
  61.3 1.4 %fusion.27 = f32[192,4,896]{2,0,1:T(8,128)S(1)} fusion(bf16[4,896,512]{2,1,0:T(8,128)(2,1)S(1)} %bitcast.156, bf16[192,512]{1,0:T(8,128)(2,1)S(1)} %get-tuple-element.29), kind=kOutput, calls=%fused_computation.72 | convolution fusion | flops 704643072 | bytes 6619136 | tf_op jit(solution)/shard_map/sf,ndf->nsd/dot_general | solution.py:172
  63.4 1.3 %fusion.1 = f32[192,4,896]{2,0,1:T(8,128)S(1)} fusion(f32[192,4,896]{2,0,1:T(8,128)S(1)} %fusion.27, bf16[192,512,1]{1,0,2:T(8,128)(2,1)S(1)} %get-tuple-element.28, bf16[4,896,512]{2,1,0:T(8,128)(2,1)S(1)} %bitcast.158), kind=kOutput, calls=%fused_computation.6 | convolution fusion | flops 706707456 | bytes 9371648 | tf_op jit(solution)/shard_map/sf,ndf->nsd/dot_general | solution.py:174
  66.8 1.6 %collective-permute-done.6 = f32[192]{0:T(256)S(1)} collective-permute-done((f32[192]{0:T(256)S(1)}, f32[192]{0:T(256)S(1)}, u32[]{:S(2)}, u32[]{:S(2)}) %collective-permute-start.6) | collective-permute-done | bytes 800 | tf_op jit(solution)/shard_map/ppermute | solution.py:68
  68.4 1.5 %collective-permute-start.7 = (f32[192]{0:T(256)S(1)}, f32[192]{0:T(256)S(1)}, u32[]{:S(2)}, u32[]{:S(2)}) collective-permute-start(f32[192]{0:T(256)S(1)} %add.53), channel_id=1, source_target_pairs={{0,16},{8,24},{16,0},{24,8},{1,17},{9,25},{17,1},{25,9},{2,18},{10... | collective-permute-start | bytes 2312 | tf_op jit(solution)/shard_map/ppermute | solution.py:68
  71.8 1.5 %collective-permute-start.3 = (bf16[1,192,896]{2,1,0:T(8,128)(2,1)}, bf16[1,192,896]{2,1,0:T(8,128)(2,1)}, u32[]{:S(2)}, u32[]{:S(2)}) collective-permute-start(bf16[1,192,896]{2,1,0:T(8,128)(2,1)} %fusion.23), channel_id=1, source_target_pairs={{0,16},{8,24},{16,0},{24,8},{1,17},{9,25},{17,1},{25,9},{2,18},{10... | collective-permute-start | bytes 1032200 | tf_op jit(solution)/shard_map/ppermute | solution.py:61
  73.3 7.9 %collective-permute-done.9 = bf16[1,192,896]{2,1,0:T(8,128)(2,1)S(1)} collective-permute-done((bf16[1,192,896]{2,1,0:T(8,128)(2,1)S(1)}, bf16[1,192,896]{2,1,0:T(8,128)(2,1)S(1)}, u32[]{:S(2)}, u32[]{:S(2)}) %collective-permute-start.9) | collective-permute-done | bytes 344096 | tf_op jit(solution)/shard_map/ppermute | solution.py:61
  82.1 5.7 %all-to-all-start.3 = ((bf16[8,24,896]{2,1,0:T(8,128)(2,1)}), bf16[8,24,896]{2,1,0:T(8,128)(2,1)S(1)}, u32[]{:S(2)}, u32[]{:S(2)}) async-start(bf16[8,24,896]{2,1,0:T(8,128)(2,1)} %bitcast.56), calls=%async_computation.3 | async-start | bytes 688128 | tf_op jit(solution)/shard_map/all_to_all | solution.py:130
  87.8 0.9 concatenate.62
  88.7 0.9 concatenate.63
  89.6 1.2 %fusion.20 = bf16[1,192,896]{2,1,0:T(8,128)(2,1)S(1)} fusion(bf16[1,192,896]{2,1,0:T(8,128)(2,1)} %collective-permute-done.3, f32[1,2,192,896]{3,2,1,0:T(8,128)S(1)} %fusion.4, pred[]{:T(512)S(6)} %eq.50), kind=kLoop, calls=%fused_computation.50 | loop fusion | flops 688128 | bytes 2064385 | tf_op jit(solution)/shard_map/convert_element_type | solution.py:158
  91.6 5.1 %all-to-all-done.3 = bf16[8,24,896]{2,1,0:T(8,128)(2,1)S(1)} async-done(((bf16[8,24,896]{2,1,0:T(8,128)(2,1)}), bf16[8,24,896]{2,1,0:T(8,128)(2,1)S(1)}, u32[]{:S(2)}, u32[]{:S(2)}) %all-to-all-start.3) | async-done | bytes 344096 | tf_op jit(solution)/shard_map/all_to_all | solution.py:130
  96.7 3.6 %all-to-all-start.2 = ((bf16[8,24,1024]{2,1,0:T(8,128)(2,1)}), bf16[8,24,1024]{2,1,0:T(8,128)(2,1)S(1)}, u32[]{:S(2)}, u32[]{:S(2)}) async-start(bf16[8,24,1024]{2,1,0:T(8,128)(2,1)} %maximum_maximum_fusion.1), calls=%async_computation.2 | async-start | bytes 786432 | tf_op jit(solution)/shard_map/all_to_all | solution.py:130
  100.3 3.9 %convolution_convert_fusion = bf16[4,896,512]{2,1,0:T(8,128)(2,1)} fusion(bf16[4,192,896]{2,1,0:T(8,128)(2,1)S(1)} %bitcast.151, bf16[192,512,1]{1,0,2:T(8,128)(2,1)} %copy-done.6), kind=kOutput, calls=%fused_computation.4 | convolution fusion | flops 706478080 | bytes 5242880 | tf_op jit(solution)/shard_map/nsd,sf->ndf/dot_general | solution.py:182
  104.3 3.0 %convolution_convert_fusion.1 = bf16[4,896,512]{2,1,0:T(8,128)(2,1)} fusion(bf16[4,192,896]{2,1,0:T(8,128)(2,1)S(1)} %bitcast.152, bf16[192,512]{1,0:T(8,128)(2,1)S(1)} %get-tuple-element.29), kind=kOutput, calls=%fused_computation.5 | convolution fusion | flops 706478080 | bytes 5242880 | tf_op jit(solution)/shard_map/nsd,sf->ndf/dot_general | solution.py:179
  107.3 1.0 convolution_convert_fusion.4
  108.2 1.5 %all-to-all-done.2 = bf16[8,24,1024]{2,1,0:T(8,128)(2,1)S(1)} async-done(((bf16[8,24,1024]{2,1,0:T(8,128)(2,1)}), bf16[8,24,1024]{2,1,0:T(8,128)(2,1)S(1)}, u32[]{:S(2)}, u32[]{:S(2)}) %all-to-all-start.2) | async-done | bytes 393248 | tf_op jit(solution)/shard_map/all_to_all | solution.py:130
  (72 shorter events, 15.5 us)
Async XLA Ops:
  0.6 1.6 %copy-start = (bf16[128,896]{1,0:T(8,128)(2,1)S(1)}, bf16[128,896]{1,0:T(8,128)(2,1)}, u32[]{:S(2)}) copy-start(bf16[128,896]{1,0:T(8,128)(2,1)} %param.8) | copy-start | bytes 688132
  0.6 11.0 %copy-start.7 = (bf16[128,896]{1,0:T(8,128)(2,1)S(1)}, bf16[128,896]{1,0:T(8,128)(2,1)}, u32[]{:S(2)}) copy-start(bf16[128,896]{1,0:T(8,128)(2,1)} %param.7) | copy-start | bytes 688132
  3.2 17.9 %all-to-all-start.1 = ((bf16[8,24,896]{2,1,0:T(8,128)(2,1)}), bf16[8,24,896]{2,1,0:T(8,128)(2,1)S(1)}, u32[]{:S(2)}, u32[]{:S(2)}) async-start(bf16[8,24,896]{2,1,0:T(8,128)(2,1)} %bitcast.32), calls=%async_computation.1 | async-start | bytes 688128 | tf_op jit(solution)/shard_map/all_to_all | solution.py:130
  21.1 14.9 %all-to-all-start = ((bf16[8,24,1024]{2,1,0:T(8,128)(2,1)}), bf16[8,24,1024]{2,1,0:T(8,128)(2,1)S(1)}, u32[]{:S(2)}, u32[]{:S(2)}) async-start(bf16[8,24,1024]{2,1,0:T(8,128)(2,1)} %maximum_maximum_fusion), calls=%async_computation | async-start | bytes 786432 | tf_op jit(solution)/shard_map/all_to_all | solution.py:130
  24.7 9.1 %collective-permute-start.4 = (bf16[1,192,896]{2,1,0:T(8,128)(2,1)S(1)}, bf16[1,192,896]{2,1,0:T(8,128)(2,1)S(1)}, u32[]{:S(2)}, u32[]{:S(2)}) collective-permute-start(bf16[1,192,896]{2,1,0:T(8,128)(2,1)S(1)} %bitcast.167), channel_id=1, source_target_pairs={{0,16},{8,24},{16,0},{24,8},{1,17},{9,25},{17,1},{25,9},{2,18},{10... | collective-permute-start | bytes 1032200 | tf_op jit(solution)/shard_map/ppermute | solution.py:45
  34.7 11.0 %collective-permute-start.5 = (bf16[2,192,896]{2,1,0:T(8,128)(2,1)}, bf16[2,192,896]{2,1,0:T(8,128)(2,1)S(1)}, u32[]{:S(2)}, u32[]{:S(2)}) collective-permute-start(bf16[2,192,896]{2,1,0:T(8,128)(2,1)} %maximum_select_fusion.4), channel_id=1, source_target_pairs={{0,8},{8,0},{16,24},{24,16},{1,9},{9,1},{17,25},{25,17},{2,10},{10... | collective-permute-start | bytes 2064392 | tf_op jit(solution)/shard_map/ppermute | solution.py:45
  36.0 9.3 %collective-permute-start = (bf16[1,192,896]{2,1,0:T(8,128)(2,1)S(1)}, bf16[1,192,896]{2,1,0:T(8,128)(2,1)S(1)}, u32[]{:S(2)}, u32[]{:S(2)}) collective-permute-start(bf16[1,192,896]{2,1,0:T(8,128)(2,1)S(1)} %get-tuple-element.32), channel_id=1, source_target_pairs={{0,16},{8,24},{16,0},{24,8},{1,17},{9,25},{17,1},{25,9},{2,18},{10... | collective-permute-start | bytes 1032200 | tf_op jit(solution)/shard_map/ppermute | solution.py:45
  45.5 3.5 %collective-permute-start.1 = (bf16[2,192,896]{2,1,0:T(8,128)(2,1)S(1)}, bf16[2,192,896]{2,1,0:T(8,128)(2,1)S(1)}, u32[]{:S(2)}, u32[]{:S(2)}) collective-permute-start(bf16[2,192,896]{2,1,0:T(8,128)(2,1)S(1)} %maximum_select_fusion.3), channel_id=1, source_target_pairs={{0,8},{8,0},{16,24},{24,16},{1,9},{9,1},{17,25},{25,17},{2,10},{10... | collective-permute-start | bytes 2064392 | tf_op jit(solution)/shard_map/ppermute | solution.py:45
  45.5 2.0 %copy-start.4 = (bf16[1,512,3584]{2,1,0:T(8,128)(2,1)S(1)}, bf16[1,512,3584]{2,1,0:T(8,128)(2,1)}, u32[]{:S(2)}) copy-start(bf16[1,512,3584]{2,1,0:T(8,128)(2,1)} %param.13) | copy-start | bytes 11010052
  56.4 2.6 %copy-start.5 = (bf16[1,512,3584]{2,1,0:T(8,128)(2,1)S(1)}, bf16[1,512,3584]{2,1,0:T(8,128)(2,1)}, u32[]{:S(2)}) copy-start(bf16[1,512,3584]{2,1,0:T(8,128)(2,1)} %param.13) | copy-start | bytes 11010052
  58.5 4.2 %copy-start.6 = (bf16[192,512,1]{1,0,2:T(8,128)(2,1)}, bf16[192,512,1]{1,0,2:T(8,128)(2,1)S(1)}, u32[]{:S(2)}) copy-start(bf16[192,512,1]{1,0,2:T(8,128)(2,1)S(1)} %get-tuple-element.28) | copy-start | bytes 589828
  59.3 2.0 %copy-start.2 = (bf16[1,3584,512]{2,1,0:T(8,128)(2,1)S(1)}, bf16[1,3584,512]{2,1,0:T(8,128)(2,1)}, u32[]{:S(2)}) copy-start(bf16[1,3584,512]{2,1,0:T(8,128)(2,1)} %param.11) | copy-start | bytes 11010052
  61.3 2.0 %copy-start.3 = (bf16[1,3584,512]{2,1,0:T(8,128)(2,1)S(1)}, bf16[1,3584,512]{2,1,0:T(8,128)(2,1)}, u32[]{:S(2)}) copy-start(bf16[1,3584,512]{2,1,0:T(8,128)(2,1)} %param.12) | copy-start | bytes 11010052
  64.9 5.1 %collective-permute-start.8 = (bf16[2,192,896]{2,1,0:T(8,128)(2,1)S(1)}, bf16[2,192,896]{2,1,0:T(8,128)(2,1)S(1)}, u32[]{:S(2)}, u32[]{:S(2)}) collective-permute-start(bf16[2,192,896]{2,1,0:T(8,128)(2,1)S(1)} %fusion.18), channel_id=1, source_target_pairs={{0,8},{8,0},{16,24},{24,16},{1,9},{9,1},{17,25},{25,17},{2,10},{10... | collective-permute-start | bytes 2064392 | tf_op jit(solution)/shard_map/ppermute | solution.py:61
  66.2 4.6 %collective-permute-start.2 = (bf16[2,192,896]{2,1,0:T(8,128)(2,1)S(1)}, bf16[2,192,896]{2,1,0:T(8,128)(2,1)S(1)}, u32[]{:S(2)}, u32[]{:S(2)}) collective-permute-start(bf16[2,192,896]{2,1,0:T(8,128)(2,1)S(1)} %fusion.17), channel_id=1, source_target_pairs={{0,8},{8,0},{16,24},{24,16},{1,9},{9,1},{17,25},{25,17},{2,10},{10... | collective-permute-start | bytes 2064392 | tf_op jit(solution)/shard_map/ppermute | solution.py:61
  66.3 2.1 %collective-permute-start.6 = (f32[192]{0:T(256)S(1)}, f32[192]{0:T(256)S(1)}, u32[]{:S(2)}, u32[]{:S(2)}) collective-permute-start(f32[192]{0:T(256)S(1)} %get-tuple-element.24), channel_id=1, source_target_pairs={{0,8},{8,0},{16,24},{24,16},{1,9},{9,1},{17,25},{25,17},{2,10},{10... | collective-permute-start | bytes 2312 | tf_op jit(solution)/shard_map/ppermute | solution.py:68
  68.4 19.4 %collective-permute-start.7 = (f32[192]{0:T(256)S(1)}, f32[192]{0:T(256)S(1)}, u32[]{:S(2)}, u32[]{:S(2)}) collective-permute-start(f32[192]{0:T(256)S(1)} %add.53), channel_id=1, source_target_pairs={{0,16},{8,24},{16,0},{24,8},{1,17},{9,25},{17,1},{25,9},{2,18},{10... | collective-permute-start | bytes 2312 | tf_op jit(solution)/shard_map/ppermute | solution.py:68
  70.3 11.0 %collective-permute-start.9 = (bf16[1,192,896]{2,1,0:T(8,128)(2,1)S(1)}, bf16[1,192,896]{2,1,0:T(8,128)(2,1)S(1)}, u32[]{:S(2)}, u32[]{:S(2)}) collective-permute-start(bf16[1,192,896]{2,1,0:T(8,128)(2,1)S(1)} %fusion.24), channel_id=1, source_target_pairs={{0,16},{8,24},{16,0},{24,8},{1,17},{9,25},{17,1},{25,9},{2,18},{10... | collective-permute-start | bytes 1032200 | tf_op jit(solution)/shard_map/ppermute | solution.py:61
  71.8 17.7 %collective-permute-start.3 = (bf16[1,192,896]{2,1,0:T(8,128)(2,1)}, bf16[1,192,896]{2,1,0:T(8,128)(2,1)}, u32[]{:S(2)}, u32[]{:S(2)}) collective-permute-start(bf16[1,192,896]{2,1,0:T(8,128)(2,1)} %fusion.23), channel_id=1, source_target_pairs={{0,16},{8,24},{16,0},{24,8},{1,17},{9,25},{17,1},{25,9},{2,18},{10... | collective-permute-start | bytes 1032200 | tf_op jit(solution)/shard_map/ppermute | solution.py:61
  82.1 14.6 %all-to-all-start.3 = ((bf16[8,24,896]{2,1,0:T(8,128)(2,1)}), bf16[8,24,896]{2,1,0:T(8,128)(2,1)S(1)}, u32[]{:S(2)}, u32[]{:S(2)}) async-start(bf16[8,24,896]{2,1,0:T(8,128)(2,1)} %bitcast.56), calls=%async_computation.3 | async-start | bytes 688128 | tf_op jit(solution)/shard_map/all_to_all | solution.py:130
  89.5 1.2 %copy-start.8 = (bf16[8,24,1]{2,1,0:T(8,128)(2,1)S(1)}, bf16[8,24,1]{2,1,0:T(8,128)(2,1)}, u32[]{:S(2)}) copy-start(bf16[8,24,1]{2,1,0:T(8,128)(2,1)} %concatenate.62) | copy-start | bytes 1156
  89.5 1.2 %copy-start.9 = (bf16[8,24,1]{2,1,0:T(8,128)(2,1)S(1)}, bf16[8,24,1]{2,1,0:T(8,128)(2,1)}, u32[]{:S(2)}) copy-start(bf16[8,24,1]{2,1,0:T(8,128)(2,1)} %concatenate.63) | copy-start | bytes 1156
  89.5 10.8 %copy-start.1 = (bf16[2,2,192,896]{3,2,1,0:T(8,128)(2,1)S(1)}, bf16[2,2,192,896]{3,2,1,0:T(8,128)(2,1)}, u32[]{:S(2)}) copy-start(bf16[2,2,192,896]{3,2,1,0:T(8,128)(2,1)} %copy.37) | copy-start | bytes 4128772
  96.7 13.0 %all-to-all-start.2 = ((bf16[8,24,1024]{2,1,0:T(8,128)(2,1)}), bf16[8,24,1024]{2,1,0:T(8,128)(2,1)S(1)}, u32[]{:S(2)}, u32[]{:S(2)}) async-start(bf16[8,24,1024]{2,1,0:T(8,128)(2,1)} %maximum_maximum_fusion.1), calls=%async_computation.2 | async-start | bytes 786432 | tf_op jit(solution)/shard_map/all_to_all | solution.py:130
  107.3 2.8 %copy-start.10 = (f32[128,1]{0,1:T(1,128)S(1)}, f32[128,1]{0,1:T(1,128)}, u32[]{:S(2)}) copy-start(f32[128,1]{0,1:T(1,128)} %param.10) | copy-start | bytes 1540

commit v16 on v13

--- a/solution.py
+++ b/solution.py
@@ -48,6 +48,11 @@
         )
         held = pair.reshape((-1,) + block.shape)
     return held
+
+
+def after(values, needed):
+    zero = needed[(0,) * needed.ndim].astype(jnp.float32) * 0.0
+    return values + zero.astype(values.dtype)
 
 
 def scatter_sum(blocks, n_ctx, me):
@@ -104,7 +109,7 @@
     got_x = to_experts(with_cols(place(tokens), slot_gates, pad))
     gate_column = join_f32(got_x[:, col_width], got_x[:, col_width + 1])[:, None]
     rows_in = gather_blocks(got_x[:, :col_width], n_ctx, me)
-    got_dy = to_experts(place(cotangent))
+    got_dy = to_experts(after(place(cotangent), got_x))
     grads_in = gather_blocks(got_dy, n_ctx, me)
 
     group = w_gate.shape[2]

time: 106 us -> 109 us (1.028)
  blocking collectives: 0 us -> 19.1 us
  waiting for transfers between devices: 41.7 us -> 33.4 us
  starting transfers between devices: 28.1 us -> 20.8 us
  other arithmetic: 10.1 us -> 8.49 us
    all_to_all x0 -> x1, blocking collectives: none -> 19.1 us  [to_experts(): got = lax.all_to_all(sent, 'ep', split_axis=0, concat_axis=0, tiled=True)]
    all_to_all x4 -> x3, waiting for transfers between devices: 17.1 us -> 8.41 us  [to_experts(): got = lax.all_to_all(sent, 'ep', split_axis=0, concat_axis=0, tiled=True)]
    all_to_all x4 -> x3, starting transfers between devices: 20.2 us -> 12.8 us  [to_experts(): got = lax.all_to_all(sent, 'ep', split_axis=0, concat_axis=0, tiled=True)]
  transfers between devices with their start and end apart: 14 -> 13, of which waited for: 8 -> 7; matrix products, arithmetic and copies ran while one was open for 18% -> 15% of each run, Pallas kernels for 0% -> 0%
where the time goes in v16:
time: 109 us
  waiting for transfers between devices  33.4 us (31%)
  starting transfers between devices  20.8 us (19%)
  blocking collectives  19.1 us (18%)
  matrix products  17.3 us (16%)
  other arithmetic  8.49 us (8%)
  local copies, waits for them, and re-layouts  7.88 us (7%)
  between operations  1.69 us (2%)
    all_to_all x1, blocking collectives, to_experts(): got = lax.all_to_all(sent, 'ep', split_axis=0, concat_axis=0, tiled=True)  19.1 us
    ppermute x4, waiting for transfers between devices, gather_blocks(): other = lax.ppermute(held, 'ctx', xor_pairs(n_ctx, bit))  15.4 us
    all_to_all x3, starting transfers between devices, to_experts(): got = lax.all_to_all(sent, 'ep', split_axis=0, concat_axis=0, tiled=True)  12.8 us
    all_to_all x3, waiting for transfers between devices, to_experts(): got = lax.all_to_all(sent, 'ep', split_axis=0, concat_axis=0, tiled=True)  8.41 us
    ppermute x4, waiting for transfers between devices, scatter_sum(): got = lax.ppermute(send, 'ctx', xor_pairs(n_ctx, bit))  7.95 us
    unnamed x21, local copies, waits for them, and re-layouts  5.05 us
    ppermute x4, starting transfers between devices, gather_blocks(): other = lax.ppermute(held, 'ctx', xor_pairs(n_ctx, bit))  3.24 us
    dot_general x1, matrix products, shards(): jnp.einsum('nsd,sf->ndf', rows_in, grad_up, preferred_element_type=jnp.fl...  3 us
  transfers between devices with their start and end apart: 13, of which 7 were waited for; matrix products, arithmetic and copies ran while one was open for 15% of the time, Pallas kernels for 0%

profile of v16, /device:TPU:0, one launch (start us, length us, event | category | flops | bytes accessed | tf_op | source)
XLA Modules:
  0.0 108.7 jit_solution(12295973532550110953)
XLA Ops:
  0.7 0.9 fusion.8
  3.8 19.1 %all_to_all.20 = bf16[8,24,1024]{2,1,0:T(8,128)(2,1)S(1)} all-to-all(bf16[8,24,1024]{2,1,0:T(8,128)(2,1)S(1)} %maximum_maximum_fusion), channel_id=1, replica_groups=mesh['ctx'=4,'ep'=8] {'ep'}, dimensions={0} | all-to-all | bytes 786432 | tf_op jit(solution)/shard_map/all_to_all | solution.py:103
  24.1 1.0 fusion.7
  25.1 3.4 %all-to-all-start.1 = ((bf16[8,24,896]{2,1,0:T(8,128)(2,1)}), bf16[8,24,896]{2,1,0:T(8,128)(2,1)S(1)}, u32[]{:S(2)}, u32[]{:S(2)}) async-start(bf16[8,24,896]{2,1,0:T(8,128)(2,1)} %bitcast.35), calls=%async_computation.1 | async-start | bytes 688128 | tf_op jit(solution)/shard_map/all_to_all | solution.py:103
  28.6 1.6 %collective-permute-start = (bf16[1,192,896]{2,1,0:T(8,128)(2,1)S(1)}, bf16[1,192,896]{2,1,0:T(8,128)(2,1)S(1)}, u32[]{:S(2)}, u32[]{:S(2)}) collective-permute-start(bf16[1,192,896]{2,1,0:T(8,128)(2,1)S(1)} %get-tuple-element.33), channel_id=1, source_target_pairs={{0,16},{8,24},{16,0},{24,8},{1,17},{9,25},{17,1},{25,9},{2,18},{10... | collective-permute-start | bytes 1032200 | tf_op jit(solution)/shard_map/ppermute | solution.py:44
  30.2 7.6 %collective-permute-done = bf16[1,192,896]{2,1,0:T(8,128)(2,1)S(1)} collective-permute-done((bf16[1,192,896]{2,1,0:T(8,128)(2,1)S(1)}, bf16[1,192,896]{2,1,0:T(8,128)(2,1)S(1)}, u32[]{:S(2)}, u32[]{:S(2)}) %collective-permute-start) | collective-permute-done | bytes 344096 | tf_op jit(solution)/shard_map/ppermute | solution.py:44
  38.0 0.8 all-to-all-done.1
  38.8 1.5 %collective-permute-start.4 = (bf16[1,192,896]{2,1,0:T(8,128)(2,1)S(1)}, bf16[1,192,896]{2,1,0:T(8,128)(2,1)S(1)}, u32[]{:S(2)}, u32[]{:S(2)}) collective-permute-start(bf16[1,192,896]{2,1,0:T(8,128)(2,1)S(1)} %bitcast.175), channel_id=1, source_target_pairs={{0,16},{8,24},{16,0},{24,8},{1,17},{9,25},{17,1},{25,9},{2,18},{10... | collective-permute-start | bytes 1032200 | tf_op jit(solution)/shard_map/ppermute | solution.py:44
  40.7 7.8 %collective-permute-done.4 = bf16[1,192,896]{2,1,0:T(8,128)(2,1)S(1)} collective-permute-done((bf16[1,192,896]{2,1,0:T(8,128)(2,1)S(1)}, bf16[1,192,896]{2,1,0:T(8,128)(2,1)S(1)}, u32[]{:S(2)}, u32[]{:S(2)}) %collective-permute-start.4) | collective-permute-done | bytes 344096 | tf_op jit(solution)/shard_map/ppermute | solution.py:44
  49.1 1.6 %copy-done.2 = bf16[1,3584,512]{2,1,0:T(8,128)(2,1)S(1)} copy-done((bf16[1,3584,512]{2,1,0:T(8,128)(2,1)S(1)}, bf16[1,3584,512]{2,1,0:T(8,128)(2,1)}, u32[]{:S(2)}) %copy-start.2) | copy-done | bytes 3670040
  50.7 0.9 convolution_bitcast_fusion.4
  51.6 1.2 %copy-done.1 = bf16[1,3584,512]{2,1,0:T(8,128)(2,1)S(1)} copy-done((bf16[1,3584,512]{2,1,0:T(8,128)(2,1)S(1)}, bf16[1,3584,512]{2,1,0:T(8,128)(2,1)}, u32[]{:S(2)}) %copy-start.1) | copy-done | bytes 3670040
  52.8 0.9 convolution_bitcast_fusion.5
  54.0 1.7 %copy-done.3 = bf16[1,512,3584]{2,1,0:T(8,128)(2,1)S(1)} copy-done((bf16[1,512,3584]{2,1,0:T(8,128)(2,1)S(1)}, bf16[1,512,3584]{2,1,0:T(8,128)(2,1)}, u32[]{:S(2)}) %copy-start.3) | copy-done | bytes 3670040
  59.3 1.3 %fusion.28 = f32[192,4,896]{2,0,1:T(8,128)S(1)} fusion(bf16[4,896,512]{2,1,0:T(8,128)(2,1)S(1)} %bitcast.170, bf16[192,512]{1,0:T(8,128)(2,1)S(1)} %get-tuple-element.30), kind=kOutput, calls=%fused_computation.75 | convolution fusion | flops 704643072 | bytes 6619136 | tf_op jit(solution)/shard_map/sf,ndf->nsd/dot_general | solution.py:146
  60.6 1.3 %fusion.1 = f32[192,4,896]{2,0,1:T(8,128)S(1)} fusion(f32[192,4,896]{2,0,1:T(8,128)S(1)} %fusion.28, bf16[192,512,1]{1,0,2:T(8,128)(2,1)S(1)} %get-tuple-element.29, bf16[4,896,512]{2,1,0:T(8,128)(2,1)S(1)} %bitcast.172), kind=kOutput, calls=%fused_computation.6 | convolution fusion | flops 706707456 | bytes 9371648 | tf_op jit(solution)/shard_map/sf,ndf->nsd/dot_general | solution.py:148
  64.1 1.6 %collective-permute-done.6 = f32[192]{0:T(256)S(1)} collective-permute-done((f32[192]{0:T(256)S(1)}, f32[192]{0:T(256)S(1)}, u32[]{:S(2)}, u32[]{:S(2)}) %collective-permute-start.6) | collective-permute-done | bytes 800 | tf_op jit(solution)/shard_map/ppermute | solution.py:72
  65.7 1.5 %collective-permute-start.7 = (f32[192]{0:T(256)S(1)}, f32[192]{0:T(256)S(1)}, u32[]{:S(2)}, u32[]{:S(2)}) collective-permute-start(f32[192]{0:T(256)S(1)} %add.61), channel_id=1, source_target_pairs={{0,16},{8,24},{16,0},{24,8},{1,17},{9,25},{17,1},{25,9},{2,18},{10... | collective-permute-start | bytes 2312 | tf_op jit(solution)/shard_map/ppermute | solution.py:72
  69.0 1.5 %collective-permute-start.3 = (bf16[1,192,896]{2,1,0:T(8,128)(2,1)}, bf16[1,192,896]{2,1,0:T(8,128)(2,1)}, u32[]{:S(2)}, u32[]{:S(2)}) collective-permute-start(bf16[1,192,896]{2,1,0:T(8,128)(2,1)} %fusion.24), channel_id=1, source_target_pairs={{0,16},{8,24},{16,0},{24,8},{1,17},{9,25},{17,1},{25,9},{2,18},{10... | collective-permute-start | bytes 1032200 | tf_op jit(solution)/shard_map/ppermute | solution.py:65
  70.5 7.9 %collective-permute-done.9 = bf16[1,192,896]{2,1,0:T(8,128)(2,1)S(1)} collective-permute-done((bf16[1,192,896]{2,1,0:T(8,128)(2,1)S(1)}, bf16[1,192,896]{2,1,0:T(8,128)(2,1)S(1)}, u32[]{:S(2)}, u32[]{:S(2)}) %collective-permute-start.9) | collective-permute-done | bytes 344096 | tf_op jit(solution)/shard_map/ppermute | solution.py:65
  78.5 0.8 fusion.20
  79.3 5.7 %all-to-all-start.3 = ((bf16[8,24,896]{2,1,0:T(8,128)(2,1)}), bf16[8,24,896]{2,1,0:T(8,128)(2,1)S(1)}, u32[]{:S(2)}, u32[]{:S(2)}) async-start(bf16[8,24,896]{2,1,0:T(8,128)(2,1)} %bitcast.187), calls=%async_computation.3 | async-start | bytes 688128 | tf_op jit(solution)/shard_map/all_to_all | solution.py:103
  85.1 0.9 concatenate.62
  85.9 0.9 concatenate.63
  86.8 1.1 fusion.21
  87.9 0.8 maximum_maximum_fusion.1
  88.7 5.2 %all-to-all-done.3 = bf16[8,24,896]{2,1,0:T(8,128)(2,1)S(1)} async-done(((bf16[8,24,896]{2,1,0:T(8,128)(2,1)}), bf16[8,24,896]{2,1,0:T(8,128)(2,1)S(1)}, u32[]{:S(2)}, u32[]{:S(2)}) %all-to-all-start.3) | async-done | bytes 344096 | tf_op jit(solution)/shard_map/all_to_all | solution.py:103
  93.9 3.6 %all-to-all-start.2 = ((bf16[8,24,1024]{2,1,0:T(8,128)(2,1)}), bf16[8,24,1024]{2,1,0:T(8,128)(2,1)S(1)}, u32[]{:S(2)}, u32[]{:S(2)}) async-start(bf16[8,24,1024]{2,1,0:T(8,128)(2,1)} %maximum_maximum_fusion.1), calls=%async_computation.2 | async-start | bytes 786432 | tf_op jit(solution)/shard_map/all_to_all | solution.py:103
  97.6 3.0 %convolution_convert_fusion = bf16[4,896,512]{2,1,0:T(8,128)(2,1)} fusion(bf16[4,192,896]{2,1,0:T(8,128)(2,1)S(1)} %bitcast.161, bf16[192,512,1]{1,0,2:T(8,128)(2,1)S(1)} %copy-done.5), kind=kOutput, calls=%fused_computation.4 | convolution fusion | flops 706478080 | bytes 5242880 | tf_op jit(solution)/shard_map/nsd,sf->ndf/dot_general | solution.py:156
  100.6 3.0 %convolution_convert_fusion.1 = bf16[4,896,512]{2,1,0:T(8,128)(2,1)} fusion(bf16[4,192,896]{2,1,0:T(8,128)(2,1)S(1)} %bitcast.162, bf16[192,512]{1,0:T(8,128)(2,1)S(1)} %get-tuple-element.30), kind=kOutput, calls=%fused_computation.5 | convolution fusion | flops 706478080 | bytes 5242880 | tf_op jit(solution)/shard_map/nsd,sf->ndf/dot_general | solution.py:153
  103.6 1.0 convolution_convert_fusion.4
  104.5 2.4 %all-to-all-done.2 = bf16[8,24,1024]{2,1,0:T(8,128)(2,1)S(1)} async-done(((bf16[8,24,1024]{2,1,0:T(8,128)(2,1)}), bf16[8,24,1024]{2,1,0:T(8,128)(2,1)S(1)}, u32[]{:S(2)}, u32[]{:S(2)}) %all-to-all-start.2) | async-done | bytes 393248 | tf_op jit(solution)/shard_map/all_to_all | solution.py:103
  (71 shorter events, 13.4 us)
Async XLA Ops:
  0.6 2.7 %copy-start = (bf16[128,896]{1,0:T(8,128)(2,1)S(1)}, bf16[128,896]{1,0:T(8,128)(2,1)}, u32[]{:S(2)}) copy-start(bf16[128,896]{1,0:T(8,128)(2,1)} %param.7) | copy-start | bytes 688132
  0.6 23.5 %copy-start.6 = (bf16[128,896]{1,0:T(8,128)(2,1)S(1)}, bf16[128,896]{1,0:T(8,128)(2,1)}, u32[]{:S(2)}) copy-start(bf16[128,896]{1,0:T(8,128)(2,1)} %param.8) | copy-start | bytes 688132
  25.1 13.7 %all-to-all-start.1 = ((bf16[8,24,896]{2,1,0:T(8,128)(2,1)}), bf16[8,24,896]{2,1,0:T(8,128)(2,1)S(1)}, u32[]{:S(2)}, u32[]{:S(2)}) async-start(bf16[8,24,896]{2,1,0:T(8,128)(2,1)} %bitcast.35), calls=%async_computation.1 | async-start | bytes 688128 | tf_op jit(solution)/shard_map/all_to_all | solution.py:103
  28.6 9.2 %collective-permute-start = (bf16[1,192,896]{2,1,0:T(8,128)(2,1)S(1)}, bf16[1,192,896]{2,1,0:T(8,128)(2,1)S(1)}, u32[]{:S(2)}, u32[]{:S(2)}) collective-permute-start(bf16[1,192,896]{2,1,0:T(8,128)(2,1)S(1)} %get-tuple-element.33), channel_id=1, source_target_pairs={{0,16},{8,24},{16,0},{24,8},{1,17},{9,25},{17,1},{25,9},{2,18},{10... | collective-permute-start | bytes 1032200 | tf_op jit(solution)/shard_map/ppermute | solution.py:44
  37.9 10.9 %collective-permute-start.1 = (bf16[2,192,896]{2,1,0:T(8,128)(2,1)S(1)}, bf16[2,192,896]{2,1,0:T(8,128)(2,1)S(1)}, u32[]{:S(2)}, u32[]{:S(2)}) collective-permute-start(bf16[2,192,896]{2,1,0:T(8,128)(2,1)S(1)} %maximum_select_fusion.2), channel_id=1, source_target_pairs={{0,8},{8,0},{16,24},{24,16},{1,9},{9,1},{17,25},{25,17},{2,10},{10... | collective-permute-start | bytes 2064392 | tf_op jit(solution)/shard_map/ppermute | solution.py:44
  38.8 9.6 %collective-permute-start.4 = (bf16[1,192,896]{2,1,0:T(8,128)(2,1)S(1)}, bf16[1,192,896]{2,1,0:T(8,128)(2,1)S(1)}, u32[]{:S(2)}, u32[]{:S(2)}) collective-permute-start(bf16[1,192,896]{2,1,0:T(8,128)(2,1)S(1)} %bitcast.175), channel_id=1, source_target_pairs={{0,16},{8,24},{16,0},{24,8},{1,17},{9,25},{17,1},{25,9},{2,18},{10... | collective-permute-start | bytes 1032200 | tf_op jit(solution)/shard_map/ppermute | solution.py:44
  48.6 5.0 %collective-permute-start.5 = (bf16[2,192,896]{2,1,0:T(8,128)(2,1)S(1)}, bf16[2,192,896]{2,1,0:T(8,128)(2,1)S(1)}, u32[]{:S(2)}, u32[]{:S(2)}) collective-permute-start(bf16[2,192,896]{2,1,0:T(8,128)(2,1)S(1)} %maximum_select_fusion.4), channel_id=1, source_target_pairs={{0,8},{8,0},{16,24},{24,16},{1,9},{9,1},{17,25},{25,17},{2,10},{10... | collective-permute-start | bytes 2064392 | tf_op jit(solution)/shard_map/ppermute | solution.py:44
  48.7 2.0 %copy-start.2 = (bf16[1,3584,512]{2,1,0:T(8,128)(2,1)S(1)}, bf16[1,3584,512]{2,1,0:T(8,128)(2,1)}, u32[]{:S(2)}) copy-start(bf16[1,3584,512]{2,1,0:T(8,128)(2,1)} %param.12) | copy-start | bytes 11010052
  50.7 2.0 %copy-start.1 = (bf16[1,3584,512]{2,1,0:T(8,128)(2,1)S(1)}, bf16[1,3584,512]{2,1,0:T(8,128)(2,1)}, u32[]{:S(2)}) copy-start(bf16[1,3584,512]{2,1,0:T(8,128)(2,1)} %param.11) | copy-start | bytes 11010052
  53.7 2.0 %copy-start.3 = (bf16[1,512,3584]{2,1,0:T(8,128)(2,1)S(1)}, bf16[1,512,3584]{2,1,0:T(8,128)(2,1)}, u32[]{:S(2)}) copy-start(bf16[1,512,3584]{2,1,0:T(8,128)(2,1)} %param.13) | copy-start | bytes 11010052
  57.7 2.9 %copy-start.4 = (bf16[192,512,1]{1,0,2:T(8,128)(2,1)}, bf16[192,512,1]{1,0,2:T(8,128)(2,1)S(1)}, u32[]{:S(2)}) copy-start(bf16[192,512,1]{1,0,2:T(8,128)(2,1)S(1)} %get-tuple-element.29) | copy-start | bytes 589828
  62.1 5.1 %collective-permute-start.8 = (bf16[2,192,896]{2,1,0:T(8,128)(2,1)S(1)}, bf16[2,192,896]{2,1,0:T(8,128)(2,1)S(1)}, u32[]{:S(2)}, u32[]{:S(2)}) collective-permute-start(bf16[2,192,896]{2,1,0:T(8,128)(2,1)S(1)} %fusion.19), channel_id=1, source_target_pairs={{0,8},{8,0},{16,24},{24,16},{1,9},{9,1},{17,25},{25,17},{2,10},{10... | collective-permute-start | bytes 2064392 | tf_op jit(solution)/shard_map/ppermute | solution.py:65
  63.5 4.6 %collective-permute-start.2 = (bf16[2,192,896]{2,1,0:T(8,128)(2,1)S(1)}, bf16[2,192,896]{2,1,0:T(8,128)(2,1)S(1)}, u32[]{:S(2)}, u32[]{:S(2)}) collective-permute-start(bf16[2,192,896]{2,1,0:T(8,128)(2,1)S(1)} %fusion.18), channel_id=1, source_target_pairs={{0,8},{8,0},{16,24},{24,16},{1,9},{9,1},{17,25},{25,17},{2,10},{10... | collective-permute-start | bytes 2064392 | tf_op jit(solution)/shard_map/ppermute | solution.py:65
  63.6 2.1 %collective-permute-start.6 = (f32[192]{0:T(256)S(1)}, f32[192]{0:T(256)S(1)}, u32[]{:S(2)}, u32[]{:S(2)}) collective-permute-start(f32[192]{0:T(256)S(1)} %get-tuple-element.25), channel_id=1, source_target_pairs={{0,8},{8,0},{16,24},{24,16},{1,9},{9,1},{17,25},{25,17},{2,10},{10... | collective-permute-start | bytes 2312 | tf_op jit(solution)/shard_map/ppermute | solution.py:72
  65.7 19.3 %collective-permute-start.7 = (f32[192]{0:T(256)S(1)}, f32[192]{0:T(256)S(1)}, u32[]{:S(2)}, u32[]{:S(2)}) collective-permute-start(f32[192]{0:T(256)S(1)} %add.61), channel_id=1, source_target_pairs={{0,16},{8,24},{16,0},{24,8},{1,17},{9,25},{17,1},{25,9},{2,18},{10... | collective-permute-start | bytes 2312 | tf_op jit(solution)/shard_map/ppermute | solution.py:72
  67.5 11.0 %collective-permute-start.9 = (bf16[1,192,896]{2,1,0:T(8,128)(2,1)S(1)}, bf16[1,192,896]{2,1,0:T(8,128)(2,1)S(1)}, u32[]{:S(2)}, u32[]{:S(2)}) collective-permute-start(bf16[1,192,896]{2,1,0:T(8,128)(2,1)S(1)} %fusion.25), channel_id=1, source_target_pairs={{0,16},{8,24},{16,0},{24,8},{1,17},{9,25},{17,1},{25,9},{2,18},{10... | collective-permute-start | bytes 1032200 | tf_op jit(solution)/shard_map/ppermute | solution.py:65
  69.0 17.7 %collective-permute-start.3 = (bf16[1,192,896]{2,1,0:T(8,128)(2,1)}, bf16[1,192,896]{2,1,0:T(8,128)(2,1)}, u32[]{:S(2)}, u32[]{:S(2)}) collective-permute-start(bf16[1,192,896]{2,1,0:T(8,128)(2,1)} %fusion.24), channel_id=1, source_target_pairs={{0,16},{8,24},{16,0},{24,8},{1,17},{9,25},{17,1},{25,9},{2,18},{10... | collective-permute-start | bytes 1032200 | tf_op jit(solution)/shard_map/ppermute | solution.py:65
  79.3 14.6 %all-to-all-start.3 = ((bf16[8,24,896]{2,1,0:T(8,128)(2,1)}), bf16[8,24,896]{2,1,0:T(8,128)(2,1)S(1)}, u32[]{:S(2)}, u32[]{:S(2)}) async-start(bf16[8,24,896]{2,1,0:T(8,128)(2,1)} %bitcast.187), calls=%async_computation.3 | async-start | bytes 688128 | tf_op jit(solution)/shard_map/all_to_all | solution.py:103
  86.8 1.1 %copy-start.7 = (bf16[8,24,1]{2,1,0:T(8,128)(2,1)S(1)}, bf16[8,24,1]{2,1,0:T(8,128)(2,1)}, u32[]{:S(2)}) copy-start(bf16[8,24,1]{2,1,0:T(8,128)(2,1)} %concatenate.62) | copy-start | bytes 1156
  86.8 1.1 %copy-start.8 = (bf16[8,24,1]{2,1,0:T(8,128)(2,1)S(1)}, bf16[8,24,1]{2,1,0:T(8,128)(2,1)}, u32[]{:S(2)}) copy-start(bf16[8,24,1]{2,1,0:T(8,128)(2,1)} %concatenate.63) | copy-start | bytes 1156
  87.9 9.7 %copy-start.5 = (bf16[192,512,1]{1,0,2:T(8,128)(2,1)S(1)}, bf16[192,512,1]{1,0,2:T(8,128)(2,1)}, u32[]{:S(2)}) copy-start(bf16[192,512,1]{1,0,2:T(8,128)(2,1)} %copy-done.4) | copy-start | bytes 589828
  93.9 13.0 %all-to-all-start.2 = ((bf16[8,24,1024]{2,1,0:T(8,128)(2,1)}), bf16[8,24,1024]{2,1,0:T(8,128)(2,1)S(1)}, u32[]{:S(2)}, u32[]{:S(2)}) async-start(bf16[8,24,1024]{2,1,0:T(8,128)(2,1)} %maximum_maximum_fusion.1), calls=%async_computation.2 | async-start | bytes 786432 | tf_op jit(solution)/shard_map/all_to_all | solution.py:103
  103.5 3.7 %copy-start.9 = (f32[128,1]{0,1:T(1,128)S(1)}, f32[128,1]{0,1:T(1,128)}, u32[]{:S(2)}) copy-start(f32[128,1]{0,1:T(1,128)} %param.10) | copy-start | bytes 1540

commit v17 on v13

--- a/solution.py
+++ b/solution.py
@@ -101,11 +101,11 @@
     slot_gates = jnp.zeros((slot_count,), jnp.float32)
     for r, chosen in enumerate(route_maps):
         slot_gates = slot_gates + jnp.sum(jnp.where(chosen, route_gates[:, r][:, None], 0.0), axis=0)
-    got_x = to_experts(with_cols(place(tokens), slot_gates, pad))
-    gate_column = join_f32(got_x[:, col_width], got_x[:, col_width + 1])[:, None]
-    rows_in = gather_blocks(got_x[:, :col_width], n_ctx, me)
-    got_dy = to_experts(place(cotangent))
-    grads_in = gather_blocks(got_dy, n_ctx, me)
+    got_x = to_experts(place(tokens))
+    rows_in = gather_blocks(got_x, n_ctx, me)
+    got_dy = to_experts(with_cols(place(cotangent), slot_gates, pad))
+    gate_column = join_f32(got_dy[:, col_width], got_dy[:, col_width + 1])[:, None]
+    grads_in = gather_blocks(got_dy[:, :col_width], n_ctx, me)
 
     group = w_gate.shape[2]
     gate_w = w_gate[0].reshape(n_ctx, col_width, group)

time: 106 us -> 106 us (level)
  no operation moved by 1% of the time
where the time goes in v17:
time: 106 us
  waiting for transfers between devices  41.7 us (39%)
  starting transfers between devices  28.1 us (27%)
  matrix products  17.3 us (16%)
  other arithmetic  10.1 us (10%)
  local copies, waits for them, and re-layouts  7.34 us (7%)
    all_to_all x4, starting transfers between devices, to_experts(): got = lax.all_to_all(sent, 'ep', split_axis=0, concat_axis=0, tiled=True)  20.2 us
    all_to_all x4, waiting for transfers between devices, to_experts(): got = lax.all_to_all(sent, 'ep', split_axis=0, concat_axis=0, tiled=True)  17.1 us
    ppermute x4, waiting for transfers between devices, gather_blocks(): other = lax.ppermute(held, 'ctx', xor_pairs(n_ctx, bit))  15 us
    ppermute x4, waiting for transfers between devices, scatter_sum(): got = lax.ppermute(send, 'ctx', xor_pairs(n_ctx, bit))  7.95 us
    unnamed x21, local copies, waits for them, and re-layouts  5.02 us
    ppermute x4, starting transfers between devices, gather_blocks(): other = lax.ppermute(held, 'ctx', xor_pairs(n_ctx, bit))  3.18 us
    dot_general x1, matrix products, shards(): jnp.einsum('nsd,sf->ndf', rows_in, grad_up, preferred_element_type=jnp.fl...  3 us
    dot_general x1, matrix products, shards(): jnp.einsum('nsd,sf->ndf', rows_in, grad_gate, preferred_element_type=jnp....  3 us
  transfers between devices with their start and end apart: 14, of which 8 were waited for; matrix products, arithmetic and copies ran while one was open for 18% of the time, Pallas kernels for 0%

profile of v17, /device:TPU:0, one launch (start us, length us, event | category | flops | bytes accessed | tf_op | source)
XLA Modules:
  0.0 105.5 jit_solution(5386552149372214418)
XLA Ops:
  0.7 0.9 fusion.7
  2.2 1.0 convolution_convert_fusion.3
  3.2 7.3 %all-to-all-start = ((bf16[8,24,896]{2,1,0:T(8,128)(2,1)}), bf16[8,24,896]{2,1,0:T(8,128)(2,1)S(1)}, u32[]{:S(2)}, u32[]{:S(2)}) async-start(bf16[8,24,896]{2,1,0:T(8,128)(2,1)} %bitcast.7), calls=%async_computation | async-start | bytes 688128 | tf_op jit(solution)/shard_map/all_to_all | solution.py:98
  12.8 8.3 %all-to-all-done = bf16[8,24,896]{2,1,0:T(8,128)(2,1)S(1)} async-done(((bf16[8,24,896]{2,1,0:T(8,128)(2,1)}), bf16[8,24,896]{2,1,0:T(8,128)(2,1)S(1)}, u32[]{:S(2)}, u32[]{:S(2)}) %all-to-all-start) | async-done | bytes 344096 | tf_op jit(solution)/shard_map/all_to_all | solution.py:98
  21.1 3.6 %all-to-all-start.1 = ((bf16[8,24,1024]{2,1,0:T(8,128)(2,1)}), bf16[8,24,1024]{2,1,0:T(8,128)(2,1)S(1)}, u32[]{:S(2)}, u32[]{:S(2)}) async-start(bf16[8,24,1024]{2,1,0:T(8,128)(2,1)} %maximum_maximum_fusion), calls=%async_computation.1 | async-start | bytes 786432 | tf_op jit(solution)/shard_map/all_to_all | solution.py:98
  24.7 1.5 %collective-permute-start = (bf16[1,192,896]{2,1,0:T(8,128)(2,1)S(1)}, bf16[1,192,896]{2,1,0:T(8,128)(2,1)S(1)}, u32[]{:S(2)}, u32[]{:S(2)}) collective-permute-start(bf16[1,192,896]{2,1,0:T(8,128)(2,1)S(1)} %bitcast.174), channel_id=1, source_target_pairs={{0,16},{8,24},{16,0},{24,8},{1,17},{9,25},{17,1},{25,9},{2,18},{10... | collective-permute-start | bytes 1032200 | tf_op jit(solution)/shard_map/ppermute | solution.py:44
  26.2 7.5 %collective-permute-done = bf16[1,192,896]{2,1,0:T(8,128)(2,1)S(1)} collective-permute-done((bf16[1,192,896]{2,1,0:T(8,128)(2,1)S(1)}, bf16[1,192,896]{2,1,0:T(8,128)(2,1)S(1)}, u32[]{:S(2)}, u32[]{:S(2)}) %collective-permute-start) | collective-permute-done | bytes 344096 | tf_op jit(solution)/shard_map/ppermute | solution.py:44
  33.8 1.0 maximum_select_fusion.2
  34.7 1.2 %all-to-all-done.1 = bf16[8,24,1024]{2,1,0:T(8,128)(2,1)S(1)} async-done(((bf16[8,24,1024]{2,1,0:T(8,128)(2,1)}), bf16[8,24,1024]{2,1,0:T(8,128)(2,1)S(1)}, u32[]{:S(2)}, u32[]{:S(2)}) %all-to-all-start.1) | async-done | bytes 393248 | tf_op jit(solution)/shard_map/all_to_all | solution.py:98
  36.0 1.6 %collective-permute-start.4 = (bf16[1,192,896]{2,1,0:T(8,128)(2,1)S(1)}, bf16[1,192,896]{2,1,0:T(8,128)(2,1)S(1)}, u32[]{:S(2)}, u32[]{:S(2)}) collective-permute-start(bf16[1,192,896]{2,1,0:T(8,128)(2,1)S(1)} %get-tuple-element.33), channel_id=1, source_target_pairs={{0,16},{8,24},{16,0},{24,8},{1,17},{9,25},{17,1},{25,9},{2,18},{10... | collective-permute-start | bytes 1032200 | tf_op jit(solution)/shard_map/ppermute | solution.py:44
  37.9 7.4 %collective-permute-done.4 = bf16[1,192,896]{2,1,0:T(8,128)(2,1)S(1)} collective-permute-done((bf16[1,192,896]{2,1,0:T(8,128)(2,1)S(1)}, bf16[1,192,896]{2,1,0:T(8,128)(2,1)S(1)}, u32[]{:S(2)}, u32[]{:S(2)}) %collective-permute-start.4) | collective-permute-done | bytes 344096 | tf_op jit(solution)/shard_map/ppermute | solution.py:44
  46.0 1.6 %copy-done.2 = bf16[1,3584,512]{2,1,0:T(8,128)(2,1)S(1)} copy-done((bf16[1,3584,512]{2,1,0:T(8,128)(2,1)S(1)}, bf16[1,3584,512]{2,1,0:T(8,128)(2,1)}, u32[]{:S(2)}) %copy-start.2) | copy-done | bytes 3670040
  47.6 0.9 convolution_bitcast_fusion.4
  48.5 1.2 %copy-done.1 = bf16[1,3584,512]{2,1,0:T(8,128)(2,1)S(1)} copy-done((bf16[1,3584,512]{2,1,0:T(8,128)(2,1)S(1)}, bf16[1,3584,512]{2,1,0:T(8,128)(2,1)}, u32[]{:S(2)}) %copy-start.1) | copy-done | bytes 3670040
  49.6 0.9 convolution_bitcast_fusion.5
  50.9 1.6 %copy-done.3 = bf16[1,512,3584]{2,1,0:T(8,128)(2,1)S(1)} copy-done((bf16[1,512,3584]{2,1,0:T(8,128)(2,1)S(1)}, bf16[1,512,3584]{2,1,0:T(8,128)(2,1)}, u32[]{:S(2)}) %copy-start.3) | copy-done | bytes 3670040
  56.1 1.3 %fusion.27 = f32[192,4,896]{2,0,1:T(8,128)S(1)} fusion(bf16[4,896,512]{2,1,0:T(8,128)(2,1)S(1)} %bitcast.169, bf16[192,512]{1,0:T(8,128)(2,1)S(1)} %get-tuple-element.30), kind=kOutput, calls=%fused_computation.74 | convolution fusion | flops 704643072 | bytes 6619136 | tf_op jit(solution)/shard_map/sf,ndf->nsd/dot_general | solution.py:141
  57.5 1.3 %fusion.1 = f32[192,4,896]{2,0,1:T(8,128)S(1)} fusion(f32[192,4,896]{2,0,1:T(8,128)S(1)} %fusion.27, bf16[192,512,1]{1,0,2:T(8,128)(2,1)S(1)} %get-tuple-element.29, bf16[4,896,512]{2,1,0:T(8,128)(2,1)S(1)} %bitcast.171), kind=kOutput, calls=%fused_computation.6 | convolution fusion | flops 706707456 | bytes 9371648 | tf_op jit(solution)/shard_map/sf,ndf->nsd/dot_general | solution.py:143
  60.9 1.6 %collective-permute-done.6 = f32[192]{0:T(256)S(1)} collective-permute-done((f32[192]{0:T(256)S(1)}, f32[192]{0:T(256)S(1)}, u32[]{:S(2)}, u32[]{:S(2)}) %collective-permute-start.6) | collective-permute-done | bytes 800 | tf_op jit(solution)/shard_map/ppermute | solution.py:67
  62.6 1.5 %collective-permute-start.7 = (f32[192]{0:T(256)S(1)}, f32[192]{0:T(256)S(1)}, u32[]{:S(2)}, u32[]{:S(2)}) collective-permute-start(f32[192]{0:T(256)S(1)} %add.53), channel_id=1, source_target_pairs={{0,16},{8,24},{16,0},{24,8},{1,17},{9,25},{17,1},{25,9},{2,18},{10... | collective-permute-start | bytes 2312 | tf_op jit(solution)/shard_map/ppermute | solution.py:67
  65.9 1.5 %collective-permute-start.3 = (bf16[1,192,896]{2,1,0:T(8,128)(2,1)}, bf16[1,192,896]{2,1,0:T(8,128)(2,1)}, u32[]{:S(2)}, u32[]{:S(2)}) collective-permute-start(bf16[1,192,896]{2,1,0:T(8,128)(2,1)} %fusion.23), channel_id=1, source_target_pairs={{0,16},{8,24},{16,0},{24,8},{1,17},{9,25},{17,1},{25,9},{2,18},{10... | collective-permute-start | bytes 1032200 | tf_op jit(solution)/shard_map/ppermute | solution.py:60
  67.4 7.9 %collective-permute-done.9 = bf16[1,192,896]{2,1,0:T(8,128)(2,1)S(1)} collective-permute-done((bf16[1,192,896]{2,1,0:T(8,128)(2,1)S(1)}, bf16[1,192,896]{2,1,0:T(8,128)(2,1)S(1)}, u32[]{:S(2)}, u32[]{:S(2)}) %collective-permute-start.9) | collective-permute-done | bytes 344096 | tf_op jit(solution)/shard_map/ppermute | solution.py:60
  76.2 5.7 %all-to-all-start.3 = ((bf16[8,24,896]{2,1,0:T(8,128)(2,1)}), bf16[8,24,896]{2,1,0:T(8,128)(2,1)S(1)}, u32[]{:S(2)}, u32[]{:S(2)}) async-start(bf16[8,24,896]{2,1,0:T(8,128)(2,1)} %bitcast.185), calls=%async_computation.3 | async-start | bytes 688128 | tf_op jit(solution)/shard_map/all_to_all | solution.py:98
  81.9 0.9 concatenate.62
  82.8 0.9 concatenate.63
  83.6 1.1 %fusion.20 = bf16[1,192,896]{2,1,0:T(8,128)(2,1)S(1)} fusion(bf16[1,192,896]{2,1,0:T(8,128)(2,1)} %collective-permute-done.3, f32[1,2,192,896]{3,2,1,0:T(8,128)S(1)} %fusion.4, pred[]{:T(512)S(6)} %eq.50), kind=kLoop, calls=%fused_computation.52 | loop fusion | flops 688128 | bytes 2064385 | tf_op jit(solution)/shard_map/convert_element_type | solution.py:127
  85.6 5.2 %all-to-all-done.3 = bf16[8,24,896]{2,1,0:T(8,128)(2,1)S(1)} async-done(((bf16[8,24,896]{2,1,0:T(8,128)(2,1)}), bf16[8,24,896]{2,1,0:T(8,128)(2,1)S(1)}, u32[]{:S(2)}, u32[]{:S(2)}) %all-to-all-start.3) | async-done | bytes 344096 | tf_op jit(solution)/shard_map/all_to_all | solution.py:98
  90.7 3.6 %all-to-all-start.2 = ((bf16[8,24,1024]{2,1,0:T(8,128)(2,1)}), bf16[8,24,1024]{2,1,0:T(8,128)(2,1)S(1)}, u32[]{:S(2)}, u32[]{:S(2)}) async-start(bf16[8,24,1024]{2,1,0:T(8,128)(2,1)} %maximum_maximum_fusion.1), calls=%async_computation.2 | async-start | bytes 786432 | tf_op jit(solution)/shard_map/all_to_all | solution.py:98
  94.4 3.0 %convolution_convert_fusion = bf16[4,896,512]{2,1,0:T(8,128)(2,1)} fusion(bf16[4,192,896]{2,1,0:T(8,128)(2,1)S(1)} %bitcast.160, bf16[192,512,1]{1,0,2:T(8,128)(2,1)S(1)} %copy-done.5), kind=kOutput, calls=%fused_computation.4 | convolution fusion | flops 706478080 | bytes 5242880 | tf_op jit(solution)/shard_map/nsd,sf->ndf/dot_general | solution.py:151
  97.4 3.0 %convolution_convert_fusion.1 = bf16[4,896,512]{2,1,0:T(8,128)(2,1)} fusion(bf16[4,192,896]{2,1,0:T(8,128)(2,1)S(1)} %bitcast.161, bf16[192,512]{1,0:T(8,128)(2,1)S(1)} %get-tuple-element.30), kind=kOutput, calls=%fused_computation.5 | convolution fusion | flops 706478080 | bytes 5242880 | tf_op jit(solution)/shard_map/nsd,sf->ndf/dot_general | solution.py:148
  100.4 1.0 convolution_convert_fusion.4
  101.4 2.4 %all-to-all-done.2 = bf16[8,24,1024]{2,1,0:T(8,128)(2,1)S(1)} async-done(((bf16[8,24,1024]{2,1,0:T(8,128)(2,1)}), bf16[8,24,1024]{2,1,0:T(8,128)(2,1)S(1)}, u32[]{:S(2)}, u32[]{:S(2)}) %all-to-all-start.2) | async-done | bytes 393248 | tf_op jit(solution)/shard_map/all_to_all | solution.py:98
  (71 shorter events, 15.1 us)
Async XLA Ops:
  0.6 1.6 %copy-start = (bf16[128,896]{1,0:T(8,128)(2,1)S(1)}, bf16[128,896]{1,0:T(8,128)(2,1)}, u32[]{:S(2)}) copy-start(bf16[128,896]{1,0:T(8,128)(2,1)} %param.7) | copy-start | bytes 688132
  0.6 11.0 %copy-start.6 = (bf16[128,896]{1,0:T(8,128)(2,1)S(1)}, bf16[128,896]{1,0:T(8,128)(2,1)}, u32[]{:S(2)}) copy-start(bf16[128,896]{1,0:T(8,128)(2,1)} %param.8) | copy-start | bytes 688132
  3.2 17.9 %all-to-all-start = ((bf16[8,24,896]{2,1,0:T(8,128)(2,1)}), bf16[8,24,896]{2,1,0:T(8,128)(2,1)S(1)}, u32[]{:S(2)}, u32[]{:S(2)}) async-start(bf16[8,24,896]{2,1,0:T(8,128)(2,1)} %bitcast.7), calls=%async_computation | async-start | bytes 688128 | tf_op jit(solution)/shard_map/all_to_all | solution.py:98
  21.1 14.9 %all-to-all-start.1 = ((bf16[8,24,1024]{2,1,0:T(8,128)(2,1)}), bf16[8,24,1024]{2,1,0:T(8,128)(2,1)S(1)}, u32[]{:S(2)}, u32[]{:S(2)}) async-start(bf16[8,24,1024]{2,1,0:T(8,128)(2,1)} %maximum_maximum_fusion), calls=%async_computation.1 | async-start | bytes 786432 | tf_op jit(solution)/shard_map/all_to_all | solution.py:98
  24.7 9.1 %collective-permute-start = (bf16[1,192,896]{2,1,0:T(8,128)(2,1)S(1)}, bf16[1,192,896]{2,1,0:T(8,128)(2,1)S(1)}, u32[]{:S(2)}, u32[]{:S(2)}) collective-permute-start(bf16[1,192,896]{2,1,0:T(8,128)(2,1)S(1)} %bitcast.174), channel_id=1, source_target_pairs={{0,16},{8,24},{16,0},{24,8},{1,17},{9,25},{17,1},{25,9},{2,18},{10... | collective-permute-start | bytes 1032200 | tf_op jit(solution)/shard_map/ppermute | solution.py:44
  34.7 11.0 %collective-permute-start.1 = (bf16[2,192,896]{2,1,0:T(8,128)(2,1)}, bf16[2,192,896]{2,1,0:T(8,128)(2,1)S(1)}, u32[]{:S(2)}, u32[]{:S(2)}) collective-permute-start(bf16[2,192,896]{2,1,0:T(8,128)(2,1)} %maximum_select_fusion.2), channel_id=1, source_target_pairs={{0,8},{8,0},{16,24},{24,16},{1,9},{9,1},{17,25},{25,17},{2,10},{10... | collective-permute-start | bytes 2064392 | tf_op jit(solution)/shard_map/ppermute | solution.py:44
  36.0 9.3 %collective-permute-start.4 = (bf16[1,192,896]{2,1,0:T(8,128)(2,1)S(1)}, bf16[1,192,896]{2,1,0:T(8,128)(2,1)S(1)}, u32[]{:S(2)}, u32[]{:S(2)}) collective-permute-start(bf16[1,192,896]{2,1,0:T(8,128)(2,1)S(1)} %get-tuple-element.33), channel_id=1, source_target_pairs={{0,16},{8,24},{16,0},{24,8},{1,17},{9,25},{17,1},{25,9},{2,18},{10... | collective-permute-start | bytes 1032200 | tf_op jit(solution)/shard_map/ppermute | solution.py:44
  45.5 5.0 %collective-permute-start.5 = (bf16[2,192,896]{2,1,0:T(8,128)(2,1)S(1)}, bf16[2,192,896]{2,1,0:T(8,128)(2,1)S(1)}, u32[]{:S(2)}, u32[]{:S(2)}) collective-permute-start(bf16[2,192,896]{2,1,0:T(8,128)(2,1)S(1)} %maximum_select_fusion.4), channel_id=1, source_target_pairs={{0,8},{8,0},{16,24},{24,16},{1,9},{9,1},{17,25},{25,17},{2,10},{10... | collective-permute-start | bytes 2064392 | tf_op jit(solution)/shard_map/ppermute | solution.py:44
  45.5 2.0 %copy-start.2 = (bf16[1,3584,512]{2,1,0:T(8,128)(2,1)S(1)}, bf16[1,3584,512]{2,1,0:T(8,128)(2,1)}, u32[]{:S(2)}) copy-start(bf16[1,3584,512]{2,1,0:T(8,128)(2,1)} %param.12) | copy-start | bytes 11010052
  47.6 2.0 %copy-start.1 = (bf16[1,3584,512]{2,1,0:T(8,128)(2,1)S(1)}, bf16[1,3584,512]{2,1,0:T(8,128)(2,1)}, u32[]{:S(2)}) copy-start(bf16[1,3584,512]{2,1,0:T(8,128)(2,1)} %param.11) | copy-start | bytes 11010052
  50.5 2.0 %copy-start.3 = (bf16[1,512,3584]{2,1,0:T(8,128)(2,1)S(1)}, bf16[1,512,3584]{2,1,0:T(8,128)(2,1)}, u32[]{:S(2)}) copy-start(bf16[1,512,3584]{2,1,0:T(8,128)(2,1)} %param.13) | copy-start | bytes 11010052
  54.6 2.9 %copy-start.4 = (bf16[192,512,1]{1,0,2:T(8,128)(2,1)}, bf16[192,512,1]{1,0,2:T(8,128)(2,1)S(1)}, u32[]{:S(2)}) copy-start(bf16[192,512,1]{1,0,2:T(8,128)(2,1)S(1)} %get-tuple-element.29) | copy-start | bytes 589828
  59.0 5.1 %collective-permute-start.8 = (bf16[2,192,896]{2,1,0:T(8,128)(2,1)S(1)}, bf16[2,192,896]{2,1,0:T(8,128)(2,1)S(1)}, u32[]{:S(2)}, u32[]{:S(2)}) collective-permute-start(bf16[2,192,896]{2,1,0:T(8,128)(2,1)S(1)} %fusion.18), channel_id=1, source_target_pairs={{0,8},{8,0},{16,24},{24,16},{1,9},{9,1},{17,25},{25,17},{2,10},{10... | collective-permute-start | bytes 2064392 | tf_op jit(solution)/shard_map/ppermute | solution.py:60
  60.3 4.6 %collective-permute-start.2 = (bf16[2,192,896]{2,1,0:T(8,128)(2,1)S(1)}, bf16[2,192,896]{2,1,0:T(8,128)(2,1)S(1)}, u32[]{:S(2)}, u32[]{:S(2)}) collective-permute-start(bf16[2,192,896]{2,1,0:T(8,128)(2,1)S(1)} %fusion.17), channel_id=1, source_target_pairs={{0,8},{8,0},{16,24},{24,16},{1,9},{9,1},{17,25},{25,17},{2,10},{10... | collective-permute-start | bytes 2064392 | tf_op jit(solution)/shard_map/ppermute | solution.py:60
  60.4 2.1 %collective-permute-start.6 = (f32[192]{0:T(256)S(1)}, f32[192]{0:T(256)S(1)}, u32[]{:S(2)}, u32[]{:S(2)}) collective-permute-start(f32[192]{0:T(256)S(1)} %get-tuple-element.25), channel_id=1, source_target_pairs={{0,8},{8,0},{16,24},{24,16},{1,9},{9,1},{17,25},{25,17},{2,10},{10... | collective-permute-start | bytes 2312 | tf_op jit(solution)/shard_map/ppermute | solution.py:67
  62.6 19.3 %collective-permute-start.7 = (f32[192]{0:T(256)S(1)}, f32[192]{0:T(256)S(1)}, u32[]{:S(2)}, u32[]{:S(2)}) collective-permute-start(f32[192]{0:T(256)S(1)} %add.53), channel_id=1, source_target_pairs={{0,16},{8,24},{16,0},{24,8},{1,17},{9,25},{17,1},{25,9},{2,18},{10... | collective-permute-start | bytes 2312 | tf_op jit(solution)/shard_map/ppermute | solution.py:67
  64.3 11.0 %collective-permute-start.9 = (bf16[1,192,896]{2,1,0:T(8,128)(2,1)S(1)}, bf16[1,192,896]{2,1,0:T(8,128)(2,1)S(1)}, u32[]{:S(2)}, u32[]{:S(2)}) collective-permute-start(bf16[1,192,896]{2,1,0:T(8,128)(2,1)S(1)} %fusion.24), channel_id=1, source_target_pairs={{0,16},{8,24},{16,0},{24,8},{1,17},{9,25},{17,1},{25,9},{2,18},{10... | collective-permute-start | bytes 1032200 | tf_op jit(solution)/shard_map/ppermute | solution.py:60
  65.9 17.7 %collective-permute-start.3 = (bf16[1,192,896]{2,1,0:T(8,128)(2,1)}, bf16[1,192,896]{2,1,0:T(8,128)(2,1)}, u32[]{:S(2)}, u32[]{:S(2)}) collective-permute-start(bf16[1,192,896]{2,1,0:T(8,128)(2,1)} %fusion.23), channel_id=1, source_target_pairs={{0,16},{8,24},{16,0},{24,8},{1,17},{9,25},{17,1},{25,9},{2,18},{10... | collective-permute-start | bytes 1032200 | tf_op jit(solution)/shard_map/ppermute | solution.py:60
  76.2 14.6 %all-to-all-start.3 = ((bf16[8,24,896]{2,1,0:T(8,128)(2,1)}), bf16[8,24,896]{2,1,0:T(8,128)(2,1)S(1)}, u32[]{:S(2)}, u32[]{:S(2)}) async-start(bf16[8,24,896]{2,1,0:T(8,128)(2,1)} %bitcast.185), calls=%async_computation.3 | async-start | bytes 688128 | tf_op jit(solution)/shard_map/all_to_all | solution.py:98
  83.6 1.1 %copy-start.7 = (bf16[8,24,1]{2,1,0:T(8,128)(2,1)S(1)}, bf16[8,24,1]{2,1,0:T(8,128)(2,1)}, u32[]{:S(2)}) copy-start(bf16[8,24,1]{2,1,0:T(8,128)(2,1)} %concatenate.62) | copy-start | bytes 1156
  83.6 1.1 %copy-start.8 = (bf16[8,24,1]{2,1,0:T(8,128)(2,1)S(1)}, bf16[8,24,1]{2,1,0:T(8,128)(2,1)}, u32[]{:S(2)}) copy-start(bf16[8,24,1]{2,1,0:T(8,128)(2,1)} %concatenate.63) | copy-start | bytes 1156
  84.7 9.7 %copy-start.5 = (bf16[192,512,1]{1,0,2:T(8,128)(2,1)S(1)}, bf16[192,512,1]{1,0,2:T(8,128)(2,1)}, u32[]{:S(2)}) copy-start(bf16[192,512,1]{1,0,2:T(8,128)(2,1)} %copy-done.4) | copy-start | bytes 589828
  90.7 13.0 %all-to-all-start.2 = ((bf16[8,24,1024]{2,1,0:T(8,128)(2,1)}), bf16[8,24,1024]{2,1,0:T(8,128)(2,1)S(1)}, u32[]{:S(2)}, u32[]{:S(2)}) async-start(bf16[8,24,1024]{2,1,0:T(8,128)(2,1)} %maximum_maximum_fusion.1), calls=%async_computation.2 | async-start | bytes 786432 | tf_op jit(solution)/shard_map/all_to_all | solution.py:98
  100.4 3.7 %copy-start.9 = (f32[128,1]{0,1:T(1,128)S(1)}, f32[128,1]{0,1:T(1,128)}, u32[]{:S(2)}) copy-start(f32[128,1]{0,1:T(1,128)} %param.10) | copy-start | bytes 1540

commit v18 on v13

--- a/solution.py
+++ b/solution.py
@@ -62,6 +62,27 @@
     return acc[0]
 
 
+def pair_sum(first, second, n_ctx, me):
+    width = first.shape[2]
+    halves = jnp.concatenate([first, second], axis=2).reshape((-1, 2) + first.shape[1:2] + (2 * width,))
+    keep_first = (me & 1) == 0
+    keep = jnp.where(keep_first, halves[:, 0], halves[:, 1])
+    send = jnp.where(keep_first, halves[:, 1], halves[:, 0]).astype(jnp.bfloat16)
+    acc = keep + lax.ppermute(send, "ctx", xor_pairs(n_ctx, 0)).astype(jnp.float32)
+    return [rest_sum(acc[:, :, :width], n_ctx, me), rest_sum(acc[:, :, width:], n_ctx, me)]
+
+
+def rest_sum(acc, n_ctx, me):
+    for bit in range(1, ctx_bits(n_ctx)):
+        halves = acc.reshape((-1, 2) + acc.shape[1:])
+        keep_first = ((me >> bit) & 1) == 0
+        keep = jnp.where(keep_first, halves[:, 0], halves[:, 1])
+        send = jnp.where(keep_first, halves[:, 1], halves[:, 0]).astype(jnp.bfloat16)
+        got = lax.ppermute(send, "ctx", xor_pairs(n_ctx, bit))
+        acc = keep + got.astype(jnp.float32)
+    return acc[0]
+
+
 def all_sum(values, n_ctx):
     for bit in range(ctx_bits(n_ctx)):
         values = values + lax.ppermute(values, "ctx", xor_pairs(n_ctx, bit))
@@ -124,9 +145,7 @@
     gate_part = jnp.einsum(
         "nsd,nsd->s", partial_out.astype(jnp.float32), grads_in.astype(jnp.float32)
     )
-    expert_out = scatter_sum(partial_out.astype(jnp.float32), n_ctx, me).astype(jnp.bfloat16)
     gate_sum = all_sum(gate_part, n_ctx)
-    back_out = to_experts(with_cols(expert_out, gate_sum, pad))
 
     contract_last = (((1,), (1,)), ((), ()))
     down_t = sum(
@@ -142,7 +161,10 @@
         "sf,ndf->nsd", grad_gate, gate_w, preferred_element_type=jnp.float32
     ) + jnp.einsum("sf,ndf->nsd", grad_up, up_w, preferred_element_type=jnp.float32)
     back_terms = back_terms.astype(jnp.bfloat16).astype(jnp.float32)
-    slot_grad = scatter_sum(back_terms, n_ctx, me).astype(jnp.bfloat16)
+    out_sum, grad_sum = pair_sum(partial_out.astype(jnp.float32), back_terms, n_ctx, me)
+    expert_out = out_sum.astype(jnp.bfloat16)
+    slot_grad = grad_sum.astype(jnp.bfloat16)
+    back_out = to_experts(with_cols(expert_out, gate_sum, pad))
     back_grad = to_experts(slot_grad)
 
     w_gate_grad = jnp.einsum(

time: 106 us -> 108 us (1.019)
  matrix products: 17.2 us -> 19.2 us
  other arithmetic: 10.1 us -> 11.5 us
    ppermute x2, starting transfers between devices: 2 us -> 0.64 us  [all_sum(): values = values + lax.ppermute(values, 'ctx', xor_pairs(n_ctx, bit))]
    ppermute x4 -> x3, starting transfers between devices: 2.73 us -> 3.68 us  [the longest x2 3.13 us: rest_sum(): got = lax.ppermute(send, 'ctx', xor_pairs(n_ctx, bit))]
    ppermute x4 -> x3, waiting for transfers between devices: 7.95 us -> 7.64 us  [the longest x2 4.88 us: rest_sum(): got = lax.ppermute(send, 'ctx', xor_pairs(n_ctx, bit))]
    convert_element_type x7 -> x5, other arithmetic: 3.23 us -> 3.02 us  [the longest x1 1.07 us: shards(): expert_out = out_sum.astype(jnp.bfloat16)]
    unnamed x21 -> x13, local copies, waits for them, and re-layouts: 4.71 us -> 4.7 us
  transfers between devices with their start and end apart: 14 -> 13, of which waited for: 8 -> 9; matrix products, arithmetic and copies ran while one was open for 18% -> 20% of each run, Pallas kernels for 0% -> 0%
where the time goes in v18:
time: 108 us; the launch traced here: 107 us
  waiting for transfers between devices  40.7 us (38%)
  starting transfers between devices  27.7 us (26%)
  matrix products  19.2 us (18%)
  other arithmetic  11.5 us (11%)
  local copies, waits for them, and re-layouts  7.19 us (7%)
    all_to_all x4, starting transfers between devices, to_experts(): got = lax.all_to_all(sent, 'ep', split_axis=0, concat_axis=0, tiled=True)  20.2 us
    all_to_all x4, waiting for transfers between devices, to_experts(): got = lax.all_to_all(sent, 'ep', split_axis=0, concat_axis=0, tiled=True)  17.1 us
    ppermute x4, waiting for transfers between devices, gather_blocks(): other = lax.ppermute(held, 'ctx', xor_pairs(n_ctx, bit))  15 us
    ppermute x2, waiting for transfers between devices, rest_sum(): got = lax.ppermute(send, 'ctx', xor_pairs(n_ctx, bit))  4.88 us
    unnamed x13, local copies, waits for them, and re-layouts  4.7 us
    dot_general x1, matrix products, shards(): jnp.einsum('nsd,sf->ndf', rows_in, grad_up, preferred_element_type=jnp.fl...  3.91 us
    ppermute x4, starting transfers between devices, gather_blocks(): other = lax.ppermute(held, 'ctx', xor_pairs(n_ctx, bit))  3.17 us
    ppermute x2, starting transfers between devices, rest_sum(): got = lax.ppermute(send, 'ctx', xor_pairs(n_ctx, bit))  3.13 us
  transfers between devices with their start and end apart: 13, of which 9 were waited for; matrix products, arithmetic and copies ran while one was open for 20% of the time, Pallas kernels for 0%

profile of v18, /device:TPU:0, one launch (start us, length us, event | category | flops | bytes accessed | tf_op | source)
XLA Modules:
  0.0 107.2 jit_solution(9528324493633293142)
XLA Ops:
  0.6 0.9 fusion.10
  2.2 1.0 convolution_convert_fusion.2
  3.2 7.2 %all-to-all-start.1 = ((bf16[8,24,896]{2,1,0:T(8,128)(2,1)}), bf16[8,24,896]{2,1,0:T(8,128)(2,1)S(1)}, u32[]{:S(2)}, u32[]{:S(2)}) async-start(bf16[8,24,896]{2,1,0:T(8,128)(2,1)} %bitcast.23), calls=%async_computation.1 | async-start | bytes 688128 | tf_op jit(solution)/shard_map/all_to_all | solution.py:119
  11.7 1.2 %convolution_convert_fusion.7 = bf16[192,896]{1,0:T(8,128)(2,1)S(1)} fusion(bf16[128,896]{1,0:T(8,128)(2,1)} %param.7, s32[128]{0:T(128)S(1)} %fusion.37), kind=kOutput, calls=%fused_computation.23 | convolution fusion | flops 44236800 | bytes 573952 | tf_op jit(solution)/shard_map/ts,tc->sc/dot_general | solution.py:112
  13.7 7.4 %all-to-all-done.1 = bf16[8,24,896]{2,1,0:T(8,128)(2,1)S(1)} async-done(((bf16[8,24,896]{2,1,0:T(8,128)(2,1)}), bf16[8,24,896]{2,1,0:T(8,128)(2,1)S(1)}, u32[]{:S(2)}, u32[]{:S(2)}) %all-to-all-start.1) | async-done | bytes 344096 | tf_op jit(solution)/shard_map/all_to_all | solution.py:119
  21.1 3.6 %all-to-all-start = ((bf16[8,24,1024]{2,1,0:T(8,128)(2,1)}), bf16[8,24,1024]{2,1,0:T(8,128)(2,1)S(1)}, u32[]{:S(2)}, u32[]{:S(2)}) async-start(bf16[8,24,1024]{2,1,0:T(8,128)(2,1)} %maximum_maximum_fusion), calls=%async_computation | async-start | bytes 786432 | tf_op jit(solution)/shard_map/all_to_all | solution.py:119
  24.7 1.5 %collective-permute-start.2 = (bf16[1,192,896]{2,1,0:T(8,128)(2,1)S(1)}, bf16[1,192,896]{2,1,0:T(8,128)(2,1)S(1)}, u32[]{:S(2)}, u32[]{:S(2)}) collective-permute-start(bf16[1,192,896]{2,1,0:T(8,128)(2,1)S(1)} %bitcast.147), channel_id=1, source_target_pairs={{0,16},{8,24},{16,0},{24,8},{1,17},{9,25},{17,1},{25,9},{2,18},{10... | collective-permute-start | bytes 1032200 | tf_op jit(solution)/shard_map/ppermute | solution.py:44
  26.2 7.5 %collective-permute-done.2 = bf16[1,192,896]{2,1,0:T(8,128)(2,1)S(1)} collective-permute-done((bf16[1,192,896]{2,1,0:T(8,128)(2,1)S(1)}, bf16[1,192,896]{2,1,0:T(8,128)(2,1)S(1)}, u32[]{:S(2)}, u32[]{:S(2)}) %collective-permute-start.2) | collective-permute-done | bytes 344096 | tf_op jit(solution)/shard_map/ppermute | solution.py:44
  33.8 1.0 maximum_select_fusion.4
  34.7 1.2 %all-to-all-done = bf16[8,24,1024]{2,1,0:T(8,128)(2,1)S(1)} async-done(((bf16[8,24,1024]{2,1,0:T(8,128)(2,1)}), bf16[8,24,1024]{2,1,0:T(8,128)(2,1)S(1)}, u32[]{:S(2)}, u32[]{:S(2)}) %all-to-all-start) | async-done | bytes 393248 | tf_op jit(solution)/shard_map/all_to_all | solution.py:119
  36.0 1.6 %collective-permute-start = (bf16[1,192,896]{2,1,0:T(8,128)(2,1)S(1)}, bf16[1,192,896]{2,1,0:T(8,128)(2,1)S(1)}, u32[]{:S(2)}, u32[]{:S(2)}) collective-permute-start(bf16[1,192,896]{2,1,0:T(8,128)(2,1)S(1)} %get-tuple-element.33), channel_id=1, source_target_pairs={{0,16},{8,24},{16,0},{24,8},{1,17},{9,25},{17,1},{25,9},{2,18},{10... | collective-permute-start | bytes 1032200 | tf_op jit(solution)/shard_map/ppermute | solution.py:44
  37.9 7.4 %collective-permute-done = bf16[1,192,896]{2,1,0:T(8,128)(2,1)S(1)} collective-permute-done((bf16[1,192,896]{2,1,0:T(8,128)(2,1)S(1)}, bf16[1,192,896]{2,1,0:T(8,128)(2,1)S(1)}, u32[]{:S(2)}, u32[]{:S(2)}) %collective-permute-start) | collective-permute-done | bytes 344096 | tf_op jit(solution)/shard_map/ppermute | solution.py:44
  46.1 1.6 %copy-done.3 = bf16[1,512,3584]{2,1,0:T(8,128)(2,1)S(1)} copy-done((bf16[1,512,3584]{2,1,0:T(8,128)(2,1)S(1)}, bf16[1,512,3584]{2,1,0:T(8,128)(2,1)}, u32[]{:S(2)}) %copy-start.3) | copy-done | bytes 3670040
  49.4 1.3 %copy-done.2 = bf16[1,3584,512]{2,1,0:T(8,128)(2,1)S(1)} copy-done((bf16[1,3584,512]{2,1,0:T(8,128)(2,1)S(1)}, bf16[1,3584,512]{2,1,0:T(8,128)(2,1)}, u32[]{:S(2)}) %copy-start.2) | copy-done | bytes 3670040
  51.6 1.2 %copy-done.1 = bf16[1,3584,512]{2,1,0:T(8,128)(2,1)S(1)} copy-done((bf16[1,3584,512]{2,1,0:T(8,128)(2,1)S(1)}, bf16[1,3584,512]{2,1,0:T(8,128)(2,1)}, u32[]{:S(2)}) %copy-start.1) | copy-done | bytes 3670040
  52.7 0.9 convolution_bitcast_fusion.1
  55.8 1.4 %fusion.28 = f32[192,4,896]{2,0,1:T(8,128)S(1)} fusion(bf16[4,896,512]{2,1,0:T(8,128)(2,1)S(1)} %bitcast.142, bf16[192,512]{1,0:T(8,128)(2,1)S(1)} %get-tuple-element.30), kind=kOutput, calls=%fused_computation.74 | convolution fusion | flops 704643072 | bytes 6619136 | tf_op jit(solution)/shard_map/sf,ndf->nsd/dot_general | solution.py:160
  57.1 1.4 %fusion.3 = bf16[4,192,896]{2,1,0:T(8,128)(2,1)S(1)} fusion(f32[192,4,896]{2,0,1:T(8,128)S(1)} %fusion.28, bf16[192,512,1]{1,0,2:T(8,128)(2,1)S(1)} %get-tuple-element.29, bf16[4,896,512]{2,1,0:T(8,128)(2,1)S(1)} %bitcast.146), kind=kOutput, calls=%fused_computation.10 | convolution fusion | flops 706019328 | bytes 7995392 | tf_op jit(solution)/shard_map/sf,ndf->nsd/dot_general | solution.py:162
  60.1 2.8 %collective-permute-done.4 = bf16[2,192,1792]{2,1,0:T(8,128)(2,1)S(1)} collective-permute-done((bf16[2,192,1792]{2,1,0:T(8,128)(2,1)S(1)}, bf16[2,192,1792]{2,1,0:T(8,128)(2,1)S(1)}, u32[]{:S(2)}, u32[]{:S(2)}) %collective-permute-start.4) | collective-permute-done | bytes 1376288 | tf_op jit(solution)/shard_map/ppermute | solution.py:71
  63.5 1.6 %collective-permute-start.8 = (bf16[1,192,896]{2,1,0:T(8,128)(2,1)S(1)}, bf16[1,192,896]{2,1,0:T(8,128)(2,1)S(1)}, u32[]{:S(2)}, u32[]{:S(2)}) collective-permute-start(bf16[1,192,896]{2,1,0:T(8,128)(2,1)S(1)} %fusion.25), channel_id=1, source_target_pairs={{0,16},{8,24},{16,0},{24,8},{1,17},{9,25},{17,1},{25,9},{2,18},{10... | collective-permute-start | bytes 1032200 | tf_op jit(solution)/shard_map/ppermute | solution.py:81
  65.7 1.1 collective-permute-done.6
  68.1 1.5 %collective-permute-start.5 = (bf16[1,192,896]{2,1,0:T(8,128)(2,1)}, bf16[1,192,896]{2,1,0:T(8,128)(2,1)}, u32[]{:S(2)}, u32[]{:S(2)}) collective-permute-start(bf16[1,192,896]{2,1,0:T(8,128)(2,1)} %fusion.24), channel_id=1, source_target_pairs={{0,16},{8,24},{16,0},{24,8},{1,17},{9,25},{17,1},{25,9},{2,18},{10... | collective-permute-start | bytes 1032200 | tf_op jit(solution)/shard_map/ppermute | solution.py:81
  69.6 4.9 %collective-permute-done.8 = bf16[1,192,896]{2,1,0:T(8,128)(2,1)S(1)} collective-permute-done((bf16[1,192,896]{2,1,0:T(8,128)(2,1)S(1)}, bf16[1,192,896]{2,1,0:T(8,128)(2,1)S(1)}, u32[]{:S(2)}, u32[]{:S(2)}) %collective-permute-start.8) | collective-permute-done | bytes 344096 | tf_op jit(solution)/shard_map/ppermute | solution.py:81
  75.3 5.7 %all-to-all-start.3 = ((bf16[8,24,896]{2,1,0:T(8,128)(2,1)}), bf16[8,24,896]{2,1,0:T(8,128)(2,1)S(1)}, u32[]{:S(2)}, u32[]{:S(2)}) async-start(bf16[8,24,896]{2,1,0:T(8,128)(2,1)} %bitcast.158), calls=%async_computation.3 | async-start | bytes 688128 | tf_op jit(solution)/shard_map/all_to_all | solution.py:119
  82.8 1.1 fusion.21
  83.8 1.7 %maximum_maximum_fusion.1 = bf16[8,24,1024]{2,1,0:T(8,128)(2,1)} fusion(bf16[8,24,1]{2,1,0:T(8,128)(2,1)} %concatenate.68, bf16[8,24,1]{2,1,0:T(8,128)(2,1)} %concatenate.67, bf16[8,24,896]{2,1,0:T(8,128)(2,1)S(1)} %bitcast.157, bf16[1024]{0:T(1024)(128)(2,1)S(1)} %pad.40.clone), kind=kLoop, calls=%fused_computation.58 | loop fusion | flops 1572864 | bytes 740096 | tf_op jit(solution)/shard_map/concatenate | solution.py:95
  85.5 5.3 %all-to-all-done.3 = bf16[8,24,896]{2,1,0:T(8,128)(2,1)S(1)} async-done(((bf16[8,24,896]{2,1,0:T(8,128)(2,1)}), bf16[8,24,896]{2,1,0:T(8,128)(2,1)S(1)}, u32[]{:S(2)}, u32[]{:S(2)}) %all-to-all-start.3) | async-done | bytes 344096 | tf_op jit(solution)/shard_map/all_to_all | solution.py:119
  90.8 3.6 %all-to-all-start.2 = ((bf16[8,24,1024]{2,1,0:T(8,128)(2,1)}), bf16[8,24,1024]{2,1,0:T(8,128)(2,1)S(1)}, u32[]{:S(2)}, u32[]{:S(2)}) async-start(bf16[8,24,1024]{2,1,0:T(8,128)(2,1)} %maximum_maximum_fusion.1), calls=%async_computation.2 | async-start | bytes 786432 | tf_op jit(solution)/shard_map/all_to_all | solution.py:119
  94.5 3.9 %convolution_convert_fusion = bf16[4,896,512]{2,1,0:T(8,128)(2,1)} fusion(bf16[4,192,896]{2,1,0:T(8,128)(2,1)S(1)} %bitcast.133, bf16[192,512,1]{1,0,2:T(8,128)(2,1)} %copy-done.4), kind=kOutput, calls=%fused_computation.8 | convolution fusion | flops 706478080 | bytes 5242880 | tf_op jit(solution)/shard_map/nsd,sf->ndf/dot_general | solution.py:173
  98.4 3.0 %convolution_convert_fusion.1 = bf16[4,896,512]{2,1,0:T(8,128)(2,1)} fusion(bf16[4,192,896]{2,1,0:T(8,128)(2,1)S(1)} %bitcast.134, bf16[192,512]{1,0:T(8,128)(2,1)S(1)} %get-tuple-element.30), kind=kOutput, calls=%fused_computation.9 | convolution fusion | flops 706478080 | bytes 5242880 | tf_op jit(solution)/shard_map/nsd,sf->ndf/dot_general | solution.py:170
  101.4 1.0 convolution_convert_fusion.8
  102.3 3.2 %all-to-all-done.2 = bf16[8,24,1024]{2,1,0:T(8,128)(2,1)S(1)} async-done(((bf16[8,24,1024]{2,1,0:T(8,128)(2,1)}), bf16[8,24,1024]{2,1,0:T(8,128)(2,1)S(1)}, u32[]{:S(2)}, u32[]{:S(2)}) %all-to-all-start.2) | async-done | bytes 393248 | tf_op jit(solution)/shard_map/all_to_all | solution.py:119
  (61 shorter events, 16.8 us)
Async XLA Ops:
  0.6 1.6 %copy-start = (bf16[128,896]{1,0:T(8,128)(2,1)S(1)}, bf16[128,896]{1,0:T(8,128)(2,1)}, u32[]{:S(2)}) copy-start(bf16[128,896]{1,0:T(8,128)(2,1)} %param.8) | copy-start | bytes 688132
  3.2 17.9 %all-to-all-start.1 = ((bf16[8,24,896]{2,1,0:T(8,128)(2,1)}), bf16[8,24,896]{2,1,0:T(8,128)(2,1)S(1)}, u32[]{:S(2)}, u32[]{:S(2)}) async-start(bf16[8,24,896]{2,1,0:T(8,128)(2,1)} %bitcast.23), calls=%async_computation.1 | async-start | bytes 688128 | tf_op jit(solution)/shard_map/all_to_all | solution.py:119
  21.1 14.9 %all-to-all-start = ((bf16[8,24,1024]{2,1,0:T(8,128)(2,1)}), bf16[8,24,1024]{2,1,0:T(8,128)(2,1)S(1)}, u32[]{:S(2)}, u32[]{:S(2)}) async-start(bf16[8,24,1024]{2,1,0:T(8,128)(2,1)} %maximum_maximum_fusion), calls=%async_computation | async-start | bytes 786432 | tf_op jit(solution)/shard_map/all_to_all | solution.py:119
  24.7 9.1 %collective-permute-start.2 = (bf16[1,192,896]{2,1,0:T(8,128)(2,1)S(1)}, bf16[1,192,896]{2,1,0:T(8,128)(2,1)S(1)}, u32[]{:S(2)}, u32[]{:S(2)}) collective-permute-start(bf16[1,192,896]{2,1,0:T(8,128)(2,1)S(1)} %bitcast.147), channel_id=1, source_target_pairs={{0,16},{8,24},{16,0},{24,8},{1,17},{9,25},{17,1},{25,9},{2,18},{10... | collective-permute-start | bytes 1032200 | tf_op jit(solution)/shard_map/ppermute | solution.py:44
  34.7 10.9 %collective-permute-start.3 = (bf16[2,192,896]{2,1,0:T(8,128)(2,1)}, bf16[2,192,896]{2,1,0:T(8,128)(2,1)S(1)}, u32[]{:S(2)}, u32[]{:S(2)}) collective-permute-start(bf16[2,192,896]{2,1,0:T(8,128)(2,1)} %maximum_select_fusion.4), channel_id=1, source_target_pairs={{0,8},{8,0},{16,24},{24,16},{1,9},{9,1},{17,25},{25,17},{2,10},{10... | collective-permute-start | bytes 2064392 | tf_op jit(solution)/shard_map/ppermute | solution.py:44
  36.0 9.3 %collective-permute-start = (bf16[1,192,896]{2,1,0:T(8,128)(2,1)S(1)}, bf16[1,192,896]{2,1,0:T(8,128)(2,1)S(1)}, u32[]{:S(2)}, u32[]{:S(2)}) collective-permute-start(bf16[1,192,896]{2,1,0:T(8,128)(2,1)S(1)} %get-tuple-element.33), channel_id=1, source_target_pairs={{0,16},{8,24},{16,0},{24,8},{1,17},{9,25},{17,1},{25,9},{2,18},{10... | collective-permute-start | bytes 1032200 | tf_op jit(solution)/shard_map/ppermute | solution.py:44
  45.5 3.7 %collective-permute-start.1 = (bf16[2,192,896]{2,1,0:T(8,128)(2,1)S(1)}, bf16[2,192,896]{2,1,0:T(8,128)(2,1)S(1)}, u32[]{:S(2)}, u32[]{:S(2)}) collective-permute-start(bf16[2,192,896]{2,1,0:T(8,128)(2,1)S(1)} %maximum_select_fusion.2), channel_id=1, source_target_pairs={{0,8},{8,0},{16,24},{24,16},{1,9},{9,1},{17,25},{25,17},{2,10},{10... | collective-permute-start | bytes 2064392 | tf_op jit(solution)/shard_map/ppermute | solution.py:44
  45.7 2.0 %copy-start.3 = (bf16[1,512,3584]{2,1,0:T(8,128)(2,1)S(1)}, bf16[1,512,3584]{2,1,0:T(8,128)(2,1)}, u32[]{:S(2)}) copy-start(bf16[1,512,3584]{2,1,0:T(8,128)(2,1)} %param.13) | copy-start | bytes 11010052
  48.7 2.0 %copy-start.2 = (bf16[1,3584,512]{2,1,0:T(8,128)(2,1)S(1)}, bf16[1,3584,512]{2,1,0:T(8,128)(2,1)}, u32[]{:S(2)}) copy-start(bf16[1,3584,512]{2,1,0:T(8,128)(2,1)} %param.12) | copy-start | bytes 11010052
  50.7 2.0 %copy-start.1 = (bf16[1,3584,512]{2,1,0:T(8,128)(2,1)S(1)}, bf16[1,3584,512]{2,1,0:T(8,128)(2,1)}, u32[]{:S(2)}) copy-start(bf16[1,3584,512]{2,1,0:T(8,128)(2,1)} %param.11) | copy-start | bytes 11010052
  54.2 4.3 %copy-start.4 = (bf16[192,512,1]{1,0,2:T(8,128)(2,1)}, bf16[192,512,1]{1,0,2:T(8,128)(2,1)S(1)}, u32[]{:S(2)}) copy-start(bf16[192,512,1]{1,0,2:T(8,128)(2,1)S(1)} %get-tuple-element.29) | copy-start | bytes 589828
  59.5 3.3 %collective-permute-start.4 = (bf16[2,192,1792]{2,1,0:T(8,128)(2,1)S(1)}, bf16[2,192,1792]{2,1,0:T(8,128)(2,1)S(1)}, u32[]{:S(2)}, u32[]{:S(2)}) collective-permute-start(bf16[2,192,1792]{2,1,0:T(8,128)(2,1)S(1)} %fusion.4), channel_id=1, source_target_pairs={{0,8},{8,0},{16,24},{24,16},{1,9},{9,1},{17,25},{25,17},{2,10},{10... | collective-permute-start | bytes 4128776 | tf_op jit(solution)/shard_map/ppermute | solution.py:71
  63.5 11.0 %collective-permute-start.8 = (bf16[1,192,896]{2,1,0:T(8,128)(2,1)S(1)}, bf16[1,192,896]{2,1,0:T(8,128)(2,1)S(1)}, u32[]{:S(2)}, u32[]{:S(2)}) collective-permute-start(bf16[1,192,896]{2,1,0:T(8,128)(2,1)S(1)} %fusion.25), channel_id=1, source_target_pairs={{0,16},{8,24},{16,0},{24,8},{1,17},{9,25},{17,1},{25,9},{2,18},{10... | collective-permute-start | bytes 1032200 | tf_op jit(solution)/shard_map/ppermute | solution.py:81
  65.6 1.2 %collective-permute-start.6 = (f32[192]{0:T(256)S(1)}, f32[192]{0:T(256)S(1)}, u32[]{:S(2)}, u32[]{:S(2)}) collective-permute-start(f32[192]{0:T(256)S(1)} %fusion.2), channel_id=1, source_target_pairs={{0,8},{8,0},{16,24},{24,16},{1,9},{9,1},{17,25},{25,17},{2,10},{10... | collective-permute-start | bytes 2312 | tf_op jit(solution)/shard_map/ppermute | solution.py:88
  66.8 14.3 %collective-permute-start.7 = (f32[192]{0:T(256)S(1)}, f32[192]{0:T(256)S(1)}, u32[]{:S(2)}, u32[]{:S(2)}) collective-permute-start(f32[192]{0:T(256)S(1)} %add.56), channel_id=1, source_target_pairs={{0,16},{8,24},{16,0},{24,8},{1,17},{9,25},{17,1},{25,9},{2,18},{10... | collective-permute-start | bytes 2312 | tf_op jit(solution)/shard_map/ppermute | solution.py:88
  68.1 14.7 %collective-permute-start.5 = (bf16[1,192,896]{2,1,0:T(8,128)(2,1)}, bf16[1,192,896]{2,1,0:T(8,128)(2,1)}, u32[]{:S(2)}, u32[]{:S(2)}) collective-permute-start(bf16[1,192,896]{2,1,0:T(8,128)(2,1)} %fusion.24), channel_id=1, source_target_pairs={{0,16},{8,24},{16,0},{24,8},{1,17},{9,25},{17,1},{25,9},{2,18},{10... | collective-permute-start | bytes 1032200 | tf_op jit(solution)/shard_map/ppermute | solution.py:81
  75.3 15.5 %all-to-all-start.3 = ((bf16[8,24,896]{2,1,0:T(8,128)(2,1)}), bf16[8,24,896]{2,1,0:T(8,128)(2,1)S(1)}, u32[]{:S(2)}, u32[]{:S(2)}) async-start(bf16[8,24,896]{2,1,0:T(8,128)(2,1)} %bitcast.158), calls=%async_computation.3 | async-start | bytes 688128 | tf_op jit(solution)/shard_map/all_to_all | solution.py:119
  90.8 14.7 %all-to-all-start.2 = ((bf16[8,24,1024]{2,1,0:T(8,128)(2,1)}), bf16[8,24,1024]{2,1,0:T(8,128)(2,1)S(1)}, u32[]{:S(2)}, u32[]{:S(2)}) async-start(bf16[8,24,1024]{2,1,0:T(8,128)(2,1)} %maximum_maximum_fusion.1), calls=%async_computation.2 | async-start | bytes 786432 | tf_op jit(solution)/shard_map/all_to_all | solution.py:119
  98.4 7.5 %copy-start.5 = (f32[128,1]{0,1:T(1,128)S(1)}, f32[128,1]{0,1:T(1,128)}, u32[]{:S(2)}) copy-start(f32[128,1]{0,1:T(1,128)} %param.10) | copy-start | bytes 1540

commit v19 on v13

--- a/solution.py
+++ b/solution.py
@@ -40,14 +40,16 @@
 
 def gather_blocks(block, n_ctx, me):
     held = block[None]
+    masks = [0]
     for bit in reversed(range(ctx_bits(n_ctx))):
         other = lax.ppermute(held, "ctx", xor_pairs(n_ctx, bit))
-        mine_first = ((me >> bit) & 1) == 0
-        pair = jnp.where(
-            mine_first, jnp.stack([held, other], axis=1), jnp.stack([other, held], axis=1)
-        )
-        held = pair.reshape((-1,) + block.shape)
-    return held
+        held = jnp.concatenate([held, other], axis=0)
+        masks = masks + [m ^ (1 << bit) for m in masks]
+    slot_of = [0] * n_ctx
+    for j, m in enumerate(masks):
+        slot_of[m] = j
+    order = jnp.asarray(slot_of, jnp.int32)[jnp.arange(n_ctx, dtype=jnp.int32) ^ me]
+    return jnp.take(held, order, axis=0)
 
 
 def scatter_sum(blocks, n_ctx, me):

time: 106 us -> 116 us (1.094)
  other arithmetic: 10.1 us -> 16.6 us
  matrix products: 17.2 us -> 21.2 us
  waiting for transfers between devices: 41.7 us -> 37.9 us
  local copies, waits for them, and re-layouts: 7.04 us -> 10.5 us
    ppermute x4, waiting for transfers between devices: 15 us -> 5.11 us  [gather_blocks(): other = lax.ppermute(held, 'ctx', xor_pairs(n_ctx, bit))]
    all_to_all x4, waiting for transfers between devices: 17.1 us -> 24.4 us  [to_experts(): got = lax.all_to_all(sent, 'ep', split_axis=0, concat_axis=0, tiled=True)]
    concatenate x0 -> x4, other arithmetic: none -> 3.65 us  [gather_blocks(): held = jnp.concatenate([held, other], axis=0)]
    gather x0 -> x3, local copies, waits for them, and re-layouts: none -> 3.2 us  [the longest x2 2.56 us: gather_blocks(): return jnp.take(held, order, axis=0)]
    dot_general x1, matrix products: 0.87 us -> 3.52 us  [shards(): jnp.einsum('nsd,ndf->sf', rows_in, gate_w, preferred_element_type=jnp.flo...]
    reshape x2, other arithmetic: 0.34 us -> 2.75 us  [scatter_sum(): halves = acc.reshape((-1, 2) + acc.shape[1:])]
    select_n x6 -> x2, other arithmetic: 1.87 us -> 0.01 us  [the longest x1 0.01 us: gather_blocks(): jnp.asarray(slot_of, jnp.int32)[jnp.arange(n_ctx, dtype=jnp.int32) ^ me]]
    convert_element_type x4, other arithmetic: 1.15 us -> 2.85 us  [scatter_sum(): jnp.where(keep_first, halves[:, 1], halves[:, 0]).astype(jnp.bfloat16)]
  transfers between devices with their start and end apart: 14 -> 14, of which waited for: 8 -> 8; matrix products, arithmetic and copies ran while one was open for 18% -> 21% of each run, Pallas kernels for 0% -> 0%
where the time goes in v19:
time: 116 us; the launch traced here: 115 us
  waiting for transfers between devices  37.9 us (33%)
  starting transfers between devices  27.7 us (24%)
  matrix products  21.2 us (18%)
  other arithmetic  16.6 us (14%)
  local copies, waits for them, and re-layouts  10.5 us (9%)
    all_to_all x4, waiting for transfers between devices, to_experts(): got = lax.all_to_all(sent, 'ep', split_axis=0, concat_axis=0, tiled=True)  24.4 us
    all_to_all x4, starting transfers between devices, to_experts(): got = lax.all_to_all(sent, 'ep', split_axis=0, concat_axis=0, tiled=True)  20.1 us
    ppermute x4, waiting for transfers between devices, scatter_sum(): got = lax.ppermute(send, 'ctx', xor_pairs(n_ctx, bit))  6.78 us
    unnamed x31, local copies, waits for them, and re-layouts  5.17 us
    ppermute x4, waiting for transfers between devices, gather_blocks(): other = lax.ppermute(held, 'ctx', xor_pairs(n_ctx, bit))  5.11 us
    dot_general x1, matrix products, shards(): jnp.einsum('nsd,sf->ndf', rows_in, grad_up, preferred_element_type=jnp.fl...  4.09 us
    concatenate x4, other arithmetic, gather_blocks(): held = jnp.concatenate([held, other], axis=0)  3.65 us
    dot_general x1, matrix products, shards(): jnp.einsum('nsd,ndf->sf', rows_in, gate_w, preferred_element_type=jnp.flo...  3.52 us
  transfers between devices with their start and end apart: 14, of which 8 were waited for; matrix products, arithmetic and copies ran while one was open for 21% of the time, Pallas kernels for 0%

profile of v19, /device:TPU:0, one launch (start us, length us, event | category | flops | bytes accessed | tf_op | source)
XLA Modules:
  0.0 115.0 jit_solution(7218255082982144651)
XLA Ops:
  2.2 1.0 convolution_convert_fusion.2
  3.2 7.3 %all-to-all-start.1 = ((bf16[8,24,896]{2,1,0:T(8,128)(2,1)}), bf16[8,24,896]{2,1,0:T(8,128)(2,1)S(1)}, u32[]{:S(2)}, u32[]{:S(2)}) async-start(bf16[8,24,896]{2,1,0:T(8,128)(2,1)} %bitcast.30), calls=%async_computation.1 | async-start | bytes 688128 | tf_op jit(solution)/shard_map/all_to_all | solution.py:100
  12.8 8.3 %all-to-all-done.1 = bf16[8,24,896]{2,1,0:T(8,128)(2,1)S(1)} async-done(((bf16[8,24,896]{2,1,0:T(8,128)(2,1)}), bf16[8,24,896]{2,1,0:T(8,128)(2,1)S(1)}, u32[]{:S(2)}, u32[]{:S(2)}) %all-to-all-start.1) | async-done | bytes 344096 | tf_op jit(solution)/shard_map/all_to_all | solution.py:100
  21.1 3.6 %all-to-all-start = ((bf16[8,24,1024]{2,1,0:T(8,128)(2,1)}), bf16[8,24,1024]{2,1,0:T(8,128)(2,1)S(1)}, u32[]{:S(2)}, u32[]{:S(2)}) async-start(bf16[8,24,1024]{2,1,0:T(8,128)(2,1)} %maximum_maximum_fusion), calls=%async_computation | async-start | bytes 786432 | tf_op jit(solution)/shard_map/all_to_all | solution.py:100
  24.7 1.5 %collective-permute-start.4 = (bf16[1,192,896]{2,1,0:T(8,128)(2,1)S(1)}, bf16[1,192,896]{2,1,0:T(8,128)(2,1)S(1)}, u32[]{:S(2)}, u32[]{:S(2)}) collective-permute-start(bf16[1,192,896]{2,1,0:T(8,128)(2,1)S(1)} %bitcast.150), channel_id=1, source_target_pairs={{0,16},{8,24},{16,0},{24,8},{1,17},{9,25},{17,1},{25,9},{2,18},{10... | collective-permute-start | bytes 1032200 | tf_op jit(solution)/shard_map/ppermute | solution.py:45
  26.2 9.7 %all-to-all-done = bf16[8,24,1024]{2,1,0:T(8,128)(2,1)S(1)} async-done(((bf16[8,24,1024]{2,1,0:T(8,128)(2,1)}), bf16[8,24,1024]{2,1,0:T(8,128)(2,1)S(1)}, u32[]{:S(2)}, u32[]{:S(2)}) %all-to-all-start) | async-done | bytes 393248 | tf_op jit(solution)/shard_map/all_to_all | solution.py:100
  36.0 1.6 %collective-permute-start = (bf16[1,192,896]{2,1,0:T(8,128)(2,1)S(1)}, bf16[1,192,896]{2,1,0:T(8,128)(2,1)S(1)}, u32[]{:S(2)}, u32[]{:S(2)}) collective-permute-start(bf16[1,192,896]{2,1,0:T(8,128)(2,1)S(1)} %slice_bitcast_fusion.10), channel_id=1, source_target_pairs={{0,16},{8,24},{16,0},{24,8},{1,17},{9,25},{17,1},{25,9},{2,18},{10... | collective-permute-start | bytes 1032200 | tf_op jit(solution)/shard_map/ppermute | solution.py:45
  38.4 4.9 %collective-permute-done = bf16[1,192,896]{2,1,0:T(8,128)(2,1)S(1)} collective-permute-done((bf16[1,192,896]{2,1,0:T(8,128)(2,1)S(1)}, bf16[1,192,896]{2,1,0:T(8,128)(2,1)S(1)}, u32[]{:S(2)}, u32[]{:S(2)}) %collective-permute-start) | collective-permute-done | bytes 344096 | tf_op jit(solution)/shard_map/ppermute | solution.py:45
  44.5 1.3 %pad_maximum_fusion.1 = bf16[4,192,896]{2,1,0:T(8,128)(2,1)S(1)} fusion(bf16[2,192,896]{2,1,0:T(8,128)(2,1)} %collective-permute-done.5, bf16[1,192,896]{2,1,0:T(8,128)(2,1)S(1)} %collective-permute-done.4, bf16[1,192,896]{2,1,0:T(8,128)(2,1)S(1)} %bitcast.152), kind=kLoop, calls=%fused_computation.13 | loop fusion | flops 1376256 | bytes 2752512 | tf_op jit(solution)/shard_map/concatenate | solution.py:46
  46.8 1.4 %pad_maximum_fusion = bf16[4,192,896]{2,1,0:T(8,128)(2,1)S(1)} fusion(bf16[2,192,896]{2,1,0:T(8,128)(2,1)} %collective-permute-done.1, bf16[1,192,896]{2,1,0:T(8,128)(2,1)} %copy-done.8, bf16[1,192,896]{2,1,0:T(8,128)(2,1)S(1)} %slice_bitcast_fusion.10), kind=kLoop, calls=%fused_computation.12 | loop fusion | flops 1376256 | bytes 2752512 | tf_op jit(solution)/shard_map/concatenate | solution.py:46
  48.1 1.8 %gather_fusion.1 = bf16[4,192,896]{2,1,0:T(8,128)(2,1)} fusion(bf16[4,192,896]{2,1,0:T(8,128)(2,1)S(1)} %pad_maximum_fusion, s32[1024]{0:T(1024)S(1)} %pad_clamp_fusion), kind=kCustom, calls=%fused_computation.clone | custom fusion | bytes 2752528 | tf_op jit(solution)/shard_map/jit(_take)/gather | solution.py:52
  49.9 3.5 %convolution_bitcast_fusion.5 = f32[192,512]{1,0:T(8,128)S(1)} fusion(bf16[4,896,512]{2,1,0:T(8,128)(2,1)} %bitcast.146, bf16[4,192,896]{2,1,0:T(8,128)(2,1)} %gather_fusion.1, pred[4]{0:T(512)(128)(4,1)S(1)} %compare_and_fusion), kind=kOutput, calls=%fused_computation.34 | convolution fusion | flops 705331200 | bytes 5439492 | tf_op jit(solution)/shard_map/nsd,ndf->sf/dot_general | solution.py:118
  54.8 1.1 copy-done.9
  60.3 1.5 %copy-done.4 = bf16[1,3584,512]{2,1,0:T(8,128)(2,1)S(1)} copy-done((bf16[1,3584,512]{2,1,0:T(8,128)(2,1)S(1)}, bf16[1,3584,512]{2,1,0:T(8,128)(2,1)}, u32[]{:S(2)}) %copy-start.4) | copy-done | bytes 3670040
  61.9 1.3 %fusion.27 = f32[192,4,896]{2,0,1:T(8,128)S(1)} fusion(bf16[4,896,512]{2,1,0:T(8,128)(2,1)S(1)} %bitcast.147, bf16[192,512]{1,0:T(8,128)(2,1)S(1)} %get-tuple-element.32), kind=kOutput, calls=%fused_computation.76 | convolution fusion | flops 704643072 | bytes 6619136 | tf_op jit(solution)/shard_map/sf,ndf->nsd/dot_general | solution.py:143
  63.2 1.4 %fusion.1 = f32[192,4,896]{2,0,1:T(8,128)S(1)} fusion(f32[192,4,896]{2,0,1:T(8,128)S(1)} %fusion.27, bf16[192,512,1]{1,0,2:T(8,128)(2,1)S(1)} %get-tuple-element.31, bf16[4,896,512]{2,1,0:T(8,128)(2,1)S(1)} %bitcast.149), kind=kOutput, calls=%fused_computation.9 | convolution fusion | flops 706707456 | bytes 9371648 | tf_op jit(solution)/shard_map/sf,ndf->nsd/dot_general | solution.py:145
  64.6 1.0 fusion.18
  66.1 1.5 %copy-done.2 = f32[2,2,192,896]{3,2,1,0:T(8,128)} copy-done((f32[2,2,192,896]{3,2,1,0:T(8,128)}, f32[2,2,192,896]{3,2,1,0:T(8,128)S(1)}, u32[]{:S(2)}) %copy-start.2) | copy-done | bytes 2752536
  67.6 1.0 fusion.17
  69.1 1.6 %collective-permute-done.6 = f32[192]{0:T(256)S(1)} collective-permute-done((f32[192]{0:T(256)S(1)}, f32[192]{0:T(256)S(1)}, u32[]{:S(2)}, u32[]{:S(2)}) %collective-permute-start.6) | collective-permute-done | bytes 800 | tf_op jit(solution)/shard_map/ppermute | solution.py:69
  70.7 1.5 %collective-permute-start.7 = (f32[192]{0:T(256)S(1)}, f32[192]{0:T(256)S(1)}, u32[]{:S(2)}, u32[]{:S(2)}) collective-permute-start(f32[192]{0:T(256)S(1)} %add.68), channel_id=1, source_target_pairs={{0,16},{8,24},{16,0},{24,8},{1,17},{9,25},{17,1},{25,9},{2,18},{10... | collective-permute-start | bytes 2312 | tf_op jit(solution)/shard_map/ppermute | solution.py:69
  72.2 1.4 %fusion.5 = f32[1,2,192,896]{3,2,1,0:T(8,128)S(1)} fusion(bf16[2,192,896]{2,1,0:T(8,128)(2,1)} %collective-permute-done.8, f32[2,2,192,896]{3,2,1,0:T(8,128)S(1)} %bitcast.144, pred[]{:T(512)S(6)} %eq.47), kind=kLoop, calls=%fused_computation.19 | loop fusion | flops 1032192 | bytes 4816897 | tf_op jit(solution)/shard_map/reshape | solution.py:58
  74.3 1.3 %fusion.4 = f32[1,2,192,896]{3,2,1,0:T(8,128)S(1)} fusion(bf16[2,192,896]{2,1,0:T(8,128)(2,1)} %collective-permute-done.2, f32[2,2,192,896]{3,2,1,0:T(8,128)S(1)} %copy-done.3, pred[]{:T(512)S(6)} %eq.47), kind=kLoop, calls=%fused_computation.17 | loop fusion | flops 1032192 | bytes 4816897 | tf_op jit(solution)/shard_map/reshape | solution.py:58
  76.5 1.5 %collective-permute-start.3 = (bf16[1,192,896]{2,1,0:T(8,128)(2,1)}, bf16[1,192,896]{2,1,0:T(8,128)(2,1)}, u32[]{:S(2)}, u32[]{:S(2)}) collective-permute-start(bf16[1,192,896]{2,1,0:T(8,128)(2,1)} %fusion.23), channel_id=1, source_target_pairs={{0,16},{8,24},{16,0},{24,8},{1,17},{9,25},{17,1},{25,9},{2,18},{10... | collective-permute-start | bytes 1032200 | tf_op jit(solution)/shard_map/ppermute | solution.py:62
  78.0 6.8 %collective-permute-done.9 = bf16[1,192,896]{2,1,0:T(8,128)(2,1)S(1)} collective-permute-done((bf16[1,192,896]{2,1,0:T(8,128)(2,1)S(1)}, bf16[1,192,896]{2,1,0:T(8,128)(2,1)S(1)}, u32[]{:S(2)}, u32[]{:S(2)}) %collective-permute-start.9) | collective-permute-done | bytes 344096 | tf_op jit(solution)/shard_map/ppermute | solution.py:62
  85.6 5.6 %all-to-all-start.3 = ((bf16[8,24,896]{2,1,0:T(8,128)(2,1)}), bf16[8,24,896]{2,1,0:T(8,128)(2,1)S(1)}, u32[]{:S(2)}, u32[]{:S(2)}) async-start(bf16[8,24,896]{2,1,0:T(8,128)(2,1)} %bitcast.47), calls=%async_computation.3 | async-start | bytes 688128 | tf_op jit(solution)/shard_map/all_to_all | solution.py:100
  93.0 1.2 %fusion.20 = bf16[1,192,896]{2,1,0:T(8,128)(2,1)S(1)} fusion(bf16[1,192,896]{2,1,0:T(8,128)(2,1)} %collective-permute-done.3, f32[1,2,192,896]{3,2,1,0:T(8,128)S(1)} %fusion.4, pred[]{:T(512)S(6)} %eq.46), kind=kLoop, calls=%fused_computation.55 | loop fusion | flops 688128 | bytes 2064385 | tf_op jit(solution)/shard_map/convert_element_type | solution.py:129
  95.0 5.1 %all-to-all-done.3 = bf16[8,24,896]{2,1,0:T(8,128)(2,1)S(1)} async-done(((bf16[8,24,896]{2,1,0:T(8,128)(2,1)}), bf16[8,24,896]{2,1,0:T(8,128)(2,1)S(1)}, u32[]{:S(2)}, u32[]{:S(2)}) %all-to-all-start.3) | async-done | bytes 344096 | tf_op jit(solution)/shard_map/all_to_all | solution.py:100
  100.1 3.6 %all-to-all-start.2 = ((bf16[8,24,1024]{2,1,0:T(8,128)(2,1)}), bf16[8,24,1024]{2,1,0:T(8,128)(2,1)S(1)}, u32[]{:S(2)}, u32[]{:S(2)}) async-start(bf16[8,24,1024]{2,1,0:T(8,128)(2,1)} %maximum_maximum_fusion.1), calls=%async_computation.2 | async-start | bytes 786432 | tf_op jit(solution)/shard_map/all_to_all | solution.py:100
  103.7 4.1 %convolution_convert_fusion = bf16[4,896,512]{2,1,0:T(8,128)(2,1)} fusion(bf16[192,512,1]{1,0,2:T(8,128)(2,1)} %copy-done.13, bf16[4,192,896]{2,1,0:T(8,128)(2,1)S(1)} %copy-done.7, pred[4]{0:T(512)(128)(4,1)S(1)} %compare_and_fusion), kind=kOutput, calls=%fused_computation.7 | convolution fusion | flops 707166208 | bytes 5242884 | tf_op jit(solution)/shard_map/nsd,sf->ndf/dot_general | solution.py:153
  107.8 3.2 %convolution_convert_fusion.1 = bf16[4,896,512]{2,1,0:T(8,128)(2,1)} fusion(bf16[192,512]{1,0:T(8,128)(2,1)S(1)} %get-tuple-element.32, bf16[4,192,896]{2,1,0:T(8,128)(2,1)S(1)} %copy-done.7, pred[4]{0:T(512)(128)(4,1)S(1)} %compare_and_fusion), kind=kOutput, calls=%fused_computation.8 | convolution fusion | flops 707166208 | bytes 5242884 | tf_op jit(solution)/shard_map/nsd,sf->ndf/dot_general | solution.py:150
  111.9 1.3 %all-to-all-done.2 = bf16[8,24,1024]{2,1,0:T(8,128)(2,1)S(1)} async-done(((bf16[8,24,1024]{2,1,0:T(8,128)(2,1)}), bf16[8,24,1024]{2,1,0:T(8,128)(2,1)S(1)}, u32[]{:S(2)}, u32[]{:S(2)}) %all-to-all-start.2) | async-done | bytes 393248 | tf_op jit(solution)/shard_map/all_to_all | solution.py:100
  (86 shorter events, 21.2 us)
Async XLA Ops:
  0.6 1.6 %copy-start = (bf16[128,896]{1,0:T(8,128)(2,1)S(1)}, bf16[128,896]{1,0:T(8,128)(2,1)}, u32[]{:S(2)}) copy-start(bf16[128,896]{1,0:T(8,128)(2,1)} %param.12) | copy-start | bytes 688132
  0.6 11.0 %copy-start.10 = (bf16[128,896]{1,0:T(8,128)(2,1)S(1)}, bf16[128,896]{1,0:T(8,128)(2,1)}, u32[]{:S(2)}) copy-start(bf16[128,896]{1,0:T(8,128)(2,1)} %param.11) | copy-start | bytes 688132
  3.2 17.9 %all-to-all-start.1 = ((bf16[8,24,896]{2,1,0:T(8,128)(2,1)}), bf16[8,24,896]{2,1,0:T(8,128)(2,1)S(1)}, u32[]{:S(2)}, u32[]{:S(2)}) async-start(bf16[8,24,896]{2,1,0:T(8,128)(2,1)} %bitcast.30), calls=%async_computation.1 | async-start | bytes 688128 | tf_op jit(solution)/shard_map/all_to_all | solution.py:100
  11.7 25.9 %copy-start.1 = (s32[4]{0:T(128)S(1)}, s32[4]{0:T(128)}, u32[]{:S(2)}) copy-start(s32[4]{0:T(128)} %constant.11.clone) | copy-start | bytes 52
  21.1 14.9 %all-to-all-start = ((bf16[8,24,1024]{2,1,0:T(8,128)(2,1)}), bf16[8,24,1024]{2,1,0:T(8,128)(2,1)S(1)}, u32[]{:S(2)}, u32[]{:S(2)}) async-start(bf16[8,24,1024]{2,1,0:T(8,128)(2,1)} %maximum_maximum_fusion), calls=%async_computation | async-start | bytes 786432 | tf_op jit(solution)/shard_map/all_to_all | solution.py:100
  24.7 13.5 %collective-permute-start.4 = (bf16[1,192,896]{2,1,0:T(8,128)(2,1)S(1)}, bf16[1,192,896]{2,1,0:T(8,128)(2,1)S(1)}, u32[]{:S(2)}, u32[]{:S(2)}) collective-permute-start(bf16[1,192,896]{2,1,0:T(8,128)(2,1)S(1)} %bitcast.150), channel_id=1, source_target_pairs={{0,16},{8,24},{16,0},{24,8},{1,17},{9,25},{17,1},{25,9},{2,18},{10... | collective-permute-start | bytes 1032200 | tf_op jit(solution)/shard_map/ppermute | solution.py:45
  36.0 7.3 %collective-permute-start = (bf16[1,192,896]{2,1,0:T(8,128)(2,1)S(1)}, bf16[1,192,896]{2,1,0:T(8,128)(2,1)S(1)}, u32[]{:S(2)}, u32[]{:S(2)}) collective-permute-start(bf16[1,192,896]{2,1,0:T(8,128)(2,1)S(1)} %slice_bitcast_fusion.10), channel_id=1, source_target_pairs={{0,16},{8,24},{16,0},{24,8},{1,17},{9,25},{17,1},{25,9},{2,18},{10... | collective-permute-start | bytes 1032200 | tf_op jit(solution)/shard_map/ppermute | solution.py:45
  38.3 6.2 %collective-permute-start.5 = (bf16[2,192,896]{2,1,0:T(8,128)(2,1)S(1)}, bf16[2,192,896]{2,1,0:T(8,128)(2,1)}, u32[]{:S(2)}, u32[]{:S(2)}) collective-permute-start(bf16[2,192,896]{2,1,0:T(8,128)(2,1)S(1)} %pad_maximum_fusion.3), channel_id=1, source_target_pairs={{0,8},{8,0},{16,24},{24,16},{1,9},{9,1},{17,25},{25,17},{2,10},{10... | collective-permute-start | bytes 2064392 | tf_op jit(solution)/shard_map/ppermute | solution.py:45
  43.3 1.2 %copy-start.8 = (bf16[1,192,896]{2,1,0:T(8,128)(2,1)}, bf16[1,192,896]{2,1,0:T(8,128)(2,1)S(1)}, u32[]{:S(2)}) copy-start(bf16[1,192,896]{2,1,0:T(8,128)(2,1)S(1)} %collective-permute-done) | copy-start | bytes 1032196
  44.3 2.5 %collective-permute-start.1 = (bf16[2,192,896]{2,1,0:T(8,128)(2,1)}, bf16[2,192,896]{2,1,0:T(8,128)(2,1)}, u32[]{:S(2)}, u32[]{:S(2)}) collective-permute-start(bf16[2,192,896]{2,1,0:T(8,128)(2,1)} %pad_maximum_fusion.2), channel_id=1, source_target_pairs={{0,8},{8,0},{16,24},{24,16},{1,9},{9,1},{17,25},{25,17},{2,10},{10... | collective-permute-start | bytes 2064392 | tf_op jit(solution)/shard_map/ppermute | solution.py:45
  49.9 3.5 %copy-start.5 = (bf16[1,3584,512]{2,1,0:T(8,128)(2,1)S(1)}, bf16[1,3584,512]{2,1,0:T(8,128)(2,1)}, u32[]{:S(2)}) copy-start(bf16[1,3584,512]{2,1,0:T(8,128)(2,1)} %param.16) | copy-start | bytes 11010052
  49.9 3.9 %copy-start.6 = (bf16[4,192,896]{2,1,0:T(8,128)(2,1)S(1)}, bf16[4,192,896]{2,1,0:T(8,128)(2,1)}, u32[]{:S(2)}) copy-start(bf16[4,192,896]{2,1,0:T(8,128)(2,1)} %gather_fusion.1) | copy-start | bytes 4128772
  53.9 2.0 %copy-start.9 = (bf16[1,512,3584]{2,1,0:T(8,128)(2,1)S(1)}, bf16[1,512,3584]{2,1,0:T(8,128)(2,1)}, u32[]{:S(2)}) copy-start(bf16[1,512,3584]{2,1,0:T(8,128)(2,1)} %param.17) | copy-start | bytes 11010052
  59.8 2.1 %copy-start.4 = (bf16[1,3584,512]{2,1,0:T(8,128)(2,1)S(1)}, bf16[1,3584,512]{2,1,0:T(8,128)(2,1)}, u32[]{:S(2)}) copy-start(bf16[1,3584,512]{2,1,0:T(8,128)(2,1)} %param.15) | copy-start | bytes 11010052
  60.3 4.2 %copy-start.13 = (bf16[192,512,1]{1,0,2:T(8,128)(2,1)}, bf16[192,512,1]{1,0,2:T(8,128)(2,1)S(1)}, u32[]{:S(2)}) copy-start(bf16[192,512,1]{1,0,2:T(8,128)(2,1)S(1)} %get-tuple-element.31) | copy-start | bytes 589828
  65.6 6.7 %collective-permute-start.8 = (bf16[2,192,896]{2,1,0:T(8,128)(2,1)}, bf16[2,192,896]{2,1,0:T(8,128)(2,1)}, u32[]{:S(2)}, u32[]{:S(2)}) collective-permute-start(bf16[2,192,896]{2,1,0:T(8,128)(2,1)} %fusion.18), channel_id=1, source_target_pairs={{0,8},{8,0},{16,24},{24,16},{1,9},{9,1},{17,25},{25,17},{2,10},{10... | collective-permute-start | bytes 2064392 | tf_op jit(solution)/shard_map/ppermute | solution.py:62
  66.1 1.5 %copy-start.2 = (f32[2,2,192,896]{3,2,1,0:T(8,128)}, f32[2,2,192,896]{3,2,1,0:T(8,128)S(1)}, u32[]{:S(2)}) copy-start(f32[2,2,192,896]{3,2,1,0:T(8,128)S(1)} %convert.5) | copy-start | bytes 8257540
  68.6 5.7 %collective-permute-start.2 = (bf16[2,192,896]{2,1,0:T(8,128)(2,1)}, bf16[2,192,896]{2,1,0:T(8,128)(2,1)}, u32[]{:S(2)}, u32[]{:S(2)}) collective-permute-start(bf16[2,192,896]{2,1,0:T(8,128)(2,1)} %fusion.17), channel_id=1, source_target_pairs={{0,8},{8,0},{16,24},{24,16},{1,9},{9,1},{17,25},{25,17},{2,10},{10... | collective-permute-start | bytes 2064392 | tf_op jit(solution)/shard_map/ppermute | solution.py:62
  68.8 1.9 %collective-permute-start.6 = (f32[192]{0:T(256)S(1)}, f32[192]{0:T(256)S(1)}, u32[]{:S(2)}, u32[]{:S(2)}) collective-permute-start(f32[192]{0:T(256)S(1)} %get-tuple-element.26), channel_id=1, source_target_pairs={{0,8},{8,0},{16,24},{24,16},{1,9},{9,1},{17,25},{25,17},{2,10},{10... | collective-permute-start | bytes 2312 | tf_op jit(solution)/shard_map/ppermute | solution.py:69
  70.7 20.5 %collective-permute-start.7 = (f32[192]{0:T(256)S(1)}, f32[192]{0:T(256)S(1)}, u32[]{:S(2)}, u32[]{:S(2)}) collective-permute-start(f32[192]{0:T(256)S(1)} %add.68), channel_id=1, source_target_pairs={{0,16},{8,24},{16,0},{24,8},{1,17},{9,25},{17,1},{25,9},{2,18},{10... | collective-permute-start | bytes 2312 | tf_op jit(solution)/shard_map/ppermute | solution.py:69
  72.2 2.1 %copy-start.3 = (f32[2,2,192,896]{3,2,1,0:T(8,128)S(1)}, f32[2,2,192,896]{3,2,1,0:T(8,128)}, u32[]{:S(2)}) copy-start(f32[2,2,192,896]{3,2,1,0:T(8,128)} %copy-done.2) | copy-start | bytes 8257540
  73.7 11.0 %collective-permute-start.9 = (bf16[1,192,896]{2,1,0:T(8,128)(2,1)S(1)}, bf16[1,192,896]{2,1,0:T(8,128)(2,1)S(1)}, u32[]{:S(2)}, u32[]{:S(2)}) collective-permute-start(bf16[1,192,896]{2,1,0:T(8,128)(2,1)S(1)} %fusion.24), channel_id=1, source_target_pairs={{0,16},{8,24},{16,0},{24,8},{1,17},{9,25},{17,1},{25,9},{2,18},{10... | collective-permute-start | bytes 1032200 | tf_op jit(solution)/shard_map/ppermute | solution.py:62
  76.5 16.5 %collective-permute-start.3 = (bf16[1,192,896]{2,1,0:T(8,128)(2,1)}, bf16[1,192,896]{2,1,0:T(8,128)(2,1)}, u32[]{:S(2)}, u32[]{:S(2)}) collective-permute-start(bf16[1,192,896]{2,1,0:T(8,128)(2,1)} %fusion.23), channel_id=1, source_target_pairs={{0,16},{8,24},{16,0},{24,8},{1,17},{9,25},{17,1},{25,9},{2,18},{10... | collective-permute-start | bytes 1032200 | tf_op jit(solution)/shard_map/ppermute | solution.py:62
  85.6 14.5 %all-to-all-start.3 = ((bf16[8,24,896]{2,1,0:T(8,128)(2,1)}), bf16[8,24,896]{2,1,0:T(8,128)(2,1)S(1)}, u32[]{:S(2)}, u32[]{:S(2)}) async-start(bf16[8,24,896]{2,1,0:T(8,128)(2,1)} %bitcast.47), calls=%async_computation.3 | async-start | bytes 688128 | tf_op jit(solution)/shard_map/all_to_all | solution.py:100
  92.9 1.2 %copy-start.11 = (bf16[8,24,1]{2,1,0:T(8,128)(2,1)S(1)}, bf16[8,24,1]{2,1,0:T(8,128)(2,1)}, u32[]{:S(2)}) copy-start(bf16[8,24,1]{2,1,0:T(8,128)(2,1)} %concatenate.40) | copy-start | bytes 1156
  92.9 1.2 %copy-start.12 = (bf16[8,24,1]{2,1,0:T(8,128)(2,1)S(1)}, bf16[8,24,1]{2,1,0:T(8,128)(2,1)}, u32[]{:S(2)}) copy-start(bf16[8,24,1]{2,1,0:T(8,128)(2,1)} %concatenate.41) | copy-start | bytes 1156
  92.9 10.8 %copy-start.7 = (bf16[4,192,896]{2,1,0:T(8,128)(2,1)S(1)}, bf16[4,192,896]{2,1,0:T(8,128)(2,1)}, u32[]{:S(2)}) copy-start(bf16[4,192,896]{2,1,0:T(8,128)(2,1)} %gather_fusion.1) | copy-start | bytes 4128772
  100.1 13.1 %all-to-all-start.2 = ((bf16[8,24,1024]{2,1,0:T(8,128)(2,1)}), bf16[8,24,1024]{2,1,0:T(8,128)(2,1)S(1)}, u32[]{:S(2)}, u32[]{:S(2)}) async-start(bf16[8,24,1024]{2,1,0:T(8,128)(2,1)} %maximum_maximum_fusion.1), calls=%async_computation.2 | async-start | bytes 786432 | tf_op jit(solution)/shard_map/all_to_all | solution.py:100
  111.0 2.6 %copy-start.14 = (f32[128,1]{0,1:T(1,128)S(1)}, f32[128,1]{0,1:T(1,128)}, u32[]{:S(2)}) copy-start(f32[128,1]{0,1:T(1,128)} %param.14) | copy-start | bytes 1540

commit v20 on v13

--- a/solution.py
+++ b/solution.py
@@ -58,7 +58,7 @@
         keep = jnp.where(keep_first, halves[:, 0], halves[:, 1])
         send = jnp.where(keep_first, halves[:, 1], halves[:, 0]).astype(jnp.bfloat16)
         got = lax.ppermute(send, "ctx", xor_pairs(n_ctx, bit))
-        acc = keep + got.astype(jnp.float32)
+        acc = keep.astype(jnp.float32) + got.astype(jnp.float32)
     return acc[0]
 
 
@@ -124,7 +124,7 @@
     gate_part = jnp.einsum(
         "nsd,nsd->s", partial_out.astype(jnp.float32), grads_in.astype(jnp.float32)
     )
-    expert_out = scatter_sum(partial_out.astype(jnp.float32), n_ctx, me).astype(jnp.bfloat16)
+    expert_out = scatter_sum(partial_out, n_ctx, me).astype(jnp.bfloat16)
     gate_sum = all_sum(gate_part, n_ctx)
     back_out = to_experts(with_cols(expert_out, gate_sum, pad))
 
@@ -141,7 +141,7 @@
     back_terms = jnp.einsum(
         "sf,ndf->nsd", grad_gate, gate_w, preferred_element_type=jnp.float32
     ) + jnp.einsum("sf,ndf->nsd", grad_up, up_w, preferred_element_type=jnp.float32)
-    back_terms = back_terms.astype(jnp.bfloat16).astype(jnp.float32)
+    back_terms = back_terms.astype(jnp.bfloat16)
     slot_grad = scatter_sum(back_terms, n_ctx, me).astype(jnp.bfloat16)
     back_grad = to_experts(slot_grad)
 

time: 106 us -> 107 us (level)
  waiting for transfers between devices: 41.7 us -> 43.3 us
    all_to_all x4, waiting for transfers between devices: 17.1 us -> 18.8 us  [to_experts(): got = lax.all_to_all(sent, 'ep', split_axis=0, concat_axis=0, tiled=True)]
where the time goes in v20:
time: 107 us
  waiting for transfers between devices  43.3 us (40%)
  starting transfers between devices  28.1 us (26%)
  matrix products  17.3 us (16%)
  other arithmetic  9.97 us (9%)
  local copies, waits for them, and re-layouts  7.04 us (7%)
    all_to_all x4, starting transfers between devices, to_experts(): got = lax.all_to_all(sent, 'ep', split_axis=0, concat_axis=0, tiled=True)  20.2 us
    all_to_all x4, waiting for transfers between devices, to_experts(): got = lax.all_to_all(sent, 'ep', split_axis=0, concat_axis=0, tiled=True)  18.8 us
    ppermute x4, waiting for transfers between devices, gather_blocks(): other = lax.ppermute(held, 'ctx', xor_pairs(n_ctx, bit))  15 us
    ppermute x4, waiting for transfers between devices, scatter_sum(): got = lax.ppermute(send, 'ctx', xor_pairs(n_ctx, bit))  7.83 us
    unnamed x21, local copies, waits for them, and re-layouts  4.71 us
    ppermute x4, starting transfers between devices, gather_blocks(): other = lax.ppermute(held, 'ctx', xor_pairs(n_ctx, bit))  3.18 us
    dot_general x1, matrix products, shards(): jnp.einsum('nsd,sf->ndf', rows_in, grad_up, preferred_element_type=jnp.fl...  3 us
    dot_general x1, matrix products, shards(): jnp.einsum('nsd,sf->ndf', rows_in, grad_gate, preferred_element_type=jnp....  3 us
  transfers between devices with their start and end apart: 14, of which 8 were waited for; matrix products, arithmetic and copies ran while one was open for 18% of the time, Pallas kernels for 0%

profile of v20, /device:TPU:0, one launch (start us, length us, event | category | flops | bytes accessed | tf_op | source)
XLA Modules:
  0.0 106.7 jit_solution(2679942987179783121)
XLA Ops:
  0.7 0.9 fusion.4
  2.2 1.0 convolution_convert_fusion.2
  3.2 7.3 %all-to-all-start.1 = ((bf16[8,24,896]{2,1,0:T(8,128)(2,1)}), bf16[8,24,896]{2,1,0:T(8,128)(2,1)S(1)}, u32[]{:S(2)}, u32[]{:S(2)}) async-start(bf16[8,24,896]{2,1,0:T(8,128)(2,1)} %bitcast.33), calls=%async_computation.1 | async-start | bytes 688128 | tf_op jit(solution)/shard_map/all_to_all | solution.py:98
  12.8 8.3 %all-to-all-done.1 = bf16[8,24,896]{2,1,0:T(8,128)(2,1)S(1)} async-done(((bf16[8,24,896]{2,1,0:T(8,128)(2,1)}), bf16[8,24,896]{2,1,0:T(8,128)(2,1)S(1)}, u32[]{:S(2)}, u32[]{:S(2)}) %all-to-all-start.1) | async-done | bytes 344096 | tf_op jit(solution)/shard_map/all_to_all | solution.py:98
  21.1 3.6 %all-to-all-start = ((bf16[8,24,1024]{2,1,0:T(8,128)(2,1)}), bf16[8,24,1024]{2,1,0:T(8,128)(2,1)S(1)}, u32[]{:S(2)}, u32[]{:S(2)}) async-start(bf16[8,24,1024]{2,1,0:T(8,128)(2,1)} %maximum_maximum_fusion), calls=%async_computation | async-start | bytes 786432 | tf_op jit(solution)/shard_map/all_to_all | solution.py:98
  24.7 1.5 %collective-permute-start.4 = (bf16[1,192,896]{2,1,0:T(8,128)(2,1)S(1)}, bf16[1,192,896]{2,1,0:T(8,128)(2,1)S(1)}, u32[]{:S(2)}, u32[]{:S(2)}) collective-permute-start(bf16[1,192,896]{2,1,0:T(8,128)(2,1)S(1)} %bitcast.166), channel_id=1, source_target_pairs={{0,16},{8,24},{16,0},{24,8},{1,17},{9,25},{17,1},{25,9},{2,18},{10... | collective-permute-start | bytes 1032200 | tf_op jit(solution)/shard_map/ppermute | solution.py:44
  26.2 7.5 %collective-permute-done.4 = bf16[1,192,896]{2,1,0:T(8,128)(2,1)S(1)} collective-permute-done((bf16[1,192,896]{2,1,0:T(8,128)(2,1)S(1)}, bf16[1,192,896]{2,1,0:T(8,128)(2,1)S(1)}, u32[]{:S(2)}, u32[]{:S(2)}) %collective-permute-start.4) | collective-permute-done | bytes 344096 | tf_op jit(solution)/shard_map/ppermute | solution.py:44
  33.8 1.0 maximum_select_fusion.4
  34.7 1.2 %all-to-all-done = bf16[8,24,1024]{2,1,0:T(8,128)(2,1)S(1)} async-done(((bf16[8,24,1024]{2,1,0:T(8,128)(2,1)}), bf16[8,24,1024]{2,1,0:T(8,128)(2,1)S(1)}, u32[]{:S(2)}, u32[]{:S(2)}) %all-to-all-start) | async-done | bytes 393248 | tf_op jit(solution)/shard_map/all_to_all | solution.py:98
  36.0 1.6 %collective-permute-start = (bf16[1,192,896]{2,1,0:T(8,128)(2,1)S(1)}, bf16[1,192,896]{2,1,0:T(8,128)(2,1)S(1)}, u32[]{:S(2)}, u32[]{:S(2)}) collective-permute-start(bf16[1,192,896]{2,1,0:T(8,128)(2,1)S(1)} %get-tuple-element.33), channel_id=1, source_target_pairs={{0,16},{8,24},{16,0},{24,8},{1,17},{9,25},{17,1},{25,9},{2,18},{10... | collective-permute-start | bytes 1032200 | tf_op jit(solution)/shard_map/ppermute | solution.py:44
  37.9 7.4 %collective-permute-done = bf16[1,192,896]{2,1,0:T(8,128)(2,1)S(1)} collective-permute-done((bf16[1,192,896]{2,1,0:T(8,128)(2,1)S(1)}, bf16[1,192,896]{2,1,0:T(8,128)(2,1)S(1)}, u32[]{:S(2)}, u32[]{:S(2)}) %collective-permute-start) | collective-permute-done | bytes 344096 | tf_op jit(solution)/shard_map/ppermute | solution.py:44
  46.1 1.6 %copy-done.3 = bf16[1,512,3584]{2,1,0:T(8,128)(2,1)S(1)} copy-done((bf16[1,512,3584]{2,1,0:T(8,128)(2,1)S(1)}, bf16[1,512,3584]{2,1,0:T(8,128)(2,1)}, u32[]{:S(2)}) %copy-start.3) | copy-done | bytes 3670040
  49.4 1.3 %copy-done.2 = bf16[1,3584,512]{2,1,0:T(8,128)(2,1)S(1)} copy-done((bf16[1,3584,512]{2,1,0:T(8,128)(2,1)S(1)}, bf16[1,3584,512]{2,1,0:T(8,128)(2,1)}, u32[]{:S(2)}) %copy-start.2) | copy-done | bytes 3670040
  50.7 0.9 convolution_bitcast_fusion.4
  51.6 1.2 %copy-done.1 = bf16[1,3584,512]{2,1,0:T(8,128)(2,1)S(1)} copy-done((bf16[1,3584,512]{2,1,0:T(8,128)(2,1)S(1)}, bf16[1,3584,512]{2,1,0:T(8,128)(2,1)}, u32[]{:S(2)}) %copy-start.1) | copy-done | bytes 3670040
  52.7 0.9 convolution_bitcast_fusion.5
  55.8 1.4 %fusion.24 = f32[192,4,896]{2,0,1:T(8,128)S(1)} fusion(bf16[4,896,512]{2,1,0:T(8,128)(2,1)S(1)} %bitcast.161, bf16[192,512]{1,0:T(8,128)(2,1)S(1)} %get-tuple-element.30), kind=kOutput, calls=%fused_computation.72 | convolution fusion | flops 704643072 | bytes 6619136 | tf_op jit(solution)/shard_map/sf,ndf->nsd/dot_general | solution.py:141
  57.2 1.3 %add_convert_fusion = bf16[192,4,896]{2,0,1:T(8,128)(2,1)S(1)} fusion(f32[192,4,896]{2,0,1:T(8,128)S(1)} %fusion.24, bf16[192,512,1]{1,0,2:T(8,128)(2,1)S(1)} %get-tuple-element.29, bf16[4,896,512]{2,1,0:T(8,128)(2,1)S(1)} %bitcast.165), kind=kOutput, calls=%fused_computation.3 | convolution fusion | flops 706019328 | bytes 7995392 | tf_op jit(solution)/shard_map/sf,ndf->nsd/dot_general | solution.py:143
  60.3 1.6 %collective-permute-done.6 = f32[192]{0:T(256)S(1)} collective-permute-done((f32[192]{0:T(256)S(1)}, f32[192]{0:T(256)S(1)}, u32[]{:S(2)}, u32[]{:S(2)}) %collective-permute-start.6) | collective-permute-done | bytes 800 | tf_op jit(solution)/shard_map/ppermute | solution.py:67
  61.9 1.5 %collective-permute-start.7 = (f32[192]{0:T(256)S(1)}, f32[192]{0:T(256)S(1)}, u32[]{:S(2)}, u32[]{:S(2)}) collective-permute-start(f32[192]{0:T(256)S(1)} %add.53), channel_id=1, source_target_pairs={{0,16},{8,24},{16,0},{24,8},{1,17},{9,25},{17,1},{25,9},{2,18},{10... | collective-permute-start | bytes 2312 | tf_op jit(solution)/shard_map/ppermute | solution.py:67
  65.4 1.5 %collective-permute-start.3 = (bf16[1,192,896]{2,1,0:T(8,128)(2,1)}, bf16[1,192,896]{2,1,0:T(8,128)(2,1)}, u32[]{:S(2)}, u32[]{:S(2)}) collective-permute-start(bf16[1,192,896]{2,1,0:T(8,128)(2,1)} %fusion.20), channel_id=1, source_target_pairs={{0,16},{8,24},{16,0},{24,8},{1,17},{9,25},{17,1},{25,9},{2,18},{10... | collective-permute-start | bytes 1032200 | tf_op jit(solution)/shard_map/ppermute | solution.py:60
  66.9 7.8 %collective-permute-done.9 = bf16[1,192,896]{2,1,0:T(8,128)(2,1)S(1)} collective-permute-done((bf16[1,192,896]{2,1,0:T(8,128)(2,1)S(1)}, bf16[1,192,896]{2,1,0:T(8,128)(2,1)S(1)}, u32[]{:S(2)}, u32[]{:S(2)}) %collective-permute-start.9) | collective-permute-done | bytes 344096 | tf_op jit(solution)/shard_map/ppermute | solution.py:60
  75.6 5.7 %all-to-all-start.3 = ((bf16[8,24,896]{2,1,0:T(8,128)(2,1)}), bf16[8,24,896]{2,1,0:T(8,128)(2,1)S(1)}, u32[]{:S(2)}, u32[]{:S(2)}) async-start(bf16[8,24,896]{2,1,0:T(8,128)(2,1)} %bitcast.177), calls=%async_computation.3 | async-start | bytes 688128 | tf_op jit(solution)/shard_map/all_to_all | solution.py:98
  81.3 0.9 concatenate.62
  82.2 0.9 concatenate.63
  83.1 1.1 %fusion.17 = bf16[1,192,896]{2,1,0:T(8,128)(2,1)S(1)} fusion(bf16[1,192,896]{2,1,0:T(8,128)(2,1)} %collective-permute-done.3, f32[1,2,192,896]{3,2,1,0:T(8,128)S(1)} %fusion.2, pred[]{:T(512)S(6)} %eq.50), kind=kLoop, calls=%fused_computation.49 | loop fusion | flops 688128 | bytes 2064385 | tf_op jit(solution)/shard_map/convert_element_type | solution.py:127
  85.0 5.4 %all-to-all-done.3 = bf16[8,24,896]{2,1,0:T(8,128)(2,1)S(1)} async-done(((bf16[8,24,896]{2,1,0:T(8,128)(2,1)}), bf16[8,24,896]{2,1,0:T(8,128)(2,1)S(1)}, u32[]{:S(2)}, u32[]{:S(2)}) %all-to-all-start.3) | async-done | bytes 344096 | tf_op jit(solution)/shard_map/all_to_all | solution.py:98
  90.5 3.6 %all-to-all-start.2 = ((bf16[8,24,1024]{2,1,0:T(8,128)(2,1)}), bf16[8,24,1024]{2,1,0:T(8,128)(2,1)S(1)}, u32[]{:S(2)}, u32[]{:S(2)}) async-start(bf16[8,24,1024]{2,1,0:T(8,128)(2,1)} %maximum_maximum_fusion.1), calls=%async_computation.2 | async-start | bytes 786432 | tf_op jit(solution)/shard_map/all_to_all | solution.py:98
  94.1 3.0 %convolution_convert_fusion = bf16[4,896,512]{2,1,0:T(8,128)(2,1)} fusion(bf16[4,192,896]{2,1,0:T(8,128)(2,1)S(1)} %bitcast.149, bf16[192,512,1]{1,0,2:T(8,128)(2,1)S(1)} %copy-done.5), kind=kOutput, calls=%fused_computation.4 | convolution fusion | flops 706478080 | bytes 5242880 | tf_op jit(solution)/shard_map/nsd,sf->ndf/dot_general | solution.py:151
  97.1 3.0 %convolution_convert_fusion.1 = bf16[4,896,512]{2,1,0:T(8,128)(2,1)} fusion(bf16[4,192,896]{2,1,0:T(8,128)(2,1)S(1)} %bitcast.150, bf16[192,512]{1,0:T(8,128)(2,1)S(1)} %get-tuple-element.30), kind=kOutput, calls=%fused_computation.5 | convolution fusion | flops 706478080 | bytes 5242880 | tf_op jit(solution)/shard_map/nsd,sf->ndf/dot_general | solution.py:148
  100.1 1.0 convolution_convert_fusion.4
  101.1 3.9 %all-to-all-done.2 = bf16[8,24,1024]{2,1,0:T(8,128)(2,1)S(1)} async-done(((bf16[8,24,1024]{2,1,0:T(8,128)(2,1)}), bf16[8,24,1024]{2,1,0:T(8,128)(2,1)S(1)}, u32[]{:S(2)}, u32[]{:S(2)}) %all-to-all-start.2) | async-done | bytes 393248 | tf_op jit(solution)/shard_map/all_to_all | solution.py:98
  (70 shorter events, 15.0 us)
Async XLA Ops:
  0.6 1.6 %copy-start = (bf16[128,896]{1,0:T(8,128)(2,1)S(1)}, bf16[128,896]{1,0:T(8,128)(2,1)}, u32[]{:S(2)}) copy-start(bf16[128,896]{1,0:T(8,128)(2,1)} %param.8) | copy-start | bytes 688132
  0.6 11.0 %copy-start.6 = (bf16[128,896]{1,0:T(8,128)(2,1)S(1)}, bf16[128,896]{1,0:T(8,128)(2,1)}, u32[]{:S(2)}) copy-start(bf16[128,896]{1,0:T(8,128)(2,1)} %param.7) | copy-start | bytes 688132
  3.2 17.9 %all-to-all-start.1 = ((bf16[8,24,896]{2,1,0:T(8,128)(2,1)}), bf16[8,24,896]{2,1,0:T(8,128)(2,1)S(1)}, u32[]{:S(2)}, u32[]{:S(2)}) async-start(bf16[8,24,896]{2,1,0:T(8,128)(2,1)} %bitcast.33), calls=%async_computation.1 | async-start | bytes 688128 | tf_op jit(solution)/shard_map/all_to_all | solution.py:98
  21.1 14.9 %all-to-all-start = ((bf16[8,24,1024]{2,1,0:T(8,128)(2,1)}), bf16[8,24,1024]{2,1,0:T(8,128)(2,1)S(1)}, u32[]{:S(2)}, u32[]{:S(2)}) async-start(bf16[8,24,1024]{2,1,0:T(8,128)(2,1)} %maximum_maximum_fusion), calls=%async_computation | async-start | bytes 786432 | tf_op jit(solution)/shard_map/all_to_all | solution.py:98
  24.7 9.1 %collective-permute-start.4 = (bf16[1,192,896]{2,1,0:T(8,128)(2,1)S(1)}, bf16[1,192,896]{2,1,0:T(8,128)(2,1)S(1)}, u32[]{:S(2)}, u32[]{:S(2)}) collective-permute-start(bf16[1,192,896]{2,1,0:T(8,128)(2,1)S(1)} %bitcast.166), channel_id=1, source_target_pairs={{0,16},{8,24},{16,0},{24,8},{1,17},{9,25},{17,1},{25,9},{2,18},{10... | collective-permute-start | bytes 1032200 | tf_op jit(solution)/shard_map/ppermute | solution.py:44
  34.7 10.9 %collective-permute-start.5 = (bf16[2,192,896]{2,1,0:T(8,128)(2,1)}, bf16[2,192,896]{2,1,0:T(8,128)(2,1)S(1)}, u32[]{:S(2)}, u32[]{:S(2)}) collective-permute-start(bf16[2,192,896]{2,1,0:T(8,128)(2,1)} %maximum_select_fusion.4), channel_id=1, source_target_pairs={{0,8},{8,0},{16,24},{24,16},{1,9},{9,1},{17,25},{25,17},{2,10},{10... | collective-permute-start | bytes 2064392 | tf_op jit(solution)/shard_map/ppermute | solution.py:44
  36.0 9.3 %collective-permute-start = (bf16[1,192,896]{2,1,0:T(8,128)(2,1)S(1)}, bf16[1,192,896]{2,1,0:T(8,128)(2,1)S(1)}, u32[]{:S(2)}, u32[]{:S(2)}) collective-permute-start(bf16[1,192,896]{2,1,0:T(8,128)(2,1)S(1)} %get-tuple-element.33), channel_id=1, source_target_pairs={{0,16},{8,24},{16,0},{24,8},{1,17},{9,25},{17,1},{25,9},{2,18},{10... | collective-permute-start | bytes 1032200 | tf_op jit(solution)/shard_map/ppermute | solution.py:44
  45.5 3.7 %collective-permute-start.1 = (bf16[2,192,896]{2,1,0:T(8,128)(2,1)S(1)}, bf16[2,192,896]{2,1,0:T(8,128)(2,1)S(1)}, u32[]{:S(2)}, u32[]{:S(2)}) collective-permute-start(bf16[2,192,896]{2,1,0:T(8,128)(2,1)S(1)} %maximum_select_fusion.2), channel_id=1, source_target_pairs={{0,8},{8,0},{16,24},{24,16},{1,9},{9,1},{17,25},{25,17},{2,10},{10... | collective-permute-start | bytes 2064392 | tf_op jit(solution)/shard_map/ppermute | solution.py:44
  45.7 2.0 %copy-start.3 = (bf16[1,512,3584]{2,1,0:T(8,128)(2,1)S(1)}, bf16[1,512,3584]{2,1,0:T(8,128)(2,1)}, u32[]{:S(2)}) copy-start(bf16[1,512,3584]{2,1,0:T(8,128)(2,1)} %param.13) | copy-start | bytes 11010052
  48.7 2.0 %copy-start.2 = (bf16[1,3584,512]{2,1,0:T(8,128)(2,1)S(1)}, bf16[1,3584,512]{2,1,0:T(8,128)(2,1)}, u32[]{:S(2)}) copy-start(bf16[1,3584,512]{2,1,0:T(8,128)(2,1)} %param.12) | copy-start | bytes 11010052
  50.7 2.0 %copy-start.1 = (bf16[1,3584,512]{2,1,0:T(8,128)(2,1)S(1)}, bf16[1,3584,512]{2,1,0:T(8,128)(2,1)}, u32[]{:S(2)}) copy-start(bf16[1,3584,512]{2,1,0:T(8,128)(2,1)} %param.11) | copy-start | bytes 11010052
  54.2 2.9 %copy-start.4 = (bf16[192,512,1]{1,0,2:T(8,128)(2,1)}, bf16[192,512,1]{1,0,2:T(8,128)(2,1)S(1)}, u32[]{:S(2)}) copy-start(bf16[192,512,1]{1,0,2:T(8,128)(2,1)S(1)} %get-tuple-element.29) | copy-start | bytes 589828
  58.6 4.9 %collective-permute-start.8 = (bf16[2,192,896]{2,1,0:T(8,128)(2,1)S(1)}, bf16[2,192,896]{2,1,0:T(8,128)(2,1)S(1)}, u32[]{:S(2)}, u32[]{:S(2)}) collective-permute-start(bf16[2,192,896]{2,1,0:T(8,128)(2,1)S(1)} %select_bitcast_fusion), channel_id=1, source_target_pairs={{0,8},{8,0},{16,24},{24,16},{1,9},{9,1},{17,25},{25,17},{2,10},{10... | collective-permute-start | bytes 2064392 | tf_op jit(solution)/shard_map/ppermute | solution.py:60
  59.7 4.6 %collective-permute-start.2 = (bf16[2,192,896]{2,1,0:T(8,128)(2,1)S(1)}, bf16[2,192,896]{2,1,0:T(8,128)(2,1)S(1)}, u32[]{:S(2)}, u32[]{:S(2)}) collective-permute-start(bf16[2,192,896]{2,1,0:T(8,128)(2,1)S(1)} %fusion.14), channel_id=1, source_target_pairs={{0,8},{8,0},{16,24},{24,16},{1,9},{9,1},{17,25},{25,17},{2,10},{10... | collective-permute-start | bytes 2064392 | tf_op jit(solution)/shard_map/ppermute | solution.py:60
  59.8 2.1 %collective-permute-start.6 = (f32[192]{0:T(256)S(1)}, f32[192]{0:T(256)S(1)}, u32[]{:S(2)}, u32[]{:S(2)}) collective-permute-start(f32[192]{0:T(256)S(1)} %get-tuple-element.25), channel_id=1, source_target_pairs={{0,8},{8,0},{16,24},{24,16},{1,9},{9,1},{17,25},{25,17},{2,10},{10... | collective-permute-start | bytes 2312 | tf_op jit(solution)/shard_map/ppermute | solution.py:67
  61.9 19.4 %collective-permute-start.7 = (f32[192]{0:T(256)S(1)}, f32[192]{0:T(256)S(1)}, u32[]{:S(2)}, u32[]{:S(2)}) collective-permute-start(f32[192]{0:T(256)S(1)} %add.53), channel_id=1, source_target_pairs={{0,16},{8,24},{16,0},{24,8},{1,17},{9,25},{17,1},{25,9},{2,18},{10... | collective-permute-start | bytes 2312 | tf_op jit(solution)/shard_map/ppermute | solution.py:67
  63.8 11.0 %collective-permute-start.9 = (bf16[1,192,896]{2,1,0:T(8,128)(2,1)S(1)}, bf16[1,192,896]{2,1,0:T(8,128)(2,1)S(1)}, u32[]{:S(2)}, u32[]{:S(2)}) collective-permute-start(bf16[1,192,896]{2,1,0:T(8,128)(2,1)S(1)} %fusion.21), channel_id=1, source_target_pairs={{0,16},{8,24},{16,0},{24,8},{1,17},{9,25},{17,1},{25,9},{2,18},{10... | collective-permute-start | bytes 1032200 | tf_op jit(solution)/shard_map/ppermute | solution.py:60
  65.4 17.6 %collective-permute-start.3 = (bf16[1,192,896]{2,1,0:T(8,128)(2,1)}, bf16[1,192,896]{2,1,0:T(8,128)(2,1)}, u32[]{:S(2)}, u32[]{:S(2)}) collective-permute-start(bf16[1,192,896]{2,1,0:T(8,128)(2,1)} %fusion.20), channel_id=1, source_target_pairs={{0,16},{8,24},{16,0},{24,8},{1,17},{9,25},{17,1},{25,9},{2,18},{10... | collective-permute-start | bytes 1032200 | tf_op jit(solution)/shard_map/ppermute | solution.py:60
  75.6 14.9 %all-to-all-start.3 = ((bf16[8,24,896]{2,1,0:T(8,128)(2,1)}), bf16[8,24,896]{2,1,0:T(8,128)(2,1)S(1)}, u32[]{:S(2)}, u32[]{:S(2)}) async-start(bf16[8,24,896]{2,1,0:T(8,128)(2,1)} %bitcast.177), calls=%async_computation.3 | async-start | bytes 688128 | tf_op jit(solution)/shard_map/all_to_all | solution.py:98
  83.0 1.1 %copy-start.7 = (bf16[8,24,1]{2,1,0:T(8,128)(2,1)S(1)}, bf16[8,24,1]{2,1,0:T(8,128)(2,1)}, u32[]{:S(2)}) copy-start(bf16[8,24,1]{2,1,0:T(8,128)(2,1)} %concatenate.62) | copy-start | bytes 1156
  83.1 1.1 %copy-start.8 = (bf16[8,24,1]{2,1,0:T(8,128)(2,1)S(1)}, bf16[8,24,1]{2,1,0:T(8,128)(2,1)}, u32[]{:S(2)}) copy-start(bf16[8,24,1]{2,1,0:T(8,128)(2,1)} %concatenate.63) | copy-start | bytes 1156
  84.1 10.0 %copy-start.5 = (bf16[192,512,1]{1,0,2:T(8,128)(2,1)S(1)}, bf16[192,512,1]{1,0,2:T(8,128)(2,1)}, u32[]{:S(2)}) copy-start(bf16[192,512,1]{1,0,2:T(8,128)(2,1)} %copy-done.4) | copy-start | bytes 589828
  90.5 14.5 %all-to-all-start.2 = ((bf16[8,24,1024]{2,1,0:T(8,128)(2,1)}), bf16[8,24,1024]{2,1,0:T(8,128)(2,1)S(1)}, u32[]{:S(2)}, u32[]{:S(2)}) async-start(bf16[8,24,1024]{2,1,0:T(8,128)(2,1)} %maximum_maximum_fusion.1), calls=%async_computation.2 | async-start | bytes 786432 | tf_op jit(solution)/shard_map/all_to_all | solution.py:98
  100.1 5.2 %copy-start.9 = (f32[128,1]{0,1:T(1,128)S(1)}, f32[128,1]{0,1:T(1,128)}, u32[]{:S(2)}) copy-start(f32[128,1]{0,1:T(1,128)} %param.10) | copy-start | bytes 1540

commit v21 on v13

--- a/solution.py
+++ b/solution.py
@@ -121,8 +121,8 @@
     partial_out = jnp.stack(
         [jnp.dot(hidden, cols, preferred_element_type=jnp.float32) for cols in down_cols]
     ).astype(jnp.bfloat16)
-    gate_part = jnp.einsum(
-        "nsd,nsd->s", partial_out.astype(jnp.float32), grads_in.astype(jnp.float32)
+    gate_part = jnp.sum(
+        partial_out.astype(jnp.float32) * grads_in.astype(jnp.float32), axis=(0, 2)
     )
     expert_out = scatter_sum(partial_out.astype(jnp.float32), n_ctx, me).astype(jnp.bfloat16)
     gate_sum = all_sum(gate_part, n_ctx)

time: 106 us -> 108 us (1.019)
  waiting for transfers between devices: 41.7 us -> 43.2 us
    all_to_all x4, waiting for transfers between devices: 17.1 us -> 18.9 us  [to_experts(): got = lax.all_to_all(sent, 'ep', split_axis=0, concat_axis=0, tiled=True)]
where the time goes in v21:
time: 108 us; the launch traced here: 107 us
  waiting for transfers between devices  43.2 us (40%)
  starting transfers between devices  28.2 us (26%)
  matrix products  17.3 us (16%)
  other arithmetic  10.1 us (9%)
  local copies, waits for them, and re-layouts  7.51 us (7%)
    all_to_all x4, starting transfers between devices, to_experts(): got = lax.all_to_all(sent, 'ep', split_axis=0, concat_axis=0, tiled=True)  20.2 us
    all_to_all x4, waiting for transfers between devices, to_experts(): got = lax.all_to_all(sent, 'ep', split_axis=0, concat_axis=0, tiled=True)  18.9 us
    ppermute x4, waiting for transfers between devices, gather_blocks(): other = lax.ppermute(held, 'ctx', xor_pairs(n_ctx, bit))  15.1 us
    ppermute x4, waiting for transfers between devices, scatter_sum(): got = lax.ppermute(send, 'ctx', xor_pairs(n_ctx, bit))  7.92 us
    unnamed x21, local copies, waits for them, and re-layouts  5.07 us
    ppermute x4, starting transfers between devices, gather_blocks(): other = lax.ppermute(held, 'ctx', xor_pairs(n_ctx, bit))  3.18 us
    dot_general x1, matrix products, shards(): jnp.einsum('nsd,sf->ndf', rows_in, grad_up, preferred_element_type=jnp.fl...  3 us
    dot_general x1, matrix products, shards(): jnp.einsum('nsd,sf->ndf', rows_in, grad_gate, preferred_element_type=jnp....  3 us
  transfers between devices with their start and end apart: 14, of which 8 were waited for; matrix products, arithmetic and copies ran while one was open for 18% of the time, Pallas kernels for 0%

profile of v21, /device:TPU:0, one launch (start us, length us, event | category | flops | bytes accessed | tf_op | source)
XLA Modules:
  0.0 107.2 jit_solution(14854611483710810439)
XLA Ops:
  0.7 0.9 fusion.7
  2.2 1.0 convolution_convert_fusion.2
  3.2 7.3 %all-to-all-start.1 = ((bf16[8,24,896]{2,1,0:T(8,128)(2,1)}), bf16[8,24,896]{2,1,0:T(8,128)(2,1)S(1)}, u32[]{:S(2)}, u32[]{:S(2)}) async-start(bf16[8,24,896]{2,1,0:T(8,128)(2,1)} %bitcast.30), calls=%async_computation.1 | async-start | bytes 688128 | tf_op jit(solution)/shard_map/all_to_all | solution.py:98
  12.8 8.3 %all-to-all-done.1 = bf16[8,24,896]{2,1,0:T(8,128)(2,1)S(1)} async-done(((bf16[8,24,896]{2,1,0:T(8,128)(2,1)}), bf16[8,24,896]{2,1,0:T(8,128)(2,1)S(1)}, u32[]{:S(2)}, u32[]{:S(2)}) %all-to-all-start.1) | async-done | bytes 344096 | tf_op jit(solution)/shard_map/all_to_all | solution.py:98
  21.1 3.6 %all-to-all-start = ((bf16[8,24,1024]{2,1,0:T(8,128)(2,1)}), bf16[8,24,1024]{2,1,0:T(8,128)(2,1)S(1)}, u32[]{:S(2)}, u32[]{:S(2)}) async-start(bf16[8,24,1024]{2,1,0:T(8,128)(2,1)} %maximum_maximum_fusion), calls=%async_computation | async-start | bytes 786432 | tf_op jit(solution)/shard_map/all_to_all | solution.py:98
  24.7 1.5 %collective-permute-start.4 = (bf16[1,192,896]{2,1,0:T(8,128)(2,1)S(1)}, bf16[1,192,896]{2,1,0:T(8,128)(2,1)S(1)}, u32[]{:S(2)}, u32[]{:S(2)}) collective-permute-start(bf16[1,192,896]{2,1,0:T(8,128)(2,1)S(1)} %bitcast.176), channel_id=1, source_target_pairs={{0,16},{8,24},{16,0},{24,8},{1,17},{9,25},{17,1},{25,9},{2,18},{10... | collective-permute-start | bytes 1032200 | tf_op jit(solution)/shard_map/ppermute | solution.py:44
  26.2 7.5 %collective-permute-done.4 = bf16[1,192,896]{2,1,0:T(8,128)(2,1)S(1)} collective-permute-done((bf16[1,192,896]{2,1,0:T(8,128)(2,1)S(1)}, bf16[1,192,896]{2,1,0:T(8,128)(2,1)S(1)}, u32[]{:S(2)}, u32[]{:S(2)}) %collective-permute-start.4) | collective-permute-done | bytes 344096 | tf_op jit(solution)/shard_map/ppermute | solution.py:44
  33.8 1.0 maximum_select_fusion.4
  34.7 1.2 %all-to-all-done = bf16[8,24,1024]{2,1,0:T(8,128)(2,1)S(1)} async-done(((bf16[8,24,1024]{2,1,0:T(8,128)(2,1)}), bf16[8,24,1024]{2,1,0:T(8,128)(2,1)S(1)}, u32[]{:S(2)}, u32[]{:S(2)}) %all-to-all-start) | async-done | bytes 393248 | tf_op jit(solution)/shard_map/all_to_all | solution.py:98
  36.0 1.6 %collective-permute-start = (bf16[1,192,896]{2,1,0:T(8,128)(2,1)S(1)}, bf16[1,192,896]{2,1,0:T(8,128)(2,1)S(1)}, u32[]{:S(2)}, u32[]{:S(2)}) collective-permute-start(bf16[1,192,896]{2,1,0:T(8,128)(2,1)S(1)} %get-tuple-element.31), channel_id=1, source_target_pairs={{0,16},{8,24},{16,0},{24,8},{1,17},{9,25},{17,1},{25,9},{2,18},{10... | collective-permute-start | bytes 1032200 | tf_op jit(solution)/shard_map/ppermute | solution.py:44
  37.8 7.6 %collective-permute-done = bf16[1,192,896]{2,1,0:T(8,128)(2,1)S(1)} collective-permute-done((bf16[1,192,896]{2,1,0:T(8,128)(2,1)S(1)}, bf16[1,192,896]{2,1,0:T(8,128)(2,1)S(1)}, u32[]{:S(2)}, u32[]{:S(2)}) %collective-permute-start) | collective-permute-done | bytes 344096 | tf_op jit(solution)/shard_map/ppermute | solution.py:44
  46.2 1.6 %copy-done.3 = bf16[1,512,3584]{2,1,0:T(8,128)(2,1)S(1)} copy-done((bf16[1,512,3584]{2,1,0:T(8,128)(2,1)S(1)}, bf16[1,512,3584]{2,1,0:T(8,128)(2,1)}, u32[]{:S(2)}) %copy-start.3) | copy-done | bytes 3670040
  49.6 1.7 %copy-done.2 = bf16[1,3584,512]{2,1,0:T(8,128)(2,1)S(1)} copy-done((bf16[1,3584,512]{2,1,0:T(8,128)(2,1)S(1)}, bf16[1,3584,512]{2,1,0:T(8,128)(2,1)}, u32[]{:S(2)}) %copy-start.2) | copy-done | bytes 3670040
  51.3 0.9 convolution_bitcast_fusion.4
  52.2 1.2 %copy-done.1 = bf16[1,3584,512]{2,1,0:T(8,128)(2,1)S(1)} copy-done((bf16[1,3584,512]{2,1,0:T(8,128)(2,1)S(1)}, bf16[1,3584,512]{2,1,0:T(8,128)(2,1)}, u32[]{:S(2)}) %copy-start.1) | copy-done | bytes 3670040
  53.3 0.9 convolution_bitcast_fusion.5
  56.4 1.3 %fusion.28 = f32[192,4,896]{2,0,1:T(8,128)S(1)} fusion(bf16[4,896,512]{2,1,0:T(8,128)(2,1)S(1)} %bitcast.171, bf16[192,512]{1,0:T(8,128)(2,1)S(1)} %get-tuple-element.28), kind=kOutput, calls=%fused_computation.76 | convolution fusion | flops 704643072 | bytes 6619136 | tf_op jit(solution)/shard_map/sf,ndf->nsd/dot_general | solution.py:141
  57.7 1.3 %fusion = f32[192,4,896]{2,0,1:T(8,128)S(1)} fusion(f32[192,4,896]{2,0,1:T(8,128)S(1)} %fusion.28, bf16[192,512,1]{1,0,2:T(8,128)(2,1)S(1)} %get-tuple-element.27, bf16[4,896,512]{2,1,0:T(8,128)(2,1)S(1)} %bitcast.173), kind=kOutput, calls=%fused_computation.5 | convolution fusion | flops 706707456 | bytes 9371648 | tf_op jit(solution)/shard_map/sf,ndf->nsd/dot_general | solution.py:143
  61.2 1.3 %collective-permute-done.6 = f32[192]{0:T(256)S(1)} collective-permute-done((f32[192]{0:T(256)S(1)}, f32[192]{0:T(256)S(1)}, u32[]{:S(2)}, u32[]{:S(2)}) %collective-permute-start.6) | collective-permute-done | bytes 800 | tf_op jit(solution)/shard_map/ppermute | solution.py:67
  62.6 1.5 %collective-permute-start.7 = (f32[192]{0:T(256)S(1)}, f32[192]{0:T(256)S(1)}, u32[]{:S(2)}, u32[]{:S(2)}) collective-permute-start(f32[192]{0:T(256)S(1)} %add.53), channel_id=1, source_target_pairs={{0,16},{8,24},{16,0},{24,8},{1,17},{9,25},{17,1},{25,9},{2,18},{10... | collective-permute-start | bytes 2312 | tf_op jit(solution)/shard_map/ppermute | solution.py:67
  65.9 1.5 %collective-permute-start.3 = (bf16[1,192,896]{2,1,0:T(8,128)(2,1)}, bf16[1,192,896]{2,1,0:T(8,128)(2,1)}, u32[]{:S(2)}, u32[]{:S(2)}) collective-permute-start(bf16[1,192,896]{2,1,0:T(8,128)(2,1)} %fusion.24), channel_id=1, source_target_pairs={{0,16},{8,24},{16,0},{24,8},{1,17},{9,25},{17,1},{25,9},{2,18},{10... | collective-permute-start | bytes 1032200 | tf_op jit(solution)/shard_map/ppermute | solution.py:60
  67.4 7.9 %collective-permute-done.9 = bf16[1,192,896]{2,1,0:T(8,128)(2,1)S(1)} collective-permute-done((bf16[1,192,896]{2,1,0:T(8,128)(2,1)S(1)}, bf16[1,192,896]{2,1,0:T(8,128)(2,1)S(1)}, u32[]{:S(2)}, u32[]{:S(2)}) %collective-permute-start.9) | collective-permute-done | bytes 344096 | tf_op jit(solution)/shard_map/ppermute | solution.py:60
  76.1 5.7 %all-to-all-start.3 = ((bf16[8,24,896]{2,1,0:T(8,128)(2,1)}), bf16[8,24,896]{2,1,0:T(8,128)(2,1)S(1)}, u32[]{:S(2)}, u32[]{:S(2)}) async-start(bf16[8,24,896]{2,1,0:T(8,128)(2,1)} %bitcast.187), calls=%async_computation.3 | async-start | bytes 688128 | tf_op jit(solution)/shard_map/all_to_all | solution.py:98
  81.9 0.9 concatenate.62
  82.7 0.9 concatenate.63
  83.6 1.1 %fusion.21 = bf16[1,192,896]{2,1,0:T(8,128)(2,1)S(1)} fusion(bf16[1,192,896]{2,1,0:T(8,128)(2,1)} %collective-permute-done.3, f32[1,2,192,896]{3,2,1,0:T(8,128)S(1)} %fusion.4, pred[]{:T(512)S(6)} %eq.50), kind=kLoop, calls=%fused_computation.54 | loop fusion | flops 688128 | bytes 2064385 | tf_op jit(solution)/shard_map/convert_element_type | solution.py:127
  85.6 5.4 %all-to-all-done.3 = bf16[8,24,896]{2,1,0:T(8,128)(2,1)S(1)} async-done(((bf16[8,24,896]{2,1,0:T(8,128)(2,1)}), bf16[8,24,896]{2,1,0:T(8,128)(2,1)S(1)}, u32[]{:S(2)}, u32[]{:S(2)}) %all-to-all-start.3) | async-done | bytes 344096 | tf_op jit(solution)/shard_map/all_to_all | solution.py:98
  91.0 3.6 %all-to-all-start.2 = ((bf16[8,24,1024]{2,1,0:T(8,128)(2,1)}), bf16[8,24,1024]{2,1,0:T(8,128)(2,1)S(1)}, u32[]{:S(2)}, u32[]{:S(2)}) async-start(bf16[8,24,1024]{2,1,0:T(8,128)(2,1)} %maximum_maximum_fusion.1), calls=%async_computation.2 | async-start | bytes 786432 | tf_op jit(solution)/shard_map/all_to_all | solution.py:98
  94.7 3.0 %convolution_convert_fusion = bf16[4,896,512]{2,1,0:T(8,128)(2,1)} fusion(bf16[4,192,896]{2,1,0:T(8,128)(2,1)S(1)} %bitcast.163, bf16[192,512,1]{1,0,2:T(8,128)(2,1)S(1)} %copy-done.5), kind=kOutput, calls=%fused_computation.3 | convolution fusion | flops 706478080 | bytes 5242880 | tf_op jit(solution)/shard_map/nsd,sf->ndf/dot_general | solution.py:151
  97.7 3.0 %convolution_convert_fusion.1 = bf16[4,896,512]{2,1,0:T(8,128)(2,1)} fusion(bf16[4,192,896]{2,1,0:T(8,128)(2,1)S(1)} %bitcast.164, bf16[192,512]{1,0:T(8,128)(2,1)S(1)} %get-tuple-element.28), kind=kOutput, calls=%fused_computation.4 | convolution fusion | flops 706478080 | bytes 5242880 | tf_op jit(solution)/shard_map/nsd,sf->ndf/dot_general | solution.py:148
  100.7 1.0 convolution_convert_fusion.4
  101.6 3.9 %all-to-all-done.2 = bf16[8,24,1024]{2,1,0:T(8,128)(2,1)S(1)} async-done(((bf16[8,24,1024]{2,1,0:T(8,128)(2,1)}), bf16[8,24,1024]{2,1,0:T(8,128)(2,1)S(1)}, u32[]{:S(2)}, u32[]{:S(2)}) %all-to-all-start.2) | async-done | bytes 393248 | tf_op jit(solution)/shard_map/all_to_all | solution.py:98
  (71 shorter events, 15.3 us)
Async XLA Ops:
  0.6 1.6 %copy-start = (bf16[128,896]{1,0:T(8,128)(2,1)S(1)}, bf16[128,896]{1,0:T(8,128)(2,1)}, u32[]{:S(2)}) copy-start(bf16[128,896]{1,0:T(8,128)(2,1)} %param.8) | copy-start | bytes 688132
  0.6 11.0 %copy-start.6 = (bf16[128,896]{1,0:T(8,128)(2,1)S(1)}, bf16[128,896]{1,0:T(8,128)(2,1)}, u32[]{:S(2)}) copy-start(bf16[128,896]{1,0:T(8,128)(2,1)} %param.7) | copy-start | bytes 688132
  3.2 17.9 %all-to-all-start.1 = ((bf16[8,24,896]{2,1,0:T(8,128)(2,1)}), bf16[8,24,896]{2,1,0:T(8,128)(2,1)S(1)}, u32[]{:S(2)}, u32[]{:S(2)}) async-start(bf16[8,24,896]{2,1,0:T(8,128)(2,1)} %bitcast.30), calls=%async_computation.1 | async-start | bytes 688128 | tf_op jit(solution)/shard_map/all_to_all | solution.py:98
  21.1 14.9 %all-to-all-start = ((bf16[8,24,1024]{2,1,0:T(8,128)(2,1)}), bf16[8,24,1024]{2,1,0:T(8,128)(2,1)S(1)}, u32[]{:S(2)}, u32[]{:S(2)}) async-start(bf16[8,24,1024]{2,1,0:T(8,128)(2,1)} %maximum_maximum_fusion), calls=%async_computation | async-start | bytes 786432 | tf_op jit(solution)/shard_map/all_to_all | solution.py:98
  24.7 9.1 %collective-permute-start.4 = (bf16[1,192,896]{2,1,0:T(8,128)(2,1)S(1)}, bf16[1,192,896]{2,1,0:T(8,128)(2,1)S(1)}, u32[]{:S(2)}, u32[]{:S(2)}) collective-permute-start(bf16[1,192,896]{2,1,0:T(8,128)(2,1)S(1)} %bitcast.176), channel_id=1, source_target_pairs={{0,16},{8,24},{16,0},{24,8},{1,17},{9,25},{17,1},{25,9},{2,18},{10... | collective-permute-start | bytes 1032200 | tf_op jit(solution)/shard_map/ppermute | solution.py:44
  34.7 11.1 %collective-permute-start.5 = (bf16[2,192,896]{2,1,0:T(8,128)(2,1)}, bf16[2,192,896]{2,1,0:T(8,128)(2,1)S(1)}, u32[]{:S(2)}, u32[]{:S(2)}) collective-permute-start(bf16[2,192,896]{2,1,0:T(8,128)(2,1)} %maximum_select_fusion.4), channel_id=1, source_target_pairs={{0,8},{8,0},{16,24},{24,16},{1,9},{9,1},{17,25},{25,17},{2,10},{10... | collective-permute-start | bytes 2064392 | tf_op jit(solution)/shard_map/ppermute | solution.py:44
  36.0 9.3 %collective-permute-start = (bf16[1,192,896]{2,1,0:T(8,128)(2,1)S(1)}, bf16[1,192,896]{2,1,0:T(8,128)(2,1)S(1)}, u32[]{:S(2)}, u32[]{:S(2)}) collective-permute-start(bf16[1,192,896]{2,1,0:T(8,128)(2,1)S(1)} %get-tuple-element.31), channel_id=1, source_target_pairs={{0,16},{8,24},{16,0},{24,8},{1,17},{9,25},{17,1},{25,9},{2,18},{10... | collective-permute-start | bytes 1032200 | tf_op jit(solution)/shard_map/ppermute | solution.py:44
  45.5 3.8 %collective-permute-start.1 = (bf16[2,192,896]{2,1,0:T(8,128)(2,1)S(1)}, bf16[2,192,896]{2,1,0:T(8,128)(2,1)S(1)}, u32[]{:S(2)}, u32[]{:S(2)}) collective-permute-start(bf16[2,192,896]{2,1,0:T(8,128)(2,1)S(1)} %maximum_select_fusion.3), channel_id=1, source_target_pairs={{0,8},{8,0},{16,24},{24,16},{1,9},{9,1},{17,25},{25,17},{2,10},{10... | collective-permute-start | bytes 2064392 | tf_op jit(solution)/shard_map/ppermute | solution.py:44
  45.8 2.0 %copy-start.3 = (bf16[1,512,3584]{2,1,0:T(8,128)(2,1)S(1)}, bf16[1,512,3584]{2,1,0:T(8,128)(2,1)}, u32[]{:S(2)}) copy-start(bf16[1,512,3584]{2,1,0:T(8,128)(2,1)} %param.13) | copy-start | bytes 11010052
  49.3 2.0 %copy-start.2 = (bf16[1,3584,512]{2,1,0:T(8,128)(2,1)S(1)}, bf16[1,3584,512]{2,1,0:T(8,128)(2,1)}, u32[]{:S(2)}) copy-start(bf16[1,3584,512]{2,1,0:T(8,128)(2,1)} %param.12) | copy-start | bytes 11010052
  51.3 2.0 %copy-start.1 = (bf16[1,3584,512]{2,1,0:T(8,128)(2,1)S(1)}, bf16[1,3584,512]{2,1,0:T(8,128)(2,1)}, u32[]{:S(2)}) copy-start(bf16[1,3584,512]{2,1,0:T(8,128)(2,1)} %param.11) | copy-start | bytes 11010052
  54.8 2.9 %copy-start.4 = (bf16[192,512,1]{1,0,2:T(8,128)(2,1)}, bf16[192,512,1]{1,0,2:T(8,128)(2,1)S(1)}, u32[]{:S(2)}) copy-start(bf16[192,512,1]{1,0,2:T(8,128)(2,1)S(1)} %get-tuple-element.27) | copy-start | bytes 589828
  59.2 4.9 %collective-permute-start.8 = (bf16[2,192,896]{2,1,0:T(8,128)(2,1)S(1)}, bf16[2,192,896]{2,1,0:T(8,128)(2,1)S(1)}, u32[]{:S(2)}, u32[]{:S(2)}) collective-permute-start(bf16[2,192,896]{2,1,0:T(8,128)(2,1)S(1)} %fusion.18), channel_id=1, source_target_pairs={{0,8},{8,0},{16,24},{24,16},{1,9},{9,1},{17,25},{25,17},{2,10},{10... | collective-permute-start | bytes 2064392 | tf_op jit(solution)/shard_map/ppermute | solution.py:60
  60.2 4.7 %collective-permute-start.2 = (bf16[2,192,896]{2,1,0:T(8,128)(2,1)S(1)}, bf16[2,192,896]{2,1,0:T(8,128)(2,1)S(1)}, u32[]{:S(2)}, u32[]{:S(2)}) collective-permute-start(bf16[2,192,896]{2,1,0:T(8,128)(2,1)S(1)} %fusion.17), channel_id=1, source_target_pairs={{0,8},{8,0},{16,24},{24,16},{1,9},{9,1},{17,25},{25,17},{2,10},{10... | collective-permute-start | bytes 2064392 | tf_op jit(solution)/shard_map/ppermute | solution.py:60
  60.7 1.8 %collective-permute-start.6 = (f32[192]{0:T(256)S(1)}, f32[192]{0:T(256)S(1)}, u32[]{:S(2)}, u32[]{:S(2)}) collective-permute-start(f32[192]{0:T(256)S(1)} %multiply_reduce_fusion), channel_id=1, source_target_pairs={{0,8},{8,0},{16,24},{24,16},{1,9},{9,1},{17,25},{25,17},{2,10},{10... | collective-permute-start | bytes 2312 | tf_op jit(solution)/shard_map/ppermute | solution.py:67
  62.6 19.3 %collective-permute-start.7 = (f32[192]{0:T(256)S(1)}, f32[192]{0:T(256)S(1)}, u32[]{:S(2)}, u32[]{:S(2)}) collective-permute-start(f32[192]{0:T(256)S(1)} %add.53), channel_id=1, source_target_pairs={{0,16},{8,24},{16,0},{24,8},{1,17},{9,25},{17,1},{25,9},{2,18},{10... | collective-permute-start | bytes 2312 | tf_op jit(solution)/shard_map/ppermute | solution.py:67
  64.3 11.0 %collective-permute-start.9 = (bf16[1,192,896]{2,1,0:T(8,128)(2,1)S(1)}, bf16[1,192,896]{2,1,0:T(8,128)(2,1)S(1)}, u32[]{:S(2)}, u32[]{:S(2)}) collective-permute-start(bf16[1,192,896]{2,1,0:T(8,128)(2,1)S(1)} %fusion.25), channel_id=1, source_target_pairs={{0,16},{8,24},{16,0},{24,8},{1,17},{9,25},{17,1},{25,9},{2,18},{10... | collective-permute-start | bytes 1032200 | tf_op jit(solution)/shard_map/ppermute | solution.py:60
  65.9 17.7 %collective-permute-start.3 = (bf16[1,192,896]{2,1,0:T(8,128)(2,1)}, bf16[1,192,896]{2,1,0:T(8,128)(2,1)}, u32[]{:S(2)}, u32[]{:S(2)}) collective-permute-start(bf16[1,192,896]{2,1,0:T(8,128)(2,1)} %fusion.24), channel_id=1, source_target_pairs={{0,16},{8,24},{16,0},{24,8},{1,17},{9,25},{17,1},{25,9},{2,18},{10... | collective-permute-start | bytes 1032200 | tf_op jit(solution)/shard_map/ppermute | solution.py:60
  76.1 14.9 %all-to-all-start.3 = ((bf16[8,24,896]{2,1,0:T(8,128)(2,1)}), bf16[8,24,896]{2,1,0:T(8,128)(2,1)S(1)}, u32[]{:S(2)}, u32[]{:S(2)}) async-start(bf16[8,24,896]{2,1,0:T(8,128)(2,1)} %bitcast.187), calls=%async_computation.3 | async-start | bytes 688128 | tf_op jit(solution)/shard_map/all_to_all | solution.py:98
  83.6 1.1 %copy-start.7 = (bf16[8,24,1]{2,1,0:T(8,128)(2,1)S(1)}, bf16[8,24,1]{2,1,0:T(8,128)(2,1)}, u32[]{:S(2)}) copy-start(bf16[8,24,1]{2,1,0:T(8,128)(2,1)} %concatenate.62) | copy-start | bytes 1156
  83.6 1.1 %copy-start.8 = (bf16[8,24,1]{2,1,0:T(8,128)(2,1)S(1)}, bf16[8,24,1]{2,1,0:T(8,128)(2,1)}, u32[]{:S(2)}) copy-start(bf16[8,24,1]{2,1,0:T(8,128)(2,1)} %concatenate.63) | copy-start | bytes 1156
  84.7 10.0 %copy-start.5 = (bf16[192,512,1]{1,0,2:T(8,128)(2,1)S(1)}, bf16[192,512,1]{1,0,2:T(8,128)(2,1)}, u32[]{:S(2)}) copy-start(bf16[192,512,1]{1,0,2:T(8,128)(2,1)} %copy-done.4) | copy-start | bytes 589828
  91.0 14.5 %all-to-all-start.2 = ((bf16[8,24,1024]{2,1,0:T(8,128)(2,1)}), bf16[8,24,1024]{2,1,0:T(8,128)(2,1)S(1)}, u32[]{:S(2)}, u32[]{:S(2)}) async-start(bf16[8,24,1024]{2,1,0:T(8,128)(2,1)} %maximum_maximum_fusion.1), calls=%async_computation.2 | async-start | bytes 786432 | tf_op jit(solution)/shard_map/all_to_all | solution.py:98
  100.7 5.2 %copy-start.9 = (f32[128,1]{0,1:T(1,128)S(1)}, f32[128,1]{0,1:T(1,128)}, u32[]{:S(2)}) copy-start(f32[128,1]{0,1:T(1,128)} %param.10) | copy-start | bytes 1540
